TPU v7x, 256 devices: a whole 4x4x8 slice. The times are simulated.
256 devices in a mesh: blk: 16 (over z, x_lo), inner: 16 (over y, x_hi, core).
Axes of the slice: x: 4 (x_hi: 2, x_lo: 2; x = x_hi * 2 + x_lo), y: 4, z: 8, core: 2. Of those that a mesh axis runs over, the one named last changes fastest.
Arguments:
- tokens: bfloat16 [32768, 4096], P(('blk', 'inner')), may hold values from -6 to 6
- expert_ids: int32 [32768, 8], P(('blk', 'inner')), may hold values from 0 to 127, all different within a row; in each aligned block of 128 rows (0 to 127, 128 to 255, ...) at most 12 rows name the same one
- route_weights: float32 [32768, 8], P(('blk', 'inner')), may hold values from 0.1 to 1
- w_in: bfloat16 [256, 4096, 768], P(('blk', 'inner')), may hold values from -0.09375 to 0.09375
- w_out: bfloat16 [256, 384, 4096], P(('blk', 'inner')), may hold values from -0.3125 to 0.3125
Outputs:
- moe_out: bfloat16 [32768, 4096], P(('blk', 'inner'))
Inputs may be any that keep to these rules, and one draw needn't show every extreme that they name: `expert_ids`: each row names 8 different experts; among the 128 rows of one device no expert is named more than 12 times, a bound that some block reaches.
All inputs are finite; a program needn't handle non-finite values.
Results may differ from a plain program's by a relative error of at most 0.0085.
Values may be sent and summed in bfloat16 or wider, within the bound.
No kernel may reach another device: no remote copies, remote signals or barrier semaphores. Data moves between devices by JAX's collectives and lax.ppermute only.
A program may use at most 128 MiB of HBM per device.

v0:
```python
import jax
import jax.numpy as jnp
from jax import lax
from jax.sharding import PartitionSpec as P

TOPK = 8
SPLIT = 2
STEPS = 3


def passed_along(value, axis, steps):
    count = lax.axis_size(axis)
    pairs = [(source, (source + steps) % count) for source in range(count)]
    return lax.ppermute(value, axis, pairs)


def expert_rows(arrived, w_in_now, w_out_now):
    hidden = w_out_now.shape[1]
    projected = jnp.einsum("jcd,de->jce", arrived, w_in_now[0], preferred_element_type=jnp.float32)
    activated = (jax.nn.silu(projected[..., :hidden]) * projected[..., hidden:]).astype(
        jnp.bfloat16
    )
    return jnp.einsum(
        "jce,ed->jcd", activated, w_out_now[0], preferred_element_type=jnp.float32
    ).astype(jnp.bfloat16)


def dispatch(tokens, expert_ids, route_weights, home_group, group_count, capacity):
    firsts = home_group * group_count + jnp.arange(group_count, dtype=jnp.int32)
    matches = expert_ids[:, :, None] == firsts[None, None, :]
    chosen = jnp.any(matches, axis=1).astype(jnp.int32)
    weighting = jnp.sum(jnp.where(matches, route_weights[:, :, None], 0.0), axis=1)
    position = jnp.cumsum(chosen, axis=0) - chosen
    slot_ids = jnp.arange(capacity, dtype=jnp.int32)
    one_hot = (
        (chosen.T[:, None, :] == 1) & (position.T[:, None, :] == slot_ids[None, :, None])
    ).astype(jnp.bfloat16)
    picked = jnp.einsum("qct,td->qcd", one_hot, tokens, preferred_element_type=jnp.float32).astype(
        jnp.bfloat16
    )
    outgoing = jnp.repeat(picked, SPLIT, axis=0)
    return (one_hot, weighting, outgoing)


def combine(one_hot, weighting, partials):
    group_count, capacity, tok_rows = one_hot.shape
    paired = partials.reshape(group_count, SPLIT, capacity, partials.shape[-1])
    gathered = jnp.einsum("qct,qkcd->qtd", one_hot, paired, preferred_element_type=jnp.float32)
    return jnp.sum(weighting.T[:, :, None] * gathered, axis=0)


def on_device(tokens, expert_ids, route_weights, w_in, w_out):
    inner_count = lax.axis_size("inner")
    blk_count = lax.axis_size("blk")
    group_index = lax.axis_index("blk")
    group_count = inner_count // SPLIT
    tok_rows = tokens.shape[0]
    experts_all = group_count * blk_count
    capacity = max(2, 3 * tok_rows * TOPK // (2 * experts_all))
    current = (w_in, w_out)
    result = jnp.zeros(tokens.shape, jnp.float32)
    for rotation in range(STEPS):
        home_group = jnp.mod(group_index - rotation, blk_count)
        one_hot, weighting, outgoing = dispatch(
            tokens, expert_ids, route_weights, home_group, group_count, capacity
        )
        if rotation > 0:
            current = passed_along((current[0], current[1]), "blk", 1)

        def apply_rows(arrived, weights_now=current):
            return expert_rows(arrived, weights_now[0], weights_now[1])

        def run_rows(arrived, apply_now=apply_rows):
            return lax.all_to_all(
                apply_now(arrived), "inner", split_axis=0, concat_axis=0, tiled=True
            )

        partials = run_rows(
            lax.all_to_all(outgoing, "inner", split_axis=0, concat_axis=0, tiled=True)
        )
        result = result + combine(one_hot, weighting, partials)
    return result.astype(jnp.bfloat16)


def solution(mesh):
    return jax.shard_map(
        on_device,
        mesh=mesh,
        in_specs=(
            P(("blk", "inner"), None),
            P(("blk", "inner"), None),
            P(("blk", "inner"), None),
            P(("blk", "inner"), None, None),
            P(("blk", "inner"), None, None),
        ),
        out_specs=P(("blk", "inner"), None),
        check_vma=False,
    )
```

profile of v0, /device:TPU:2, one launch (start us, length us, event | category | flops | bytes accessed | tf_op | source)
XLA Modules:
  0.0 620.7 jit_solution(4923664993203882777)
XLA Ops:
  0.0 1.9 collective-permute-start
  3.1 134.4 %collective-permute-done = bf16[1,4096,768]{2,1,0:T(8,128)(2,1)} collective-permute-done((bf16[1,4096,768]{2,1,0:T(8,128)(2,1)}, bf16[1,4096,768]{2,1,0:T(8,128)(2,1)}, u32[]{:S(2)}, u32[]{:S(2)}) %collective-permute-start) | collective-permute-done | bytes 6291488 | tf_op jit(solution)/shard_map/ppermute | solution.py:14
  137.6 2.8 collective-permute-start.2
  140.8 1.5 broadcast_in_dim.30
  142.3 6.5 %all-to-all-start.4 = ((bf16[16,12,4096]{2,1,0:T(8,128)(2,1)}), bf16[16,12,4096]{2,1,0:T(8,128)(2,1)}, u32[]{:S(2)}, u32[]{:S(2)}) async-start(bf16[16,12,4096]{2,1,0:T(8,128)(2,1)} %bitcast.22), calls=%async_computation.4 | async-start | bytes 4194304 | tf_op jit(solution)/shard_map/all_to_all | solution.py:79
  150.7 224.0 %all-to-all-done.4 = bf16[16,12,4096]{2,1,0:T(8,128)(2,1)} async-done(((bf16[16,12,4096]{2,1,0:T(8,128)(2,1)}), bf16[16,12,4096]{2,1,0:T(8,128)(2,1)}, u32[]{:S(2)}, u32[]{:S(2)}) %all-to-all-start.4) | async-done | bytes 1572896 | tf_op jit(solution)/shard_map/all_to_all | solution.py:79
  374.7 1.6 broadcast_in_dim.28
  376.3 4.4 all-to-all-start
  381.6 28.7 %all-to-all-done = bf16[16,12,4096]{2,1,0:T(8,128)(2,1)} async-done(((bf16[16,12,4096]{2,1,0:T(8,128)(2,1)}), bf16[16,12,4096]{2,1,0:T(8,128)(2,1)}, u32[]{:S(2)}, u32[]{:S(2)}) %all-to-all-start) | async-done | bytes 1572896 | tf_op jit(solution)/shard_map/all_to_all | solution.py:79
  410.3 1.6 broadcast_in_dim.29
  411.9 3.7 all-to-all-start.2
  415.6 5.3 fusion.4
  422.2 2.2 copy.41
  424.4 87.8 %all-to-all-done.2 = bf16[16,12,4096]{2,1,0:T(8,128)(2,1)S(1)} async-done(((bf16[16,12,4096]{2,1,0:T(8,128)(2,1)}), bf16[16,12,4096]{2,1,0:T(8,128)(2,1)S(1)}, u32[]{:S(2)}, u32[]{:S(2)}) %all-to-all-start.2) | async-done | bytes 1572896 | tf_op jit(solution)/shard_map/all_to_all | solution.py:79
  513.5 3.9 all-to-all-start.1
  517.4 5.2 fusion.2
  522.8 2.9 convolution_convert_fusion.1
  525.6 2.2 copy.48
  527.9 18.9 %all-to-all-done.1 = bf16[16,12,4096]{2,1,0:T(8,128)(2,1)S(1)} async-done(((bf16[16,12,4096]{2,1,0:T(8,128)(2,1)}), bf16[16,12,4096]{2,1,0:T(8,128)(2,1)S(1)}, u32[]{:S(2)}, u32[]{:S(2)}) %all-to-all-start.1) | async-done | bytes 1572896 | tf_op jit(solution)/shard_map/all_to_all | solution.py:74
  546.8 4.4 all-to-all-start.3
  551.2 5.2 fusion
  556.6 2.9 convolution_convert_fusion
  559.5 2.3 copy.55
  561.7 19.1 %all-to-all-done.3 = bf16[16,12,4096]{2,1,0:T(8,128)(2,1)} async-done(((bf16[16,12,4096]{2,1,0:T(8,128)(2,1)}), bf16[16,12,4096]{2,1,0:T(8,128)(2,1)}, u32[]{:S(2)}, u32[]{:S(2)}) %all-to-all-start.3) | async-done | bytes 1572896 | tf_op jit(solution)/shard_map/all_to_all | solution.py:74
  580.8 4.7 all-to-all-start.5
  586.0 2.4 multiply_reduce_fusion.2
  588.4 2.0 convert_reduce_fusion.1
  590.4 3.8 multiply_reduce_fusion.1
  594.1 20.7 %all-to-all-done.5 = bf16[16,12,4096]{2,1,0:T(8,128)(2,1)} async-done(((bf16[16,12,4096]{2,1,0:T(8,128)(2,1)}), bf16[16,12,4096]{2,1,0:T(8,128)(2,1)}, u32[]{:S(2)}, u32[]{:S(2)}) %all-to-all-start.5) | async-done | bytes 1572896 | tf_op jit(solution)/shard_map/all_to_all | solution.py:74
  614.8 2.0 convert_reduce_fusion
  616.8 2.4 multiply_reduce_fusion
  619.3 1.4 add_convert_fusion
  (49 shorter events, 7.7 us)
Async XLA Ops:
  0.0 140.4 %copy-start = (bf16[128,4096]{1,0:T(8,128)(2,1)S(1)}, bf16[128,4096]{1,0:T(8,128)(2,1)}, u32[]{:S(2)}) copy-start(bf16[128,4096]{1,0:T(8,128)(2,1)} %param.5) | copy-start | bytes 3145732
  0.0 137.6 %collective-permute-start = (bf16[1,4096,768]{2,1,0:T(8,128)(2,1)}, bf16[1,4096,768]{2,1,0:T(8,128)(2,1)}, u32[]{:S(2)}, u32[]{:S(2)}) collective-permute-start(bf16[1,4096,768]{2,1,0:T(8,128)(2,1)} %param.8), channel_id=1, source_target_pairs={{0,16},{16,32},{32,48},{48,64},{64,80},{80,96},{96,112},{112,128},... | collective-permute-start | bytes 18874376 | tf_op jit(solution)/shard_map/ppermute | solution.py:14
  137.6 413.6 %collective-permute-start.2 = (bf16[1,4096,768]{2,1,0:T(8,128)(2,1)}, bf16[1,4096,768]{2,1,0:T(8,128)(2,1)}, u32[]{:S(2)}, u32[]{:S(2)}) collective-permute-start(bf16[1,4096,768]{2,1,0:T(8,128)(2,1)} %collective-permute-done), channel_id=1, source_target_pairs={{0,16},{16,32},{32,48},{48,64},{64,80},{80,96},{96,112},{112,128},... | collective-permute-start | bytes 18874376 | tf_op jit(solution)/shard_map/ppermute | solution.py:14
  142.3 232.4 %all-to-all-start.4 = ((bf16[16,12,4096]{2,1,0:T(8,128)(2,1)}), bf16[16,12,4096]{2,1,0:T(8,128)(2,1)}, u32[]{:S(2)}, u32[]{:S(2)}) async-start(bf16[16,12,4096]{2,1,0:T(8,128)(2,1)} %bitcast.22), calls=%async_computation.4 | async-start | bytes 4194304 | tf_op jit(solution)/shard_map/all_to_all | solution.py:79
  148.8 272.1 %collective-permute-start.1 = (bf16[1,384,4096]{2,1,0:T(8,128)(2,1)}, bf16[1,384,4096]{2,1,0:T(8,128)(2,1)}, u32[]{:S(2)}, u32[]{:S(2)}) collective-permute-start(bf16[1,384,4096]{2,1,0:T(8,128)(2,1)} %param.9), channel_id=1, source_target_pairs={{0,16},{16,32},{32,48},{48,64},{64,80},{80,96},{96,112},{112,128},... | collective-permute-start | bytes 9437192 | tf_op jit(solution)/shard_map/ppermute | solution.py:14
  376.3 34.0 %all-to-all-start = ((bf16[16,12,4096]{2,1,0:T(8,128)(2,1)}), bf16[16,12,4096]{2,1,0:T(8,128)(2,1)}, u32[]{:S(2)}, u32[]{:S(2)}) async-start(bf16[16,12,4096]{2,1,0:T(8,128)(2,1)} %bitcast.4), calls=%async_computation | async-start | bytes 4194304 | tf_op jit(solution)/shard_map/all_to_all | solution.py:79
  411.9 100.3 %all-to-all-start.2 = ((bf16[16,12,4096]{2,1,0:T(8,128)(2,1)}), bf16[16,12,4096]{2,1,0:T(8,128)(2,1)S(1)}, u32[]{:S(2)}, u32[]{:S(2)}) async-start(bf16[16,12,4096]{2,1,0:T(8,128)(2,1)} %bitcast.13), calls=%async_computation.2 | async-start | bytes 4194304 | tf_op jit(solution)/shard_map/all_to_all | solution.py:79
  415.6 5.6 copy-start.2
  421.0 135.6 %collective-permute-start.3 = (bf16[1,384,4096]{2,1,0:T(8,128)(2,1)}, bf16[1,384,4096]{2,1,0:T(8,128)(2,1)}, u32[]{:S(2)}, u32[]{:S(2)}) collective-permute-start(bf16[1,384,4096]{2,1,0:T(8,128)(2,1)} %collective-permute-done.1), channel_id=1, source_target_pairs={{0,16},{16,32},{32,48},{48,64},{64,80},{80,96},{96,112},{112,128},... | collective-permute-start | bytes 9437192 | tf_op jit(solution)/shard_map/ppermute | solution.py:14
  512.2 1.3 copy-start.4
  513.5 33.3 %all-to-all-start.1 = ((bf16[16,12,4096]{2,1,0:T(8,128)(2,1)}), bf16[16,12,4096]{2,1,0:T(8,128)(2,1)S(1)}, u32[]{:S(2)}, u32[]{:S(2)}) async-start(bf16[16,12,4096]{2,1,0:T(8,128)(2,1)} %copy.41), calls=%async_computation.1 | async-start | bytes 4194304 | tf_op jit(solution)/shard_map/all_to_all | solution.py:74
  546.8 34.0 %all-to-all-start.3 = ((bf16[16,12,4096]{2,1,0:T(8,128)(2,1)}), bf16[16,12,4096]{2,1,0:T(8,128)(2,1)}, u32[]{:S(2)}, u32[]{:S(2)}) async-start(bf16[16,12,4096]{2,1,0:T(8,128)(2,1)} %copy.48), calls=%async_computation.3 | async-start | bytes 4194304 | tf_op jit(solution)/shard_map/all_to_all | solution.py:74
  561.7 23.8 %copy-start.5 = (s32[128,8]{0,1:T(8,128)S(1)}, s32[128,8]{0,1:T(8,128)}, u32[]{:S(2)}) copy-start(s32[128,8]{0,1:T(8,128)} %param.6) | copy-start | bytes 12292
  561.7 23.8 %copy-start.6 = (f32[128,8]{0,1:T(8,128)S(1)}, f32[128,8]{0,1:T(8,128)}, u32[]{:S(2)}) copy-start(f32[128,8]{0,1:T(8,128)} %param.7) | copy-start | bytes 12292
  580.8 34.0 %all-to-all-start.5 = ((bf16[16,12,4096]{2,1,0:T(8,128)(2,1)}), bf16[16,12,4096]{2,1,0:T(8,128)(2,1)}, u32[]{:S(2)}, u32[]{:S(2)}) async-start(bf16[16,12,4096]{2,1,0:T(8,128)(2,1)} %copy.55), calls=%async_computation.5 | async-start | bytes 4194304 | tf_op jit(solution)/shard_map/all_to_all | solution.py:74
  616.8 2.5 copy-start.3
  616.8 3.9 copy-start.1
where the time goes:
time: 621 us
  waiting for transfers between devices  534 us (86%)
  starting transfers between devices  33.3 us (5%)
  matrix products  32.4 us (5%)
  local copies, waits for them, and re-layouts  13.6 us (2%)
  other arithmetic  7.54 us (1%)
    all_to_all x3, waiting for transfers between devices, on_device(): lax.all_to_all(outgoing, 'inner', split_axis=0, concat_axis=0, tiled=True)  340 us
    ppermute x4, waiting for transfers between devices, passed_along(): return lax.ppermute(value, axis, pairs)  134 us
    all_to_all x3, waiting for transfers between devices, run_rows(): lax.all_to_all(apply_now(arrived), 'inner', split_axis=0, concat_axis=0,...  58.7 us
    dot_general x3, matrix products, expert_rows(): jnp.einsum('jcd,de->jce', arrived, w_in_now[0], preferred_element_type=jn...  15.8 us
    all_to_all x3, starting transfers between devices, on_device(): lax.all_to_all(outgoing, 'inner', split_axis=0, concat_axis=0, tiled=True)  14.6 us
    all_to_all x3, starting transfers between devices, run_rows(): lax.all_to_all(apply_now(arrived), 'inner', split_axis=0, concat_axis=0,...  13 us
  transfers between devices with their start and end apart: 10, of which 7 were waited for; matrix products, arithmetic and copies ran while one was open for 7% of the time, Pallas kernels for 0%

commit v1 on v0

v1 whole, which is shorter than its diff:
```python
import jax
import jax.numpy as jnp
from jax import lax
from jax.sharding import PartitionSpec as P

TOPK = 8
SPLIT = 2
STEPS = 3


def shifted(value, axis, steps):
    count = lax.axis_size(axis)
    pairs = [(source, (source + steps) % count) for source in range(count)]
    return lax.ppermute(value, axis, pairs)


def swapped_with_partner(value, axis):
    count = lax.axis_size(axis)
    pairs = [(source, source ^ 1) for source in range(count)]
    return lax.ppermute(value, axis, pairs)


def whole_expert(rows, w_in_a, w_out_a, w_in_b, w_out_b):
    hidden = w_out_a.shape[0]

    def one_half(w_in_now, w_out_now):
        projected = jnp.dot(rows, w_in_now, preferred_element_type=jnp.float32)
        activated = (jax.nn.silu(projected[:, :hidden]) * projected[:, hidden:]).astype(
            jnp.bfloat16
        )
        return jnp.dot(activated, w_out_now, preferred_element_type=jnp.float32)

    return (one_half(w_in_a, w_out_a) + one_half(w_in_b, w_out_b)).astype(jnp.bfloat16)


def on_device(tokens, expert_ids, route_weights, w_in, w_out):
    inner_count = lax.axis_size("inner")
    blk_count = lax.axis_size("blk")
    group_index = lax.axis_index("blk")
    group_count = inner_count // SPLIT
    tok_rows, width = tokens.shape
    experts_all = group_count * blk_count
    capacity = max(2, 3 * tok_rows * TOPK // (2 * experts_all))
    capacity = -(-capacity // SPLIT) * SPLIT
    half_cap = capacity // SPLIT

    w_in_other = swapped_with_partner(w_in, "inner")
    w_out_other = swapped_with_partner(w_out, "inner")

    homes = jnp.mod(group_index - jnp.arange(STEPS, dtype=jnp.int32), blk_count)
    targets = (
        homes[:, None] * group_count + jnp.arange(group_count, dtype=jnp.int32)[None, :]
    ).reshape(-1)
    matches = expert_ids[:, :, None] == targets[None, None, :]
    chosen = jnp.any(matches, axis=1).astype(jnp.int32)
    weighting = jnp.sum(jnp.where(matches, route_weights[:, :, None], 0.0), axis=1)
    position = jnp.cumsum(chosen, axis=0) - chosen
    slot_ids = jnp.arange(capacity, dtype=jnp.int32)
    one_hot = (chosen.T[:, None, :] == 1) & (position.T[:, None, :] == slot_ids[None, :, None])
    one_hot = one_hot.reshape(STEPS, group_count, SPLIT, half_cap, tok_rows).transpose(
        1, 2, 0, 3, 4
    )
    scale = jnp.where(
        one_hot,
        weighting.T.reshape(STEPS, group_count, 1, 1, tok_rows).transpose(1, 2, 0, 3, 4),
        0.0,
    )
    picked = jnp.einsum(
        "qcrht,td->qcrhd",
        one_hot.astype(jnp.bfloat16),
        tokens,
        preferred_element_type=jnp.float32,
    ).astype(jnp.bfloat16)
    outgoing = picked.reshape(inner_count, STEPS, half_cap, width)

    arrived = lax.all_to_all(outgoing, "inner", split_axis=0, concat_axis=0, tiled=True)
    parts = [arrived[:, 0]]
    for rotation in range(1, STEPS):
        parts.append(shifted(arrived[:, rotation], "blk", -rotation))

    results = []
    for rotation in range(STEPS):
        rows = parts[rotation].reshape(inner_count * half_cap, width)
        done = whole_expert(rows, w_in[0], w_out[0], w_in_other[0], w_out_other[0])
        done = done.reshape(inner_count, half_cap, width)
        if rotation > 0:
            done = shifted(done, "blk", rotation)
        results.append(done)
    returned = jnp.stack(results, axis=1)
    returned = lax.all_to_all(returned, "inner", split_axis=0, concat_axis=0, tiled=True)
    returned = returned.reshape(group_count, SPLIT, STEPS, half_cap, width)

    scale_hi = scale.astype(jnp.bfloat16)
    scale_lo = (scale - scale_hi.astype(jnp.float32)).astype(jnp.bfloat16)
    combined = jnp.einsum(
        "qcrht,qcrhd->td", scale_hi, returned, preferred_element_type=jnp.float32
    ) + jnp.einsum("qcrht,qcrhd->td", scale_lo, returned, preferred_element_type=jnp.float32)
    return combined.astype(jnp.bfloat16)


def solution(mesh):
    return jax.shard_map(
        on_device,
        mesh=mesh,
        in_specs=(
            P(("blk", "inner"), None),
            P(("blk", "inner"), None),
            P(("blk", "inner"), None),
            P(("blk", "inner"), None, None),
            P(("blk", "inner"), None, None),
        ),
        out_specs=P(("blk", "inner"), None),
        check_vma=False,
    )
```

time: 621 us -> 219 us (0.35)
  waiting for transfers between devices: 534 us -> 106 us
  local copies, waits for them, and re-layouts: 13.6 us -> 28.4 us
  matrix products: 32.4 us -> 45.3 us
    all_to_all x3 -> x1, waiting for transfers between devices: 340 us -> 40.3 us  [on_device(): lax.all_to_all(outgoing, 'inner', split_axis=0, concat_axis=0, tiled=True)]
    ppermute x4 -> x6, waiting for transfers between devices: 134 us -> 25.6 us  [the longest x4 25.6 us: shifted(): return lax.ppermute(value, axis, pairs)]
    ppermute x4 -> x6, starting transfers between devices: 5.75 us -> 24.8 us  [the longest x4 24.4 us: shifted(): return lax.ppermute(value, axis, pairs)]
    all_to_all x3 -> x1, waiting for transfers between devices: 58.7 us -> 40.5 us  [on_device(): lax.all_to_all(returned, 'inner', split_axis=0, concat_axis=0, tiled=True)]
    reshape x0 -> x7, local copies, waits for them, and re-layouts: none -> 13.2 us  [the longest x4 6.64 us: on_device(): done = done.reshape(inner_count, half_cap, width)]
    dot_general x12 -> x15, matrix products: 32.4 us -> 45.3 us  [the longest x6 21.1 us: one_half(): projected = jnp.dot(rows, w_in_now, preferred_element_type=jnp.float32)]
    all_to_all x3 -> x1, starting transfers between devices: 14.6 us -> 6.21 us  [on_device(): lax.all_to_all(outgoing, 'inner', split_axis=0, concat_axis=0, tiled=True)]
    all_to_all x3 -> x1, starting transfers between devices: 13 us -> 4.61 us  [on_device(): lax.all_to_all(returned, 'inner', split_axis=0, concat_axis=0, tiled=True)]
  transfers between devices with their start and end apart: 10 -> 8, of which waited for: 7 -> 6; matrix products, arithmetic and copies ran while one was open for 7% -> 24% of each run, Pallas kernels for 0% -> 0%
where the time goes in v1:
time: 219 us; the launch traced here: 218 us
  waiting for transfers between devices  106 us (48%)
  matrix products  45.3 us (21%)
  starting transfers between devices  35.6 us (16%)
  local copies, waits for them, and re-layouts  28.4 us (13%)
    all_to_all x1, waiting for transfers between devices, on_device(): lax.all_to_all(returned, 'inner', split_axis=0, concat_axis=0, tiled=True)  40.5 us
    all_to_all x1, waiting for transfers between devices, on_device(): lax.all_to_all(outgoing, 'inner', split_axis=0, concat_axis=0, tiled=True)  40.3 us
    ppermute x4, waiting for transfers between devices, shifted(): return lax.ppermute(value, axis, pairs)  25.6 us
    ppermute x4, starting transfers between devices, shifted(): return lax.ppermute(value, axis, pairs)  24.4 us
    dot_general x6, matrix products, one_half(): projected = jnp.dot(rows, w_in_now, preferred_element_type=jnp.float32)  21.1 us
    dot_general x6, matrix products, one_half(): return jnp.dot(activated, w_out_now, preferred_element_type=jnp.float32)  15 us
    ppermute x4, local copies, waits for them, and re-layouts, shifted(): return lax.ppermute(value, axis, pairs)  7.27 us
    reshape x4, local copies, waits for them, and re-layouts, on_device(): done = done.reshape(inner_count, half_cap, width)  6.64 us
  transfers between devices with their start and end apart: 8, of which 6 were waited for; matrix products, arithmetic and copies ran while one was open for 24% of the time, Pallas kernels for 0%

profile of v1, /device:TPU:2, one launch (start us, length us, event | category | flops | bytes accessed | tf_op | source)
XLA Modules:
  0.0 217.9 jit_solution(2505985838600838011)
XLA Ops:
  2.4 3.0 %copy.78 = bf16[8,2,3,6,4096]{4,3,2,1,0:T(8,128)(2,1)} copy(bf16[8,2,3,6,4096]{4,0,3,2,1:T(8,128)(2,1)S(1)} %convolution_convert_fusion) | data formatting | bytes 4718592 | tf_op jit(solution)/shard_map/reshape | solution.py:74
  5.4 6.2 %all-to-all-start = ((bf16[16,3,6,4096]{3,2,1,0:T(8,128)(2,1)}), bf16[16,3,6,4096]{3,2,1,0:T(8,128)(2,1)}, u32[]{:S(2)}, u32[]{:S(2)}) async-start(bf16[16,3,6,4096]{3,2,1,0:T(8,128)(2,1)} %bitcast.82), calls=%async_computation | async-start | bytes 6291456 | tf_op jit(solution)/shard_map/all_to_all | solution.py:76
  11.9 40.3 %all-to-all-done = bf16[16,3,6,4096]{3,2,1,0:T(8,128)(2,1)} async-done(((bf16[16,3,6,4096]{3,2,1,0:T(8,128)(2,1)}), bf16[16,3,6,4096]{3,2,1,0:T(8,128)(2,1)}, u32[]{:S(2)}, u32[]{:S(2)}) %all-to-all-start) | async-done | bytes 2359328 | tf_op jit(solution)/shard_map/all_to_all | solution.py:76
  52.2 2.1 fusion.65
  55.7 1.4 collective-permute-start.2
  57.8 6.1 %collective-permute-start.4 = (bf16[16,6,4096]{2,0,1:T(8,128)(2,1)S(1)}, bf16[16,6,4096]{2,0,1:T(8,128)(2,1)}, u32[]{:S(2)}, u32[]{:S(2)}) collective-permute-start(bf16[16,6,4096]{2,0,1:T(8,128)(2,1)S(1)} %copy.67), channel_id=1, source_target_pairs={{0,224},{16,240},{32,0},{48,16},{64,32},{80,48},{96,64},{112,80},{... | collective-permute-start | bytes 2359304 | tf_op jit(solution)/shard_map/ppermute | solution.py:14
  63.9 3.9 %fusion.10 = f32[96,768]{1,0:T(8,128)S(1)} fusion(bf16[96,4096]{1,0:T(8,128)(2,1)S(1)} %reshape_squeeze.3, bf16[1,4096,768]{2,1,0:T(8,128)(2,1)} %param.8), kind=kOutput, calls=%fused_computation.10 | convolution fusion | flops 603979776 | bytes 7372800 | tf_op jit(solution)/shard_map/dot_general | solution.py:27
  67.8 1.9 fusion.24
  69.7 7.6 %collective-permute-done.2 = bf16[16,6,4096]{2,0,1:T(8,128)(2,1)} collective-permute-done((bf16[16,6,4096]{2,0,1:T(8,128)(2,1)}, bf16[16,6,4096]{2,0,1:T(8,128)(2,1)}, u32[]{:S(2)}, u32[]{:S(2)}) %collective-permute-start.2) | collective-permute-done | bytes 786464 | tf_op jit(solution)/shard_map/ppermute | solution.py:14
  77.3 1.6 copy.64
  80.2 2.5 %copy.68 = bf16[16,6,4096]{2,1,0:T(8,128)(2,1)} copy(bf16[16,6,4096]{2,0,1:T(8,128)(2,1)} %collective-permute-done.4) | data formatting | bytes 1572864 | tf_op jit(solution)/shard_map/ppermute | solution.py:14
  82.7 2.4 %reshape.67 = bf16[96,4096]{1,0:T(8,128)(2,1)} reshape(bf16[16,6,4096]{2,1,0:T(8,128)(2,1)} %copy.68) | data formatting | bytes 1572864 | tf_op jit(solution)/shard_map/reshape | solution.py:83
  85.2 4.3 %fusion.8 = f32[96,768]{1,0:T(8,128)S(1)} fusion(bf16[96,4096]{1,0:T(8,128)(2,1)} %reshape.65, bf16[1,4096,768]{2,1,0:T(8,128)(2,1)} %param.8), kind=kOutput, calls=%fused_computation.8 | convolution fusion | flops 603979776 | bytes 7372800 | tf_op jit(solution)/shard_map/dot_general | solution.py:27
  89.5 2.7 %fusion.22 = f32[96,4096]{1,0:T(8,128)S(1)} fusion(bf16[1,384,4096]{2,1,0:T(8,128)(2,1)} %param.9, f32[96,768]{1,0:T(8,128)S(1)} %fusion.8), kind=kOutput, calls=%fused_computation.29 | convolution fusion | flops 302211072 | bytes 5013504 | tf_op jit(solution)/shard_map/dot_general | solution.py:31
  95.2 3.9 %fusion.2 = f32[96,768]{1,0:T(8,128)S(1)} fusion(bf16[96,4096]{1,0:T(8,128)(2,1)S(1)} %copy-done.6, bf16[1,4096,768]{2,1,0:T(8,128)(2,1)} %collective-permute-done), kind=kOutput, calls=%fused_computation.2 | convolution fusion | flops 603979776 | bytes 7372800 | tf_op jit(solution)/shard_map/dot_general | solution.py:27
  99.2 3.5 %fusion.15 = bf16[96,4096]{1,0:T(8,128)(2,1)} fusion(f32[96,4096]{1,0:T(8,128)S(1)} %fusion.22, bf16[1,384,4096]{2,1,0:T(8,128)(2,1)} %collective-permute-done.1, f32[96,768]{1,0:T(8,128)S(1)} %fusion.2), kind=kOutput, calls=%fused_computation.21 | convolution fusion | flops 302997504 | bytes 5799936 | tf_op jit(solution)/shard_map/dot_general | solution.py:31
  102.7 2.3 %reshape.66 = bf16[16,6,4096]{2,1,0:T(8,128)(2,1)} reshape(bf16[96,4096]{1,0:T(8,128)(2,1)} %fusion.15) | data formatting | bytes 1572864 | tf_op jit(solution)/shard_map/reshape | solution.py:85
  105.0 2.5 %copy.65 = bf16[16,6,4096]{2,0,1:T(8,128)(2,1)} copy(bf16[16,6,4096]{2,1,0:T(8,128)(2,1)} %reshape.66) | data formatting | bytes 1572864 | tf_op jit(solution)/shard_map/reshape | solution.py:85
  107.5 14.6 %collective-permute-start.3 = (bf16[16,6,4096]{2,0,1:T(8,128)(2,1)}, bf16[16,6,4096]{2,0,1:T(8,128)(2,1)}, u32[]{:S(2)}, u32[]{:S(2)}) collective-permute-start(bf16[16,6,4096]{2,0,1:T(8,128)(2,1)} %copy.65), channel_id=1, source_target_pairs={{0,16},{16,32},{32,48},{48,64},{64,80},{80,96},{96,112},{112,128},... | collective-permute-start | bytes 2359304 | tf_op jit(solution)/shard_map/ppermute | solution.py:14
  122.1 3.9 %fusion = f32[96,768]{1,0:T(8,128)S(1)} fusion(bf16[96,4096]{1,0:T(8,128)(2,1)S(1)} %copy-done.5, bf16[1,4096,768]{2,1,0:T(8,128)(2,1)} %collective-permute-done), kind=kOutput, calls=%fused_computation | convolution fusion | flops 603979776 | bytes 7372800 | tf_op jit(solution)/shard_map/dot_general | solution.py:27
  126.0 3.5 %fusion.16 = bf16[96,4096]{1,0:T(8,128)(2,1)} fusion(f32[96,4096]{1,0:T(8,128)S(1)} %fusion.20, bf16[1,384,4096]{2,1,0:T(8,128)(2,1)} %collective-permute-done.1, f32[96,768]{1,0:T(8,128)S(1)} %fusion), kind=kOutput, calls=%fused_computation.22 | convolution fusion | flops 302997504 | bytes 5799936 | tf_op jit(solution)/shard_map/dot_general | solution.py:31
  131.4 2.2 %collective-permute-start.5 = (bf16[16,6,4096]{2,0,1:T(8,128)(2,1)S(1)}, bf16[16,6,4096]{2,0,1:T(8,128)(2,1)}, u32[]{:S(2)}, u32[]{:S(2)}) collective-permute-start(bf16[16,6,4096]{2,0,1:T(8,128)(2,1)S(1)} %copy.69), channel_id=1, source_target_pairs={{0,32},{16,48},{32,64},{48,80},{64,96},{80,112},{96,128},{112,144}... | collective-permute-start | bytes 2359304 | tf_op jit(solution)/shard_map/ppermute | solution.py:14
  133.6 3.9 %fusion.4 = f32[96,768]{1,0:T(8,128)S(1)} fusion(bf16[96,4096]{1,0:T(8,128)(2,1)S(1)} %reshape_squeeze.3, bf16[1,4096,768]{2,1,0:T(8,128)(2,1)} %collective-permute-done), kind=kOutput, calls=%fused_computation.4 | convolution fusion | flops 603979776 | bytes 7372800 | tf_op jit(solution)/shard_map/dot_general | solution.py:27
  137.6 2.6 %fusion.14 = bf16[96,4096]{1,0:T(8,128)(2,1)S(1)} fusion(f32[96,4096]{1,0:T(8,128)S(1)} %copy-done.7, bf16[1,384,4096]{2,1,0:T(8,128)(2,1)} %collective-permute-done.1, f32[96,768]{1,0:T(8,128)S(1)} %fusion.4), kind=kOutput, calls=%fused_computation.20 | convolution fusion | flops 302997504 | bytes 5799936 | tf_op jit(solution)/shard_map/dot_general | solution.py:31
  140.6 1.6 copy.92
  142.2 17.7 %collective-permute-done.5 = bf16[16,6,4096]{2,0,1:T(8,128)(2,1)} collective-permute-done((bf16[16,6,4096]{2,0,1:T(8,128)(2,1)S(1)}, bf16[16,6,4096]{2,0,1:T(8,128)(2,1)}, u32[]{:S(2)}, u32[]{:S(2)}) %collective-permute-start.5) | collective-permute-done | bytes 786464 | tf_op jit(solution)/shard_map/ppermute | solution.py:14
  159.9 1.6 copy.91
  162.2 2.0 copy.71
  164.3 4.6 %all-to-all-start.1 = ((bf16[16,3,6,4096]{3,2,1,0:T(8,128)(2,1)}), bf16[16,3,6,4096]{3,2,1,0:T(8,128)(2,1)}, u32[]{:S(2)}, u32[]{:S(2)}) async-start(bf16[16,3,6,4096]{3,2,1,0:T(8,128)(2,1)} %copy.71), calls=%async_computation.1 | async-start | bytes 6291456 | tf_op jit(solution)/shard_map/all_to_all | solution.py:90
  169.0 40.5 %all-to-all-done.1 = bf16[16,3,6,4096]{3,2,1,0:T(8,128)(2,1)} async-done(((bf16[16,3,6,4096]{3,2,1,0:T(8,128)(2,1)}), bf16[16,3,6,4096]{3,2,1,0:T(8,128)(2,1)}, u32[]{:S(2)}, u32[]{:S(2)}) %all-to-all-start.1) | async-done | bytes 2359328 | tf_op jit(solution)/shard_map/all_to_all | solution.py:90
  209.5 3.8 %convolution_bitcast_fusion = f32[128,4096]{1,0:T(8,128)S(1)} fusion(bf16[8,2,3,6,4096]{4,3,2,1,0:T(8,128)(2,1)} %bitcast.21, f32[8,3,128]{2,0,1:T(8,128)S(1)} %bitcast.88, s32[2,6]{1,0:T(2,128)S(1)} %multiply_add_fusion, s32[8,3,128]{2,0,1:T(8,128)S(1)} %bitcast.86, pred[8,3,128]{2,0,1:T(8,128)(4,1)S(1)} %bitcast.91), kind=kOutput, calls=%fused_computation.13 | convolution fusion | flops 302247936 | bytes 4484144 | tf_op jit(solution)/shard_map/qcrht,qcrhd->td/dot_general | solution.py:97
  213.2 4.7 %fusion.13 = bf16[128,4096]{1,0:T(8,128)(2,1)} fusion(f32[128,4096]{1,0:T(8,128)S(1)} %convolution_bitcast_fusion, bf16[8,2,3,6,4096]{4,3,2,1,0:T(8,128)(2,1)} %bitcast.21, f32[8,3,128]{2,0,1:T(8,128)S(1)} %bitcast.89, s32[2,6]{1,0:T(2,128)S(1)} %multiply_add_fusion, s32[8,3,128]{2,0,1:T(8,128)S(1)} %bitcast.87, pred[8,3,128]{2,0,1:T(8,128)(4,1)S(1)} %bitcast.92), kind=kOutput, calls=%fused_computation.16 | convolution fusion | flops 303149056 | bytes 5532720 | tf_op jit(solution)/shard_map/qcrht,qcrhd->td/dot_general | solution.py:95
  (54 shorter events, 12.1 us)
Async XLA Ops:
  0.0 1.6 copy-start
  0.0 94.8 %collective-permute-start = (bf16[1,4096,768]{2,1,0:T(8,128)(2,1)}, bf16[1,4096,768]{2,1,0:T(8,128)(2,1)}, u32[]{:S(2)}, u32[]{:S(2)}) collective-permute-start(bf16[1,4096,768]{2,1,0:T(8,128)(2,1)} %param.8), channel_id=1, source_target_pairs={{0,1},{1,0},{2,3},{3,2},{4,5},{5,4},{6,7},{7,6},{8,9},{9,8},{10,11... | collective-permute-start | bytes 18874376 | tf_op jit(solution)/shard_map/ppermute | solution.py:20
  5.4 46.9 %all-to-all-start = ((bf16[16,3,6,4096]{3,2,1,0:T(8,128)(2,1)}), bf16[16,3,6,4096]{3,2,1,0:T(8,128)(2,1)}, u32[]{:S(2)}, u32[]{:S(2)}) async-start(bf16[16,3,6,4096]{3,2,1,0:T(8,128)(2,1)} %bitcast.82), calls=%async_computation | async-start | bytes 6291456 | tf_op jit(solution)/shard_map/all_to_all | solution.py:76
  11.6 87.6 %collective-permute-start.1 = (bf16[1,384,4096]{2,1,0:T(8,128)(2,1)}, bf16[1,384,4096]{2,1,0:T(8,128)(2,1)}, u32[]{:S(2)}, u32[]{:S(2)}) collective-permute-start(bf16[1,384,4096]{2,1,0:T(8,128)(2,1)} %param.9), channel_id=1, source_target_pairs={{0,1},{1,0},{2,3},{3,2},{4,5},{5,4},{6,7},{7,6},{8,9},{9,8},{10,11... | collective-permute-start | bytes 9437192 | tf_op jit(solution)/shard_map/ppermute | solution.py:20
  55.7 21.7 %collective-permute-start.2 = (bf16[16,6,4096]{2,0,1:T(8,128)(2,1)}, bf16[16,6,4096]{2,0,1:T(8,128)(2,1)}, u32[]{:S(2)}, u32[]{:S(2)}) collective-permute-start(bf16[16,6,4096]{2,0,1:T(8,128)(2,1)} %copy.63), channel_id=1, source_target_pairs={{0,240},{16,0},{32,16},{48,32},{64,48},{80,64},{96,80},{112,96},{1... | collective-permute-start | bytes 2359304 | tf_op jit(solution)/shard_map/ppermute | solution.py:14
  57.8 10.0 %copy-start.2 = (bf16[1,384,4096]{2,1,0:T(8,128)(2,1)S(1)}, bf16[1,384,4096]{2,1,0:T(8,128)(2,1)}, u32[]{:S(2)}) copy-start(bf16[1,384,4096]{2,1,0:T(8,128)(2,1)} %param.9) | copy-start | bytes 9437188
  57.8 22.4 %collective-permute-start.4 = (bf16[16,6,4096]{2,0,1:T(8,128)(2,1)S(1)}, bf16[16,6,4096]{2,0,1:T(8,128)(2,1)}, u32[]{:S(2)}, u32[]{:S(2)}) collective-permute-start(bf16[16,6,4096]{2,0,1:T(8,128)(2,1)S(1)} %copy.67), channel_id=1, source_target_pairs={{0,224},{16,240},{32,0},{48,16},{64,32},{80,48},{96,64},{112,80},{... | collective-permute-start | bytes 2359304 | tf_op jit(solution)/shard_map/ppermute | solution.py:14
  82.7 9.5 %slice-start = ((s8[6291456]{0:T(1024)(128)(4,1)}), s8[2097152]{0:T(1024)(128)(4,1)S(1)}, s32[]{:S(2)}) async-start(s8[6291456]{0:T(1024)(128)(4,1)} %bitcast.80), calls=%async_computation.2 | async-start | bytes 4194304
  85.2 7.0 %slice-start.1 = ((s8[6291456]{0:T(1024)(128)(4,1)}), s8[4194304]{0:T(1024)(128)(4,1)S(1)}, s32[]{:S(2)}) async-start(s8[6291456]{0:T(1024)(128)(4,1)} %bitcast.80), calls=%async_computation.3 | async-start | bytes 8388608
  89.5 2.7 %copy-start.4 = (bf16[96,4096]{1,0:T(8,128)(2,1)S(1)}, bf16[96,4096]{1,0:T(8,128)(2,1)}, u32[]{:S(2)}) copy-start(bf16[96,4096]{1,0:T(8,128)(2,1)} %reshape.67) | copy-start | bytes 2359300
  92.2 1.9 copy-start.3
  94.1 1.1 copy-start.6
  102.7 19.5 %copy-start.5 = (bf16[96,4096]{1,0:T(8,128)(2,1)S(1)}, bf16[96,4096]{1,0:T(8,128)(2,1)}, u32[]{:S(2)}) copy-start(bf16[96,4096]{1,0:T(8,128)(2,1)} %reshape.67) | copy-start | bytes 2359300
  107.5 33.1 %collective-permute-start.3 = (bf16[16,6,4096]{2,0,1:T(8,128)(2,1)}, bf16[16,6,4096]{2,0,1:T(8,128)(2,1)}, u32[]{:S(2)}, u32[]{:S(2)}) collective-permute-start(bf16[16,6,4096]{2,0,1:T(8,128)(2,1)} %copy.65), channel_id=1, source_target_pairs={{0,16},{16,32},{32,48},{48,64},{64,80},{80,96},{96,112},{112,128},... | collective-permute-start | bytes 2359304 | tf_op jit(solution)/shard_map/ppermute | solution.py:14
  131.4 6.1 %copy-start.7 = (f32[96,4096]{1,0:T(8,128)S(1)}, f32[96,4096]{1,0:T(8,128)}, u32[]{:S(2)}) copy-start(f32[96,4096]{1,0:T(8,128)} %fusion.24) | copy-start | bytes 4718596
  131.4 28.4 %collective-permute-start.5 = (bf16[16,6,4096]{2,0,1:T(8,128)(2,1)S(1)}, bf16[16,6,4096]{2,0,1:T(8,128)(2,1)}, u32[]{:S(2)}, u32[]{:S(2)}) collective-permute-start(bf16[16,6,4096]{2,0,1:T(8,128)(2,1)S(1)} %copy.69), channel_id=1, source_target_pairs={{0,32},{16,48},{32,64},{48,80},{64,96},{80,112},{96,128},{112,144}... | collective-permute-start | bytes 2359304 | tf_op jit(solution)/shard_map/ppermute | solution.py:14
  164.2 4.6 %copy-start.8 = (s32[128,8]{0,1:T(8,128)S(1)}, s32[128,8]{0,1:T(8,128)}, u32[]{:S(2)}) copy-start(s32[128,8]{0,1:T(8,128)} %param.6) | copy-start | bytes 12292
  164.3 4.6 %copy-start.9 = (f32[128,8]{0,1:T(8,128)S(1)}, f32[128,8]{0,1:T(8,128)}, u32[]{:S(2)}) copy-start(f32[128,8]{0,1:T(8,128)} %param.7) | copy-start | bytes 12292
  164.3 45.2 %all-to-all-start.1 = ((bf16[16,3,6,4096]{3,2,1,0:T(8,128)(2,1)}), bf16[16,3,6,4096]{3,2,1,0:T(8,128)(2,1)}, u32[]{:S(2)}, u32[]{:S(2)}) async-start(bf16[16,3,6,4096]{3,2,1,0:T(8,128)(2,1)} %copy.71), calls=%async_computation.1 | async-start | bytes 6291456 | tf_op jit(solution)/shard_map/all_to_all | solution.py:90
  209.5 8.5 %copy-start.1 = (bf16[128,4096]{1,0:T(8,128)(2,1)S(1)}, bf16[128,4096]{1,0:T(8,128)(2,1)}, u32[]{:S(2)}) copy-start(bf16[128,4096]{1,0:T(8,128)(2,1)} %param.5) | copy-start | bytes 3145732

commit v2 on v1

--- a/solution.py
+++ b/solution.py
@@ -57,44 +57,42 @@
     position = jnp.cumsum(chosen, axis=0) - chosen
     slot_ids = jnp.arange(capacity, dtype=jnp.int32)
     one_hot = (chosen.T[:, None, :] == 1) & (position.T[:, None, :] == slot_ids[None, :, None])
-    one_hot = one_hot.reshape(STEPS, group_count, SPLIT, half_cap, tok_rows).transpose(
-        1, 2, 0, 3, 4
+    one_hot = one_hot.reshape(STEPS, group_count, SPLIT, half_cap, tok_rows)
+    scale = jnp.where(
+        one_hot, weighting.T.reshape(STEPS, group_count, 1, 1, tok_rows), 0.0
     )
-    scale = jnp.where(
-        one_hot,
-        weighting.T.reshape(STEPS, group_count, 1, 1, tok_rows).transpose(1, 2, 0, 3, 4),
-        0.0,
-    )
+    scale_hi = scale.astype(jnp.bfloat16)
+    scale_lo = (scale - scale_hi.astype(jnp.float32)).astype(jnp.bfloat16)
     picked = jnp.einsum(
-        "qcrht,td->qcrhd",
+        "rqcht,td->rqchd",
         one_hot.astype(jnp.bfloat16),
         tokens,
         preferred_element_type=jnp.float32,
     ).astype(jnp.bfloat16)
-    outgoing = picked.reshape(inner_count, STEPS, half_cap, width)
 
-    arrived = lax.all_to_all(outgoing, "inner", split_axis=0, concat_axis=0, tiled=True)
-    parts = [arrived[:, 0]]
-    for rotation in range(1, STEPS):
-        parts.append(shifted(arrived[:, rotation], "blk", -rotation))
+    arrived = [None] * STEPS
+    for rotation in reversed(range(STEPS)):
+        outgoing = picked[rotation].reshape(inner_count, half_cap, width)
+        here = lax.all_to_all(outgoing, "inner", split_axis=0, concat_axis=0, tiled=True)
+        if rotation > 0:
+            here = shifted(here, "blk", -rotation)
+        arrived[rotation] = here
 
-    results = []
+    combined = jnp.zeros((tok_rows, width), jnp.float32)
     for rotation in range(STEPS):
-        rows = parts[rotation].reshape(inner_count * half_cap, width)
+        rows = arrived[rotation].reshape(inner_count * half_cap, width)
         done = whole_expert(rows, w_in[0], w_out[0], w_in_other[0], w_out_other[0])
         done = done.reshape(inner_count, half_cap, width)
         if rotation > 0:
             done = shifted(done, "blk", rotation)
-        results.append(done)
-    returned = jnp.stack(results, axis=1)
-    returned = lax.all_to_all(returned, "inner", split_axis=0, concat_axis=0, tiled=True)
-    returned = returned.reshape(group_count, SPLIT, STEPS, half_cap, width)
-
-    scale_hi = scale.astype(jnp.bfloat16)
-    scale_lo = (scale - scale_hi.astype(jnp.float32)).astype(jnp.bfloat16)
-    combined = jnp.einsum(
-        "qcrht,qcrhd->td", scale_hi, returned, preferred_element_type=jnp.float32
-    ) + jnp.einsum("qcrht,qcrhd->td", scale_lo, returned, preferred_element_type=jnp.float32)
+        back = lax.all_to_all(done, "inner", split_axis=0, concat_axis=0, tiled=True)
+        back = back.reshape(group_count, SPLIT, half_cap, width)
+        combined = combined + jnp.einsum(
+            "qcht,qchd->td", scale_hi[rotation], back, preferred_element_type=jnp.float32
+        )
+        combined = combined + jnp.einsum(
+            "qcht,qchd->td", scale_lo[rotation], back, preferred_element_type=jnp.float32
+        )
     return combined.astype(jnp.bfloat16)
 
 

time: 219 us -> 220 us (level)
  the two profiles are of different devices: /device:TPU:2 before, /device:TPU:1 now
where the time goes in v2:
time: 220 us; the launch traced here: 219 us
  waiting for transfers between devices  95.1 us (43%)
  matrix products  50.9 us (23%)
  starting transfers between devices  43.4 us (20%)
  local copies, waits for them, and re-layouts  28.2 us (13%)
    all_to_all x3, waiting for transfers between devices, on_device(): lax.all_to_all(outgoing, 'inner', split_axis=0, concat_axis=0, tiled=True)  56.4 us
    all_to_all x3, waiting for transfers between devices, on_device(): lax.all_to_all(done, 'inner', split_axis=0, concat_axis=0, tiled=True)  24.7 us
    dot_general x6, matrix products, one_half(): projected = jnp.dot(rows, w_in_now, preferred_element_type=jnp.float32)  21.5 us
    all_to_all x3, starting transfers between devices, on_device(): lax.all_to_all(done, 'inner', split_axis=0, concat_axis=0, tiled=True)  19.3 us
    dot_general x6, matrix products, one_half(): return jnp.dot(activated, w_out_now, preferred_element_type=jnp.float32)  15.6 us
    all_to_all x3, starting transfers between devices, on_device(): lax.all_to_all(outgoing, 'inner', split_axis=0, concat_axis=0, tiled=True)  14.1 us
    ppermute x4, waiting for transfers between devices, shifted(): return lax.ppermute(value, axis, pairs)  14 us
    ppermute x4, local copies, waits for them, and re-layouts, shifted(): return lax.ppermute(value, axis, pairs)  9.27 us
  transfers between devices with their start and end apart: 12, of which 6 were waited for; matrix products, arithmetic and copies ran while one was open for 31% of the time, Pallas kernels for 0%

profile of v2, /device:TPU:1, one launch (start us, length us, event | category | flops | bytes accessed | tf_op | source)
XLA Modules:
  0.0 219.3 jit_solution(1230998513859788319)
XLA Ops:
  0.0 3.2 %collective-permute-start = (bf16[1,4096,768]{2,1,0:T(8,128)(2,1)}, bf16[1,4096,768]{2,1,0:T(8,128)(2,1)}, u32[]{:S(2)}, u32[]{:S(2)}) collective-permute-start(bf16[1,4096,768]{2,1,0:T(8,128)(2,1)} %param.8), channel_id=1, source_target_pairs={{0,1},{1,0},{2,3},{3,2},{4,5},{5,4},{6,7},{7,6},{8,9},{9,8},{10,11... | collective-permute-start | bytes 18874376 | tf_op jit(solution)/shard_map/ppermute | solution.py:20
  7.1 5.3 %all-to-all-start.2 = ((bf16[16,6,4096]{2,1,0:T(8,128)(2,1)}), bf16[16,6,4096]{2,1,0:T(8,128)(2,1)S(1)}, u32[]{:S(2)}, u32[]{:S(2)}) async-start(bf16[16,6,4096]{2,1,0:T(8,128)(2,1)} %bitcast.21), calls=%async_computation.2 | async-start | bytes 2097152 | tf_op jit(solution)/shard_map/all_to_all | solution.py:76
  13.8 15.8 %all-to-all-done.2 = bf16[16,6,4096]{2,1,0:T(8,128)(2,1)S(1)} async-done(((bf16[16,6,4096]{2,1,0:T(8,128)(2,1)}), bf16[16,6,4096]{2,1,0:T(8,128)(2,1)S(1)}, u32[]{:S(2)}, u32[]{:S(2)}) %all-to-all-start.2) | async-done | bytes 786464 | tf_op jit(solution)/shard_map/all_to_all | solution.py:76
  29.6 4.4 %all-to-all-start.4 = ((bf16[16,6,4096]{2,1,0:T(8,128)(2,1)}), bf16[16,6,4096]{2,1,0:T(8,128)(2,1)S(1)}, u32[]{:S(2)}, u32[]{:S(2)}) async-start(bf16[16,6,4096]{2,1,0:T(8,128)(2,1)} %bitcast.29), calls=%async_computation.4 | async-start | bytes 2097152 | tf_op jit(solution)/shard_map/all_to_all | solution.py:76
  35.5 15.8 %all-to-all-done.4 = bf16[16,6,4096]{2,1,0:T(8,128)(2,1)S(1)} async-done(((bf16[16,6,4096]{2,1,0:T(8,128)(2,1)}), bf16[16,6,4096]{2,1,0:T(8,128)(2,1)S(1)}, u32[]{:S(2)}, u32[]{:S(2)}) %all-to-all-start.4) | async-done | bytes 786464 | tf_op jit(solution)/shard_map/all_to_all | solution.py:76
  51.3 4.4 %all-to-all-start = ((bf16[16,6,4096]{2,1,0:T(8,128)(2,1)}), bf16[16,6,4096]{2,1,0:T(8,128)(2,1)S(1)}, u32[]{:S(2)}, u32[]{:S(2)}) async-start(bf16[16,6,4096]{2,1,0:T(8,128)(2,1)} %bitcast.9), calls=%async_computation | async-start | bytes 2097152 | tf_op jit(solution)/shard_map/all_to_all | solution.py:76
  57.3 5.7 %collective-permute-start.2 = (bf16[16,6,4096]{2,0,1:T(8,128)(2,1)}, bf16[16,6,4096]{2,0,1:T(8,128)(2,1)}, u32[]{:S(2)}, u32[]{:S(2)}) collective-permute-start(bf16[16,6,4096]{2,0,1:T(8,128)(2,1)} %copy.85), channel_id=1, source_target_pairs={{0,240},{16,0},{32,16},{48,32},{64,48},{80,64},{96,80},{112,96},{1... | collective-permute-start | bytes 2359304 | tf_op jit(solution)/shard_map/ppermute | solution.py:14
  65.0 24.8 %all-to-all-done = bf16[16,6,4096]{2,1,0:T(8,128)(2,1)S(1)} async-done(((bf16[16,6,4096]{2,1,0:T(8,128)(2,1)}), bf16[16,6,4096]{2,1,0:T(8,128)(2,1)S(1)}, u32[]{:S(2)}, u32[]{:S(2)}) %all-to-all-start) | async-done | bytes 786464 | tf_op jit(solution)/shard_map/all_to_all | solution.py:76
  90.1 4.2 %fusion.10 = f32[96,768]{1,0:T(8,128)S(1)} fusion(bf16[96,4096]{1,0:T(8,128)(2,1)S(1)} %reshape.71, bf16[1,4096,768]{2,1,0:T(8,128)(2,1)} %param.8), kind=kOutput, calls=%fused_computation.10 | convolution fusion | flops 603979776 | bytes 7372800 | tf_op jit(solution)/shard_map/dot_general | solution.py:27
  98.1 2.5 %copy.95 = bf16[16,6,4096]{2,1,0:T(8,128)(2,1)} copy(bf16[16,6,4096]{2,0,1:T(8,128)(2,1)} %collective-permute-done.4) | data formatting | bytes 1572864 | tf_op jit(solution)/shard_map/ppermute | solution.py:14
  100.7 2.4 %reshape.77 = bf16[96,4096]{1,0:T(8,128)(2,1)} reshape(bf16[16,6,4096]{2,1,0:T(8,128)(2,1)} %copy.95) | data formatting | bytes 1572864 | tf_op jit(solution)/shard_map/reshape | solution.py:83
  103.0 4.1 %fusion.8 = f32[96,768]{1,0:T(8,128)S(1)} fusion(bf16[96,4096]{1,0:T(8,128)(2,1)S(1)} %reshape.74, bf16[1,4096,768]{2,1,0:T(8,128)(2,1)} %param.8), kind=kOutput, calls=%fused_computation.8 | convolution fusion | flops 603979776 | bytes 7372800 | tf_op jit(solution)/shard_map/dot_general | solution.py:27
  107.1 3.9 %fusion.26 = f32[96,4096]{1,0:T(8,128)} fusion(bf16[1,384,4096]{2,1,0:T(8,128)(2,1)} %param.9, f32[96,768]{1,0:T(8,128)S(1)} %fusion.8), kind=kOutput, calls=%fused_computation.36 | convolution fusion | flops 302211072 | bytes 5013504 | tf_op jit(solution)/shard_map/dot_general | solution.py:31
  114.8 4.0 %fusion.4 = f32[96,768]{1,0:T(8,128)S(1)} fusion(bf16[96,4096]{1,0:T(8,128)(2,1)S(1)} %copy-done.6, bf16[1,4096,768]{2,1,0:T(8,128)(2,1)} %collective-permute-done), kind=kOutput, calls=%fused_computation.4 | convolution fusion | flops 603979776 | bytes 7372800 | tf_op jit(solution)/shard_map/dot_general | solution.py:27
  118.8 2.6 %fusion.18 = bf16[96,4096]{1,0:T(8,128)(2,1)S(1)} fusion(f32[96,4096]{1,0:T(8,128)S(1)} %copy-done.14, bf16[1,384,4096]{2,1,0:T(8,128)(2,1)} %collective-permute-done.1, f32[96,768]{1,0:T(8,128)S(1)} %fusion.4), kind=kOutput, calls=%fused_computation.28 | convolution fusion | flops 302997504 | bytes 5799936 | tf_op jit(solution)/shard_map/dot_general | solution.py:31
  122.7 7.4 %all-to-all-start.1 = ((bf16[16,6,4096]{2,1,0:T(8,128)(2,1)}), bf16[16,6,4096]{2,1,0:T(8,128)(2,1)S(1)}, u32[]{:S(2)}, u32[]{:S(2)}) async-start(bf16[16,6,4096]{2,1,0:T(8,128)(2,1)} %reshape.72), calls=%async_computation.1 | async-start | bytes 2097152 | tf_op jit(solution)/shard_map/all_to_all | solution.py:88
  130.2 4.0 %fusion = f32[96,768]{1,0:T(8,128)S(1)} fusion(bf16[96,4096]{1,0:T(8,128)(2,1)S(1)} %copy-done.8, bf16[1,4096,768]{2,1,0:T(8,128)(2,1)} %collective-permute-done), kind=kOutput, calls=%fused_computation | convolution fusion | flops 603979776 | bytes 7372800 | tf_op jit(solution)/shard_map/dot_general | solution.py:27
  134.2 2.6 %fusion.20 = bf16[96,4096]{1,0:T(8,128)(2,1)S(1)} fusion(f32[96,4096]{1,0:T(8,128)S(1)} %copy-done.15, bf16[1,384,4096]{2,1,0:T(8,128)(2,1)} %collective-permute-done.1, f32[96,768]{1,0:T(8,128)S(1)} %fusion), kind=kOutput, calls=%fused_computation.30 | convolution fusion | flops 302997504 | bytes 5799936 | tf_op jit(solution)/shard_map/dot_general | solution.py:31
  138.1 2.6 %copy.96 = bf16[16,6,4096]{2,0,1:T(8,128)(2,1)} copy(bf16[16,6,4096]{2,1,0:T(8,128)(2,1)} %reshape.78) | data formatting | bytes 1572864 | tf_op jit(solution)/shard_map/reshape | solution.py:85
  140.7 4.0 %fusion.2 = f32[96,768]{1,0:T(8,128)S(1)} fusion(bf16[96,4096]{1,0:T(8,128)(2,1)S(1)} %reshape.74, bf16[1,4096,768]{2,1,0:T(8,128)(2,1)} %collective-permute-done), kind=kOutput, calls=%fused_computation.2 | convolution fusion | flops 603979776 | bytes 7372800 | tf_op jit(solution)/shard_map/dot_general | solution.py:27
  144.7 2.6 %fusion.19 = bf16[96,4096]{1,0:T(8,128)(2,1)S(1)} fusion(f32[96,4096]{1,0:T(8,128)S(1)} %copy-done.13, bf16[1,384,4096]{2,1,0:T(8,128)(2,1)} %collective-permute-done.1, f32[96,768]{1,0:T(8,128)S(1)} %fusion.2), kind=kOutput, calls=%fused_computation.29 | convolution fusion | flops 302997504 | bytes 5799936 | tf_op jit(solution)/shard_map/dot_general | solution.py:31
  148.2 14.0 %collective-permute-done.5 = bf16[16,6,4096]{2,0,1:T(8,128)(2,1)} collective-permute-done((bf16[16,6,4096]{2,0,1:T(8,128)(2,1)}, bf16[16,6,4096]{2,0,1:T(8,128)(2,1)}, u32[]{:S(2)}, u32[]{:S(2)}) %collective-permute-start.5) | collective-permute-done | bytes 786464 | tf_op jit(solution)/shard_map/ppermute | solution.py:14
  162.2 2.5 %copy.97 = bf16[16,6,4096]{2,1,0:T(8,128)(2,1)} copy(bf16[16,6,4096]{2,0,1:T(8,128)(2,1)} %collective-permute-done.5) | data formatting | bytes 1572864 | tf_op jit(solution)/shard_map/ppermute | solution.py:14
  164.8 7.5 %all-to-all-start.5 = ((bf16[16,6,4096]{2,1,0:T(8,128)(2,1)}), bf16[16,6,4096]{2,1,0:T(8,128)(2,1)S(1)}, u32[]{:S(2)}, u32[]{:S(2)}) async-start(bf16[16,6,4096]{2,1,0:T(8,128)(2,1)} %copy.97), calls=%async_computation.5 | async-start | bytes 2097152 | tf_op jit(solution)/shard_map/all_to_all | solution.py:88
  172.6 2.6 %copy.88 = bf16[16,6,4096]{2,1,0:T(8,128)(2,1)} copy(bf16[16,6,4096]{2,0,1:T(8,128)(2,1)} %collective-permute-done.3) | data formatting | bytes 1572864 | tf_op jit(solution)/shard_map/ppermute | solution.py:14
  175.2 14.3 %all-to-all-done.5 = bf16[16,6,4096]{2,1,0:T(8,128)(2,1)S(1)} async-done(((bf16[16,6,4096]{2,1,0:T(8,128)(2,1)}), bf16[16,6,4096]{2,1,0:T(8,128)(2,1)S(1)}, u32[]{:S(2)}, u32[]{:S(2)}) %all-to-all-start.5) | async-done | bytes 786464 | tf_op jit(solution)/shard_map/all_to_all | solution.py:88
  190.5 4.4 %all-to-all-start.3 = ((bf16[16,6,4096]{2,1,0:T(8,128)(2,1)}), bf16[16,6,4096]{2,1,0:T(8,128)(2,1)S(1)}, u32[]{:S(2)}, u32[]{:S(2)}) async-start(bf16[16,6,4096]{2,1,0:T(8,128)(2,1)} %copy.88), calls=%async_computation.3 | async-start | bytes 2097152 | tf_op jit(solution)/shard_map/all_to_all | solution.py:88
  195.6 2.1 fusion.12
  199.7 2.1 convolution_bitcast_fusion
  201.7 10.4 %all-to-all-done.3 = bf16[16,6,4096]{2,1,0:T(8,128)(2,1)S(1)} async-done(((bf16[16,6,4096]{2,1,0:T(8,128)(2,1)}), bf16[16,6,4096]{2,1,0:T(8,128)(2,1)S(1)}, u32[]{:S(2)}, u32[]{:S(2)}) %all-to-all-start.3) | async-done | bytes 786464 | tf_op jit(solution)/shard_map/all_to_all | solution.py:88
  213.2 2.1 convolution_bitcast_fusion.2
  215.2 4.0 %fusion.17 = bf16[128,4096]{1,0:T(8,128)(2,1)} fusion(f32[128,4096]{1,0:T(8,128)} %convolution_bitcast_fusion, f32[128,4096]{1,0:T(8,128)S(1)} %copy-done.4, f32[128,4096]{1,0:T(8,128)S(1)} %convolution_bitcast_fusion.2, f32[128,4096]{1,0:T(8,128)S(1)} %fusion.12, bf16[8,2,6,4096]{3,2,1,0:T(8,128)(2,1)} %bitcast.113, ...), kind=kOutput, calls=%fused_computation.24 | convolution fusion | flops 103284736 | bytes 10248192 | tf_op jit(solution)/shard_map/qcht,qchd->td/dot_general | solution.py:90
  (84 shorter events, 26.5 us)
Async XLA Ops:
  0.0 4.7 %copy-start = (bf16[128,4096]{1,0:T(8,128)(2,1)S(1)}, bf16[128,4096]{1,0:T(8,128)(2,1)}, u32[]{:S(2)}) copy-start(bf16[128,4096]{1,0:T(8,128)(2,1)} %param.5) | copy-start | bytes 3145732
  0.0 114.8 %collective-permute-start = (bf16[1,4096,768]{2,1,0:T(8,128)(2,1)}, bf16[1,4096,768]{2,1,0:T(8,128)(2,1)}, u32[]{:S(2)}, u32[]{:S(2)}) collective-permute-start(bf16[1,4096,768]{2,1,0:T(8,128)(2,1)} %param.8), channel_id=1, source_target_pairs={{0,1},{1,0},{2,3},{3,2},{4,5},{5,4},{6,7},{7,6},{8,9},{9,8},{10,11... | collective-permute-start | bytes 18874376 | tf_op jit(solution)/shard_map/ppermute | solution.py:20
  7.1 22.6 %all-to-all-start.2 = ((bf16[16,6,4096]{2,1,0:T(8,128)(2,1)}), bf16[16,6,4096]{2,1,0:T(8,128)(2,1)S(1)}, u32[]{:S(2)}, u32[]{:S(2)}) async-start(bf16[16,6,4096]{2,1,0:T(8,128)(2,1)} %bitcast.21), calls=%async_computation.2 | async-start | bytes 2097152 | tf_op jit(solution)/shard_map/all_to_all | solution.py:76
  29.6 21.6 %all-to-all-start.4 = ((bf16[16,6,4096]{2,1,0:T(8,128)(2,1)}), bf16[16,6,4096]{2,1,0:T(8,128)(2,1)S(1)}, u32[]{:S(2)}, u32[]{:S(2)}) async-start(bf16[16,6,4096]{2,1,0:T(8,128)(2,1)} %bitcast.29), calls=%async_computation.4 | async-start | bytes 2097152 | tf_op jit(solution)/shard_map/all_to_all | solution.py:76
  51.3 38.5 %all-to-all-start = ((bf16[16,6,4096]{2,1,0:T(8,128)(2,1)}), bf16[16,6,4096]{2,1,0:T(8,128)(2,1)S(1)}, u32[]{:S(2)}, u32[]{:S(2)}) async-start(bf16[16,6,4096]{2,1,0:T(8,128)(2,1)} %bitcast.9), calls=%async_computation | async-start | bytes 2097152 | tf_op jit(solution)/shard_map/all_to_all | solution.py:76
  55.6 63.2 %collective-permute-start.1 = (bf16[1,384,4096]{2,1,0:T(8,128)(2,1)}, bf16[1,384,4096]{2,1,0:T(8,128)(2,1)}, u32[]{:S(2)}, u32[]{:S(2)}) collective-permute-start(bf16[1,384,4096]{2,1,0:T(8,128)(2,1)} %param.9), channel_id=1, source_target_pairs={{0,1},{1,0},{2,3},{3,2},{4,5},{5,4},{6,7},{7,6},{8,9},{9,8},{10,11... | collective-permute-start | bytes 9437192 | tf_op jit(solution)/shard_map/ppermute | solution.py:20
  57.3 39.0 %collective-permute-start.2 = (bf16[16,6,4096]{2,0,1:T(8,128)(2,1)}, bf16[16,6,4096]{2,0,1:T(8,128)(2,1)}, u32[]{:S(2)}, u32[]{:S(2)}) collective-permute-start(bf16[16,6,4096]{2,0,1:T(8,128)(2,1)} %copy.85), channel_id=1, source_target_pairs={{0,240},{16,0},{32,16},{48,32},{64,48},{80,64},{96,80},{112,96},{1... | collective-permute-start | bytes 2359304 | tf_op jit(solution)/shard_map/ppermute | solution.py:14
  64.3 33.8 %collective-permute-start.4 = (bf16[16,6,4096]{2,0,1:T(8,128)(2,1)}, bf16[16,6,4096]{2,0,1:T(8,128)(2,1)}, u32[]{:S(2)}, u32[]{:S(2)}) collective-permute-start(bf16[16,6,4096]{2,0,1:T(8,128)(2,1)} %copy.94), channel_id=1, source_target_pairs={{0,224},{16,240},{32,0},{48,16},{64,32},{80,48},{96,64},{112,80},{... | collective-permute-start | bytes 2359304 | tf_op jit(solution)/shard_map/ppermute | solution.py:14
  90.1 4.3 %copy-start.5 = (bf16[96,4096]{1,0:T(8,128)(2,1)}, bf16[96,4096]{1,0:T(8,128)(2,1)S(1)}, u32[]{:S(2)}) copy-start(bf16[96,4096]{1,0:T(8,128)(2,1)S(1)} %reshape.71) | copy-start | bytes 2359300
  90.1 4.3 %copy-start.2 = (bf16[1,384,4096]{2,1,0:T(8,128)(2,1)S(1)}, bf16[1,384,4096]{2,1,0:T(8,128)(2,1)}, u32[]{:S(2)}) copy-start(bf16[1,384,4096]{2,1,0:T(8,128)(2,1)} %param.9) | copy-start | bytes 9437188
  100.7 10.3 %slice-start = ((s8[6291456]{0:T(1024)(128)(4,1)}), s8[2097152]{0:T(1024)(128)(4,1)S(1)}, s32[]{:S(2)}) async-start(s8[6291456]{0:T(1024)(128)(4,1)} %bitcast.108), calls=%async_computation.6 | async-start | bytes 4194304
  103.0 7.9 %slice-start.1 = ((s8[6291456]{0:T(1024)(128)(4,1)}), s8[4194304]{0:T(1024)(128)(4,1)S(1)}, s32[]{:S(2)}) async-start(s8[6291456]{0:T(1024)(128)(4,1)} %bitcast.108), calls=%async_computation.7 | async-start | bytes 8388608
  107.1 3.9 %copy-start.7 = (bf16[96,4096]{1,0:T(8,128)(2,1)S(1)}, bf16[96,4096]{1,0:T(8,128)(2,1)}, u32[]{:S(2)}) copy-start(bf16[96,4096]{1,0:T(8,128)(2,1)} %reshape.77) | copy-start | bytes 2359300
  111.0 1.9 copy-start.3
  112.9 1.9 copy-start.6
  114.8 4.1 %copy-start.14 = (f32[96,4096]{1,0:T(8,128)S(1)}, f32[96,4096]{1,0:T(8,128)}, u32[]{:S(2)}) copy-start(f32[96,4096]{1,0:T(8,128)} %fusion.28) | copy-start | bytes 4718596
  121.5 8.7 %copy-start.8 = (bf16[96,4096]{1,0:T(8,128)(2,1)S(1)}, bf16[96,4096]{1,0:T(8,128)(2,1)}, u32[]{:S(2)}) copy-start(bf16[96,4096]{1,0:T(8,128)(2,1)} %reshape.77) | copy-start | bytes 2359300
  122.7 42.0 %all-to-all-start.1 = ((bf16[16,6,4096]{2,1,0:T(8,128)(2,1)}), bf16[16,6,4096]{2,1,0:T(8,128)(2,1)S(1)}, u32[]{:S(2)}, u32[]{:S(2)}) async-start(bf16[16,6,4096]{2,1,0:T(8,128)(2,1)} %reshape.72), calls=%async_computation.1 | async-start | bytes 2097152 | tf_op jit(solution)/shard_map/all_to_all | solution.py:88
  130.2 4.0 %copy-start.15 = (f32[96,4096]{1,0:T(8,128)S(1)}, f32[96,4096]{1,0:T(8,128)}, u32[]{:S(2)}) copy-start(f32[96,4096]{1,0:T(8,128)} %fusion.24) | copy-start | bytes 4718596
  140.7 4.0 %copy-start.13 = (f32[96,4096]{1,0:T(8,128)S(1)}, f32[96,4096]{1,0:T(8,128)}, u32[]{:S(2)}) copy-start(f32[96,4096]{1,0:T(8,128)} %fusion.26) | copy-start | bytes 4718596
  140.7 21.5 %collective-permute-start.5 = (bf16[16,6,4096]{2,0,1:T(8,128)(2,1)}, bf16[16,6,4096]{2,0,1:T(8,128)(2,1)}, u32[]{:S(2)}, u32[]{:S(2)}) collective-permute-start(bf16[16,6,4096]{2,0,1:T(8,128)(2,1)} %copy.96), channel_id=1, source_target_pairs={{0,32},{16,48},{32,64},{48,80},{64,96},{80,112},{96,128},{112,144}... | collective-permute-start | bytes 2359304 | tf_op jit(solution)/shard_map/ppermute | solution.py:14
  147.6 24.7 %copy-start.16 = (s32[128,8]{0,1:T(8,128)S(1)}, s32[128,8]{0,1:T(8,128)}, u32[]{:S(2)}) copy-start(s32[128,8]{0,1:T(8,128)} %param.6) | copy-start | bytes 12292
  147.6 24.7 %copy-start.17 = (f32[128,8]{0,1:T(8,128)S(1)}, f32[128,8]{0,1:T(8,128)}, u32[]{:S(2)}) copy-start(f32[128,8]{0,1:T(8,128)} %param.7) | copy-start | bytes 12292
  148.1 24.5 %collective-permute-start.3 = (bf16[16,6,4096]{2,0,1:T(8,128)(2,1)S(1)}, bf16[16,6,4096]{2,0,1:T(8,128)(2,1)}, u32[]{:S(2)}, u32[]{:S(2)}) collective-permute-start(bf16[16,6,4096]{2,0,1:T(8,128)(2,1)S(1)} %copy.87), channel_id=1, source_target_pairs={{0,16},{16,32},{32,48},{48,64},{64,80},{80,96},{96,112},{112,128},... | collective-permute-start | bytes 2359304 | tf_op jit(solution)/shard_map/ppermute | solution.py:14
  164.8 30.1 %copy-start.9 = (bf16[16,6,4096]{2,1,0:T(8,128)(2,1)}, bf16[16,6,4096]{2,1,0:T(8,128)(2,1)S(1)}, u32[]{:S(2)}) copy-start(bf16[16,6,4096]{2,1,0:T(8,128)(2,1)S(1)} %all-to-all-done.1) | copy-start | bytes 2359300
  164.8 24.7 %all-to-all-start.5 = ((bf16[16,6,4096]{2,1,0:T(8,128)(2,1)}), bf16[16,6,4096]{2,1,0:T(8,128)(2,1)S(1)}, u32[]{:S(2)}, u32[]{:S(2)}) async-start(bf16[16,6,4096]{2,1,0:T(8,128)(2,1)} %copy.97), calls=%async_computation.5 | async-start | bytes 2097152 | tf_op jit(solution)/shard_map/all_to_all | solution.py:88
  189.5 1.0 copy-start.11
  190.5 21.6 %all-to-all-start.3 = ((bf16[16,6,4096]{2,1,0:T(8,128)(2,1)}), bf16[16,6,4096]{2,1,0:T(8,128)(2,1)S(1)}, u32[]{:S(2)}, u32[]{:S(2)}) async-start(bf16[16,6,4096]{2,1,0:T(8,128)(2,1)} %copy.88), calls=%async_computation.3 | async-start | bytes 2097152 | tf_op jit(solution)/shard_map/all_to_all | solution.py:88
  195.5 2.1 copy-start.12
  212.1 1.0 copy-start.10
  213.2 2.1 copy-start.4
  213.2 6.1 %copy-start.1 = (bf16[128,4096]{1,0:T(8,128)(2,1)S(1)}, bf16[128,4096]{1,0:T(8,128)(2,1)}, u32[]{:S(2)}) copy-start(bf16[128,4096]{1,0:T(8,128)(2,1)} %param.5) | copy-start | bytes 3145732

commit v3 on v2

--- a/solution.py
+++ b/solution.py
@@ -63,36 +63,43 @@
     )
     scale_hi = scale.astype(jnp.bfloat16)
     scale_lo = (scale - scale_hi.astype(jnp.float32)).astype(jnp.bfloat16)
+    lanes_major = width // 128
+    dense = tokens.reshape(tok_rows, lanes_major, 128)
     picked = jnp.einsum(
-        "rqcht,td->rqchd",
+        "rqcht,tkl->qcrhkl",
         one_hot.astype(jnp.bfloat16),
-        tokens,
+        dense,
         preferred_element_type=jnp.float32,
     ).astype(jnp.bfloat16)
+    outgoing = picked.reshape(inner_count, STEPS * half_cap * lanes_major, 128)
+    arrived = lax.all_to_all(outgoing, "inner", split_axis=0, concat_axis=0, tiled=True)
+    arrived = arrived.reshape(inner_count, STEPS, half_cap, lanes_major, 128)
 
-    arrived = [None] * STEPS
-    for rotation in reversed(range(STEPS)):
-        outgoing = picked[rotation].reshape(inner_count, half_cap, width)
-        here = lax.all_to_all(outgoing, "inner", split_axis=0, concat_axis=0, tiled=True)
+    parts = []
+    for rotation in range(STEPS):
+        part = arrived[:, rotation]
         if rotation > 0:
-            here = shifted(here, "blk", -rotation)
-        arrived[rotation] = here
+            part = shifted(part, "blk", -rotation)
+        parts.append(part.reshape(inner_count * half_cap, width))
+    rows = jnp.concatenate(parts, axis=0)
+    done = whole_expert(rows, w_in[0], w_out[0], w_in_other[0], w_out_other[0])
+    done = done.reshape(STEPS, inner_count, half_cap, lanes_major, 128)
 
-    combined = jnp.zeros((tok_rows, width), jnp.float32)
+    results = []
     for rotation in range(STEPS):
-        rows = arrived[rotation].reshape(inner_count * half_cap, width)
-        done = whole_expert(rows, w_in[0], w_out[0], w_in_other[0], w_out_other[0])
-        done = done.reshape(inner_count, half_cap, width)
+        result = done[rotation]
         if rotation > 0:
-            done = shifted(done, "blk", rotation)
-        back = lax.all_to_all(done, "inner", split_axis=0, concat_axis=0, tiled=True)
-        back = back.reshape(group_count, SPLIT, half_cap, width)
-        combined = combined + jnp.einsum(
-            "qcht,qchd->td", scale_hi[rotation], back, preferred_element_type=jnp.float32
-        )
-        combined = combined + jnp.einsum(
-            "qcht,qchd->td", scale_lo[rotation], back, preferred_element_type=jnp.float32
-        )
+            result = shifted(result, "blk", rotation)
+        results.append(result)
+    returned = jnp.stack(results, axis=1)
+    returned = returned.reshape(inner_count, STEPS * half_cap * lanes_major, 128)
+    returned = lax.all_to_all(returned, "inner", split_axis=0, concat_axis=0, tiled=True)
+    returned = returned.reshape(group_count, SPLIT, STEPS, half_cap, lanes_major, 128)
+
+    combined = jnp.einsum(
+        "rqcht,qcrhkl->tkl", scale_hi, returned, preferred_element_type=jnp.float32
+    ) + jnp.einsum("rqcht,qcrhkl->tkl", scale_lo, returned, preferred_element_type=jnp.float32)
+    combined = combined.reshape(tok_rows, width)
     return combined.astype(jnp.bfloat16)
 
 

time: 220 us -> 181 us (0.82)
  the two profiles are of different devices: /device:TPU:1 before, /device:TPU:2 now
where the time goes in v3:
time: 181 us
  waiting for transfers between devices  115 us (64%)
  starting transfers between devices  35.4 us (20%)
  matrix products  20.2 us (11%)
  local copies, waits for them, and re-layouts  7 us (4%)
  other arithmetic  2.79 us (2%)
    ppermute x4, waiting for transfers between devices, shifted(): return lax.ppermute(value, axis, pairs)  51 us
    all_to_all x1, waiting for transfers between devices, on_device(): lax.all_to_all(returned, 'inner', split_axis=0, concat_axis=0, tiled=True)  32.3 us
    all_to_all x1, waiting for transfers between devices, on_device(): lax.all_to_all(outgoing, 'inner', split_axis=0, concat_axis=0, tiled=True)  31.8 us
    ppermute x4, starting transfers between devices, shifted(): return lax.ppermute(value, axis, pairs)  24.8 us
    dot_general x2, matrix products, one_half(): projected = jnp.dot(rows, w_in_now, preferred_element_type=jnp.float32)  9.69 us
    all_to_all x1, starting transfers between devices, on_device(): lax.all_to_all(outgoing, 'inner', split_axis=0, concat_axis=0, tiled=True)  6.13 us
    dot_general x2, matrix products, one_half(): return jnp.dot(activated, w_out_now, preferred_element_type=jnp.float32)  4.86 us
    all_to_all x1, starting transfers between devices, on_device(): lax.all_to_all(returned, 'inner', split_axis=0, concat_axis=0, tiled=True)  3.86 us
  transfers between devices with their start and end apart: 8, of which 6 were waited for; matrix products, arithmetic and copies ran while one was open for 7% of the time, Pallas kernels for 0%

profile of v3, /device:TPU:2, one launch (start us, length us, event | category | flops | bytes accessed | tf_op | source)
XLA Modules:
  0.0 180.7 jit_solution(7556535968105635578)
XLA Ops:
  0.2 0.8 compare_reduce_fusion
  1.1 0.2 reduce_window_sum.11
  1.4 1.5 copy.44
  2.9 0.8 convert_bitcast_fusion
  3.7 2.0 %copy.29 = bf16[8,2,3,6,32,128]{5,4,3,2,1,0:T(8,128)(2,1)} copy(bf16[8,2,3,6,32,128]{5,0,4,3,1,2:T(8,128)(2,1)S(1)} %convert_bitcast_fusion) | data formatting | bytes 4718592 | tf_op jit(solution)/shard_map/convert_element_type | solution.py:73
  5.7 6.1 %all-to-all-start = ((bf16[16,576,128]{2,1,0:T(8,128)(2,1)}), bf16[16,576,128]{2,1,0:T(8,128)(2,1)S(1)}, u32[]{:S(2)}, u32[]{:S(2)}) async-start(bf16[16,576,128]{2,1,0:T(8,128)(2,1)} %bitcast.94), calls=%async_computation | async-start | bytes 4718592 | tf_op jit(solution)/shard_map/all_to_all | solution.py:75
  11.9 0.4 collective-permute-start.2
  12.3 0.2 collective-permute-start.3
  12.5 31.8 %all-to-all-done = bf16[16,576,128]{2,1,0:T(8,128)(2,1)S(1)} async-done(((bf16[16,576,128]{2,1,0:T(8,128)(2,1)}), bf16[16,576,128]{2,1,0:T(8,128)(2,1)S(1)}, u32[]{:S(2)}, u32[]{:S(2)}) %all-to-all-start) | async-done | bytes 2359328 | tf_op jit(solution)/shard_map/all_to_all | solution.py:75
  44.3 0.4 slice_bitcast_fusion.3
  44.7 1.2 collective-permute-start
  46.0 5.9 %collective-permute-start.1 = (bf16[16,6,32,128]{3,2,1,0:T(8,128)(2,1)S(1)}, bf16[16,6,32,128]{3,2,1,0:T(8,128)(2,1)S(1)}, u32[]{:S(2)}, u32[]{:S(2)}) collective-permute-start(bf16[16,6,32,128]{3,2,1,0:T(8,128)(2,1)S(1)} %get-tuple-element.8), channel_id=1, source_target_pairs={{0,224},{16,240},{32,0},{48,16},{64,32},{80,48},{96,64},{112,80},{... | collective-permute-start | bytes 2359304 | tf_op jit(solution)/shard_map/ppermute | solution.py:14
  51.8 0.3 bitcast_dynamic-update-slice_fusion.2
  52.1 14.1 %collective-permute-done = bf16[16,6,32,128]{3,2,1,0:T(8,128)(2,1)S(1)} collective-permute-done((bf16[16,6,32,128]{3,2,1,0:T(8,128)(2,1)S(1)}, bf16[16,6,32,128]{3,2,1,0:T(8,128)(2,1)S(1)}, u32[]{:S(2)}, u32[]{:S(2)}) %collective-permute-start) | collective-permute-done | bytes 786464 | tf_op jit(solution)/shard_map/ppermute | solution.py:14
  66.2 0.3 bitcast_dynamic-update-slice_fusion.1
  66.4 1.7 collective-permute-done.1
  68.1 0.3 bitcast_dynamic-update-slice_fusion
  68.4 4.9 %fusion.2 = f32[288,768]{1,0:T(8,128)S(1)} fusion(bf16[288,4096]{1,0:T(8,128)(2,1)S(1)} %bitcast_dynamic-update-slice_fusion, bf16[1,4096,768]{2,1,0:T(8,128)(2,1)} %param.8), kind=kOutput, calls=%fused_computation.2 | convolution fusion | flops 1811939328 | bytes 9535488 | tf_op jit(solution)/shard_map/dot_general | solution.py:27
  73.3 1.4 fusion.6
  74.8 4.8 %fusion = f32[288,768]{1,0:T(8,128)S(1)} fusion(bf16[288,4096]{1,0:T(8,128)(2,1)S(1)} %bitcast_dynamic-update-slice_fusion, bf16[1,4096,768]{2,1,0:T(8,128)(2,1)} %collective-permute-done.2), kind=kOutput, calls=%fused_computation | convolution fusion | flops 1811939328 | bytes 9535488 | tf_op jit(solution)/shard_map/dot_general | solution.py:27
  79.6 3.4 %fusion.4 = bf16[288,4096]{1,0:T(8,128)(2,1)S(1)} fusion(f32[288,4096]{1,0:T(8,128)S(1)} %fusion.6, bf16[1,384,4096]{2,1,0:T(8,128)(2,1)} %collective-permute-done.3, f32[288,768]{1,0:T(8,128)S(1)} %fusion), kind=kOutput, calls=%fused_computation.5 | convolution fusion | flops 908992512 | bytes 11108352 | tf_op jit(solution)/shard_map/dot_general | solution.py:31
  83.2 0.2 copy.49
  83.3 15.7 %collective-permute-start.4 = (bf16[16,6,32,128]{3,2,1,0:T(8,128)(2,1)S(1)}, bf16[16,6,32,128]{3,2,1,0:T(8,128)(2,1)S(1)}, u32[]{:S(2)}, u32[]{:S(2)}) collective-permute-start(bf16[16,6,32,128]{3,2,1,0:T(8,128)(2,1)S(1)} %bitcast.104), channel_id=1, source_target_pairs={{0,16},{16,32},{32,48},{48,64},{64,80},{80,96},{96,112},{112,128},... | collective-permute-start | bytes 2359304 | tf_op jit(solution)/shard_map/ppermute | solution.py:14
  99.2 2.0 %collective-permute-start.5 = (bf16[16,6,32,128]{3,2,1,0:T(8,128)(2,1)S(1)}, bf16[16,6,32,128]{3,2,1,0:T(8,128)(2,1)S(1)}, u32[]{:S(2)}, u32[]{:S(2)}) collective-permute-start(bf16[16,6,32,128]{3,2,1,0:T(8,128)(2,1)S(1)} %bitcast.106), channel_id=1, source_target_pairs={{0,32},{16,48},{32,64},{48,80},{64,96},{80,112},{96,128},{112,144}... | collective-permute-start | bytes 2359304 | tf_op jit(solution)/shard_map/ppermute | solution.py:14
  101.3 16.1 %collective-permute-done.4 = bf16[16,6,32,128]{3,2,1,0:T(8,128)(2,1)S(1)} collective-permute-done((bf16[16,6,32,128]{3,2,1,0:T(8,128)(2,1)S(1)}, bf16[16,6,32,128]{3,2,1,0:T(8,128)(2,1)S(1)}, u32[]{:S(2)}, u32[]{:S(2)}) %collective-permute-start.4) | collective-permute-done | bytes 786464 | tf_op jit(solution)/shard_map/ppermute | solution.py:14
  117.4 19.2 %collective-permute-done.5 = bf16[16,6,32,128]{3,2,1,0:T(8,128)(2,1)S(1)} collective-permute-done((bf16[16,6,32,128]{3,2,1,0:T(8,128)(2,1)S(1)}, bf16[16,6,32,128]{3,2,1,0:T(8,128)(2,1)S(1)}, u32[]{:S(2)}, u32[]{:S(2)}) %collective-permute-start.5) | collective-permute-done | bytes 786464 | tf_op jit(solution)/shard_map/ppermute | solution.py:14
  136.6 1.7 pad_maximum_fusion
  138.3 3.9 %all-to-all-start.1 = ((bf16[16,576,128]{2,1,0:T(8,128)(2,1)}), bf16[16,576,128]{2,1,0:T(8,128)(2,1)S(1)}, u32[]{:S(2)}, u32[]{:S(2)}) async-start(bf16[16,576,128]{2,1,0:T(8,128)(2,1)} %bitcast.95), calls=%async_computation.1 | async-start | bytes 4718592 | tf_op jit(solution)/shard_map/all_to_all | solution.py:96
  142.3 32.3 %all-to-all-done.1 = bf16[16,576,128]{2,1,0:T(8,128)(2,1)S(1)} async-done(((bf16[16,576,128]{2,1,0:T(8,128)(2,1)}), bf16[16,576,128]{2,1,0:T(8,128)(2,1)S(1)}, u32[]{:S(2)}, u32[]{:S(2)}) %all-to-all-start.1) | async-done | bytes 2359328 | tf_op jit(solution)/shard_map/all_to_all | solution.py:96
  174.6 2.3 %fusion.9 = f32[128,32,128,1,1,1]{0,2,5,1,4,3:T(8,128)S(1)} fusion(bf16[8,2,3,6,32,128]{5,4,3,2,1,0:T(8,128)(2,1)S(1)} %bitcast.91, f32[3,8,128]{2,1,0:T(8,128)S(1)} %bitcast.110, s32[2,6]{1,0:T(2,128)S(1)} %multiply_add_fusion, s32[3,8,128]{2,1,0:T(8,128)S(1)} %bitcast.108, pred[3,8,128]{2,1,0:T(8,128)(4,1)S(1)} %bitcast.113), kind=kOutput, calls=%fused_computation.13 | convolution fusion | flops 302247936 | bytes 4484144 | tf_op jit(solution)/shard_map/rqcht,qcrhkl->tkl/dot_general | solution.py:101
  176.9 2.4 %fusion.8 = bf16[128,32,128]{0,2,1:T(8,128)(2,1)S(1)} fusion(f32[128,32,128,1,1,1]{0,2,5,1,4,3:T(8,128)S(1)} %fusion.9, bf16[8,2,3,6,32,128]{5,4,3,2,1,0:T(8,128)(2,1)S(1)} %bitcast.92, f32[3,8,128]{2,1,0:T(8,128)S(1)} %bitcast.111, s32[2,6]{1,0:T(2,128)S(1)} %multiply_add_fusion, s32[3,8,128]{2,1,0:T(8,128)S(1)} %bitcast.109, ...), kind=kOutput, calls=%fused_computation.12 | convolution fusion | flops 303149056 | bytes 5532720 | tf_op jit(solution)/shard_map/rqcht,qcrhkl->tkl/dot_general | solution.py:99
  179.4 1.3 copy.33
  (21 shorter events, 1.0 us)
Async XLA Ops:
  5.7 38.6 %all-to-all-start = ((bf16[16,576,128]{2,1,0:T(8,128)(2,1)}), bf16[16,576,128]{2,1,0:T(8,128)(2,1)S(1)}, u32[]{:S(2)}, u32[]{:S(2)}) async-start(bf16[16,576,128]{2,1,0:T(8,128)(2,1)} %bitcast.94), calls=%async_computation | async-start | bytes 4718592 | tf_op jit(solution)/shard_map/all_to_all | solution.py:75
  11.9 62.9 %collective-permute-start.2 = (bf16[1,4096,768]{2,1,0:T(8,128)(2,1)}, bf16[1,4096,768]{2,1,0:T(8,128)(2,1)}, u32[]{:S(2)}, u32[]{:S(2)}) collective-permute-start(bf16[1,4096,768]{2,1,0:T(8,128)(2,1)} %param.8), channel_id=1, source_target_pairs={{0,1},{1,0},{2,3},{3,2},{4,5},{5,4},{6,7},{7,6},{8,9},{9,8},{10,11... | collective-permute-start | bytes 18874376 | tf_op jit(solution)/shard_map/ppermute | solution.py:20
  12.3 67.3 %collective-permute-start.3 = (bf16[1,384,4096]{2,1,0:T(8,128)(2,1)}, bf16[1,384,4096]{2,1,0:T(8,128)(2,1)}, u32[]{:S(2)}, u32[]{:S(2)}) collective-permute-start(bf16[1,384,4096]{2,1,0:T(8,128)(2,1)} %param.9), channel_id=1, source_target_pairs={{0,1},{1,0},{2,3},{3,2},{4,5},{5,4},{6,7},{7,6},{8,9},{9,8},{10,11... | collective-permute-start | bytes 9437192 | tf_op jit(solution)/shard_map/ppermute | solution.py:20
  44.7 21.4 %collective-permute-start = (bf16[16,6,32,128]{3,2,1,0:T(8,128)(2,1)S(1)}, bf16[16,6,32,128]{3,2,1,0:T(8,128)(2,1)S(1)}, u32[]{:S(2)}, u32[]{:S(2)}) collective-permute-start(bf16[16,6,32,128]{3,2,1,0:T(8,128)(2,1)S(1)} %get-tuple-element.9), channel_id=1, source_target_pairs={{0,240},{16,0},{32,16},{48,32},{64,48},{80,64},{96,80},{112,96},{1... | collective-permute-start | bytes 2359304 | tf_op jit(solution)/shard_map/ppermute | solution.py:14
  46.0 22.1 %collective-permute-start.1 = (bf16[16,6,32,128]{3,2,1,0:T(8,128)(2,1)S(1)}, bf16[16,6,32,128]{3,2,1,0:T(8,128)(2,1)S(1)}, u32[]{:S(2)}, u32[]{:S(2)}) collective-permute-start(bf16[16,6,32,128]{3,2,1,0:T(8,128)(2,1)S(1)} %get-tuple-element.8), channel_id=1, source_target_pairs={{0,224},{16,240},{32,0},{48,16},{64,32},{80,48},{96,64},{112,80},{... | collective-permute-start | bytes 2359304 | tf_op jit(solution)/shard_map/ppermute | solution.py:14
  68.4 4.9 %copy-start = (bf16[1,384,4096]{2,1,0:T(8,128)(2,1)S(1)}, bf16[1,384,4096]{2,1,0:T(8,128)(2,1)}, u32[]{:S(2)}) copy-start(bf16[1,384,4096]{2,1,0:T(8,128)(2,1)} %param.9) | copy-start | bytes 9437188
  83.3 34.1 %collective-permute-start.4 = (bf16[16,6,32,128]{3,2,1,0:T(8,128)(2,1)S(1)}, bf16[16,6,32,128]{3,2,1,0:T(8,128)(2,1)S(1)}, u32[]{:S(2)}, u32[]{:S(2)}) collective-permute-start(bf16[16,6,32,128]{3,2,1,0:T(8,128)(2,1)S(1)} %bitcast.104), channel_id=1, source_target_pairs={{0,16},{16,32},{32,48},{48,64},{64,80},{80,96},{96,112},{112,128},... | collective-permute-start | bytes 2359304 | tf_op jit(solution)/shard_map/ppermute | solution.py:14
  99.2 37.5 %collective-permute-start.5 = (bf16[16,6,32,128]{3,2,1,0:T(8,128)(2,1)S(1)}, bf16[16,6,32,128]{3,2,1,0:T(8,128)(2,1)S(1)}, u32[]{:S(2)}, u32[]{:S(2)}) collective-permute-start(bf16[16,6,32,128]{3,2,1,0:T(8,128)(2,1)S(1)} %bitcast.106), channel_id=1, source_target_pairs={{0,32},{16,48},{32,64},{48,80},{64,96},{80,112},{96,128},{112,144}... | collective-permute-start | bytes 2359304 | tf_op jit(solution)/shard_map/ppermute | solution.py:14
  138.3 3.9 %copy-start.1 = (s32[128,8]{0,1:T(8,128)S(1)}, s32[128,8]{0,1:T(8,128)}, u32[]{:S(2)}) copy-start(s32[128,8]{0,1:T(8,128)} %param.6) | copy-start | bytes 12292
  138.3 3.9 %copy-start.2 = (f32[128,8]{0,1:T(8,128)S(1)}, f32[128,8]{0,1:T(8,128)}, u32[]{:S(2)}) copy-start(f32[128,8]{0,1:T(8,128)} %param.7) | copy-start | bytes 12292
  138.3 36.3 %all-to-all-start.1 = ((bf16[16,576,128]{2,1,0:T(8,128)(2,1)}), bf16[16,576,128]{2,1,0:T(8,128)(2,1)S(1)}, u32[]{:S(2)}, u32[]{:S(2)}) async-start(bf16[16,576,128]{2,1,0:T(8,128)(2,1)} %bitcast.95), calls=%async_computation.1 | async-start | bytes 4718592 | tf_op jit(solution)/shard_map/all_to_all | solution.py:96

commit v4 on v2

--- a/solution.py
+++ b/solution.py
@@ -63,36 +63,40 @@
     )
     scale_hi = scale.astype(jnp.bfloat16)
     scale_lo = (scale - scale_hi.astype(jnp.float32)).astype(jnp.bfloat16)
+    lanes_major = width // 128
+    dense = tokens.reshape(tok_rows, lanes_major, 128)
     picked = jnp.einsum(
-        "rqcht,td->rqchd",
+        "rqcht,tkl->rqchkl",
         one_hot.astype(jnp.bfloat16),
-        tokens,
+        dense,
         preferred_element_type=jnp.float32,
     ).astype(jnp.bfloat16)
 
     arrived = [None] * STEPS
     for rotation in reversed(range(STEPS)):
-        outgoing = picked[rotation].reshape(inner_count, half_cap, width)
-        here = lax.all_to_all(outgoing, "inner", split_axis=0, concat_axis=0, tiled=True)
+        outgoing = picked[rotation].reshape(inner_count, half_cap, lanes_major, 128)
         if rotation > 0:
-            here = shifted(here, "blk", -rotation)
-        arrived[rotation] = here
+            outgoing = shifted(outgoing, "blk", -rotation)
+        arrived[rotation] = lax.all_to_all(
+            outgoing, "inner", split_axis=0, concat_axis=0, tiled=True
+        )
+    rows = jnp.concatenate([part.reshape(-1, width) for part in arrived], axis=0)
+    done = whole_expert(rows, w_in[0], w_out[0], w_in_other[0], w_out_other[0])
+    done = done.reshape(STEPS, inner_count, half_cap, lanes_major, 128)
 
-    combined = jnp.zeros((tok_rows, width), jnp.float32)
-    for rotation in range(STEPS):
-        rows = arrived[rotation].reshape(inner_count * half_cap, width)
-        done = whole_expert(rows, w_in[0], w_out[0], w_in_other[0], w_out_other[0])
-        done = done.reshape(inner_count, half_cap, width)
+    combined = jnp.zeros((tok_rows, lanes_major, 128), jnp.float32)
+    for rotation in reversed(range(STEPS)):
+        back = lax.all_to_all(done[rotation], "inner", split_axis=0, concat_axis=0, tiled=True)
         if rotation > 0:
-            done = shifted(done, "blk", rotation)
-        back = lax.all_to_all(done, "inner", split_axis=0, concat_axis=0, tiled=True)
-        back = back.reshape(group_count, SPLIT, half_cap, width)
+            back = shifted(back, "blk", rotation)
+        back = back.reshape(group_count, SPLIT, half_cap, lanes_major, 128)
         combined = combined + jnp.einsum(
-            "qcht,qchd->td", scale_hi[rotation], back, preferred_element_type=jnp.float32
+            "qcht,qchkl->tkl", scale_hi[rotation], back, preferred_element_type=jnp.float32
         )
         combined = combined + jnp.einsum(
-            "qcht,qchd->td", scale_lo[rotation], back, preferred_element_type=jnp.float32
+            "qcht,qchkl->tkl", scale_lo[rotation], back, preferred_element_type=jnp.float32
         )
+    combined = combined.reshape(tok_rows, width)
     return combined.astype(jnp.bfloat16)
 
 

time: 220 us -> 185 us (0.84)
  matrix products: 50.9 us -> 21 us
  local copies, waits for them, and re-layouts: 28.2 us -> 19 us
  waiting for transfers between devices: 95.1 us -> 102 us
  starting transfers between devices: 43.4 us -> 41 us
    all_to_all x3, waiting for transfers between devices: 56.4 us -> 40.3 us  [on_device(): lax.all_to_all(outgoing, 'inner', split_axis=0, concat_axis=0, tiled=True)]
    all_to_all x3, waiting for transfers between devices: 24.7 us -> 39.3 us  [on_device(): lax.all_to_all(done[rotation], 'inner', split_axis=0, concat_axis=0, tile...]
    dot_general x6 -> x2, matrix products: 21.5 us -> 10.2 us  [one_half(): projected = jnp.dot(rows, w_in_now, preferred_element_type=jnp.float32)]
    dot_general x6 -> x2, matrix products: 15.6 us -> 4.86 us  [one_half(): return jnp.dot(activated, w_out_now, preferred_element_type=jnp.float32)]
    ppermute x4 -> x0, local copies, waits for them, and re-layouts: 9.27 us -> none  [shifted(): return lax.ppermute(value, axis, pairs)]
    reshape x8 -> x0, local copies, waits for them, and re-layouts: 8.64 us -> none  [the longest x5 5.75 us: on_device(): done = done.reshape(inner_count, half_cap, width)]
    ppermute x4, waiting for transfers between devices: 14 us -> 22.3 us  [shifted(): return lax.ppermute(value, axis, pairs)]
    dot_general x7, matrix products: 13.8 us -> 5.87 us  [the longest x3 2.77 us: on_device(): jnp.einsum('qcht,qchkl->tkl', scale_lo[rotation], back, preferred_element...]
  transfers between devices with their start and end apart: 12 -> 12, of which waited for: 6 -> 9; matrix products, arithmetic and copies ran while one was open for 31% -> 18% of each run, Pallas kernels for 0% -> 0%
where the time goes in v4:
time: 185 us; the launch traced here: 184 us
  waiting for transfers between devices  102 us (55%)
  starting transfers between devices  41 us (22%)
  matrix products  21 us (11%)
  local copies, waits for them, and re-layouts  19 us (10%)
    all_to_all x3, waiting for transfers between devices, on_device(): lax.all_to_all(outgoing, 'inner', split_axis=0, concat_axis=0, tiled=True)  40.3 us
    all_to_all x3, waiting for transfers between devices, on_device(): lax.all_to_all(done[rotation], 'inner', split_axis=0, concat_axis=0, tile...  39.3 us
    ppermute x4, waiting for transfers between devices, shifted(): return lax.ppermute(value, axis, pairs)  22.3 us
    all_to_all x3, starting transfers between devices, on_device(): lax.all_to_all(outgoing, 'inner', split_axis=0, concat_axis=0, tiled=True)  16.4 us
    all_to_all x3, starting transfers between devices, on_device(): lax.all_to_all(done[rotation], 'inner', split_axis=0, concat_axis=0, tile...  13.6 us
    dot_general x2, matrix products, one_half(): projected = jnp.dot(rows, w_in_now, preferred_element_type=jnp.float32)  10.2 us
    unnamed x15, local copies, waits for them, and re-layouts  9.63 us
    ppermute x4, starting transfers between devices, shifted(): return lax.ppermute(value, axis, pairs)  7.29 us
  transfers between devices with their start and end apart: 12, of which 9 were waited for; matrix products, arithmetic and copies ran while one was open for 18% of the time, Pallas kernels for 0%

profile of v4, /device:TPU:1, one launch (start us, length us, event | category | flops | bytes accessed | tf_op | source)
XLA Modules:
  0.0 184.3 jit_solution(15042946175550691872)
XLA Ops:
  0.0 3.2 %collective-permute-start.2 = (bf16[1,4096,768]{2,1,0:T(8,128)(2,1)}, bf16[1,4096,768]{2,1,0:T(8,128)(2,1)}, u32[]{:S(2)}, u32[]{:S(2)}) collective-permute-start(bf16[1,4096,768]{2,1,0:T(8,128)(2,1)} %param.8), channel_id=1, source_target_pairs={{0,1},{1,0},{2,3},{3,2},{4,5},{5,4},{6,7},{7,6},{8,9},{9,8},{10,11... | collective-permute-start | bytes 18874376 | tf_op jit(solution)/shard_map/ppermute | solution.py:20
  4.7 1.5 copy.57
  7.0 1.1 fusion.37
  8.1 1.1 copy.32
  9.1 4.8 %collective-permute-start = (bf16[16,6,32,128]{3,2,1,0:T(8,128)(2,1)}, bf16[16,6,32,128]{3,2,1,0:T(8,128)(2,1)}, u32[]{:S(2)}, u32[]{:S(2)}) collective-permute-start(bf16[16,6,32,128]{3,2,1,0:T(8,128)(2,1)} %bitcast.13), channel_id=1, source_target_pairs={{0,240},{16,0},{32,16},{48,32},{64,48},{80,64},{96,80},{112,96},{1... | collective-permute-start | bytes 2359304 | tf_op jit(solution)/shard_map/ppermute | solution.py:14
  13.9 1.1 copy.31
  15.0 7.1 %all-to-all-start = ((bf16[16,6,32,128]{3,2,1,0:T(8,128)(2,1)}), bf16[16,6,32,128]{3,2,1,0:T(8,128)(2,1)}, u32[]{:S(2)}, u32[]{:S(2)}) async-start(bf16[16,6,32,128]{3,2,1,0:T(8,128)(2,1)} %bitcast.137), calls=%async_computation | async-start | bytes 1572864 | tf_op jit(solution)/shard_map/all_to_all | solution.py:80
  22.0 2.2 %copy.33 = bf16[1,8,2,6,32,128]{5,4,3,2,1,0:T(8,128)(2,1)} copy(bf16[1,8,2,6,32,128]{5,1,4,3,2,0:T(8,128)(2,1)} %get-tuple-element.8) | data formatting | bytes 1572864 | tf_op jit(solution)/shard_map/slice | solution.py:77
  25.4 15.8 %all-to-all-done = bf16[16,6,32,128]{3,2,1,0:T(8,128)(2,1)} async-done(((bf16[16,6,32,128]{3,2,1,0:T(8,128)(2,1)}), bf16[16,6,32,128]{3,2,1,0:T(8,128)(2,1)}, u32[]{:S(2)}, u32[]{:S(2)}) %all-to-all-start) | async-done | bytes 786464 | tf_op jit(solution)/shard_map/all_to_all | solution.py:80
  41.2 4.5 %all-to-all-start.1 = ((bf16[16,6,32,128]{3,2,1,0:T(8,128)(2,1)}), bf16[16,6,32,128]{3,2,1,0:T(8,128)(2,1)}, u32[]{:S(2)}, u32[]{:S(2)}) async-start(bf16[16,6,32,128]{3,2,1,0:T(8,128)(2,1)} %collective-permute-done), calls=%async_computation.1 | async-start | bytes 1572864 | tf_op jit(solution)/shard_map/all_to_all | solution.py:80
  45.7 2.3 %bitcast_dynamic-update-slice_fusion.2 = bf16[288,4096]{1,0:T(8,128)(2,1)} fusion(bf16[12,8,32,128]{3,2,1,0:T(8,128)(2,1)} %bitcast.67), kind=kLoop, calls=%fused_computation.19 | loop fusion | bytes 1572864
  48.1 12.2 %all-to-all-done.1 = bf16[16,6,32,128]{3,2,1,0:T(8,128)(2,1)} async-done(((bf16[16,6,32,128]{3,2,1,0:T(8,128)(2,1)}), bf16[16,6,32,128]{3,2,1,0:T(8,128)(2,1)}, u32[]{:S(2)}, u32[]{:S(2)}) %all-to-all-start.1) | async-done | bytes 786464 | tf_op jit(solution)/shard_map/all_to_all | solution.py:80
  60.3 4.9 %all-to-all-start.2 = ((bf16[16,6,32,128]{3,2,1,0:T(8,128)(2,1)}), bf16[16,6,32,128]{3,2,1,0:T(8,128)(2,1)}, u32[]{:S(2)}, u32[]{:S(2)}) async-start(bf16[16,6,32,128]{3,2,1,0:T(8,128)(2,1)} %collective-permute-done.1), calls=%async_computation.2 | async-start | bytes 1572864 | tf_op jit(solution)/shard_map/all_to_all | solution.py:80
  65.2 2.3 %bitcast_dynamic-update-slice_fusion.1 = bf16[288,4096]{1,0:T(8,128)(2,1)} fusion(bf16[288,4096]{1,0:T(8,128)(2,1)} %bitcast_dynamic-update-slice_fusion.2, bf16[12,8,32,128]{3,2,1,0:T(8,128)(2,1)} %bitcast.70), kind=kLoop, calls=%fused_computation.18 | loop fusion | bytes 1572864
  67.4 12.3 %all-to-all-done.2 = bf16[16,6,32,128]{3,2,1,0:T(8,128)(2,1)} async-done(((bf16[16,6,32,128]{3,2,1,0:T(8,128)(2,1)}), bf16[16,6,32,128]{3,2,1,0:T(8,128)(2,1)}, u32[]{:S(2)}, u32[]{:S(2)}) %all-to-all-start.2) | async-done | bytes 786464 | tf_op jit(solution)/shard_map/all_to_all | solution.py:80
  79.7 2.3 %bitcast_dynamic-update-slice_fusion = bf16[288,4096]{1,0:T(8,128)(2,1)} fusion(bf16[288,4096]{1,0:T(8,128)(2,1)} %bitcast_dynamic-update-slice_fusion.1, bf16[12,8,32,128]{3,2,1,0:T(8,128)(2,1)} %bitcast.73), kind=kLoop, calls=%fused_computation.17 | loop fusion | bytes 1572864 | tf_op jit(solution)/shard_map/concatenate | solution.py:83
  82.0 5.5 %fusion.2 = f32[288,768]{1,0:T(8,128)S(1)} fusion(bf16[288,4096]{1,0:T(8,128)(2,1)} %bitcast_dynamic-update-slice_fusion, bf16[1,4096,768]{2,1,0:T(8,128)(2,1)} %param.8), kind=kOutput, calls=%fused_computation.2 | convolution fusion | flops 1811939328 | bytes 9535488 | tf_op jit(solution)/shard_map/dot_general | solution.py:27
  87.5 1.4 fusion.6
  89.2 4.8 %fusion = f32[288,768]{1,0:T(8,128)S(1)} fusion(bf16[288,4096]{1,0:T(8,128)(2,1)S(1)} %copy-done.1, bf16[1,4096,768]{2,1,0:T(8,128)(2,1)} %collective-permute-done.2), kind=kOutput, calls=%fused_computation | convolution fusion | flops 1811939328 | bytes 9535488 | tf_op jit(solution)/shard_map/dot_general | solution.py:27
  94.0 3.4 %fusion.4 = bf16[288,4096]{1,0:T(8,128)(2,1)S(1)} fusion(f32[288,4096]{1,0:T(8,128)S(1)} %fusion.6, bf16[1,384,4096]{2,1,0:T(8,128)(2,1)} %collective-permute-done.3, f32[288,768]{1,0:T(8,128)S(1)} %fusion), kind=kOutput, calls=%fused_computation.5 | convolution fusion | flops 908992512 | bytes 11108352 | tf_op jit(solution)/shard_map/dot_general | solution.py:31
  98.6 4.3 %all-to-all-start.4 = ((bf16[16,6,32,128]{3,2,1,0:T(8,128)(2,1)}), bf16[16,6,32,128]{3,2,1,0:T(8,128)(2,1)S(1)}, u32[]{:S(2)}, u32[]{:S(2)}) async-start(bf16[16,6,32,128]{3,2,1,0:T(8,128)(2,1)} %bitcast.80), calls=%async_computation.4 | async-start | bytes 1572864 | tf_op jit(solution)/shard_map/all_to_all | solution.py:89
  102.9 1.1 copy.61
  104.0 13.4 %all-to-all-done.4 = bf16[16,6,32,128]{3,2,1,0:T(8,128)(2,1)S(1)} async-done(((bf16[16,6,32,128]{3,2,1,0:T(8,128)(2,1)}), bf16[16,6,32,128]{3,2,1,0:T(8,128)(2,1)S(1)}, u32[]{:S(2)}, u32[]{:S(2)}) %all-to-all-start.4) | async-done | bytes 786464 | tf_op jit(solution)/shard_map/all_to_all | solution.py:89
  117.4 5.0 %all-to-all-start.3 = ((bf16[16,6,32,128]{3,2,1,0:T(8,128)(2,1)}), bf16[16,6,32,128]{3,2,1,0:T(8,128)(2,1)}, u32[]{:S(2)}, u32[]{:S(2)}) async-start(bf16[16,6,32,128]{3,2,1,0:T(8,128)(2,1)} %bitcast.77), calls=%async_computation.3 | async-start | bytes 1572864 | tf_op jit(solution)/shard_map/all_to_all | solution.py:89
  123.5 13.6 %all-to-all-done.3 = bf16[16,6,32,128]{3,2,1,0:T(8,128)(2,1)} async-done(((bf16[16,6,32,128]{3,2,1,0:T(8,128)(2,1)}), bf16[16,6,32,128]{3,2,1,0:T(8,128)(2,1)}, u32[]{:S(2)}, u32[]{:S(2)}) %all-to-all-start.3) | async-done | bytes 786464 | tf_op jit(solution)/shard_map/all_to_all | solution.py:89
  137.0 4.3 %all-to-all-start.5 = ((bf16[16,6,32,128]{3,2,1,0:T(8,128)(2,1)}), bf16[16,6,32,128]{3,2,1,0:T(8,128)(2,1)S(1)}, u32[]{:S(2)}, u32[]{:S(2)}) async-start(bf16[16,6,32,128]{3,2,1,0:T(8,128)(2,1)} %bitcast.83), calls=%async_computation.5 | async-start | bytes 1572864 | tf_op jit(solution)/shard_map/all_to_all | solution.py:89
  141.5 1.7 collective-permute-start.4
  143.4 12.4 %all-to-all-done.5 = bf16[16,6,32,128]{3,2,1,0:T(8,128)(2,1)S(1)} async-done(((bf16[16,6,32,128]{3,2,1,0:T(8,128)(2,1)}), bf16[16,6,32,128]{3,2,1,0:T(8,128)(2,1)S(1)}, u32[]{:S(2)}, u32[]{:S(2)}) %all-to-all-start.5) | async-done | bytes 786464 | tf_op jit(solution)/shard_map/all_to_all | solution.py:89
  157.3 9.1 %collective-permute-done.4 = bf16[16,6,32,128]{3,2,1,0:T(8,128)(2,1)S(1)} collective-permute-done((bf16[16,6,32,128]{3,2,1,0:T(8,128)(2,1)}, bf16[16,6,32,128]{3,2,1,0:T(8,128)(2,1)S(1)}, u32[]{:S(2)}, u32[]{:S(2)}) %collective-permute-start.4) | collective-permute-done | bytes 786464 | tf_op jit(solution)/shard_map/ppermute | solution.py:14
  167.9 13.1 %collective-permute-done.5 = bf16[16,6,32,128]{3,2,1,0:T(8,128)(2,1)S(1)} collective-permute-done((bf16[16,6,32,128]{3,2,1,0:T(8,128)(2,1)S(1)}, bf16[16,6,32,128]{3,2,1,0:T(8,128)(2,1)S(1)}, u32[]{:S(2)}, u32[]{:S(2)}) %collective-permute-start.5) | collective-permute-done | bytes 786464 | tf_op jit(solution)/shard_map/ppermute | solution.py:14
  181.7 1.3 fusion.8
  183.0 1.3 copy.40
  (38 shorter events, 10.2 us)
Async XLA Ops:
  0.0 89.0 %collective-permute-start.2 = (bf16[1,4096,768]{2,1,0:T(8,128)(2,1)}, bf16[1,4096,768]{2,1,0:T(8,128)(2,1)}, u32[]{:S(2)}, u32[]{:S(2)}) collective-permute-start(bf16[1,4096,768]{2,1,0:T(8,128)(2,1)} %param.8), channel_id=1, source_target_pairs={{0,1},{1,0},{2,3},{3,2},{4,5},{5,4},{6,7},{7,6},{8,9},{9,8},{10,11... | collective-permute-start | bytes 18874376 | tf_op jit(solution)/shard_map/ppermute | solution.py:20
  9.1 32.1 %collective-permute-start = (bf16[16,6,32,128]{3,2,1,0:T(8,128)(2,1)}, bf16[16,6,32,128]{3,2,1,0:T(8,128)(2,1)}, u32[]{:S(2)}, u32[]{:S(2)}) collective-permute-start(bf16[16,6,32,128]{3,2,1,0:T(8,128)(2,1)} %bitcast.13), channel_id=1, source_target_pairs={{0,240},{16,0},{32,16},{48,32},{64,48},{80,64},{96,80},{112,96},{1... | collective-permute-start | bytes 2359304 | tf_op jit(solution)/shard_map/ppermute | solution.py:14
  13.9 11.0 %copy-start = (bf16[1,384,4096]{2,1,0:T(8,128)(2,1)S(1)}, bf16[1,384,4096]{2,1,0:T(8,128)(2,1)}, u32[]{:S(2)}) copy-start(bf16[1,384,4096]{2,1,0:T(8,128)(2,1)} %param.9) | copy-start | bytes 9437188
  15.0 26.2 %all-to-all-start = ((bf16[16,6,32,128]{3,2,1,0:T(8,128)(2,1)}), bf16[16,6,32,128]{3,2,1,0:T(8,128)(2,1)}, u32[]{:S(2)}, u32[]{:S(2)}) async-start(bf16[16,6,32,128]{3,2,1,0:T(8,128)(2,1)} %bitcast.137), calls=%async_computation | async-start | bytes 1572864 | tf_op jit(solution)/shard_map/all_to_all | solution.py:80
  24.2 23.9 %collective-permute-start.1 = (bf16[16,6,32,128]{3,2,1,0:T(8,128)(2,1)}, bf16[16,6,32,128]{3,2,1,0:T(8,128)(2,1)}, u32[]{:S(2)}, u32[]{:S(2)}) collective-permute-start(bf16[16,6,32,128]{3,2,1,0:T(8,128)(2,1)} %bitcast.14), channel_id=1, source_target_pairs={{0,224},{16,240},{32,0},{48,16},{64,32},{80,48},{96,64},{112,80},{... | collective-permute-start | bytes 2359304 | tf_op jit(solution)/shard_map/ppermute | solution.py:14
  25.0 69.0 %collective-permute-start.3 = (bf16[1,384,4096]{2,1,0:T(8,128)(2,1)S(1)}, bf16[1,384,4096]{2,1,0:T(8,128)(2,1)}, u32[]{:S(2)}, u32[]{:S(2)}) collective-permute-start(bf16[1,384,4096]{2,1,0:T(8,128)(2,1)S(1)} %copy-done), channel_id=1, source_target_pairs={{0,1},{1,0},{2,3},{3,2},{4,5},{5,4},{6,7},{7,6},{8,9},{9,8},{10,11... | collective-permute-start | bytes 9437192 | tf_op jit(solution)/shard_map/ppermute | solution.py:20
  41.2 19.0 %all-to-all-start.1 = ((bf16[16,6,32,128]{3,2,1,0:T(8,128)(2,1)}), bf16[16,6,32,128]{3,2,1,0:T(8,128)(2,1)}, u32[]{:S(2)}, u32[]{:S(2)}) async-start(bf16[16,6,32,128]{3,2,1,0:T(8,128)(2,1)} %collective-permute-done), calls=%async_computation.1 | async-start | bytes 1572864 | tf_op jit(solution)/shard_map/all_to_all | solution.py:80
  60.3 19.5 %all-to-all-start.2 = ((bf16[16,6,32,128]{3,2,1,0:T(8,128)(2,1)}), bf16[16,6,32,128]{3,2,1,0:T(8,128)(2,1)}, u32[]{:S(2)}, u32[]{:S(2)}) async-start(bf16[16,6,32,128]{3,2,1,0:T(8,128)(2,1)} %collective-permute-done.1), calls=%async_computation.2 | async-start | bytes 1572864 | tf_op jit(solution)/shard_map/all_to_all | solution.py:80
  87.5 1.7 copy-start.1
  98.6 18.8 %all-to-all-start.4 = ((bf16[16,6,32,128]{3,2,1,0:T(8,128)(2,1)}), bf16[16,6,32,128]{3,2,1,0:T(8,128)(2,1)S(1)}, u32[]{:S(2)}, u32[]{:S(2)}) async-start(bf16[16,6,32,128]{3,2,1,0:T(8,128)(2,1)} %bitcast.80), calls=%async_computation.4 | async-start | bytes 1572864 | tf_op jit(solution)/shard_map/all_to_all | solution.py:89
  117.4 23.9 %copy-start.2 = (s32[128,8]{0,1:T(8,128)S(1)}, s32[128,8]{0,1:T(8,128)}, u32[]{:S(2)}) copy-start(s32[128,8]{0,1:T(8,128)} %param.6) | copy-start | bytes 12292
  117.4 23.9 %copy-start.3 = (f32[128,8]{0,1:T(8,128)S(1)}, f32[128,8]{0,1:T(8,128)}, u32[]{:S(2)}) copy-start(f32[128,8]{0,1:T(8,128)} %param.7) | copy-start | bytes 12292
  117.4 19.6 %all-to-all-start.3 = ((bf16[16,6,32,128]{3,2,1,0:T(8,128)(2,1)}), bf16[16,6,32,128]{3,2,1,0:T(8,128)(2,1)}, u32[]{:S(2)}, u32[]{:S(2)}) async-start(bf16[16,6,32,128]{3,2,1,0:T(8,128)(2,1)} %bitcast.77), calls=%async_computation.3 | async-start | bytes 1572864 | tf_op jit(solution)/shard_map/all_to_all | solution.py:89
  137.0 18.8 %all-to-all-start.5 = ((bf16[16,6,32,128]{3,2,1,0:T(8,128)(2,1)}), bf16[16,6,32,128]{3,2,1,0:T(8,128)(2,1)S(1)}, u32[]{:S(2)}, u32[]{:S(2)}) async-start(bf16[16,6,32,128]{3,2,1,0:T(8,128)(2,1)} %bitcast.83), calls=%async_computation.5 | async-start | bytes 1572864 | tf_op jit(solution)/shard_map/all_to_all | solution.py:89
  141.5 24.9 %collective-permute-start.4 = (bf16[16,6,32,128]{3,2,1,0:T(8,128)(2,1)}, bf16[16,6,32,128]{3,2,1,0:T(8,128)(2,1)S(1)}, u32[]{:S(2)}, u32[]{:S(2)}) collective-permute-start(bf16[16,6,32,128]{3,2,1,0:T(8,128)(2,1)} %all-to-all-done.3), channel_id=1, source_target_pairs={{0,32},{16,48},{32,64},{48,80},{64,96},{80,112},{96,128},{112,144}... | collective-permute-start | bytes 2359304 | tf_op jit(solution)/shard_map/ppermute | solution.py:14
  143.3 37.6 %collective-permute-start.5 = (bf16[16,6,32,128]{3,2,1,0:T(8,128)(2,1)S(1)}, bf16[16,6,32,128]{3,2,1,0:T(8,128)(2,1)S(1)}, u32[]{:S(2)}, u32[]{:S(2)}) collective-permute-start(bf16[16,6,32,128]{3,2,1,0:T(8,128)(2,1)S(1)} %all-to-all-done.4), channel_id=1, source_target_pairs={{0,16},{16,32},{32,48},{48,64},{64,80},{80,96},{96,112},{112,128},... | collective-permute-start | bytes 2359304 | tf_op jit(solution)/shard_map/ppermute | solution.py:14

commit v5 on v4

--- a/solution.py
+++ b/solution.py
@@ -72,24 +72,31 @@
         preferred_element_type=jnp.float32,
     ).astype(jnp.bfloat16)
 
-    arrived = [None] * STEPS
-    for rotation in reversed(range(STEPS)):
+    far = []
+    for rotation in range(1, STEPS):
         outgoing = picked[rotation].reshape(inner_count, half_cap, lanes_major, 128)
-        if rotation > 0:
-            outgoing = shifted(outgoing, "blk", -rotation)
-        arrived[rotation] = lax.all_to_all(
-            outgoing, "inner", split_axis=0, concat_axis=0, tiled=True
-        )
-    rows = jnp.concatenate([part.reshape(-1, width) for part in arrived], axis=0)
+        far.append(shifted(outgoing, "blk", -rotation))
+    near = picked[0].reshape(inner_count, half_cap, lanes_major, 128)
+    near = lax.all_to_all(near, "inner", split_axis=0, concat_axis=0, tiled=True)
+    far = jnp.stack(far, axis=1)
+    far = lax.all_to_all(far, "inner", split_axis=0, concat_axis=0, tiled=True)
+    rows = jnp.concatenate(
+        [near.reshape(-1, width), far.transpose(1, 0, 2, 3, 4).reshape(-1, width)], axis=0
+    )
     done = whole_expert(rows, w_in[0], w_out[0], w_in_other[0], w_out_other[0])
     done = done.reshape(STEPS, inner_count, half_cap, lanes_major, 128)
 
+    far_back = lax.all_to_all(
+        done[1:].transpose(1, 0, 2, 3, 4), "inner", split_axis=0, concat_axis=0, tiled=True
+    )
+    near_back = lax.all_to_all(done[0], "inner", split_axis=0, concat_axis=0, tiled=True)
+    backs = [near_back]
+    for rotation in range(1, STEPS):
+        backs.append(shifted(far_back[:, rotation - 1], "blk", rotation))
+
     combined = jnp.zeros((tok_rows, lanes_major, 128), jnp.float32)
-    for rotation in reversed(range(STEPS)):
-        back = lax.all_to_all(done[rotation], "inner", split_axis=0, concat_axis=0, tiled=True)
-        if rotation > 0:
-            back = shifted(back, "blk", rotation)
-        back = back.reshape(group_count, SPLIT, half_cap, lanes_major, 128)
+    for rotation in range(STEPS):
+        back = backs[rotation].reshape(group_count, SPLIT, half_cap, lanes_major, 128)
         combined = combined + jnp.einsum(
             "qcht,qchkl->tkl", scale_hi[rotation], back, preferred_element_type=jnp.float32
         )

time: 185 us -> 173 us (0.935)
  the two profiles are of different devices: /device:TPU:1 before, /device:TPU:2 now
where the time goes in v5:
time: 173 us; the launch traced here: 172 us
  waiting for transfers between devices  93.5 us (54%)
  starting transfers between devices  41.1 us (24%)
  matrix products  20.4 us (12%)
  local copies, waits for them, and re-layouts  14.3 us (8%)
  other arithmetic  2.62 us (2%)
    ppermute x4, waiting for transfers between devices, shifted(): return lax.ppermute(value, axis, pairs)  43.5 us
    all_to_all x1, waiting for transfers between devices, on_device(): lax.all_to_all(done[1:].transpose(1, 0, 2, 3, 4), 'inner', split_axis=0,...  22.7 us
    ppermute x4, starting transfers between devices, shifted(): return lax.ppermute(value, axis, pairs)  22.6 us
    all_to_all x1, waiting for transfers between devices, on_device(): far = lax.all_to_all(far, 'inner', split_axis=0, concat_axis=0, tiled=True)  22.2 us
    dot_general x2, matrix products, one_half(): projected = jnp.dot(rows, w_in_now, preferred_element_type=jnp.float32)  9.69 us
    all_to_all x1, starting transfers between devices, on_device(): lax.all_to_all(near, 'inner', split_axis=0, concat_axis=0, tiled=True)  6.43 us
    unnamed x14, local copies, waits for them, and re-layouts  5.6 us
    all_to_all x1, waiting for transfers between devices, on_device(): lax.all_to_all(near, 'inner', split_axis=0, concat_axis=0, tiled=True)  5.15 us
  transfers between devices with their start and end apart: 10, of which 7 were waited for; matrix products, arithmetic and copies ran while one was open for 16% of the time, Pallas kernels for 0%

profile of v5, /device:TPU:2, one launch (start us, length us, event | category | flops | bytes accessed | tf_op | source)
XLA Modules:
  0.0 172.3 jit_solution(14191056098565139179)
XLA Ops:
  0.2 0.8 compare_reduce_fusion
  1.4 1.5 copy.103
  2.9 0.8 convolution_convert_fusion
  4.1 2.3 %collective-permute-start = (bf16[16,6,32,128]{3,2,1,0:T(8,128)(2,1)S(1)}, bf16[16,6,32,128]{3,2,1,0:T(8,128)(2,1)S(1)}, u32[]{:S(2)}, u32[]{:S(2)}) collective-permute-start(bf16[16,6,32,128]{3,2,1,0:T(8,128)(2,1)S(1)} %bitcast.153), channel_id=1, source_target_pairs={{0,240},{16,0},{32,16},{48,32},{64,48},{80,64},{96,80},{112,96},{1... | collective-permute-start | bytes 2359304 | tf_op jit(solution)/shard_map/ppermute | solution.py:14
  6.6 4.2 %collective-permute-start.1 = (bf16[16,6,32,128]{3,2,1,0:T(8,128)(2,1)S(1)}, bf16[16,6,32,128]{3,2,1,0:T(8,128)(2,1)}, u32[]{:S(2)}, u32[]{:S(2)}) collective-permute-start(bf16[16,6,32,128]{3,2,1,0:T(8,128)(2,1)S(1)} %bitcast.154), channel_id=1, source_target_pairs={{0,224},{16,240},{32,0},{48,16},{64,32},{80,48},{96,64},{112,80},{... | collective-permute-start | bytes 2359304 | tf_op jit(solution)/shard_map/ppermute | solution.py:14
  10.8 1.0 copy.70
  11.9 6.4 %all-to-all-start = ((bf16[16,6,32,128]{3,2,1,0:T(8,128)(2,1)}), bf16[16,6,32,128]{3,2,1,0:T(8,128)(2,1)S(1)}, u32[]{:S(2)}, u32[]{:S(2)}) async-start(bf16[16,6,32,128]{3,2,1,0:T(8,128)(2,1)} %bitcast.12), calls=%async_computation | async-start | bytes 1572864 | tf_op jit(solution)/shard_map/all_to_all | solution.py:80
  18.3 7.2 %collective-permute-done = bf16[16,6,32,128]{3,2,1,0:T(8,128)(2,1)S(1)} collective-permute-done((bf16[16,6,32,128]{3,2,1,0:T(8,128)(2,1)S(1)}, bf16[16,6,32,128]{3,2,1,0:T(8,128)(2,1)S(1)}, u32[]{:S(2)}, u32[]{:S(2)}) %collective-permute-start) | collective-permute-done | bytes 786464 | tf_op jit(solution)/shard_map/ppermute | solution.py:14
  25.5 2.5 %collective-permute-done.1 = bf16[16,6,32,128]{3,2,1,0:T(8,128)(2,1)} collective-permute-done((bf16[16,6,32,128]{3,2,1,0:T(8,128)(2,1)S(1)}, bf16[16,6,32,128]{3,2,1,0:T(8,128)(2,1)}, u32[]{:S(2)}, u32[]{:S(2)}) %collective-permute-start.1) | collective-permute-done | bytes 786464 | tf_op jit(solution)/shard_map/ppermute | solution.py:14
  28.0 1.3 pad_maximum_fusion
  29.3 1.5 copy.73
  30.8 5.2 %all-to-all-done = bf16[16,6,32,128]{3,2,1,0:T(8,128)(2,1)S(1)} async-done(((bf16[16,6,32,128]{3,2,1,0:T(8,128)(2,1)}), bf16[16,6,32,128]{3,2,1,0:T(8,128)(2,1)S(1)}, u32[]{:S(2)}, u32[]{:S(2)}) %all-to-all-start) | async-done | bytes 786464 | tf_op jit(solution)/shard_map/all_to_all | solution.py:80
  36.0 3.7 %all-to-all-start.1 = ((bf16[16,2,6,32,128]{4,3,2,1,0:T(8,128)(2,1)}), bf16[16,2,6,32,128]{4,3,2,1,0:T(8,128)(2,1)S(1)}, u32[]{:S(2)}, u32[]{:S(2)}) async-start(bf16[16,2,6,32,128]{4,3,2,1,0:T(8,128)(2,1)} %copy.73), calls=%async_computation.1 | async-start | bytes 3145728 | tf_op jit(solution)/shard_map/all_to_all | solution.py:82
  40.0 1.1 bitcast_dynamic-update-slice_fusion.1
  41.2 22.2 %all-to-all-done.1 = bf16[16,2,6,32,128]{4,3,2,1,0:T(8,128)(2,1)S(1)} async-done(((bf16[16,2,6,32,128]{4,3,2,1,0:T(8,128)(2,1)}), bf16[16,2,6,32,128]{4,3,2,1,0:T(8,128)(2,1)S(1)}, u32[]{:S(2)}, u32[]{:S(2)}) %all-to-all-start.1) | async-done | bytes 1572896 | tf_op jit(solution)/shard_map/all_to_all | solution.py:82
  63.7 1.4 copy-done.1
  65.7 4.9 %fusion.2 = f32[288,768]{1,0:T(8,128)S(1)} fusion(bf16[288,4096]{1,0:T(8,128)(2,1)S(1)} %bitcast_dynamic-update-slice_fusion, bf16[1,4096,768]{2,1,0:T(8,128)(2,1)} %param.8), kind=kOutput, calls=%fused_computation.2 | convolution fusion | flops 1811939328 | bytes 9535488 | tf_op jit(solution)/shard_map/dot_general | solution.py:27
  70.7 1.4 fusion.6
  72.1 4.8 %fusion = f32[288,768]{1,0:T(8,128)S(1)} fusion(bf16[288,4096]{1,0:T(8,128)(2,1)S(1)} %bitcast_dynamic-update-slice_fusion, bf16[1,4096,768]{2,1,0:T(8,128)(2,1)} %collective-permute-done.2), kind=kOutput, calls=%fused_computation | convolution fusion | flops 1811939328 | bytes 9535488 | tf_op jit(solution)/shard_map/dot_general | solution.py:27
  76.9 3.4 %fusion.4 = bf16[288,4096]{1,0:T(8,128)(2,1)S(1)} fusion(f32[288,4096]{1,0:T(8,128)S(1)} %fusion.6, bf16[1,384,4096]{2,1,0:T(8,128)(2,1)} %collective-permute-done.3, f32[288,768]{1,0:T(8,128)S(1)} %fusion), kind=kOutput, calls=%fused_computation.5 | convolution fusion | flops 908992512 | bytes 11108352 | tf_op jit(solution)/shard_map/dot_general | solution.py:31
  80.9 1.4 copy.125
  82.3 4.4 %all-to-all-start.3 = ((bf16[16,2,6,32,128]{4,3,2,1,0:T(8,128)(2,1)}), bf16[16,2,6,32,128]{4,3,2,1,0:T(8,128)(2,1)}, u32[]{:S(2)}, u32[]{:S(2)}) async-start(bf16[16,2,6,32,128]{4,3,2,1,0:T(8,128)(2,1)} %bitcast.142), calls=%async_computation.3 | async-start | bytes 3145728 | tf_op jit(solution)/shard_map/all_to_all | solution.py:89
  86.8 1.0 copy.106
  87.8 22.7 %all-to-all-done.3 = bf16[16,2,6,32,128]{4,3,2,1,0:T(8,128)(2,1)} async-done(((bf16[16,2,6,32,128]{4,3,2,1,0:T(8,128)(2,1)}), bf16[16,2,6,32,128]{4,3,2,1,0:T(8,128)(2,1)}, u32[]{:S(2)}, u32[]{:S(2)}) %all-to-all-start.3) | async-done | bytes 1572896 | tf_op jit(solution)/shard_map/all_to_all | solution.py:89
  110.5 3.6 %all-to-all-start.2 = ((bf16[16,6,32,128]{3,2,1,0:T(8,128)(2,1)}), bf16[16,6,32,128]{3,2,1,0:T(8,128)(2,1)S(1)}, u32[]{:S(2)}, u32[]{:S(2)}) async-start(bf16[16,6,32,128]{3,2,1,0:T(8,128)(2,1)} %bitcast.84), calls=%async_computation.2 | async-start | bytes 1572864 | tf_op jit(solution)/shard_map/all_to_all | solution.py:92
  114.3 1.7 slice_bitcast_fusion.2
  116.0 13.8 %collective-permute-start.4 = (bf16[16,6,32,128]{3,2,1,0:T(8,128)(2,1)S(1)}, bf16[16,6,32,128]{3,2,1,0:T(8,128)(2,1)S(1)}, u32[]{:S(2)}, u32[]{:S(2)}) collective-permute-start(bf16[16,6,32,128]{3,2,1,0:T(8,128)(2,1)S(1)} %get-tuple-element.8), channel_id=1, source_target_pairs={{0,16},{16,32},{32,48},{48,64},{64,80},{80,96},{96,112},{112,128},... | collective-permute-start | bytes 2359304 | tf_op jit(solution)/shard_map/ppermute | solution.py:14
  130.7 2.2 %collective-permute-start.5 = (bf16[16,6,32,128]{3,2,1,0:T(8,128)(2,1)S(1)}, bf16[16,6,32,128]{3,2,1,0:T(8,128)(2,1)S(1)}, u32[]{:S(2)}, u32[]{:S(2)}) collective-permute-start(bf16[16,6,32,128]{3,2,1,0:T(8,128)(2,1)S(1)} %get-tuple-element.9), channel_id=1, source_target_pairs={{0,32},{16,48},{32,64},{48,80},{64,96},{80,112},{96,128},{112,144}... | collective-permute-start | bytes 2359304 | tf_op jit(solution)/shard_map/ppermute | solution.py:14
  133.6 22.8 %collective-permute-done.4 = bf16[16,6,32,128]{3,2,1,0:T(8,128)(2,1)S(1)} collective-permute-done((bf16[16,6,32,128]{3,2,1,0:T(8,128)(2,1)S(1)}, bf16[16,6,32,128]{3,2,1,0:T(8,128)(2,1)S(1)}, u32[]{:S(2)}, u32[]{:S(2)}) %collective-permute-start.4) | collective-permute-done | bytes 786464 | tf_op jit(solution)/shard_map/ppermute | solution.py:14
  157.9 11.1 %collective-permute-done.5 = bf16[16,6,32,128]{3,2,1,0:T(8,128)(2,1)S(1)} collective-permute-done((bf16[16,6,32,128]{3,2,1,0:T(8,128)(2,1)S(1)}, bf16[16,6,32,128]{3,2,1,0:T(8,128)(2,1)S(1)}, u32[]{:S(2)}, u32[]{:S(2)}) %collective-permute-start.5) | collective-permute-done | bytes 786464 | tf_op jit(solution)/shard_map/ppermute | solution.py:14
  169.7 1.3 fusion.8
  171.0 1.3 copy.84
  (38 shorter events, 7.1 us)
Async XLA Ops:
  0.0 72.1 %collective-permute-start.2 = (bf16[1,4096,768]{2,1,0:T(8,128)(2,1)}, bf16[1,4096,768]{2,1,0:T(8,128)(2,1)}, u32[]{:S(2)}, u32[]{:S(2)}) collective-permute-start(bf16[1,4096,768]{2,1,0:T(8,128)(2,1)} %param.8), channel_id=1, source_target_pairs={{0,1},{1,0},{2,3},{3,2},{4,5},{5,4},{6,7},{7,6},{8,9},{9,8},{10,11... | collective-permute-start | bytes 18874376 | tf_op jit(solution)/shard_map/ppermute | solution.py:20
  4.1 21.4 %collective-permute-start = (bf16[16,6,32,128]{3,2,1,0:T(8,128)(2,1)S(1)}, bf16[16,6,32,128]{3,2,1,0:T(8,128)(2,1)S(1)}, u32[]{:S(2)}, u32[]{:S(2)}) collective-permute-start(bf16[16,6,32,128]{3,2,1,0:T(8,128)(2,1)S(1)} %bitcast.153), channel_id=1, source_target_pairs={{0,240},{16,0},{32,16},{48,32},{64,48},{80,64},{96,80},{112,96},{1... | collective-permute-start | bytes 2359304 | tf_op jit(solution)/shard_map/ppermute | solution.py:14
  6.6 21.4 %collective-permute-start.1 = (bf16[16,6,32,128]{3,2,1,0:T(8,128)(2,1)S(1)}, bf16[16,6,32,128]{3,2,1,0:T(8,128)(2,1)}, u32[]{:S(2)}, u32[]{:S(2)}) collective-permute-start(bf16[16,6,32,128]{3,2,1,0:T(8,128)(2,1)S(1)} %bitcast.154), channel_id=1, source_target_pairs={{0,224},{16,240},{32,0},{48,16},{64,32},{80,48},{96,64},{112,80},{... | collective-permute-start | bytes 2359304 | tf_op jit(solution)/shard_map/ppermute | solution.py:14
  11.9 24.1 %all-to-all-start = ((bf16[16,6,32,128]{3,2,1,0:T(8,128)(2,1)}), bf16[16,6,32,128]{3,2,1,0:T(8,128)(2,1)S(1)}, u32[]{:S(2)}, u32[]{:S(2)}) async-start(bf16[16,6,32,128]{3,2,1,0:T(8,128)(2,1)} %bitcast.12), calls=%async_computation | async-start | bytes 1572864 | tf_op jit(solution)/shard_map/all_to_all | solution.py:80
  36.0 27.4 %all-to-all-start.1 = ((bf16[16,2,6,32,128]{4,3,2,1,0:T(8,128)(2,1)}), bf16[16,2,6,32,128]{4,3,2,1,0:T(8,128)(2,1)S(1)}, u32[]{:S(2)}, u32[]{:S(2)}) async-start(bf16[16,2,6,32,128]{4,3,2,1,0:T(8,128)(2,1)} %copy.73), calls=%async_computation.1 | async-start | bytes 3145728 | tf_op jit(solution)/shard_map/all_to_all | solution.py:82
  39.7 37.2 %collective-permute-start.3 = (bf16[1,384,4096]{2,1,0:T(8,128)(2,1)}, bf16[1,384,4096]{2,1,0:T(8,128)(2,1)}, u32[]{:S(2)}, u32[]{:S(2)}) collective-permute-start(bf16[1,384,4096]{2,1,0:T(8,128)(2,1)} %param.9), channel_id=1, source_target_pairs={{0,1},{1,0},{2,3},{3,2},{4,5},{5,4},{6,7},{7,6},{8,9},{9,8},{10,11... | collective-permute-start | bytes 9437192 | tf_op jit(solution)/shard_map/ppermute | solution.py:20
  63.4 1.7 copy-start.1
  65.7 4.9 %copy-start = (bf16[1,384,4096]{2,1,0:T(8,128)(2,1)S(1)}, bf16[1,384,4096]{2,1,0:T(8,128)(2,1)}, u32[]{:S(2)}) copy-start(bf16[1,384,4096]{2,1,0:T(8,128)(2,1)} %param.9) | copy-start | bytes 9437188
  82.3 28.2 %all-to-all-start.3 = ((bf16[16,2,6,32,128]{4,3,2,1,0:T(8,128)(2,1)}), bf16[16,2,6,32,128]{4,3,2,1,0:T(8,128)(2,1)}, u32[]{:S(2)}, u32[]{:S(2)}) async-start(bf16[16,2,6,32,128]{4,3,2,1,0:T(8,128)(2,1)} %bitcast.142), calls=%async_computation.3 | async-start | bytes 3145728 | tf_op jit(solution)/shard_map/all_to_all | solution.py:89
  86.7 27.4 %copy-start.2 = (s32[128,8]{0,1:T(8,128)S(1)}, s32[128,8]{0,1:T(8,128)}, u32[]{:S(2)}) copy-start(s32[128,8]{0,1:T(8,128)} %param.6) | copy-start | bytes 12292
  86.7 27.4 %copy-start.3 = (f32[128,8]{0,1:T(8,128)S(1)}, f32[128,8]{0,1:T(8,128)}, u32[]{:S(2)}) copy-start(f32[128,8]{0,1:T(8,128)} %param.7) | copy-start | bytes 12292
  110.5 19.4 %all-to-all-start.2 = ((bf16[16,6,32,128]{3,2,1,0:T(8,128)(2,1)}), bf16[16,6,32,128]{3,2,1,0:T(8,128)(2,1)S(1)}, u32[]{:S(2)}, u32[]{:S(2)}) async-start(bf16[16,6,32,128]{3,2,1,0:T(8,128)(2,1)} %bitcast.84), calls=%async_computation.2 | async-start | bytes 1572864 | tf_op jit(solution)/shard_map/all_to_all | solution.py:92
  116.0 40.4 %collective-permute-start.4 = (bf16[16,6,32,128]{3,2,1,0:T(8,128)(2,1)S(1)}, bf16[16,6,32,128]{3,2,1,0:T(8,128)(2,1)S(1)}, u32[]{:S(2)}, u32[]{:S(2)}) collective-permute-start(bf16[16,6,32,128]{3,2,1,0:T(8,128)(2,1)S(1)} %get-tuple-element.8), channel_id=1, source_target_pairs={{0,16},{16,32},{32,48},{48,64},{64,80},{80,96},{96,112},{112,128},... | collective-permute-start | bytes 2359304 | tf_op jit(solution)/shard_map/ppermute | solution.py:14
  130.7 38.3 %collective-permute-start.5 = (bf16[16,6,32,128]{3,2,1,0:T(8,128)(2,1)S(1)}, bf16[16,6,32,128]{3,2,1,0:T(8,128)(2,1)S(1)}, u32[]{:S(2)}, u32[]{:S(2)}) collective-permute-start(bf16[16,6,32,128]{3,2,1,0:T(8,128)(2,1)S(1)} %get-tuple-element.9), channel_id=1, source_target_pairs={{0,32},{16,48},{32,64},{48,80},{64,96},{80,112},{96,128},{112,144}... | collective-permute-start | bytes 2359304 | tf_op jit(solution)/shard_map/ppermute | solution.py:14

commit v6 on v5

--- a/solution.py
+++ b/solution.py
@@ -86,23 +86,16 @@
     done = whole_expert(rows, w_in[0], w_out[0], w_in_other[0], w_out_other[0])
     done = done.reshape(STEPS, inner_count, half_cap, lanes_major, 128)
 
-    far_back = lax.all_to_all(
-        done[1:].transpose(1, 0, 2, 3, 4), "inner", split_axis=0, concat_axis=0, tiled=True
-    )
-    near_back = lax.all_to_all(done[0], "inner", split_axis=0, concat_axis=0, tiled=True)
-    backs = [near_back]
+    results = [done[0]]
     for rotation in range(1, STEPS):
-        backs.append(shifted(far_back[:, rotation - 1], "blk", rotation))
+        results.append(shifted(done[rotation], "blk", rotation))
+    returned = jnp.stack(results, axis=1)
+    returned = lax.all_to_all(returned, "inner", split_axis=0, concat_axis=0, tiled=True)
+    returned = returned.reshape(group_count, SPLIT, STEPS, half_cap, lanes_major, 128)
 
-    combined = jnp.zeros((tok_rows, lanes_major, 128), jnp.float32)
-    for rotation in range(STEPS):
-        back = backs[rotation].reshape(group_count, SPLIT, half_cap, lanes_major, 128)
-        combined = combined + jnp.einsum(
-            "qcht,qchkl->tkl", scale_hi[rotation], back, preferred_element_type=jnp.float32
-        )
-        combined = combined + jnp.einsum(
-            "qcht,qchkl->tkl", scale_lo[rotation], back, preferred_element_type=jnp.float32
-        )
+    combined = jnp.einsum(
+        "rqcht,qcrhkl->tkl", scale_hi, returned, preferred_element_type=jnp.float32
+    ) + jnp.einsum("rqcht,qcrhkl->tkl", scale_lo, returned, preferred_element_type=jnp.float32)
     combined = combined.reshape(tok_rows, width)
     return combined.astype(jnp.bfloat16)
 

time: 173 us -> 178 us (1.029)
  waiting for transfers between devices: 93.5 us -> 105 us
  starting transfers between devices: 41.1 us -> 37 us
  local copies, waits for them, and re-layouts: 14.3 us -> 10.3 us
    all_to_all x2 -> x1, waiting for transfers between devices: 22.7 us -> 32.1 us  [on_device(): lax.all_to_all(returned, 'inner', split_axis=0, concat_axis=0, tiled=True)]
    all_to_all x2 -> x1, starting transfers between devices: 8.01 us -> 4.08 us  [on_device(): lax.all_to_all(returned, 'inner', split_axis=0, concat_axis=0, tiled=True)]
    ppermute x4, waiting for transfers between devices: 43.5 us -> 45.8 us  [shifted(): return lax.ppermute(value, axis, pairs)]
    dot_general x6 -> x2, matrix products: 5.05 us -> 4.81 us  [the longest x1 2.47 us: on_device(): jnp.einsum('rqcht,qcrhkl->tkl', scale_lo, returned, preferred_element_typ...]
  transfers between devices with their start and end apart: 10 -> 9, of which waited for: 7 -> 7; matrix products, arithmetic and copies ran while one was open for 16% -> 12% of each run, Pallas kernels for 0% -> 0%
where the time goes in v6:
time: 178 us; the launch traced here: 177 us
  waiting for transfers between devices  105 us (59%)
  starting transfers between devices  37 us (21%)
  matrix products  20.2 us (11%)
  local copies, waits for them, and re-layouts  10.3 us (6%)
  other arithmetic  4.08 us (2%)
    ppermute x4, waiting for transfers between devices, shifted(): return lax.ppermute(value, axis, pairs)  45.8 us
    all_to_all x1, waiting for transfers between devices, on_device(): lax.all_to_all(returned, 'inner', split_axis=0, concat_axis=0, tiled=True)  32.1 us
    ppermute x4, starting transfers between devices, shifted(): return lax.ppermute(value, axis, pairs)  22.4 us
    all_to_all x1, waiting for transfers between devices, on_device(): far = lax.all_to_all(far, 'inner', split_axis=0, concat_axis=0, tiled=True)  22.2 us
    dot_general x2, matrix products, one_half(): projected = jnp.dot(rows, w_in_now, preferred_element_type=jnp.float32)  9.73 us
    all_to_all x1, starting transfers between devices, on_device(): lax.all_to_all(near, 'inner', split_axis=0, concat_axis=0, tiled=True)  6.43 us
    all_to_all x1, waiting for transfers between devices, on_device(): lax.all_to_all(near, 'inner', split_axis=0, concat_axis=0, tiled=True)  5.16 us
    dot_general x2, matrix products, one_half(): return jnp.dot(activated, w_out_now, preferred_element_type=jnp.float32)  4.86 us
  transfers between devices with their start and end apart: 9, of which 7 were waited for; matrix products, arithmetic and copies ran while one was open for 12% of the time, Pallas kernels for 0%

profile of v6, /device:TPU:2, one launch (start us, length us, event | category | flops | bytes accessed | tf_op | source)
XLA Modules:
  0.0 177.1 jit_solution(13988125427013247673)
XLA Ops:
  0.2 0.8 compare_reduce_fusion
  1.4 1.5 copy.79
  2.9 0.8 convolution_convert_fusion
  4.1 2.3 %collective-permute-start = (bf16[16,6,32,128]{3,2,1,0:T(8,128)(2,1)S(1)}, bf16[16,6,32,128]{3,2,1,0:T(8,128)(2,1)S(1)}, u32[]{:S(2)}, u32[]{:S(2)}) collective-permute-start(bf16[16,6,32,128]{3,2,1,0:T(8,128)(2,1)S(1)} %bitcast.95), channel_id=1, source_target_pairs={{0,240},{16,0},{32,16},{48,32},{64,48},{80,64},{96,80},{112,96},{1... | collective-permute-start | bytes 2359304 | tf_op jit(solution)/shard_map/ppermute | solution.py:14
  6.6 4.2 %collective-permute-start.1 = (bf16[16,6,32,128]{3,2,1,0:T(8,128)(2,1)S(1)}, bf16[16,6,32,128]{3,2,1,0:T(8,128)(2,1)}, u32[]{:S(2)}, u32[]{:S(2)}) collective-permute-start(bf16[16,6,32,128]{3,2,1,0:T(8,128)(2,1)S(1)} %bitcast.96), channel_id=1, source_target_pairs={{0,224},{16,240},{32,0},{48,16},{64,32},{80,48},{96,64},{112,80},{... | collective-permute-start | bytes 2359304 | tf_op jit(solution)/shard_map/ppermute | solution.py:14
  10.8 1.0 copy.60
  11.8 6.4 %all-to-all-start = ((bf16[16,6,32,128]{3,2,1,0:T(8,128)(2,1)}), bf16[16,6,32,128]{3,2,1,0:T(8,128)(2,1)S(1)}, u32[]{:S(2)}, u32[]{:S(2)}) async-start(bf16[16,6,32,128]{3,2,1,0:T(8,128)(2,1)} %bitcast.10), calls=%async_computation | async-start | bytes 1572864 | tf_op jit(solution)/shard_map/all_to_all | solution.py:80
  18.3 7.2 %collective-permute-done = bf16[16,6,32,128]{3,2,1,0:T(8,128)(2,1)S(1)} collective-permute-done((bf16[16,6,32,128]{3,2,1,0:T(8,128)(2,1)S(1)}, bf16[16,6,32,128]{3,2,1,0:T(8,128)(2,1)S(1)}, u32[]{:S(2)}, u32[]{:S(2)}) %collective-permute-start) | collective-permute-done | bytes 786464 | tf_op jit(solution)/shard_map/ppermute | solution.py:14
  25.5 2.5 %collective-permute-done.1 = bf16[16,6,32,128]{3,2,1,0:T(8,128)(2,1)} collective-permute-done((bf16[16,6,32,128]{3,2,1,0:T(8,128)(2,1)S(1)}, bf16[16,6,32,128]{3,2,1,0:T(8,128)(2,1)}, u32[]{:S(2)}, u32[]{:S(2)}) %collective-permute-start.1) | collective-permute-done | bytes 786464 | tf_op jit(solution)/shard_map/ppermute | solution.py:14
  28.0 1.3 pad_maximum_fusion.1
  29.3 1.5 copy.63
  30.8 5.2 %all-to-all-done = bf16[16,6,32,128]{3,2,1,0:T(8,128)(2,1)S(1)} async-done(((bf16[16,6,32,128]{3,2,1,0:T(8,128)(2,1)}), bf16[16,6,32,128]{3,2,1,0:T(8,128)(2,1)S(1)}, u32[]{:S(2)}, u32[]{:S(2)}) %all-to-all-start) | async-done | bytes 786464 | tf_op jit(solution)/shard_map/all_to_all | solution.py:80
  35.9 3.7 %all-to-all-start.1 = ((bf16[16,2,6,32,128]{4,3,2,1,0:T(8,128)(2,1)}), bf16[16,2,6,32,128]{4,3,2,1,0:T(8,128)(2,1)S(1)}, u32[]{:S(2)}, u32[]{:S(2)}) async-start(bf16[16,2,6,32,128]{4,3,2,1,0:T(8,128)(2,1)} %copy.63), calls=%async_computation.1 | async-start | bytes 3145728 | tf_op jit(solution)/shard_map/all_to_all | solution.py:82
  39.6 0.4 collective-permute-start.3
  40.0 1.2 bitcast_dynamic-update-slice_fusion.1
  41.2 22.2 %all-to-all-done.1 = bf16[16,2,6,32,128]{4,3,2,1,0:T(8,128)(2,1)S(1)} async-done(((bf16[16,2,6,32,128]{4,3,2,1,0:T(8,128)(2,1)}), bf16[16,2,6,32,128]{4,3,2,1,0:T(8,128)(2,1)S(1)}, u32[]{:S(2)}, u32[]{:S(2)}) %all-to-all-start.1) | async-done | bytes 1572896 | tf_op jit(solution)/shard_map/all_to_all | solution.py:82
  63.7 1.4 copy-done.1
  65.0 0.7 bitcast_dynamic-update-slice_fusion
  65.7 4.9 %fusion.2 = f32[288,768]{1,0:T(8,128)S(1)} fusion(bf16[288,4096]{1,0:T(8,128)(2,1)S(1)} %bitcast_dynamic-update-slice_fusion, bf16[1,4096,768]{2,1,0:T(8,128)(2,1)} %param.8), kind=kOutput, calls=%fused_computation.2 | convolution fusion | flops 1811939328 | bytes 9535488 | tf_op jit(solution)/shard_map/dot_general | solution.py:27
  70.7 1.4 fusion.6
  72.1 4.8 %fusion = f32[288,768]{1,0:T(8,128)S(1)} fusion(bf16[288,4096]{1,0:T(8,128)(2,1)S(1)} %bitcast_dynamic-update-slice_fusion, bf16[1,4096,768]{2,1,0:T(8,128)(2,1)} %collective-permute-done.2), kind=kOutput, calls=%fused_computation | convolution fusion | flops 1811939328 | bytes 9535488 | tf_op jit(solution)/shard_map/dot_general | solution.py:27
  76.9 3.4 %fusion.4 = bf16[288,4096]{1,0:T(8,128)(2,1)S(1)} fusion(f32[288,4096]{1,0:T(8,128)S(1)} %fusion.6, bf16[1,384,4096]{2,1,0:T(8,128)(2,1)} %collective-permute-done.3, f32[288,768]{1,0:T(8,128)S(1)} %fusion), kind=kOutput, calls=%fused_computation.5 | convolution fusion | flops 908992512 | bytes 11108352 | tf_op jit(solution)/shard_map/dot_general | solution.py:31
  80.7 13.9 %collective-permute-start.4 = (bf16[16,6,32,128]{3,2,1,0:T(8,128)(2,1)S(1)}, bf16[16,6,32,128]{3,2,1,0:T(8,128)(2,1)S(1)}, u32[]{:S(2)}, u32[]{:S(2)}) collective-permute-start(bf16[16,6,32,128]{3,2,1,0:T(8,128)(2,1)S(1)} %bitcast.97), channel_id=1, source_target_pairs={{0,16},{16,32},{32,48},{48,64},{64,80},{80,96},{96,112},{112,128},... | collective-permute-start | bytes 2359304 | tf_op jit(solution)/shard_map/ppermute | solution.py:14
  94.7 2.0 %collective-permute-start.5 = (bf16[16,6,32,128]{3,2,1,0:T(8,128)(2,1)S(1)}, bf16[16,6,32,128]{3,2,1,0:T(8,128)(2,1)S(1)}, u32[]{:S(2)}, u32[]{:S(2)}) collective-permute-start(bf16[16,6,32,128]{3,2,1,0:T(8,128)(2,1)S(1)} %bitcast.98), channel_id=1, source_target_pairs={{0,32},{16,48},{32,64},{48,80},{64,96},{80,112},{96,128},{112,144}... | collective-permute-start | bytes 2359304 | tf_op jit(solution)/shard_map/ppermute | solution.py:14
  96.9 16.9 %collective-permute-done.4 = bf16[16,6,32,128]{3,2,1,0:T(8,128)(2,1)S(1)} collective-permute-done((bf16[16,6,32,128]{3,2,1,0:T(8,128)(2,1)S(1)}, bf16[16,6,32,128]{3,2,1,0:T(8,128)(2,1)S(1)}, u32[]{:S(2)}, u32[]{:S(2)}) %collective-permute-start.4) | collective-permute-done | bytes 786464 | tf_op jit(solution)/shard_map/ppermute | solution.py:14
  113.8 19.2 %collective-permute-done.5 = bf16[16,6,32,128]{3,2,1,0:T(8,128)(2,1)S(1)} collective-permute-done((bf16[16,6,32,128]{3,2,1,0:T(8,128)(2,1)S(1)}, bf16[16,6,32,128]{3,2,1,0:T(8,128)(2,1)S(1)}, u32[]{:S(2)}, u32[]{:S(2)}) %collective-permute-start.5) | collective-permute-done | bytes 786464 | tf_op jit(solution)/shard_map/ppermute | solution.py:14
  133.0 1.7 pad_maximum_fusion
  134.7 4.1 %all-to-all-start.2 = ((bf16[16,3,6,32,128]{4,3,2,1,0:T(8,128)(2,1)}), bf16[16,3,6,32,128]{4,3,2,1,0:T(8,128)(2,1)S(1)}, u32[]{:S(2)}, u32[]{:S(2)}) async-start(bf16[16,3,6,32,128]{4,3,2,1,0:T(8,128)(2,1)} %pad_maximum_fusion), calls=%async_computation.2 | async-start | bytes 4718592 | tf_op jit(solution)/shard_map/all_to_all | solution.py:93
  138.9 32.1 %all-to-all-done.2 = bf16[16,3,6,32,128]{4,3,2,1,0:T(8,128)(2,1)S(1)} async-done(((bf16[16,3,6,32,128]{4,3,2,1,0:T(8,128)(2,1)}), bf16[16,3,6,32,128]{4,3,2,1,0:T(8,128)(2,1)S(1)}, u32[]{:S(2)}, u32[]{:S(2)}) %all-to-all-start.2) | async-done | bytes 2359328 | tf_op jit(solution)/shard_map/all_to_all | solution.py:93
  170.9 2.3 %fusion.11 = f32[128,32,128,1,1,1]{0,2,5,1,4,3:T(8,128)S(1)} fusion(bf16[8,2,3,6,32,128]{5,4,3,2,1,0:T(8,128)(2,1)S(1)} %bitcast.84, f32[3,8,128]{2,1,0:T(8,128)S(1)} %bitcast.103, s32[2,6]{1,0:T(2,128)S(1)} %multiply_add_fusion, s32[3,8,128]{2,1,0:T(8,128)S(1)} %bitcast.101, pred[3,8,128]{2,1,0:T(8,128)(4,1)S(1)} %bitcast.106), kind=kOutput, calls=%fused_computation.14 | convolution fusion | flops 302100480 | bytes 4484144 | tf_op jit(solution)/shard_map/rqcht,qcrhkl->tkl/dot_general | solution.py:96
  173.3 2.5 %fusion.8 = bf16[128,32,128]{0,2,1:T(8,128)(2,1)S(1)} fusion(f32[128,32,128,1,1,1]{0,2,5,1,4,3:T(8,128)S(1)} %fusion.11, bf16[8,2,3,6,32,128]{5,4,3,2,1,0:T(8,128)(2,1)S(1)} %bitcast.85, f32[3,8,128]{2,1,0:T(8,128)S(1)} %bitcast.104, s32[2,6]{1,0:T(2,128)S(1)} %multiply_add_fusion, s32[3,8,128]{2,1,0:T(8,128)S(1)} %bitcast.102, ...), kind=kOutput, calls=%fused_computation.11 | convolution fusion | flops 303296512 | bytes 5532720 | tf_op jit(solution)/shard_map/rqcht,qcrhkl->tkl/dot_general | solution.py:98
  175.8 1.3 copy.68
  (29 shorter events, 2.1 us)
Async XLA Ops:
  0.0 72.1 %collective-permute-start.2 = (bf16[1,4096,768]{2,1,0:T(8,128)(2,1)}, bf16[1,4096,768]{2,1,0:T(8,128)(2,1)}, u32[]{:S(2)}, u32[]{:S(2)}) collective-permute-start(bf16[1,4096,768]{2,1,0:T(8,128)(2,1)} %param.8), channel_id=1, source_target_pairs={{0,1},{1,0},{2,3},{3,2},{4,5},{5,4},{6,7},{7,6},{8,9},{9,8},{10,11... | collective-permute-start | bytes 18874376 | tf_op jit(solution)/shard_map/ppermute | solution.py:20
  4.1 21.4 %collective-permute-start = (bf16[16,6,32,128]{3,2,1,0:T(8,128)(2,1)S(1)}, bf16[16,6,32,128]{3,2,1,0:T(8,128)(2,1)S(1)}, u32[]{:S(2)}, u32[]{:S(2)}) collective-permute-start(bf16[16,6,32,128]{3,2,1,0:T(8,128)(2,1)S(1)} %bitcast.95), channel_id=1, source_target_pairs={{0,240},{16,0},{32,16},{48,32},{64,48},{80,64},{96,80},{112,96},{1... | collective-permute-start | bytes 2359304 | tf_op jit(solution)/shard_map/ppermute | solution.py:14
  6.6 21.4 %collective-permute-start.1 = (bf16[16,6,32,128]{3,2,1,0:T(8,128)(2,1)S(1)}, bf16[16,6,32,128]{3,2,1,0:T(8,128)(2,1)}, u32[]{:S(2)}, u32[]{:S(2)}) collective-permute-start(bf16[16,6,32,128]{3,2,1,0:T(8,128)(2,1)S(1)} %bitcast.96), channel_id=1, source_target_pairs={{0,224},{16,240},{32,0},{48,16},{64,32},{80,48},{96,64},{112,80},{... | collective-permute-start | bytes 2359304 | tf_op jit(solution)/shard_map/ppermute | solution.py:14
  11.8 24.1 %all-to-all-start = ((bf16[16,6,32,128]{3,2,1,0:T(8,128)(2,1)}), bf16[16,6,32,128]{3,2,1,0:T(8,128)(2,1)S(1)}, u32[]{:S(2)}, u32[]{:S(2)}) async-start(bf16[16,6,32,128]{3,2,1,0:T(8,128)(2,1)} %bitcast.10), calls=%async_computation | async-start | bytes 1572864 | tf_op jit(solution)/shard_map/all_to_all | solution.py:80
  35.9 27.4 %all-to-all-start.1 = ((bf16[16,2,6,32,128]{4,3,2,1,0:T(8,128)(2,1)}), bf16[16,2,6,32,128]{4,3,2,1,0:T(8,128)(2,1)S(1)}, u32[]{:S(2)}, u32[]{:S(2)}) async-start(bf16[16,2,6,32,128]{4,3,2,1,0:T(8,128)(2,1)} %copy.63), calls=%async_computation.1 | async-start | bytes 3145728 | tf_op jit(solution)/shard_map/all_to_all | solution.py:82
  39.6 37.3 %collective-permute-start.3 = (bf16[1,384,4096]{2,1,0:T(8,128)(2,1)}, bf16[1,384,4096]{2,1,0:T(8,128)(2,1)}, u32[]{:S(2)}, u32[]{:S(2)}) collective-permute-start(bf16[1,384,4096]{2,1,0:T(8,128)(2,1)} %param.9), channel_id=1, source_target_pairs={{0,1},{1,0},{2,3},{3,2},{4,5},{5,4},{6,7},{7,6},{8,9},{9,8},{10,11... | collective-permute-start | bytes 9437192 | tf_op jit(solution)/shard_map/ppermute | solution.py:20
  63.4 1.7 copy-start.1
  65.7 5.0 %copy-start = (bf16[1,384,4096]{2,1,0:T(8,128)(2,1)S(1)}, bf16[1,384,4096]{2,1,0:T(8,128)(2,1)}, u32[]{:S(2)}) copy-start(bf16[1,384,4096]{2,1,0:T(8,128)(2,1)} %param.9) | copy-start | bytes 9437188
  80.7 33.1 %collective-permute-start.4 = (bf16[16,6,32,128]{3,2,1,0:T(8,128)(2,1)S(1)}, bf16[16,6,32,128]{3,2,1,0:T(8,128)(2,1)S(1)}, u32[]{:S(2)}, u32[]{:S(2)}) collective-permute-start(bf16[16,6,32,128]{3,2,1,0:T(8,128)(2,1)S(1)} %bitcast.97), channel_id=1, source_target_pairs={{0,16},{16,32},{32,48},{48,64},{64,80},{80,96},{96,112},{112,128},... | collective-permute-start | bytes 2359304 | tf_op jit(solution)/shard_map/ppermute | solution.py:14
  94.7 38.3 %collective-permute-start.5 = (bf16[16,6,32,128]{3,2,1,0:T(8,128)(2,1)S(1)}, bf16[16,6,32,128]{3,2,1,0:T(8,128)(2,1)S(1)}, u32[]{:S(2)}, u32[]{:S(2)}) collective-permute-start(bf16[16,6,32,128]{3,2,1,0:T(8,128)(2,1)S(1)} %bitcast.98), channel_id=1, source_target_pairs={{0,32},{16,48},{32,64},{48,80},{64,96},{80,112},{96,128},{112,144}... | collective-permute-start | bytes 2359304 | tf_op jit(solution)/shard_map/ppermute | solution.py:14
  134.7 4.1 %copy-start.2 = (s32[128,8]{0,1:T(8,128)S(1)}, s32[128,8]{0,1:T(8,128)}, u32[]{:S(2)}) copy-start(s32[128,8]{0,1:T(8,128)} %param.6) | copy-start | bytes 12292
  134.7 4.1 %copy-start.3 = (f32[128,8]{0,1:T(8,128)S(1)}, f32[128,8]{0,1:T(8,128)}, u32[]{:S(2)}) copy-start(f32[128,8]{0,1:T(8,128)} %param.7) | copy-start | bytes 12292
  134.7 36.3 %all-to-all-start.2 = ((bf16[16,3,6,32,128]{4,3,2,1,0:T(8,128)(2,1)}), bf16[16,3,6,32,128]{4,3,2,1,0:T(8,128)(2,1)S(1)}, u32[]{:S(2)}, u32[]{:S(2)}) async-start(bf16[16,3,6,32,128]{4,3,2,1,0:T(8,128)(2,1)} %pad_maximum_fusion), calls=%async_computation.2 | async-start | bytes 4718592 | tf_op jit(solution)/shard_map/all_to_all | solution.py:93

commit v7 on v6

--- a/solution.py
+++ b/solution.py
@@ -12,6 +12,31 @@
     count = lax.axis_size(axis)
     pairs = [(source, (source + steps) % count) for source in range(count)]
     return lax.ppermute(value, axis, pairs)
+
+
+def one_step(value, axis, direction):
+    count = lax.axis_size(axis)
+    here = lax.axis_index(axis)
+
+    def same_row(source):
+        return source // 2 == ((source + direction) % count) // 2
+
+    near = [s for s in range(count) if same_row(s)]
+    far = [s for s in range(count) if not same_row(s)]
+    direct = lax.ppermute(value, axis, [(s, (s + direction) % count) for s in near])
+    half = value.shape[0] // 2
+    first, second = value[:half], value[half:]
+    first = lax.ppermute(first, axis, [(s, (s + 2 * direction) % count) for s in far])
+    first = lax.ppermute(
+        first, axis, [((s + 2 * direction) % count, (s + direction) % count) for s in far]
+    )
+    second = lax.ppermute(second, axis, [(s, (s - direction) % count) for s in far])
+    second = lax.ppermute(
+        second, axis, [((s - direction) % count, (s + direction) % count) for s in far]
+    )
+    routed = jnp.concatenate([first, second], axis=0)
+    arrived_direct = ((here - direction) % count) // 2 == here // 2
+    return jnp.where(arrived_direct, direct, routed)
 
 
 def swapped_with_partner(value, axis):
@@ -75,7 +100,10 @@
     far = []
     for rotation in range(1, STEPS):
         outgoing = picked[rotation].reshape(inner_count, half_cap, lanes_major, 128)
-        far.append(shifted(outgoing, "blk", -rotation))
+        if rotation == 1:
+            far.append(one_step(outgoing, "blk", -1))
+        else:
+            far.append(shifted(outgoing, "blk", -rotation))
     near = picked[0].reshape(inner_count, half_cap, lanes_major, 128)
     near = lax.all_to_all(near, "inner", split_axis=0, concat_axis=0, tiled=True)
     far = jnp.stack(far, axis=1)
@@ -88,7 +116,10 @@
 
     results = [done[0]]
     for rotation in range(1, STEPS):
-        results.append(shifted(done[rotation], "blk", rotation))
+        if rotation == 1:
+            results.append(one_step(done[rotation], "blk", 1))
+        else:
+            results.append(shifted(done[rotation], "blk", rotation))
     returned = jnp.stack(results, axis=1)
     returned = lax.all_to_all(returned, "inner", split_axis=0, concat_axis=0, tiled=True)
     returned = returned.reshape(group_count, SPLIT, STEPS, half_cap, lanes_major, 128)

time: 178 us -> 180 us (1.011)
  the two profiles are of different devices: /device:TPU:2 before, /device:TPU:1 now
where the time goes in v7:
time: 180 us; the launch traced here: 179 us
  waiting for transfers between devices  91.5 us (51%)
  starting transfers between devices  48.5 us (27%)
  matrix products  20.1 us (11%)
  local copies, waits for them, and re-layouts  12.4 us (7%)
  other arithmetic  6.31 us (4%)
    all_to_all x1, waiting for transfers between devices, on_device(): lax.all_to_all(returned, 'inner', split_axis=0, concat_axis=0, tiled=True)  31.3 us
    all_to_all x1, waiting for transfers between devices, on_device(): far = lax.all_to_all(far, 'inner', split_axis=0, concat_axis=0, tiled=True)  21.3 us
    ppermute x2, waiting for transfers between devices, one_step(): lax.ppermute(second, axis, [((s - direction) % count, (s + direction) % c...  11.7 us
    dot_general x2, matrix products, one_half(): projected = jnp.dot(rows, w_in_now, preferred_element_type=jnp.float32)  9.78 us
    all_to_all x1, starting transfers between devices, on_device(): lax.all_to_all(near, 'inner', split_axis=0, concat_axis=0, tiled=True)  8.07 us
    ppermute x2, waiting for transfers between devices, one_step(): lax.ppermute(second, axis, [(s, (s - direction) % count) for s in far])  7.83 us
    ppermute x2, starting transfers between devices, one_step(): lax.ppermute(value, axis, [(s, (s + direction) % count) for s in near])  7.67 us
    ppermute x2, starting transfers between devices, one_step(): lax.ppermute(first, axis, [(s, (s + 2 * direction) % count) for s in far])  7.19 us
  transfers between devices with their start and end apart: 17, of which 10 were waited for; matrix products, arithmetic and copies ran while one was open for 14% of the time, Pallas kernels for 0%

profile of v7, /device:TPU:1, one launch (start us, length us, event | category | flops | bytes accessed | tf_op | source)
XLA Modules:
  0.0 179.2 jit_solution(11921778664590395926)
XLA Ops:
  0.0 3.2 %collective-permute-start.6 = (bf16[1,4096,768]{2,1,0:T(8,128)(2,1)}, bf16[1,4096,768]{2,1,0:T(8,128)(2,1)}, u32[]{:S(2)}, u32[]{:S(2)}) collective-permute-start(bf16[1,4096,768]{2,1,0:T(8,128)(2,1)} %param.8), channel_id=1, source_target_pairs={{0,1},{1,0},{2,3},{3,2},{4,5},{5,4},{6,7},{7,6},{8,9},{9,8},{10,11... | collective-permute-start | bytes 18874376 | tf_op jit(solution)/shard_map/ppermute | solution.py:45
  4.7 1.5 copy.87
  9.6 5.8 %collective-permute-start.1 = (bf16[8,6,32,128]{3,2,1,0:T(8,128)(2,1)S(1)}, bf16[8,6,32,128]{3,2,1,0:T(8,128)(2,1)}, u32[]{:S(2)}, u32[]{:S(2)}) collective-permute-start(bf16[8,6,32,128]{3,2,1,0:T(8,128)(2,1)S(1)} %bitcast.111), channel_id=1, source_target_pairs={{0,224},{32,0},{64,32},{96,64},{128,96},{160,128},{192,160},{224,1... | collective-permute-start | bytes 1179656 | tf_op jit(solution)/shard_map/ppermute | solution.py:29
  15.4 2.0 %collective-permute-start.3 = (bf16[8,6,32,128]{3,2,1,0:T(8,128)(2,1)S(1)}, bf16[8,6,32,128]{3,2,1,0:T(8,128)(2,1)}, u32[]{:S(2)}, u32[]{:S(2)}) collective-permute-start(bf16[8,6,32,128]{3,2,1,0:T(8,128)(2,1)S(1)} %bitcast.109), channel_id=1, source_target_pairs={{0,16},{32,48},{64,80},{96,112},{128,144},{160,176},{192,208},{224... | collective-permute-start | bytes 1179656 | tf_op jit(solution)/shard_map/ppermute | solution.py:33
  17.6 2.3 %collective-permute-start.5 = (bf16[16,6,32,128]{3,2,1,0:T(8,128)(2,1)S(1)}, bf16[16,6,32,128]{3,2,1,0:T(8,128)(2,1)}, u32[]{:S(2)}, u32[]{:S(2)}) collective-permute-start(bf16[16,6,32,128]{3,2,1,0:T(8,128)(2,1)S(1)} %bitcast.107), channel_id=1, source_target_pairs={{0,224},{16,240},{32,0},{48,16},{64,32},{80,48},{96,64},{112,80},{... | collective-permute-start | bytes 2359304 | tf_op jit(solution)/shard_map/ppermute | solution.py:14
  20.0 3.9 %collective-permute-done.1 = bf16[8,6,32,128]{3,2,1,0:T(8,128)(2,1)} collective-permute-done((bf16[8,6,32,128]{3,2,1,0:T(8,128)(2,1)S(1)}, bf16[8,6,32,128]{3,2,1,0:T(8,128)(2,1)}, u32[]{:S(2)}, u32[]{:S(2)}) %collective-permute-start.1) | collective-permute-done | bytes 393248 | tf_op jit(solution)/shard_map/ppermute | solution.py:29
  23.9 1.3 collective-permute-start.2
  25.3 1.5 collective-permute-start.4
  27.8 8.1 %all-to-all-start = ((bf16[16,6,32,128]{3,2,1,0:T(8,128)(2,1)}), bf16[16,6,32,128]{3,2,1,0:T(8,128)(2,1)S(1)}, u32[]{:S(2)}, u32[]{:S(2)}) async-start(bf16[16,6,32,128]{3,2,1,0:T(8,128)(2,1)} %bitcast.10), calls=%async_computation | async-start | bytes 1572864 | tf_op jit(solution)/shard_map/all_to_all | solution.py:108
  37.0 3.8 %collective-permute-done.5 = bf16[16,6,32,128]{3,2,1,0:T(8,128)(2,1)} collective-permute-done((bf16[16,6,32,128]{3,2,1,0:T(8,128)(2,1)S(1)}, bf16[16,6,32,128]{3,2,1,0:T(8,128)(2,1)}, u32[]{:S(2)}, u32[]{:S(2)}) %collective-permute-start.5) | collective-permute-done | bytes 786464 | tf_op jit(solution)/shard_map/ppermute | solution.py:14
  42.0 1.5 copy.71
  43.5 6.7 %all-to-all-done = bf16[16,6,32,128]{3,2,1,0:T(8,128)(2,1)S(1)} async-done(((bf16[16,6,32,128]{3,2,1,0:T(8,128)(2,1)}), bf16[16,6,32,128]{3,2,1,0:T(8,128)(2,1)S(1)}, u32[]{:S(2)}, u32[]{:S(2)}) %all-to-all-start) | async-done | bytes 786464 | tf_op jit(solution)/shard_map/all_to_all | solution.py:108
  50.3 4.4 %all-to-all-start.1 = ((bf16[16,2,6,32,128]{4,3,2,1,0:T(8,128)(2,1)}), bf16[16,2,6,32,128]{4,3,2,1,0:T(8,128)(2,1)S(1)}, u32[]{:S(2)}, u32[]{:S(2)}) async-start(bf16[16,2,6,32,128]{4,3,2,1,0:T(8,128)(2,1)} %copy.71), calls=%async_computation.1 | async-start | bytes 3145728 | tf_op jit(solution)/shard_map/all_to_all | solution.py:110
  56.3 21.3 %all-to-all-done.1 = bf16[16,2,6,32,128]{4,3,2,1,0:T(8,128)(2,1)S(1)} async-done(((bf16[16,2,6,32,128]{4,3,2,1,0:T(8,128)(2,1)}), bf16[16,2,6,32,128]{4,3,2,1,0:T(8,128)(2,1)S(1)}, u32[]{:S(2)}, u32[]{:S(2)}) %all-to-all-start.1) | async-done | bytes 1572896 | tf_op jit(solution)/shard_map/all_to_all | solution.py:110
  77.9 1.4 copy-done.1
  79.9 5.0 %fusion.2 = f32[288,768]{1,0:T(8,128)S(1)} fusion(bf16[288,4096]{1,0:T(8,128)(2,1)S(1)} %bitcast_dynamic-update-slice_fusion, bf16[1,4096,768]{2,1,0:T(8,128)(2,1)} %param.8), kind=kOutput, calls=%fused_computation.2 | convolution fusion | flops 1811939328 | bytes 9535488 | tf_op jit(solution)/shard_map/dot_general | solution.py:52
  84.9 1.4 fusion.6
  86.3 4.8 %fusion = f32[288,768]{1,0:T(8,128)S(1)} fusion(bf16[288,4096]{1,0:T(8,128)(2,1)S(1)} %bitcast_dynamic-update-slice_fusion, bf16[1,4096,768]{2,1,0:T(8,128)(2,1)} %collective-permute-done.6), kind=kOutput, calls=%fused_computation | convolution fusion | flops 1811939328 | bytes 9535488 | tf_op jit(solution)/shard_map/dot_general | solution.py:52
  91.2 3.3 %fusion.4 = bf16[288,4096]{1,0:T(8,128)(2,1)S(1)} fusion(f32[288,4096]{1,0:T(8,128)S(1)} %fusion.6, bf16[1,384,4096]{2,1,0:T(8,128)(2,1)} %collective-permute-done.7, f32[288,768]{1,0:T(8,128)S(1)} %fusion), kind=kOutput, calls=%fused_computation.5 | convolution fusion | flops 908992512 | bytes 11108352 | tf_op jit(solution)/shard_map/dot_general | solution.py:56
  94.9 6.4 %collective-permute-start.8 = (bf16[16,6,32,128]{3,2,1,0:T(8,128)(2,1)S(1)}, bf16[16,6,32,128]{3,2,1,0:T(8,128)(2,1)S(1)}, u32[]{:S(2)}, u32[]{:S(2)}) collective-permute-start(bf16[16,6,32,128]{3,2,1,0:T(8,128)(2,1)S(1)} %bitcast.108), channel_id=1, source_target_pairs={{0,16},{32,48},{64,80},{96,112},{128,144},{160,176},{192,208},{224... | collective-permute-start | bytes 2359304 | tf_op jit(solution)/shard_map/ppermute | solution.py:26
  101.4 1.4 collective-permute-start.9
  102.9 1.3 collective-permute-start.11
  106.5 7.8 %collective-permute-done.11 = bf16[8,6,32,128]{3,2,1,0:T(8,128)(2,1)} collective-permute-done((bf16[8,6,32,128]{3,2,1,0:T(8,128)(2,1)S(1)}, bf16[8,6,32,128]{3,2,1,0:T(8,128)(2,1)}, u32[]{:S(2)}, u32[]{:S(2)}) %collective-permute-start.11) | collective-permute-done | bytes 393248 | tf_op jit(solution)/shard_map/ppermute | solution.py:33
  114.3 1.9 %collective-permute-start.12 = (bf16[8,6,32,128]{3,2,1,0:T(8,128)(2,1)}, bf16[8,6,32,128]{3,2,1,0:T(8,128)(2,1)}, u32[]{:S(2)}, u32[]{:S(2)}) collective-permute-start(bf16[8,6,32,128]{3,2,1,0:T(8,128)(2,1)} %collective-permute-done.11), channel_id=1, source_target_pairs={{0,32},{32,64},{64,96},{96,128},{128,160},{160,192},{192,224},{224... | collective-permute-start | bytes 1179656 | tf_op jit(solution)/shard_map/ppermute | solution.py:34
  117.2 4.1 %collective-permute-done.10 = bf16[8,6,32,128]{3,2,1,0:T(8,128)(2,1)S(1)} collective-permute-done((bf16[8,6,32,128]{3,2,1,0:T(8,128)(2,1)}, bf16[8,6,32,128]{3,2,1,0:T(8,128)(2,1)S(1)}, u32[]{:S(2)}, u32[]{:S(2)}) %collective-permute-start.10) | collective-permute-done | bytes 393248 | tf_op jit(solution)/shard_map/ppermute | solution.py:30
  121.3 11.7 %collective-permute-done.12 = bf16[8,6,32,128]{3,2,1,0:T(8,128)(2,1)} collective-permute-done((bf16[8,6,32,128]{3,2,1,0:T(8,128)(2,1)}, bf16[8,6,32,128]{3,2,1,0:T(8,128)(2,1)}, u32[]{:S(2)}, u32[]{:S(2)}) %collective-permute-start.12) | collective-permute-done | bytes 393248 | tf_op jit(solution)/shard_map/ppermute | solution.py:34
  134.1 1.7 pad_maximum_fusion
  135.8 5.8 %all-to-all-start.2 = ((bf16[16,3,6,32,128]{4,3,2,1,0:T(8,128)(2,1)}), bf16[16,3,6,32,128]{4,3,2,1,0:T(8,128)(2,1)S(1)}, u32[]{:S(2)}, u32[]{:S(2)}) async-start(bf16[16,3,6,32,128]{4,3,2,1,0:T(8,128)(2,1)} %pad_maximum_fusion), calls=%async_computation.2 | async-start | bytes 4718592 | tf_op jit(solution)/shard_map/all_to_all | solution.py:124
  141.7 31.3 %all-to-all-done.2 = bf16[16,3,6,32,128]{4,3,2,1,0:T(8,128)(2,1)S(1)} async-done(((bf16[16,3,6,32,128]{4,3,2,1,0:T(8,128)(2,1)}), bf16[16,3,6,32,128]{4,3,2,1,0:T(8,128)(2,1)S(1)}, u32[]{:S(2)}, u32[]{:S(2)}) %all-to-all-start.2) | async-done | bytes 2359328 | tf_op jit(solution)/shard_map/all_to_all | solution.py:124
  173.0 2.3 %fusion.11 = f32[128,32,128,1,1,1]{0,2,5,1,4,3:T(8,128)S(1)} fusion(bf16[8,2,3,6,32,128]{5,4,3,2,1,0:T(8,128)(2,1)S(1)} %bitcast.96, f32[3,8,128]{2,1,0:T(8,128)S(1)} %bitcast.116, s32[2,6]{1,0:T(2,128)S(1)} %copy-done.3, s32[3,8,128]{2,1,0:T(8,128)S(1)} %bitcast.114, pred[3,8,128]{2,1,0:T(8,128)(4,1)S(1)} %bitcast.119), kind=kOutput, calls=%fused_computation.14 | convolution fusion | flops 302100480 | bytes 4484144 | tf_op jit(solution)/shard_map/rqcht,qcrhkl->tkl/dot_general | solution.py:127
  175.4 2.5 %fusion.8 = bf16[128,32,128]{0,2,1:T(8,128)(2,1)S(1)} fusion(f32[128,32,128,1,1,1]{0,2,5,1,4,3:T(8,128)S(1)} %fusion.11, bf16[8,2,3,6,32,128]{5,4,3,2,1,0:T(8,128)(2,1)S(1)} %bitcast.97, f32[3,8,128]{2,1,0:T(8,128)S(1)} %bitcast.117, s32[2,6]{1,0:T(2,128)S(1)} %copy-done.3, s32[3,8,128]{2,1,0:T(8,128)S(1)} %bitcast.115, pred[3,8,128]{2,1,0:T(8,128)(4,1)S(1)} %bitcast.120), kind=kOutput, calls=%fused_computation.11 | convolution fusion | flops 303296512 | bytes 5532720 | tf_op jit(solution)/shard_map/rqcht,qcrhkl->tkl/dot_general | solution.py:129
  177.8 1.3 copy.76
  (61 shorter events, 16.0 us)
Async XLA Ops:
  0.0 86.3 %collective-permute-start.6 = (bf16[1,4096,768]{2,1,0:T(8,128)(2,1)}, bf16[1,4096,768]{2,1,0:T(8,128)(2,1)}, u32[]{:S(2)}, u32[]{:S(2)}) collective-permute-start(bf16[1,4096,768]{2,1,0:T(8,128)(2,1)} %param.8), channel_id=1, source_target_pairs={{0,1},{1,0},{2,3},{3,2},{4,5},{5,4},{6,7},{7,6},{8,9},{9,8},{10,11... | collective-permute-start | bytes 18874376 | tf_op jit(solution)/shard_map/ppermute | solution.py:45
  3.4 0.8 copy-start.5
  6.2 0.5 copy-start.2
  7.9 28.0 %collective-permute-start = (bf16[16,6,32,128]{3,2,1,0:T(8,128)(2,1)S(1)}, bf16[16,6,32,128]{3,2,1,0:T(8,128)(2,1)S(1)}, u32[]{:S(2)}, u32[]{:S(2)}) collective-permute-start(bf16[16,6,32,128]{3,2,1,0:T(8,128)(2,1)S(1)} %bitcast.106), channel_id=1, source_target_pairs={{16,0},{48,32},{80,64},{112,96},{144,128},{176,160},{208,192},{240... | collective-permute-start | bytes 2359304 | tf_op jit(solution)/shard_map/ppermute | solution.py:26
  9.6 14.3 %collective-permute-start.1 = (bf16[8,6,32,128]{3,2,1,0:T(8,128)(2,1)S(1)}, bf16[8,6,32,128]{3,2,1,0:T(8,128)(2,1)}, u32[]{:S(2)}, u32[]{:S(2)}) collective-permute-start(bf16[8,6,32,128]{3,2,1,0:T(8,128)(2,1)S(1)} %bitcast.111), channel_id=1, source_target_pairs={{0,224},{32,0},{64,32},{96,64},{128,96},{160,128},{192,160},{224,1... | collective-permute-start | bytes 1179656 | tf_op jit(solution)/shard_map/ppermute | solution.py:29
  15.4 9.8 %collective-permute-start.3 = (bf16[8,6,32,128]{3,2,1,0:T(8,128)(2,1)S(1)}, bf16[8,6,32,128]{3,2,1,0:T(8,128)(2,1)}, u32[]{:S(2)}, u32[]{:S(2)}) collective-permute-start(bf16[8,6,32,128]{3,2,1,0:T(8,128)(2,1)S(1)} %bitcast.109), channel_id=1, source_target_pairs={{0,16},{32,48},{64,80},{96,112},{128,144},{160,176},{192,208},{224... | collective-permute-start | bytes 1179656 | tf_op jit(solution)/shard_map/ppermute | solution.py:33
  17.6 23.1 %collective-permute-start.5 = (bf16[16,6,32,128]{3,2,1,0:T(8,128)(2,1)S(1)}, bf16[16,6,32,128]{3,2,1,0:T(8,128)(2,1)}, u32[]{:S(2)}, u32[]{:S(2)}) collective-permute-start(bf16[16,6,32,128]{3,2,1,0:T(8,128)(2,1)S(1)} %bitcast.107), channel_id=1, source_target_pairs={{0,224},{16,240},{32,0},{48,16},{64,32},{80,48},{96,64},{112,80},{... | collective-permute-start | bytes 2359304 | tf_op jit(solution)/shard_map/ppermute | solution.py:14
  23.9 12.0 %collective-permute-start.2 = (bf16[8,6,32,128]{3,2,1,0:T(8,128)(2,1)}, bf16[8,6,32,128]{3,2,1,0:T(8,128)(2,1)S(1)}, u32[]{:S(2)}, u32[]{:S(2)}) collective-permute-start(bf16[8,6,32,128]{3,2,1,0:T(8,128)(2,1)} %collective-permute-done.1), channel_id=1, source_target_pairs={{224,240},{0,16},{32,48},{64,80},{96,112},{128,144},{160,176},{192... | collective-permute-start | bytes 1179656 | tf_op jit(solution)/shard_map/ppermute | solution.py:30
  25.3 10.6 %collective-permute-start.4 = (bf16[8,6,32,128]{3,2,1,0:T(8,128)(2,1)}, bf16[8,6,32,128]{3,2,1,0:T(8,128)(2,1)}, u32[]{:S(2)}, u32[]{:S(2)}) collective-permute-start(bf16[8,6,32,128]{3,2,1,0:T(8,128)(2,1)} %collective-permute-done.3), channel_id=1, source_target_pairs={{16,240},{48,16},{80,48},{112,80},{144,112},{176,144},{208,176},{2... | collective-permute-start | bytes 1179656 | tf_op jit(solution)/shard_map/ppermute | solution.py:34
  27.8 22.5 %all-to-all-start = ((bf16[16,6,32,128]{3,2,1,0:T(8,128)(2,1)}), bf16[16,6,32,128]{3,2,1,0:T(8,128)(2,1)S(1)}, u32[]{:S(2)}, u32[]{:S(2)}) async-start(bf16[16,6,32,128]{3,2,1,0:T(8,128)(2,1)} %bitcast.10), calls=%async_computation | async-start | bytes 1572864 | tf_op jit(solution)/shard_map/all_to_all | solution.py:108
  50.3 27.3 %all-to-all-start.1 = ((bf16[16,2,6,32,128]{4,3,2,1,0:T(8,128)(2,1)}), bf16[16,2,6,32,128]{4,3,2,1,0:T(8,128)(2,1)S(1)}, u32[]{:S(2)}, u32[]{:S(2)}) async-start(bf16[16,2,6,32,128]{4,3,2,1,0:T(8,128)(2,1)} %copy.71), calls=%async_computation.1 | async-start | bytes 3145728 | tf_op jit(solution)/shard_map/all_to_all | solution.py:110
  54.6 36.5 %collective-permute-start.7 = (bf16[1,384,4096]{2,1,0:T(8,128)(2,1)}, bf16[1,384,4096]{2,1,0:T(8,128)(2,1)}, u32[]{:S(2)}, u32[]{:S(2)}) collective-permute-start(bf16[1,384,4096]{2,1,0:T(8,128)(2,1)} %param.9), channel_id=1, source_target_pairs={{0,1},{1,0},{2,3},{3,2},{4,5},{5,4},{6,7},{7,6},{8,9},{9,8},{10,11... | collective-permute-start | bytes 9437192 | tf_op jit(solution)/shard_map/ppermute | solution.py:45
  77.6 1.7 copy-start.1
  79.9 5.0 %copy-start = (bf16[1,384,4096]{2,1,0:T(8,128)(2,1)S(1)}, bf16[1,384,4096]{2,1,0:T(8,128)(2,1)}, u32[]{:S(2)}) copy-start(bf16[1,384,4096]{2,1,0:T(8,128)(2,1)} %param.9) | copy-start | bytes 9437188
  94.9 22.2 %collective-permute-start.8 = (bf16[16,6,32,128]{3,2,1,0:T(8,128)(2,1)S(1)}, bf16[16,6,32,128]{3,2,1,0:T(8,128)(2,1)S(1)}, u32[]{:S(2)}, u32[]{:S(2)}) collective-permute-start(bf16[16,6,32,128]{3,2,1,0:T(8,128)(2,1)S(1)} %bitcast.108), channel_id=1, source_target_pairs={{0,16},{32,48},{64,80},{96,112},{128,144},{160,176},{192,208},{224... | collective-permute-start | bytes 2359304 | tf_op jit(solution)/shard_map/ppermute | solution.py:26
  101.4 3.8 %collective-permute-start.9 = (bf16[8,6,32,128]{3,2,1,0:T(8,128)(2,1)S(1)}, bf16[8,6,32,128]{3,2,1,0:T(8,128)(2,1)}, u32[]{:S(2)}, u32[]{:S(2)}) collective-permute-start(bf16[8,6,32,128]{3,2,1,0:T(8,128)(2,1)S(1)} %bitcast.112), channel_id=1, source_target_pairs={{16,48},{48,80},{80,112},{112,144},{144,176},{176,208},{208,240},{... | collective-permute-start | bytes 1179656 | tf_op jit(solution)/shard_map/ppermute | solution.py:29
  102.9 11.4 %collective-permute-start.11 = (bf16[8,6,32,128]{3,2,1,0:T(8,128)(2,1)S(1)}, bf16[8,6,32,128]{3,2,1,0:T(8,128)(2,1)}, u32[]{:S(2)}, u32[]{:S(2)}) collective-permute-start(bf16[8,6,32,128]{3,2,1,0:T(8,128)(2,1)S(1)} %bitcast.110), channel_id=1, source_target_pairs={{16,0},{48,32},{80,64},{112,96},{144,128},{176,160},{208,192},{240... | collective-permute-start | bytes 1179656 | tf_op jit(solution)/shard_map/ppermute | solution.py:33
  105.2 28.9 %collective-permute-start.13 = (bf16[16,6,32,128]{3,2,1,0:T(8,128)(2,1)}, bf16[16,6,32,128]{3,2,1,0:T(8,128)(2,1)S(1)}, u32[]{:S(2)}, u32[]{:S(2)}) collective-permute-start(bf16[16,6,32,128]{3,2,1,0:T(8,128)(2,1)} %bitcast.61), channel_id=1, source_target_pairs={{0,32},{16,48},{32,64},{48,80},{64,96},{80,112},{96,128},{112,144}... | collective-permute-start | bytes 2359304 | tf_op jit(solution)/shard_map/ppermute | solution.py:14
  105.2 16.0 %collective-permute-start.10 = (bf16[8,6,32,128]{3,2,1,0:T(8,128)(2,1)}, bf16[8,6,32,128]{3,2,1,0:T(8,128)(2,1)S(1)}, u32[]{:S(2)}, u32[]{:S(2)}) collective-permute-start(bf16[8,6,32,128]{3,2,1,0:T(8,128)(2,1)} %collective-permute-done.9), channel_id=1, source_target_pairs={{48,32},{80,64},{112,96},{144,128},{176,160},{208,192},{240,224},{... | collective-permute-start | bytes 1179656 | tf_op jit(solution)/shard_map/ppermute | solution.py:30
  114.3 18.7 %collective-permute-start.12 = (bf16[8,6,32,128]{3,2,1,0:T(8,128)(2,1)}, bf16[8,6,32,128]{3,2,1,0:T(8,128)(2,1)}, u32[]{:S(2)}, u32[]{:S(2)}) collective-permute-start(bf16[8,6,32,128]{3,2,1,0:T(8,128)(2,1)} %collective-permute-done.11), channel_id=1, source_target_pairs={{0,32},{32,64},{64,96},{96,128},{128,160},{160,192},{192,224},{224... | collective-permute-start | bytes 1179656 | tf_op jit(solution)/shard_map/ppermute | solution.py:34
  135.8 5.8 %copy-start.4 = (s32[128,8]{0,1:T(8,128)S(1)}, s32[128,8]{0,1:T(8,128)}, u32[]{:S(2)}) copy-start(s32[128,8]{0,1:T(8,128)} %param.6) | copy-start | bytes 12292
  135.8 5.8 %copy-start.6 = (s32[24]{0:T(128)S(1)}, s32[24]{0:T(128)}, u32[]{:S(2)}) copy-start(s32[24]{0:T(128)} %copy-done.5) | copy-start | bytes 292
  135.8 5.8 %copy-start.7 = (f32[128,8]{0,1:T(8,128)S(1)}, f32[128,8]{0,1:T(8,128)}, u32[]{:S(2)}) copy-start(f32[128,8]{0,1:T(8,128)} %param.7) | copy-start | bytes 12292
  135.8 37.2 %copy-start.3 = (s32[2,6]{1,0:T(2,128)S(1)}, s32[2,6]{1,0:T(2,128)}, u32[]{:S(2)}) copy-start(s32[2,6]{1,0:T(2,128)} %copy-done.2) | copy-start | bytes 148
  135.8 37.2 %all-to-all-start.2 = ((bf16[16,3,6,32,128]{4,3,2,1,0:T(8,128)(2,1)}), bf16[16,3,6,32,128]{4,3,2,1,0:T(8,128)(2,1)S(1)}, u32[]{:S(2)}, u32[]{:S(2)}) async-start(bf16[16,3,6,32,128]{4,3,2,1,0:T(8,128)(2,1)} %pad_maximum_fusion), calls=%async_computation.2 | async-start | bytes 4718592 | tf_op jit(solution)/shard_map/all_to_all | solution.py:124

commit v8 on v5

--- a/solution.py
+++ b/solution.py
@@ -86,13 +86,12 @@
     done = whole_expert(rows, w_in[0], w_out[0], w_in_other[0], w_out_other[0])
     done = done.reshape(STEPS, inner_count, half_cap, lanes_major, 128)
 
+    far_back = [shifted(done[rotation], "blk", rotation) for rotation in range(1, STEPS)]
+    near_back = lax.all_to_all(done[0], "inner", split_axis=0, concat_axis=0, tiled=True)
     far_back = lax.all_to_all(
-        done[1:].transpose(1, 0, 2, 3, 4), "inner", split_axis=0, concat_axis=0, tiled=True
+        jnp.stack(far_back, axis=1), "inner", split_axis=0, concat_axis=0, tiled=True
     )
-    near_back = lax.all_to_all(done[0], "inner", split_axis=0, concat_axis=0, tiled=True)
-    backs = [near_back]
-    for rotation in range(1, STEPS):
-        backs.append(shifted(far_back[:, rotation - 1], "blk", rotation))
+    backs = [near_back] + [far_back[:, rotation - 1] for rotation in range(1, STEPS)]
 
     combined = jnp.zeros((tok_rows, lanes_major, 128), jnp.float32)
     for rotation in range(STEPS):

time: 173 us -> 171 us (0.988)
  waiting for transfers between devices: 93.5 us -> 89.2 us
  other arithmetic: 2.62 us -> 5.31 us
    another operation x0 -> x1, other arithmetic: none -> 2.69 us  [on_device(): jnp.stack(far_back, axis=1)]
    all_to_all x1, waiting for transfers between devices: 22.7 us -> 20.4 us  [on_device(): lax.all_to_all(jnp.stack(far_back, axis=1), 'inner', split_axis=0, concat...]
    ppermute x4, waiting for transfers between devices: 43.5 us -> 41.5 us  [shifted(): return lax.ppermute(value, axis, pairs)]
    unnamed x14 -> x16, local copies, waits for them, and re-layouts: 5.6 us -> 5.62 us
  transfers between devices with their start and end apart: 10 -> 10, of which waited for: 7 -> 7; matrix products, arithmetic and copies ran while one was open for 16% -> 17% of each run, Pallas kernels for 0% -> 0%
where the time goes in v8:
time: 171 us
  waiting for transfers between devices  89.2 us (52%)
  starting transfers between devices  41.3 us (24%)
  matrix products  21.5 us (13%)
  local copies, waits for them, and re-layouts  13 us (8%)
  other arithmetic  5.31 us (3%)
    ppermute x4, waiting for transfers between devices, shifted(): return lax.ppermute(value, axis, pairs)  41.5 us
    ppermute x4, starting transfers between devices, shifted(): return lax.ppermute(value, axis, pairs)  22.4 us
    all_to_all x1, waiting for transfers between devices, on_device(): far = lax.all_to_all(far, 'inner', split_axis=0, concat_axis=0, tiled=True)  22.2 us
    all_to_all x1, waiting for transfers between devices, on_device(): lax.all_to_all(jnp.stack(far_back, axis=1), 'inner', split_axis=0, concat...  20.4 us
    dot_general x2, matrix products, one_half(): projected = jnp.dot(rows, w_in_now, preferred_element_type=jnp.float32)  9.68 us
    all_to_all x1, starting transfers between devices, on_device(): lax.all_to_all(near, 'inner', split_axis=0, concat_axis=0, tiled=True)  6.43 us
    unnamed x16, local copies, waits for them, and re-layouts  5.62 us
    all_to_all x1, waiting for transfers between devices, on_device(): lax.all_to_all(near, 'inner', split_axis=0, concat_axis=0, tiled=True)  5.16 us
  transfers between devices with their start and end apart: 10, of which 7 were waited for; matrix products, arithmetic and copies ran while one was open for 17% of the time, Pallas kernels for 0%

profile of v8, /device:TPU:2, one launch (start us, length us, event | category | flops | bytes accessed | tf_op | source)
XLA Modules:
  0.0 170.6 jit_solution(7459309109841858245)
XLA Ops:
  1.4 1.5 copy.100
  2.9 0.8 convolution_convert_fusion
  4.2 2.3 %collective-permute-start = (bf16[16,6,32,128]{3,2,1,0:T(8,128)(2,1)S(1)}, bf16[16,6,32,128]{3,2,1,0:T(8,128)(2,1)S(1)}, u32[]{:S(2)}, u32[]{:S(2)}) collective-permute-start(bf16[16,6,32,128]{3,2,1,0:T(8,128)(2,1)S(1)} %bitcast.150), channel_id=1, source_target_pairs={{0,240},{16,0},{32,16},{48,32},{64,48},{80,64},{96,80},{112,96},{1... | collective-permute-start | bytes 2359304 | tf_op jit(solution)/shard_map/ppermute | solution.py:14
  6.7 4.2 %collective-permute-start.1 = (bf16[16,6,32,128]{3,2,1,0:T(8,128)(2,1)S(1)}, bf16[16,6,32,128]{3,2,1,0:T(8,128)(2,1)}, u32[]{:S(2)}, u32[]{:S(2)}) collective-permute-start(bf16[16,6,32,128]{3,2,1,0:T(8,128)(2,1)S(1)} %bitcast.152), channel_id=1, source_target_pairs={{0,224},{16,240},{32,0},{48,16},{64,32},{80,48},{96,64},{112,80},{... | collective-permute-start | bytes 2359304 | tf_op jit(solution)/shard_map/ppermute | solution.py:14
  10.9 1.0 copy.68
  11.9 6.4 %all-to-all-start = ((bf16[16,6,32,128]{3,2,1,0:T(8,128)(2,1)}), bf16[16,6,32,128]{3,2,1,0:T(8,128)(2,1)S(1)}, u32[]{:S(2)}, u32[]{:S(2)}) async-start(bf16[16,6,32,128]{3,2,1,0:T(8,128)(2,1)} %bitcast.12), calls=%async_computation | async-start | bytes 1572864 | tf_op jit(solution)/shard_map/all_to_all | solution.py:80
  18.3 7.2 %collective-permute-done = bf16[16,6,32,128]{3,2,1,0:T(8,128)(2,1)S(1)} collective-permute-done((bf16[16,6,32,128]{3,2,1,0:T(8,128)(2,1)S(1)}, bf16[16,6,32,128]{3,2,1,0:T(8,128)(2,1)S(1)}, u32[]{:S(2)}, u32[]{:S(2)}) %collective-permute-start) | collective-permute-done | bytes 786464 | tf_op jit(solution)/shard_map/ppermute | solution.py:14
  25.5 2.5 %collective-permute-done.1 = bf16[16,6,32,128]{3,2,1,0:T(8,128)(2,1)} collective-permute-done((bf16[16,6,32,128]{3,2,1,0:T(8,128)(2,1)S(1)}, bf16[16,6,32,128]{3,2,1,0:T(8,128)(2,1)}, u32[]{:S(2)}, u32[]{:S(2)}) %collective-permute-start.1) | collective-permute-done | bytes 786464 | tf_op jit(solution)/shard_map/ppermute | solution.py:14
  28.0 1.3 pad_maximum_fusion
  29.3 1.5 copy.71
  30.8 5.2 %all-to-all-done = bf16[16,6,32,128]{3,2,1,0:T(8,128)(2,1)S(1)} async-done(((bf16[16,6,32,128]{3,2,1,0:T(8,128)(2,1)}), bf16[16,6,32,128]{3,2,1,0:T(8,128)(2,1)S(1)}, u32[]{:S(2)}, u32[]{:S(2)}) %all-to-all-start) | async-done | bytes 786464 | tf_op jit(solution)/shard_map/all_to_all | solution.py:80
  36.0 3.7 %all-to-all-start.1 = ((bf16[16,2,6,32,128]{4,3,2,1,0:T(8,128)(2,1)}), bf16[16,2,6,32,128]{4,3,2,1,0:T(8,128)(2,1)S(1)}, u32[]{:S(2)}, u32[]{:S(2)}) async-start(bf16[16,2,6,32,128]{4,3,2,1,0:T(8,128)(2,1)} %copy.71), calls=%async_computation.1 | async-start | bytes 3145728 | tf_op jit(solution)/shard_map/all_to_all | solution.py:82
  40.1 1.2 bitcast_dynamic-update-slice_fusion.1
  41.2 22.2 %all-to-all-done.1 = bf16[16,2,6,32,128]{4,3,2,1,0:T(8,128)(2,1)S(1)} async-done(((bf16[16,2,6,32,128]{4,3,2,1,0:T(8,128)(2,1)}), bf16[16,2,6,32,128]{4,3,2,1,0:T(8,128)(2,1)S(1)}, u32[]{:S(2)}, u32[]{:S(2)}) %all-to-all-start.1) | async-done | bytes 1572896 | tf_op jit(solution)/shard_map/all_to_all | solution.py:82
  63.7 1.4 copy-done.2
  65.8 4.9 %fusion.2 = f32[288,768]{1,0:T(8,128)S(1)} fusion(bf16[288,4096]{1,0:T(8,128)(2,1)S(1)} %bitcast_dynamic-update-slice_fusion, bf16[1,4096,768]{2,1,0:T(8,128)(2,1)} %param.8), kind=kOutput, calls=%fused_computation.2 | convolution fusion | flops 1811939328 | bytes 9535488 | tf_op jit(solution)/shard_map/dot_general | solution.py:27
  70.7 1.4 fusion.6
  72.1 4.8 %fusion = f32[288,768]{1,0:T(8,128)S(1)} fusion(bf16[288,4096]{1,0:T(8,128)(2,1)S(1)} %bitcast_dynamic-update-slice_fusion, bf16[1,4096,768]{2,1,0:T(8,128)(2,1)} %collective-permute-done.2), kind=kOutput, calls=%fused_computation | convolution fusion | flops 1811939328 | bytes 9535488 | tf_op jit(solution)/shard_map/dot_general | solution.py:27
  76.9 3.3 %fusion.4 = bf16[288,4096]{1,0:T(8,128)(2,1)S(1)} fusion(f32[288,4096]{1,0:T(8,128)S(1)} %fusion.6, bf16[1,384,4096]{2,1,0:T(8,128)(2,1)} %collective-permute-done.3, f32[288,768]{1,0:T(8,128)S(1)} %fusion), kind=kOutput, calls=%fused_computation.5 | convolution fusion | flops 908992512 | bytes 11108352 | tf_op jit(solution)/shard_map/dot_general | solution.py:31
  80.6 13.9 %collective-permute-start.4 = (bf16[16,6,32,128]{3,2,1,0:T(8,128)(2,1)S(1)}, bf16[16,6,32,128]{3,2,1,0:T(8,128)(2,1)}, u32[]{:S(2)}, u32[]{:S(2)}) collective-permute-start(bf16[16,6,32,128]{3,2,1,0:T(8,128)(2,1)S(1)} %bitcast.151), channel_id=1, source_target_pairs={{0,16},{16,32},{32,48},{48,64},{64,80},{80,96},{96,112},{112,128},... | collective-permute-start | bytes 2359304 | tf_op jit(solution)/shard_map/ppermute | solution.py:14
  94.6 2.0 %collective-permute-start.5 = (bf16[16,6,32,128]{3,2,1,0:T(8,128)(2,1)S(1)}, bf16[16,6,32,128]{3,2,1,0:T(8,128)(2,1)}, u32[]{:S(2)}, u32[]{:S(2)}) collective-permute-start(bf16[16,6,32,128]{3,2,1,0:T(8,128)(2,1)S(1)} %bitcast.153), channel_id=1, source_target_pairs={{0,32},{16,48},{32,64},{48,80},{64,96},{80,112},{96,128},{112,144}... | collective-permute-start | bytes 2359304 | tf_op jit(solution)/shard_map/ppermute | solution.py:14
  96.6 1.0 copy.103
  97.6 3.6 %all-to-all-start.2 = ((bf16[16,6,32,128]{3,2,1,0:T(8,128)(2,1)}), bf16[16,6,32,128]{3,2,1,0:T(8,128)(2,1)S(1)}, u32[]{:S(2)}, u32[]{:S(2)}) async-start(bf16[16,6,32,128]{3,2,1,0:T(8,128)(2,1)} %bitcast.83), calls=%async_computation.2 | async-start | bytes 1572864 | tf_op jit(solution)/shard_map/all_to_all | solution.py:90
  101.3 13.6 %collective-permute-done.4 = bf16[16,6,32,128]{3,2,1,0:T(8,128)(2,1)} collective-permute-done((bf16[16,6,32,128]{3,2,1,0:T(8,128)(2,1)S(1)}, bf16[16,6,32,128]{3,2,1,0:T(8,128)(2,1)}, u32[]{:S(2)}, u32[]{:S(2)}) %collective-permute-start.4) | collective-permute-done | bytes 786464 | tf_op jit(solution)/shard_map/ppermute | solution.py:14
  114.9 18.1 %collective-permute-done.5 = bf16[16,6,32,128]{3,2,1,0:T(8,128)(2,1)} collective-permute-done((bf16[16,6,32,128]{3,2,1,0:T(8,128)(2,1)S(1)}, bf16[16,6,32,128]{3,2,1,0:T(8,128)(2,1)}, u32[]{:S(2)}, u32[]{:S(2)}) %collective-permute-start.5) | collective-permute-done | bytes 786464 | tf_op jit(solution)/shard_map/ppermute | solution.py:14
  133.0 2.7 %pad_maximum_fusion.1 = bf16[16,2,6,32,128]{4,3,2,1,0:T(8,128)(2,1)} fusion(bf16[16,1,6,32,128]{4,3,2,1,0:T(8,128)(2,1)} %bitcast.34, bf16[16,1,6,32,128]{4,3,2,1,0:T(8,128)(2,1)} %bitcast.33), kind=kLoop, calls=%fused_computation.18 | loop fusion | flops 786432 | bytes 3145728 | tf_op jit(solution)/shard_map/stack | solution.py:92
  135.7 4.8 %all-to-all-start.3 = ((bf16[16,2,6,32,128]{4,3,2,1,0:T(8,128)(2,1)}), bf16[16,2,6,32,128]{4,3,2,1,0:T(8,128)(2,1)}, u32[]{:S(2)}, u32[]{:S(2)}) async-start(bf16[16,2,6,32,128]{4,3,2,1,0:T(8,128)(2,1)} %pad_maximum_fusion.1), calls=%async_computation.3 | async-start | bytes 3145728 | tf_op jit(solution)/shard_map/all_to_all | solution.py:91
  141.6 2.1 %fusion.19 = f32[128,32,128,1,1]{0,2,4,1,3:T(8,128)} fusion(bf16[8,2,6,32,128]{4,3,2,1,0:T(8,128)(2,1)S(1)} %bitcast.139, bf16[3,8,2,6,128]{4,1,3,2,0:T(8,128)(2,1)S(1)} %select_convert_fusion), kind=kOutput, calls=%fused_computation.33 | convolution fusion | flops 100663296 | bytes 2908160 | tf_op jit(solution)/shard_map/qcht,qchkl->tkl/dot_general | solution.py:99
  143.7 20.4 %all-to-all-done.3 = bf16[16,2,6,32,128]{4,3,2,1,0:T(8,128)(2,1)} async-done(((bf16[16,2,6,32,128]{4,3,2,1,0:T(8,128)(2,1)}), bf16[16,2,6,32,128]{4,3,2,1,0:T(8,128)(2,1)}, u32[]{:S(2)}, u32[]{:S(2)}) %all-to-all-start.3) | async-done | bytes 1572896 | tf_op jit(solution)/shard_map/all_to_all | solution.py:91
  164.1 1.6 fusion.38
  168.1 1.2 fusion.8
  169.2 1.3 copy.81
  (40 shorter events, 7.1 us)
Async XLA Ops:
  0.0 72.1 %collective-permute-start.2 = (bf16[1,4096,768]{2,1,0:T(8,128)(2,1)}, bf16[1,4096,768]{2,1,0:T(8,128)(2,1)}, u32[]{:S(2)}, u32[]{:S(2)}) collective-permute-start(bf16[1,4096,768]{2,1,0:T(8,128)(2,1)} %param.8), channel_id=1, source_target_pairs={{0,1},{1,0},{2,3},{3,2},{4,5},{5,4},{6,7},{7,6},{8,9},{9,8},{10,11... | collective-permute-start | bytes 18874376 | tf_op jit(solution)/shard_map/ppermute | solution.py:20
  4.2 21.4 %collective-permute-start = (bf16[16,6,32,128]{3,2,1,0:T(8,128)(2,1)S(1)}, bf16[16,6,32,128]{3,2,1,0:T(8,128)(2,1)S(1)}, u32[]{:S(2)}, u32[]{:S(2)}) collective-permute-start(bf16[16,6,32,128]{3,2,1,0:T(8,128)(2,1)S(1)} %bitcast.150), channel_id=1, source_target_pairs={{0,240},{16,0},{32,16},{48,32},{64,48},{80,64},{96,80},{112,96},{1... | collective-permute-start | bytes 2359304 | tf_op jit(solution)/shard_map/ppermute | solution.py:14
  6.7 21.4 %collective-permute-start.1 = (bf16[16,6,32,128]{3,2,1,0:T(8,128)(2,1)S(1)}, bf16[16,6,32,128]{3,2,1,0:T(8,128)(2,1)}, u32[]{:S(2)}, u32[]{:S(2)}) collective-permute-start(bf16[16,6,32,128]{3,2,1,0:T(8,128)(2,1)S(1)} %bitcast.152), channel_id=1, source_target_pairs={{0,224},{16,240},{32,0},{48,16},{64,32},{80,48},{96,64},{112,80},{... | collective-permute-start | bytes 2359304 | tf_op jit(solution)/shard_map/ppermute | solution.py:14
  11.9 24.1 %all-to-all-start = ((bf16[16,6,32,128]{3,2,1,0:T(8,128)(2,1)}), bf16[16,6,32,128]{3,2,1,0:T(8,128)(2,1)S(1)}, u32[]{:S(2)}, u32[]{:S(2)}) async-start(bf16[16,6,32,128]{3,2,1,0:T(8,128)(2,1)} %bitcast.12), calls=%async_computation | async-start | bytes 1572864 | tf_op jit(solution)/shard_map/all_to_all | solution.py:80
  36.0 27.4 %all-to-all-start.1 = ((bf16[16,2,6,32,128]{4,3,2,1,0:T(8,128)(2,1)}), bf16[16,2,6,32,128]{4,3,2,1,0:T(8,128)(2,1)S(1)}, u32[]{:S(2)}, u32[]{:S(2)}) async-start(bf16[16,2,6,32,128]{4,3,2,1,0:T(8,128)(2,1)} %copy.71), calls=%async_computation.1 | async-start | bytes 3145728 | tf_op jit(solution)/shard_map/all_to_all | solution.py:82
  39.7 37.2 %collective-permute-start.3 = (bf16[1,384,4096]{2,1,0:T(8,128)(2,1)}, bf16[1,384,4096]{2,1,0:T(8,128)(2,1)}, u32[]{:S(2)}, u32[]{:S(2)}) collective-permute-start(bf16[1,384,4096]{2,1,0:T(8,128)(2,1)} %param.9), channel_id=1, source_target_pairs={{0,1},{1,0},{2,3},{3,2},{4,5},{5,4},{6,7},{7,6},{8,9},{9,8},{10,11... | collective-permute-start | bytes 9437192 | tf_op jit(solution)/shard_map/ppermute | solution.py:20
  63.4 1.7 copy-start.2
  65.8 4.9 %copy-start.1 = (bf16[1,384,4096]{2,1,0:T(8,128)(2,1)S(1)}, bf16[1,384,4096]{2,1,0:T(8,128)(2,1)}, u32[]{:S(2)}) copy-start(bf16[1,384,4096]{2,1,0:T(8,128)(2,1)} %param.9) | copy-start | bytes 9437188
  80.6 34.3 %collective-permute-start.4 = (bf16[16,6,32,128]{3,2,1,0:T(8,128)(2,1)S(1)}, bf16[16,6,32,128]{3,2,1,0:T(8,128)(2,1)}, u32[]{:S(2)}, u32[]{:S(2)}) collective-permute-start(bf16[16,6,32,128]{3,2,1,0:T(8,128)(2,1)S(1)} %bitcast.151), channel_id=1, source_target_pairs={{0,16},{16,32},{32,48},{48,64},{64,80},{80,96},{96,112},{112,128},... | collective-permute-start | bytes 2359304 | tf_op jit(solution)/shard_map/ppermute | solution.py:14
  94.6 38.4 %collective-permute-start.5 = (bf16[16,6,32,128]{3,2,1,0:T(8,128)(2,1)S(1)}, bf16[16,6,32,128]{3,2,1,0:T(8,128)(2,1)}, u32[]{:S(2)}, u32[]{:S(2)}) collective-permute-start(bf16[16,6,32,128]{3,2,1,0:T(8,128)(2,1)S(1)} %bitcast.153), channel_id=1, source_target_pairs={{0,32},{16,48},{32,64},{48,80},{64,96},{80,112},{96,128},{112,144}... | collective-permute-start | bytes 2359304 | tf_op jit(solution)/shard_map/ppermute | solution.py:14
  97.6 38.1 %all-to-all-start.2 = ((bf16[16,6,32,128]{3,2,1,0:T(8,128)(2,1)}), bf16[16,6,32,128]{3,2,1,0:T(8,128)(2,1)S(1)}, u32[]{:S(2)}, u32[]{:S(2)}) async-start(bf16[16,6,32,128]{3,2,1,0:T(8,128)(2,1)} %bitcast.83), calls=%async_computation.2 | async-start | bytes 1572864 | tf_op jit(solution)/shard_map/all_to_all | solution.py:90
  135.7 4.8 %copy-start.3 = (s32[128,8]{0,1:T(8,128)S(1)}, s32[128,8]{0,1:T(8,128)}, u32[]{:S(2)}) copy-start(s32[128,8]{0,1:T(8,128)} %param.6) | copy-start | bytes 12292
  135.7 4.8 %copy-start.4 = (f32[128,8]{0,1:T(8,128)S(1)}, f32[128,8]{0,1:T(8,128)}, u32[]{:S(2)}) copy-start(f32[128,8]{0,1:T(8,128)} %param.7) | copy-start | bytes 12292
  135.7 28.3 %all-to-all-start.3 = ((bf16[16,2,6,32,128]{4,3,2,1,0:T(8,128)(2,1)}), bf16[16,2,6,32,128]{4,3,2,1,0:T(8,128)(2,1)}, u32[]{:S(2)}, u32[]{:S(2)}) async-start(bf16[16,2,6,32,128]{4,3,2,1,0:T(8,128)(2,1)} %pad_maximum_fusion.1), calls=%async_computation.3 | async-start | bytes 3145728 | tf_op jit(solution)/shard_map/all_to_all | solution.py:91
  166.5 1.6 copy-start

commit v9 on v4

--- a/solution.py
+++ b/solution.py
@@ -10,6 +10,8 @@
 
 def shifted(value, axis, steps):
     count = lax.axis_size(axis)
+    if steps % count == 0:
+        return value
     pairs = [(source, (source + steps) % count) for source in range(count)]
     return lax.ppermute(value, axis, pairs)
 
@@ -72,24 +74,33 @@
         preferred_element_type=jnp.float32,
     ).astype(jnp.bfloat16)
 
+    def exchanged(value):
+        return lax.all_to_all(value, "inner", split_axis=0, concat_axis=0, tiled=True)
+
+    outgoing = [
+        picked[rotation].reshape(inner_count, half_cap, lanes_major, 128)
+        for rotation in range(STEPS)
+    ]
     arrived = [None] * STEPS
     for rotation in reversed(range(STEPS)):
-        outgoing = picked[rotation].reshape(inner_count, half_cap, lanes_major, 128)
-        if rotation > 0:
-            outgoing = shifted(outgoing, "blk", -rotation)
-        arrived[rotation] = lax.all_to_all(
-            outgoing, "inner", split_axis=0, concat_axis=0, tiled=True
-        )
+        if rotation % 2 == 0:
+            arrived[rotation] = exchanged(shifted(outgoing[rotation], "blk", -rotation))
+        else:
+            arrived[rotation] = shifted(exchanged(outgoing[rotation]), "blk", -rotation)
     rows = jnp.concatenate([part.reshape(-1, width) for part in arrived], axis=0)
     done = whole_expert(rows, w_in[0], w_out[0], w_in_other[0], w_out_other[0])
     done = done.reshape(STEPS, inner_count, half_cap, lanes_major, 128)
 
+    backs = [None] * STEPS
+    for rotation in reversed(range(STEPS)):
+        if rotation % 2 == 0:
+            backs[rotation] = exchanged(shifted(done[rotation], "blk", rotation))
+        else:
+            backs[rotation] = shifted(exchanged(done[rotation]), "blk", rotation)
+
     combined = jnp.zeros((tok_rows, lanes_major, 128), jnp.float32)
-    for rotation in reversed(range(STEPS)):
-        back = lax.all_to_all(done[rotation], "inner", split_axis=0, concat_axis=0, tiled=True)
-        if rotation > 0:
-            back = shifted(back, "blk", rotation)
-        back = back.reshape(group_count, SPLIT, half_cap, lanes_major, 128)
+    for rotation in range(STEPS):
+        back = backs[rotation].reshape(group_count, SPLIT, half_cap, lanes_major, 128)
         combined = combined + jnp.einsum(
             "qcht,qchkl->tkl", scale_hi[rotation], back, preferred_element_type=jnp.float32
         )

time: 185 us -> 185 us (level)
  the two profiles are of different devices: /device:TPU:1 before, /device:TPU:2 now
where the time goes in v9:
time: 185 us; the launch traced here: 183 us
  waiting for transfers between devices  80.3 us (43%)
  starting transfers between devices  48.7 us (26%)
  matrix products  30.8 us (17%)
  local copies, waits for them, and re-layouts  21.3 us (12%)
    all_to_all x6, waiting for transfers between devices, exchanged(): lax.all_to_all(value, 'inner', split_axis=0, concat_axis=0, tiled=True)  54.2 us
    all_to_all x6, starting transfers between devices, exchanged(): lax.all_to_all(value, 'inner', split_axis=0, concat_axis=0, tiled=True)  32.3 us
    ppermute x4, waiting for transfers between devices, shifted(): return lax.ppermute(value, axis, pairs)  26.1 us
    ppermute x4, starting transfers between devices, shifted(): return lax.ppermute(value, axis, pairs)  16.4 us
    unnamed x19, local copies, waits for them, and re-layouts  10.5 us
    dot_general x2, matrix products, one_half(): projected = jnp.dot(rows, w_in_now, preferred_element_type=jnp.float32)  10.3 us
    dot_general x3, matrix products, on_device(): jnp.einsum('qcht,qchkl->tkl', scale_lo[rotation], back, preferred_element...  7.62 us
    dot_general x3, matrix products, on_device(): jnp.einsum('qcht,qchkl->tkl', scale_hi[rotation], back, preferred_element...  7.37 us
  transfers between devices with their start and end apart: 12, of which 10 were waited for; matrix products, arithmetic and copies ran while one was open for 22% of the time, Pallas kernels for 0%

profile of v9, /device:TPU:2, one launch (start us, length us, event | category | flops | bytes accessed | tf_op | source)
XLA Modules:
  0.0 182.7 jit_solution(584068958839040519)
XLA Ops:
  1.4 1.5 copy.57
  6.1 6.3 %all-to-all-start.1 = ((bf16[16,6,32,128]{3,2,1,0:T(8,128)(2,1)}), bf16[16,6,32,128]{3,2,1,0:T(8,128)(2,1)}, u32[]{:S(2)}, u32[]{:S(2)}) async-start(bf16[16,6,32,128]{3,2,1,0:T(8,128)(2,1)} %bitcast.13), calls=%async_computation.1 | async-start | bytes 1572864 | tf_op jit(solution)/shard_map/all_to_all | solution.py:78
  12.4 2.3 %copy.31 = bf16[1,8,2,6,32,128]{5,4,3,2,1,0:T(8,128)(2,1)} copy(bf16[1,8,2,6,32,128]{5,1,4,3,2,0:T(8,128)(2,1)} %get-tuple-element.10) | data formatting | bytes 1572864 | tf_op jit(solution)/shard_map/slice | solution.py:81
  14.7 13.0 %all-to-all-done.1 = bf16[16,6,32,128]{3,2,1,0:T(8,128)(2,1)} async-done(((bf16[16,6,32,128]{3,2,1,0:T(8,128)(2,1)}), bf16[16,6,32,128]{3,2,1,0:T(8,128)(2,1)}, u32[]{:S(2)}, u32[]{:S(2)}) %all-to-all-start.1) | async-done | bytes 786464 | tf_op jit(solution)/shard_map/all_to_all | solution.py:78
  27.7 4.3 %all-to-all-start = ((bf16[16,6,32,128]{3,2,1,0:T(8,128)(2,1)}), bf16[16,6,32,128]{3,2,1,0:T(8,128)(2,1)}, u32[]{:S(2)}, u32[]{:S(2)}) async-start(bf16[16,6,32,128]{3,2,1,0:T(8,128)(2,1)} %bitcast.138), calls=%async_computation | async-start | bytes 1572864 | tf_op jit(solution)/shard_map/all_to_all | solution.py:78
  32.0 2.2 %copy.33 = bf16[1,8,2,6,32,128]{5,4,3,2,1,0:T(8,128)(2,1)} copy(bf16[1,8,2,6,32,128]{5,1,4,3,2,0:T(8,128)(2,1)} %get-tuple-element.8) | data formatting | bytes 1572864 | tf_op jit(solution)/shard_map/slice | solution.py:81
  34.2 5.9 %collective-permute-start.1 = (bf16[16,6,32,128]{3,2,1,0:T(8,128)(2,1)}, bf16[16,6,32,128]{3,2,1,0:T(8,128)(2,1)}, u32[]{:S(2)}, u32[]{:S(2)}) collective-permute-start(bf16[16,6,32,128]{3,2,1,0:T(8,128)(2,1)} %bitcast.14), channel_id=1, source_target_pairs={{0,224},{16,240},{32,0},{48,16},{64,32},{80,48},{96,64},{112,80},{... | collective-permute-start | bytes 2359304 | tf_op jit(solution)/shard_map/ppermute | solution.py:16
  41.4 5.8 %all-to-all-done = bf16[16,6,32,128]{3,2,1,0:T(8,128)(2,1)} async-done(((bf16[16,6,32,128]{3,2,1,0:T(8,128)(2,1)}), bf16[16,6,32,128]{3,2,1,0:T(8,128)(2,1)}, u32[]{:S(2)}, u32[]{:S(2)}) %all-to-all-start) | async-done | bytes 786464 | tf_op jit(solution)/shard_map/all_to_all | solution.py:78
  47.2 2.3 %bitcast_dynamic-update-slice_fusion.2 = bf16[288,4096]{1,0:T(8,128)(2,1)} fusion(bf16[12,8,32,128]{3,2,1,0:T(8,128)(2,1)} %bitcast.67), kind=kLoop, calls=%fused_computation.19 | loop fusion | bytes 1572864
  49.5 8.1 %collective-permute-done.1 = bf16[16,6,32,128]{3,2,1,0:T(8,128)(2,1)} collective-permute-done((bf16[16,6,32,128]{3,2,1,0:T(8,128)(2,1)}, bf16[16,6,32,128]{3,2,1,0:T(8,128)(2,1)}, u32[]{:S(2)}, u32[]{:S(2)}) %collective-permute-start.1) | collective-permute-done | bytes 786464 | tf_op jit(solution)/shard_map/ppermute | solution.py:16
  57.5 7.1 %all-to-all-start.2 = ((bf16[16,6,32,128]{3,2,1,0:T(8,128)(2,1)}), bf16[16,6,32,128]{3,2,1,0:T(8,128)(2,1)}, u32[]{:S(2)}, u32[]{:S(2)}) async-start(bf16[16,6,32,128]{3,2,1,0:T(8,128)(2,1)} %collective-permute-done.1), calls=%async_computation.2 | async-start | bytes 1572864 | tf_op jit(solution)/shard_map/all_to_all | solution.py:78
  64.6 7.5 %collective-permute-done = bf16[16,6,32,128]{3,2,1,0:T(8,128)(2,1)} collective-permute-done((bf16[16,6,32,128]{3,2,1,0:T(8,128)(2,1)}, bf16[16,6,32,128]{3,2,1,0:T(8,128)(2,1)}, u32[]{:S(2)}, u32[]{:S(2)}) %collective-permute-start) | collective-permute-done | bytes 786464 | tf_op jit(solution)/shard_map/ppermute | solution.py:16
  72.1 2.3 %bitcast_dynamic-update-slice_fusion.1 = bf16[288,4096]{1,0:T(8,128)(2,1)} fusion(bf16[288,4096]{1,0:T(8,128)(2,1)} %bitcast_dynamic-update-slice_fusion.2, bf16[12,8,32,128]{3,2,1,0:T(8,128)(2,1)} %bitcast.70), kind=kLoop, calls=%fused_computation.18 | loop fusion | bytes 1572864
  74.4 5.5 %all-to-all-done.2 = bf16[16,6,32,128]{3,2,1,0:T(8,128)(2,1)} async-done(((bf16[16,6,32,128]{3,2,1,0:T(8,128)(2,1)}), bf16[16,6,32,128]{3,2,1,0:T(8,128)(2,1)}, u32[]{:S(2)}, u32[]{:S(2)}) %all-to-all-start.2) | async-done | bytes 786464 | tf_op jit(solution)/shard_map/all_to_all | solution.py:78
  79.9 2.3 %bitcast_dynamic-update-slice_fusion = bf16[288,4096]{1,0:T(8,128)(2,1)} fusion(bf16[288,4096]{1,0:T(8,128)(2,1)} %bitcast_dynamic-update-slice_fusion.1, bf16[12,8,32,128]{3,2,1,0:T(8,128)(2,1)} %bitcast.73), kind=kLoop, calls=%fused_computation.17 | loop fusion | bytes 1572864 | tf_op jit(solution)/shard_map/concatenate | solution.py:90
  82.2 5.5 %fusion.2 = f32[288,768]{1,0:T(8,128)S(1)} fusion(bf16[288,4096]{1,0:T(8,128)(2,1)} %bitcast_dynamic-update-slice_fusion, bf16[1,4096,768]{2,1,0:T(8,128)(2,1)} %param.8), kind=kOutput, calls=%fused_computation.2 | convolution fusion | flops 1811939328 | bytes 9535488 | tf_op jit(solution)/shard_map/dot_general | solution.py:29
  89.3 4.8 %fusion = f32[288,768]{1,0:T(8,128)S(1)} fusion(bf16[288,4096]{1,0:T(8,128)(2,1)S(1)} %copy-done.3, bf16[1,4096,768]{2,1,0:T(8,128)(2,1)} %collective-permute-done.2), kind=kOutput, calls=%fused_computation | convolution fusion | flops 1811939328 | bytes 9535488 | tf_op jit(solution)/shard_map/dot_general | solution.py:29
  94.1 3.3 %fusion.4 = bf16[288,4096]{1,0:T(8,128)(2,1)S(1)} fusion(f32[288,4096]{1,0:T(8,128)S(1)} %fusion.6, bf16[1,384,4096]{2,1,0:T(8,128)(2,1)} %collective-permute-done.3, f32[288,768]{1,0:T(8,128)S(1)} %fusion), kind=kOutput, calls=%fused_computation.5 | convolution fusion | flops 908992512 | bytes 11108352 | tf_op jit(solution)/shard_map/dot_general | solution.py:33
  98.7 3.8 %all-to-all-start.4 = ((bf16[16,6,32,128]{3,2,1,0:T(8,128)(2,1)}), bf16[16,6,32,128]{3,2,1,0:T(8,128)(2,1)S(1)}, u32[]{:S(2)}, u32[]{:S(2)}) async-start(bf16[16,6,32,128]{3,2,1,0:T(8,128)(2,1)} %bitcast.80), calls=%async_computation.4 | async-start | bytes 1572864 | tf_op jit(solution)/shard_map/all_to_all | solution.py:78
  103.5 13.9 %all-to-all-done.4 = bf16[16,6,32,128]{3,2,1,0:T(8,128)(2,1)S(1)} async-done(((bf16[16,6,32,128]{3,2,1,0:T(8,128)(2,1)}), bf16[16,6,32,128]{3,2,1,0:T(8,128)(2,1)S(1)}, u32[]{:S(2)}, u32[]{:S(2)}) %all-to-all-start.4) | async-done | bytes 786464 | tf_op jit(solution)/shard_map/all_to_all | solution.py:78
  118.4 3.6 %all-to-all-start.3 = ((bf16[16,6,32,128]{3,2,1,0:T(8,128)(2,1)}), bf16[16,6,32,128]{3,2,1,0:T(8,128)(2,1)S(1)}, u32[]{:S(2)}, u32[]{:S(2)}) async-start(bf16[16,6,32,128]{3,2,1,0:T(8,128)(2,1)} %bitcast.137), calls=%async_computation.3 | async-start | bytes 1572864 | tf_op jit(solution)/shard_map/all_to_all | solution.py:78
  123.2 9.2 %collective-permute-start.4 = (bf16[16,6,32,128]{3,2,1,0:T(8,128)(2,1)}, bf16[16,6,32,128]{3,2,1,0:T(8,128)(2,1)}, u32[]{:S(2)}, u32[]{:S(2)}) collective-permute-start(bf16[16,6,32,128]{3,2,1,0:T(8,128)(2,1)} %copy-done.2), channel_id=1, source_target_pairs={{0,16},{16,32},{32,48},{48,64},{64,80},{80,96},{96,112},{112,128},... | collective-permute-start | bytes 2359304 | tf_op jit(solution)/shard_map/ppermute | solution.py:16
  132.5 4.6 %all-to-all-done.3 = bf16[16,6,32,128]{3,2,1,0:T(8,128)(2,1)S(1)} async-done(((bf16[16,6,32,128]{3,2,1,0:T(8,128)(2,1)}), bf16[16,6,32,128]{3,2,1,0:T(8,128)(2,1)S(1)}, u32[]{:S(2)}, u32[]{:S(2)}) %all-to-all-start.3) | async-done | bytes 786464 | tf_op jit(solution)/shard_map/all_to_all | solution.py:78
  137.9 8.0 %collective-permute-done.5 = bf16[16,6,32,128]{3,2,1,0:T(8,128)(2,1)} collective-permute-done((bf16[16,6,32,128]{3,2,1,0:T(8,128)(2,1)}, bf16[16,6,32,128]{3,2,1,0:T(8,128)(2,1)}, u32[]{:S(2)}, u32[]{:S(2)}) %collective-permute-start.5) | collective-permute-done | bytes 786464 | tf_op jit(solution)/shard_map/ppermute | solution.py:16
  145.9 7.2 %all-to-all-start.5 = ((bf16[16,6,32,128]{3,2,1,0:T(8,128)(2,1)}), bf16[16,6,32,128]{3,2,1,0:T(8,128)(2,1)}, u32[]{:S(2)}, u32[]{:S(2)}) async-start(bf16[16,6,32,128]{3,2,1,0:T(8,128)(2,1)} %collective-permute-done.5), calls=%async_computation.5 | async-start | bytes 1572864 | tf_op jit(solution)/shard_map/all_to_all | solution.py:78
  153.1 2.1 %fusion.19 = f32[128,32,128,1,1]{0,2,4,1,3:T(8,128)} fusion(bf16[8,2,6,32,128]{4,3,2,1,0:T(8,128)(2,1)S(1)} %bitcast.134, bf16[3,8,2,6,128]{4,1,3,2,0:T(8,128)(2,1)S(1)} %select_convert_fusion), kind=kOutput, calls=%fused_computation.32 | convolution fusion | flops 100663296 | bytes 2908160 | tf_op jit(solution)/shard_map/qcht,qchkl->tkl/dot_general | solution.py:104
  155.2 2.5 %collective-permute-done.4 = bf16[16,6,32,128]{3,2,1,0:T(8,128)(2,1)} collective-permute-done((bf16[16,6,32,128]{3,2,1,0:T(8,128)(2,1)}, bf16[16,6,32,128]{3,2,1,0:T(8,128)(2,1)}, u32[]{:S(2)}, u32[]{:S(2)}) %collective-permute-start.4) | collective-permute-done | bytes 786464 | tf_op jit(solution)/shard_map/ppermute | solution.py:16
  157.8 3.2 %fusion.13 = f32[128,32,128,1,1]{0,2,4,1,3:T(8,128)} fusion(bf16[8,2,6,32,128]{4,3,2,1,0:T(8,128)(2,1)} %bitcast.30, bf16[3,8,2,6,128]{4,1,3,2,0:T(8,128)(2,1)S(1)} %fusion.27), kind=kOutput, calls=%fused_computation.26 | convolution fusion | flops 100663296 | bytes 2908160 | tf_op jit(solution)/shard_map/qcht,qchkl->tkl/dot_general | solution.py:107
  161.0 3.2 %fusion.15 = f32[128,32,128,1,1]{0,2,4,1,3:T(8,128)} fusion(bf16[8,2,6,32,128]{4,3,2,1,0:T(8,128)(2,1)} %bitcast.30, bf16[3,8,2,6,128]{4,1,3,2,0:T(8,128)(2,1)S(1)} %select_convert_fusion), kind=kOutput, calls=%fused_computation.28 | convolution fusion | flops 100663296 | bytes 2908160 | tf_op jit(solution)/shard_map/qcht,qchkl->tkl/dot_general | solution.py:104
  164.2 11.4 %all-to-all-done.5 = bf16[16,6,32,128]{3,2,1,0:T(8,128)(2,1)} async-done(((bf16[16,6,32,128]{3,2,1,0:T(8,128)(2,1)}), bf16[16,6,32,128]{3,2,1,0:T(8,128)(2,1)}, u32[]{:S(2)}, u32[]{:S(2)}) %all-to-all-start.5) | async-done | bytes 786464 | tf_op jit(solution)/shard_map/all_to_all | solution.py:78
  175.7 2.0 %fusion.11 = f32[128,32,128,1,1]{0,2,4,1,3:T(8,128)S(1)} fusion(bf16[8,2,6,32,128]{4,3,2,1,0:T(8,128)(2,1)} %bitcast.41, bf16[3,8,2,6,128]{4,1,3,2,0:T(8,128)(2,1)S(1)} %select_convert_fusion), kind=kOutput, calls=%fused_computation.24 | convolution fusion | flops 100663296 | bytes 2908160 | tf_op jit(solution)/shard_map/qcht,qchkl->tkl/dot_general | solution.py:104
  177.7 3.6 %fusion.8 = bf16[128,32,128]{0,2,1:T(8,128)(2,1)S(1)} fusion(f32[128,32,128,1,1]{0,2,4,1,3:T(8,128)S(1)} %fusion.11, f32[128,32,128,1,1]{0,2,4,1,3:T(8,128)} %fusion.13, f32[128,32,128,1,1]{0,2,4,1,3:T(8,128)} %fusion.15, f32[128,32,128,1,1]{0,2,4,1,3:T(8,128)S(1)} %fusion.17, f32[128,32,128,1,1]{0,2,4,1,3:T(8,128)S(1)} %copy-done, ...), kind=kOutput, calls=%fused_computation.10 | convolution fusion | flops 103809024 | bytes 12345344 | tf_op jit(solution)/shard_map/qcht,qchkl->tkl/dot_general | solution.py:107
  (42 shorter events, 14.2 us)
Async XLA Ops:
  0.0 89.1 %collective-permute-start.2 = (bf16[1,4096,768]{2,1,0:T(8,128)(2,1)}, bf16[1,4096,768]{2,1,0:T(8,128)(2,1)}, u32[]{:S(2)}, u32[]{:S(2)}) collective-permute-start(bf16[1,4096,768]{2,1,0:T(8,128)(2,1)} %param.8), channel_id=1, source_target_pairs={{0,1},{1,0},{2,3},{3,2},{4,5},{5,4},{6,7},{7,6},{8,9},{9,8},{10,11... | collective-permute-start | bytes 18874376 | tf_op jit(solution)/shard_map/ppermute | solution.py:22
  6.1 21.6 %all-to-all-start.1 = ((bf16[16,6,32,128]{3,2,1,0:T(8,128)(2,1)}), bf16[16,6,32,128]{3,2,1,0:T(8,128)(2,1)}, u32[]{:S(2)}, u32[]{:S(2)}) async-start(bf16[16,6,32,128]{3,2,1,0:T(8,128)(2,1)} %bitcast.13), calls=%async_computation.1 | async-start | bytes 1572864 | tf_op jit(solution)/shard_map/all_to_all | solution.py:78
  12.4 27.6 %copy-start.1 = (bf16[1,384,4096]{2,1,0:T(8,128)(2,1)S(1)}, bf16[1,384,4096]{2,1,0:T(8,128)(2,1)}, u32[]{:S(2)}) copy-start(bf16[1,384,4096]{2,1,0:T(8,128)(2,1)} %param.9) | copy-start | bytes 9437188
  27.7 19.5 %all-to-all-start = ((bf16[16,6,32,128]{3,2,1,0:T(8,128)(2,1)}), bf16[16,6,32,128]{3,2,1,0:T(8,128)(2,1)}, u32[]{:S(2)}, u32[]{:S(2)}) async-start(bf16[16,6,32,128]{3,2,1,0:T(8,128)(2,1)} %bitcast.138), calls=%async_computation | async-start | bytes 1572864 | tf_op jit(solution)/shard_map/all_to_all | solution.py:78
  34.2 23.4 %collective-permute-start.1 = (bf16[16,6,32,128]{3,2,1,0:T(8,128)(2,1)}, bf16[16,6,32,128]{3,2,1,0:T(8,128)(2,1)}, u32[]{:S(2)}, u32[]{:S(2)}) collective-permute-start(bf16[16,6,32,128]{3,2,1,0:T(8,128)(2,1)} %bitcast.14), channel_id=1, source_target_pairs={{0,224},{16,240},{32,0},{48,16},{64,32},{80,48},{96,64},{112,80},{... | collective-permute-start | bytes 2359304 | tf_op jit(solution)/shard_map/ppermute | solution.py:16
  40.0 54.1 %collective-permute-start.3 = (bf16[1,384,4096]{2,1,0:T(8,128)(2,1)S(1)}, bf16[1,384,4096]{2,1,0:T(8,128)(2,1)}, u32[]{:S(2)}, u32[]{:S(2)}) collective-permute-start(bf16[1,384,4096]{2,1,0:T(8,128)(2,1)S(1)} %copy-done.1), channel_id=1, source_target_pairs={{0,1},{1,0},{2,3},{3,2},{4,5},{5,4},{6,7},{7,6},{8,9},{9,8},{10,11... | collective-permute-start | bytes 9437192 | tf_op jit(solution)/shard_map/ppermute | solution.py:22
  40.0 32.1 %collective-permute-start = (bf16[16,6,32,128]{3,2,1,0:T(8,128)(2,1)}, bf16[16,6,32,128]{3,2,1,0:T(8,128)(2,1)}, u32[]{:S(2)}, u32[]{:S(2)}) collective-permute-start(bf16[16,6,32,128]{3,2,1,0:T(8,128)(2,1)} %all-to-all-done.1), channel_id=1, source_target_pairs={{0,240},{16,0},{32,16},{48,32},{64,48},{80,64},{96,80},{112,96},{1... | collective-permute-start | bytes 2359304 | tf_op jit(solution)/shard_map/ppermute | solution.py:16
  57.5 22.3 %all-to-all-start.2 = ((bf16[16,6,32,128]{3,2,1,0:T(8,128)(2,1)}), bf16[16,6,32,128]{3,2,1,0:T(8,128)(2,1)}, u32[]{:S(2)}, u32[]{:S(2)}) async-start(bf16[16,6,32,128]{3,2,1,0:T(8,128)(2,1)} %collective-permute-done.1), calls=%async_computation.2 | async-start | bytes 1572864 | tf_op jit(solution)/shard_map/all_to_all | solution.py:78
  87.7 1.7 copy-start.3
  98.7 18.8 %all-to-all-start.4 = ((bf16[16,6,32,128]{3,2,1,0:T(8,128)(2,1)}), bf16[16,6,32,128]{3,2,1,0:T(8,128)(2,1)S(1)}, u32[]{:S(2)}, u32[]{:S(2)}) async-start(bf16[16,6,32,128]{3,2,1,0:T(8,128)(2,1)} %bitcast.80), calls=%async_computation.4 | async-start | bytes 1572864 | tf_op jit(solution)/shard_map/all_to_all | solution.py:78
  102.5 20.6 %copy-start.4 = (s32[128,8]{0,1:T(8,128)S(1)}, s32[128,8]{0,1:T(8,128)}, u32[]{:S(2)}) copy-start(s32[128,8]{0,1:T(8,128)} %param.6) | copy-start | bytes 12292
  102.5 20.5 %copy-start.5 = (f32[128,8]{0,1:T(8,128)S(1)}, f32[128,8]{0,1:T(8,128)}, u32[]{:S(2)}) copy-start(f32[128,8]{0,1:T(8,128)} %param.7) | copy-start | bytes 12292
  117.5 0.9 copy-start.2
  118.4 18.8 %all-to-all-start.3 = ((bf16[16,6,32,128]{3,2,1,0:T(8,128)(2,1)}), bf16[16,6,32,128]{3,2,1,0:T(8,128)(2,1)S(1)}, u32[]{:S(2)}, u32[]{:S(2)}) async-start(bf16[16,6,32,128]{3,2,1,0:T(8,128)(2,1)} %bitcast.137), calls=%async_computation.3 | async-start | bytes 1572864 | tf_op jit(solution)/shard_map/all_to_all | solution.py:78
  123.0 22.9 %collective-permute-start.5 = (bf16[16,6,32,128]{3,2,1,0:T(8,128)(2,1)}, bf16[16,6,32,128]{3,2,1,0:T(8,128)(2,1)}, u32[]{:S(2)}, u32[]{:S(2)}) collective-permute-start(bf16[16,6,32,128]{3,2,1,0:T(8,128)(2,1)} %bitcast.83), channel_id=1, source_target_pairs={{0,32},{16,48},{32,64},{48,80},{64,96},{80,112},{96,128},{112,144}... | collective-permute-start | bytes 2359304 | tf_op jit(solution)/shard_map/ppermute | solution.py:16
  123.2 34.5 %collective-permute-start.4 = (bf16[16,6,32,128]{3,2,1,0:T(8,128)(2,1)}, bf16[16,6,32,128]{3,2,1,0:T(8,128)(2,1)}, u32[]{:S(2)}, u32[]{:S(2)}) collective-permute-start(bf16[16,6,32,128]{3,2,1,0:T(8,128)(2,1)} %copy-done.2), channel_id=1, source_target_pairs={{0,16},{16,32},{32,48},{48,64},{64,80},{80,96},{96,112},{112,128},... | collective-permute-start | bytes 2359304 | tf_op jit(solution)/shard_map/ppermute | solution.py:16
  145.9 29.8 %all-to-all-start.5 = ((bf16[16,6,32,128]{3,2,1,0:T(8,128)(2,1)}), bf16[16,6,32,128]{3,2,1,0:T(8,128)(2,1)}, u32[]{:S(2)}, u32[]{:S(2)}) async-start(bf16[16,6,32,128]{3,2,1,0:T(8,128)(2,1)} %collective-permute-done.5), calls=%async_computation.5 | async-start | bytes 1572864 | tf_op jit(solution)/shard_map/all_to_all | solution.py:78
  175.7 2.0 %copy-start = (f32[128,32,128,1,1]{0,2,4,1,3:T(8,128)S(1)}, f32[128,32,128,1,1]{0,2,4,1,3:T(8,128)}, u32[]{:S(2)}) copy-start(f32[128,32,128,1,1]{0,2,4,1,3:T(8,128)} %fusion.19) | copy-start | bytes 6291460

commit v10 on v9

--- a/solution.py
+++ b/solution.py
@@ -10,8 +10,6 @@
 
 def shifted(value, axis, steps):
     count = lax.axis_size(axis)
-    if steps % count == 0:
-        return value
     pairs = [(source, (source + steps) % count) for source in range(count)]
     return lax.ppermute(value, axis, pairs)
 
@@ -77,26 +75,39 @@
     def exchanged(value):
         return lax.all_to_all(value, "inner", split_axis=0, concat_axis=0, tiled=True)
 
+    def far_in_halves(parts, direction):
+        cut = half_cap // 2
+        firsts = [part[:, :cut] for part in parts]
+        seconds = [part[:, cut:] for part in parts]
+        firsts = [
+            shifted(first, "blk", direction * rotation)
+            for rotation, first in enumerate(firsts, start=1)
+        ]
+        firsts, seconds = lax.optimization_barrier((firsts, seconds))
+        seconds = [
+            shifted(second, "blk", direction * rotation)
+            for rotation, second in enumerate(seconds, start=1)
+        ]
+        firsts = jnp.split(exchanged(jnp.stack(firsts, axis=1)), len(parts), axis=1)
+        seconds = jnp.split(exchanged(jnp.stack(seconds, axis=1)), len(parts), axis=1)
+        firsts = [first[:, 0] for first in firsts]
+        seconds = [second[:, 0] for second in seconds]
+        return [
+            jnp.concatenate([first, second], axis=1) for first, second in zip(firsts, seconds)
+        ]
+
     outgoing = [
         picked[rotation].reshape(inner_count, half_cap, lanes_major, 128)
         for rotation in range(STEPS)
     ]
-    arrived = [None] * STEPS
-    for rotation in reversed(range(STEPS)):
-        if rotation % 2 == 0:
-            arrived[rotation] = exchanged(shifted(outgoing[rotation], "blk", -rotation))
-        else:
-            arrived[rotation] = shifted(exchanged(outgoing[rotation]), "blk", -rotation)
+    near = exchanged(outgoing[0])
+    arrived = [near] + far_in_halves(outgoing[1:], -1)
     rows = jnp.concatenate([part.reshape(-1, width) for part in arrived], axis=0)
     done = whole_expert(rows, w_in[0], w_out[0], w_in_other[0], w_out_other[0])
     done = done.reshape(STEPS, inner_count, half_cap, lanes_major, 128)
 
-    backs = [None] * STEPS
-    for rotation in reversed(range(STEPS)):
-        if rotation % 2 == 0:
-            backs[rotation] = exchanged(shifted(done[rotation], "blk", rotation))
-        else:
-            backs[rotation] = shifted(exchanged(done[rotation]), "blk", rotation)
+    near_back = exchanged(done[0])
+    backs = [near_back] + far_in_halves([done[r] for r in range(1, STEPS)], 1)
 
     combined = jnp.zeros((tok_rows, lanes_major, 128), jnp.float32)
     for rotation in range(STEPS):

time: 185 us -> 180 us (0.973)
  matrix products: 30.8 us -> 21.2 us
  starting transfers between devices: 48.7 us -> 52.5 us
  other arithmetic: 1.34 us -> 4.8 us
  waiting for transfers between devices: 80.3 us -> 78.2 us
    all_to_all x6, waiting for transfers between devices: 54.2 us -> 24.9 us  [exchanged(): lax.all_to_all(value, 'inner', split_axis=0, concat_axis=0, tiled=True)]
    ppermute x4 -> x8, waiting for transfers between devices: 26.1 us -> 53.3 us  [shifted(): return lax.ppermute(value, axis, pairs)]
    slice x4, local copies, waits for them, and re-layouts: 6.86 us -> 1.5 us  [on_device(): picked[rotation].reshape(inner_count, half_cap, lanes_major, 128)]
    dot_general x3, matrix products: 7.62 us -> 2.77 us  [on_device(): jnp.einsum('qcht,qchkl->tkl', scale_lo[rotation], back, preferred_element...]
    dot_general x3, matrix products: 7.37 us -> 3.2 us  [on_device(): jnp.einsum('qcht,qchkl->tkl', scale_hi[rotation], back, preferred_element...]
    squeeze x0 -> x2, local copies, waits for them, and re-layouts: none -> 3.25 us  [the longest x1 1.93 us: far_in_halves(): firsts = [first[:, 0] for first in firsts]]
    ppermute x4 -> x8, starting transfers between devices: 16.4 us -> 19.5 us  [shifted(): return lax.ppermute(value, axis, pairs)]
    another operation x0 -> x3, local copies, waits for them, and re-layouts: none -> 2.96 us  [the longest x2 1.96 us: far_in_halves(): jnp.stack(seconds, axis=1)]
  transfers between devices with their start and end apart: 12 -> 16, of which waited for: 10 -> 9; matrix products, arithmetic and copies ran while one was open for 22% -> 21% of each run, Pallas kernels for 0% -> 0%
where the time goes in v10:
time: 180 us; the launch traced here: 179 us
  waiting for transfers between devices  78.2 us (43%)
  starting transfers between devices  52.5 us (29%)
  local copies, waits for them, and re-layouts  21.9 us (12%)
  matrix products  21.2 us (12%)
  other arithmetic  4.8 us (3%)
    ppermute x8, waiting for transfers between devices, shifted(): return lax.ppermute(value, axis, pairs)  53.3 us
    all_to_all x6, starting transfers between devices, exchanged(): lax.all_to_all(value, 'inner', split_axis=0, concat_axis=0, tiled=True)  33 us
    all_to_all x6, waiting for transfers between devices, exchanged(): lax.all_to_all(value, 'inner', split_axis=0, concat_axis=0, tiled=True)  24.9 us
    ppermute x8, starting transfers between devices, shifted(): return lax.ppermute(value, axis, pairs)  19.5 us
    dot_general x2, matrix products, one_half(): projected = jnp.dot(rows, w_in_now, preferred_element_type=jnp.float32)  9.62 us
    unnamed x33, local copies, waits for them, and re-layouts  7.61 us
    dot_general x2, matrix products, one_half(): return jnp.dot(activated, w_out_now, preferred_element_type=jnp.float32)  4.72 us
  transfers between devices with their start and end apart: 16, of which 9 were waited for; matrix products, arithmetic and copies ran while one was open for 21% of the time, Pallas kernels for 0%

profile of v10, /device:TPU:2, one launch (start us, length us, event | category | flops | bytes accessed | tf_op | source)
XLA Modules:
  0.0 179.0 jit_solution(9679172046422643829)
XLA Ops:
  1.5 1.5 copy.98
  4.2 2.3 %collective-permute-start = (bf16[16,3,32,128]{3,2,1,0:T(8,128)(2,1)S(1)}, bf16[16,3,32,128]{3,2,1,0:T(8,128)(2,1)S(1)}, u32[]{:S(2)}, u32[]{:S(2)}) collective-permute-start(bf16[16,3,32,128]{3,2,1,0:T(8,128)(2,1)S(1)} %get-tuple-element.42), channel_id=1, source_target_pairs={{0,240},{16,0},{32,16},{48,32},{64,48},{80,64},{96,80},{112,96},{1... | collective-permute-start | bytes 1179656 | tf_op jit(solution)/shard_map/ppermute | solution.py:14
  7.6 4.7 %all-to-all-start = ((bf16[16,6,32,128]{3,2,1,0:T(8,128)(2,1)}), bf16[16,6,32,128]{3,2,1,0:T(8,128)(2,1)}, u32[]{:S(2)}, u32[]{:S(2)}) async-start(bf16[16,6,32,128]{3,2,1,0:T(8,128)(2,1)} %bitcast.12), calls=%async_computation | async-start | bytes 1572864 | tf_op jit(solution)/shard_map/all_to_all | solution.py:76
  13.3 5.9 %collective-permute-start.1 = (bf16[16,3,32,128]{3,2,1,0:T(8,128)(2,1)S(1)}, bf16[16,3,32,128]{3,2,1,0:T(8,128)(2,1)S(1)}, u32[]{:S(2)}, u32[]{:S(2)}) collective-permute-start(bf16[16,3,32,128]{3,2,1,0:T(8,128)(2,1)S(1)} %get-tuple-element.40), channel_id=1, source_target_pairs={{0,224},{16,240},{32,0},{48,16},{64,32},{80,48},{96,64},{112,80},{... | collective-permute-start | bytes 1179656 | tf_op jit(solution)/shard_map/ppermute | solution.py:14
  19.1 8.9 %collective-permute-done.1 = bf16[16,3,32,128]{3,2,1,0:T(8,128)(2,1)S(1)} collective-permute-done((bf16[16,3,32,128]{3,2,1,0:T(8,128)(2,1)S(1)}, bf16[16,3,32,128]{3,2,1,0:T(8,128)(2,1)S(1)}, u32[]{:S(2)}, u32[]{:S(2)}) %collective-permute-start.1) | collective-permute-done | bytes 393248 | tf_op jit(solution)/shard_map/ppermute | solution.py:14
  28.0 1.2 pad_maximum_fusion
  30.3 7.0 %all-to-all-start.1 = ((bf16[16,2,3,32,128]{4,3,2,1,0:T(8,128)(2,1)}), bf16[16,2,3,32,128]{4,3,2,1,0:T(8,128)(2,1)}, u32[]{:S(2)}, u32[]{:S(2)}) async-start(bf16[16,2,3,32,128]{4,3,2,1,0:T(8,128)(2,1)} %copy.59), calls=%async_computation.1 | async-start | bytes 1572864 | tf_op jit(solution)/shard_map/all_to_all | solution.py:76
  37.3 3.8 %collective-permute-start.2 = (bf16[16,3,32,128]{3,2,1,0:T(8,128)(2,1)S(1)}, bf16[16,3,32,128]{3,2,1,0:T(8,128)(2,1)S(1)}, u32[]{:S(2)}, u32[]{:S(2)}) collective-permute-start(bf16[16,3,32,128]{3,2,1,0:T(8,128)(2,1)S(1)} %get-tuple-element.15), channel_id=1, source_target_pairs={{0,240},{16,0},{32,16},{48,32},{64,48},{80,64},{96,80},{112,96},{1... | collective-permute-start | bytes 1179656 | tf_op jit(solution)/shard_map/ppermute | solution.py:14
  41.1 2.2 %collective-permute-start.3 = (bf16[16,3,32,128]{3,2,1,0:T(8,128)(2,1)}, bf16[16,3,32,128]{3,2,1,0:T(8,128)(2,1)S(1)}, u32[]{:S(2)}, u32[]{:S(2)}) collective-permute-start(bf16[16,3,32,128]{3,2,1,0:T(8,128)(2,1)} %get-tuple-element.16), channel_id=1, source_target_pairs={{0,224},{16,240},{32,0},{48,16},{64,32},{80,48},{96,64},{112,80},{... | collective-permute-start | bytes 1179656 | tf_op jit(solution)/shard_map/ppermute | solution.py:14
  43.3 11.8 %collective-permute-done.2 = bf16[16,3,32,128]{3,2,1,0:T(8,128)(2,1)S(1)} collective-permute-done((bf16[16,3,32,128]{3,2,1,0:T(8,128)(2,1)S(1)}, bf16[16,3,32,128]{3,2,1,0:T(8,128)(2,1)S(1)}, u32[]{:S(2)}, u32[]{:S(2)}) %collective-permute-start.2) | collective-permute-done | bytes 393248 | tf_op jit(solution)/shard_map/ppermute | solution.py:14
  56.1 7.0 %all-to-all-start.2 = ((bf16[16,2,3,32,128]{4,3,2,1,0:T(8,128)(2,1)}), bf16[16,2,3,32,128]{4,3,2,1,0:T(8,128)(2,1)}, u32[]{:S(2)}, u32[]{:S(2)}) async-start(bf16[16,2,3,32,128]{4,3,2,1,0:T(8,128)(2,1)} %copy.60), calls=%async_computation.2 | async-start | bytes 1572864 | tf_op jit(solution)/shard_map/all_to_all | solution.py:76
  63.2 2.3 %bitcast_dynamic-update-slice_fusion.2 = bf16[288,4096]{1,0:T(8,128)(2,1)} fusion(bf16[12,8,32,128]{3,2,1,0:T(8,128)(2,1)} %bitcast.95), kind=kLoop, calls=%fused_computation.19 | loop fusion | bytes 1572864
  65.5 1.9 %slice_bitcast_fusion.4 = (bf16[16,3,32,128]{3,2,1,0:T(8,128)(2,1)S(1)}, bf16[16,3,32,128]{3,2,1,0:T(8,128)(2,1)}) fusion(bf16[16,2,3,32,128]{4,3,2,1,0:T(8,128)(2,1)} %all-to-all-done.1), kind=kLoop, calls=%fused_computation.38 | loop fusion | bytes 1572864 | tf_op jit(solution)/shard_map/squeeze | solution.py:93
  67.4 11.0 %all-to-all-done.2 = bf16[16,2,3,32,128]{4,3,2,1,0:T(8,128)(2,1)} async-done(((bf16[16,2,3,32,128]{4,3,2,1,0:T(8,128)(2,1)}), bf16[16,2,3,32,128]{4,3,2,1,0:T(8,128)(2,1)}, u32[]{:S(2)}, u32[]{:S(2)}) %all-to-all-start.2) | async-done | bytes 786464 | tf_op jit(solution)/shard_map/all_to_all | solution.py:76
  78.4 1.3 slice_bitcast_fusion.3
  81.5 4.8 %fusion.2 = f32[288,768]{1,0:T(8,128)S(1)} fusion(bf16[288,4096]{1,0:T(8,128)(2,1)S(1)} %bitcast_dynamic-update-slice_fusion, bf16[1,4096,768]{2,1,0:T(8,128)(2,1)} %param.8), kind=kOutput, calls=%fused_computation.2 | convolution fusion | flops 1811939328 | bytes 9535488 | tf_op jit(solution)/shard_map/dot_general | solution.py:27
  86.3 1.4 fusion.6
  87.7 4.8 %fusion = f32[288,768]{1,0:T(8,128)S(1)} fusion(bf16[288,4096]{1,0:T(8,128)(2,1)S(1)} %bitcast_dynamic-update-slice_fusion, bf16[1,4096,768]{2,1,0:T(8,128)(2,1)} %collective-permute-done.4), kind=kOutput, calls=%fused_computation | convolution fusion | flops 1811939328 | bytes 9535488 | tf_op jit(solution)/shard_map/dot_general | solution.py:27
  92.6 3.3 %fusion.4 = bf16[288,4096]{1,0:T(8,128)(2,1)S(1)} fusion(f32[288,4096]{1,0:T(8,128)S(1)} %fusion.6, bf16[1,384,4096]{2,1,0:T(8,128)(2,1)} %collective-permute-done.5, f32[288,768]{1,0:T(8,128)S(1)} %fusion), kind=kOutput, calls=%fused_computation.5 | convolution fusion | flops 908992512 | bytes 11108352 | tf_op jit(solution)/shard_map/dot_general | solution.py:31
  96.3 3.3 %collective-permute-start.6 = (bf16[16,3,32,128]{3,2,1,0:T(8,128)(2,1)S(1)}, bf16[16,3,32,128]{3,2,1,0:T(8,128)(2,1)S(1)}, u32[]{:S(2)}, u32[]{:S(2)}) collective-permute-start(bf16[16,3,32,128]{3,2,1,0:T(8,128)(2,1)S(1)} %get-tuple-element.34), channel_id=1, source_target_pairs={{0,16},{16,32},{32,48},{48,64},{64,80},{80,96},{96,112},{112,128},... | collective-permute-start | bytes 1179656 | tf_op jit(solution)/shard_map/ppermute | solution.py:14
  100.8 3.6 %all-to-all-start.3 = ((bf16[16,6,32,128]{3,2,1,0:T(8,128)(2,1)}), bf16[16,6,32,128]{3,2,1,0:T(8,128)(2,1)S(1)}, u32[]{:S(2)}, u32[]{:S(2)}) async-start(bf16[16,6,32,128]{3,2,1,0:T(8,128)(2,1)} %bitcast.105), calls=%async_computation.3 | async-start | bytes 1572864 | tf_op jit(solution)/shard_map/all_to_all | solution.py:76
  105.2 1.6 collective-permute-start.7
  107.0 4.7 %collective-permute-done.6 = bf16[16,3,32,128]{3,2,1,0:T(8,128)(2,1)S(1)} collective-permute-done((bf16[16,3,32,128]{3,2,1,0:T(8,128)(2,1)S(1)}, bf16[16,3,32,128]{3,2,1,0:T(8,128)(2,1)S(1)}, u32[]{:S(2)}, u32[]{:S(2)}) %collective-permute-start.6) | collective-permute-done | bytes 393248 | tf_op jit(solution)/shard_map/ppermute | solution.py:14
  111.7 9.8 %collective-permute-done.7 = bf16[16,3,32,128]{3,2,1,0:T(8,128)(2,1)S(1)} collective-permute-done((bf16[16,3,32,128]{3,2,1,0:T(8,128)(2,1)S(1)}, bf16[16,3,32,128]{3,2,1,0:T(8,128)(2,1)S(1)}, u32[]{:S(2)}, u32[]{:S(2)}) %collective-permute-start.7) | collective-permute-done | bytes 393248 | tf_op jit(solution)/shard_map/ppermute | solution.py:14
  122.4 5.2 %all-to-all-start.4 = ((bf16[16,2,3,32,128]{4,3,2,1,0:T(8,128)(2,1)}), bf16[16,2,3,32,128]{4,3,2,1,0:T(8,128)(2,1)}, u32[]{:S(2)}, u32[]{:S(2)}) async-start(bf16[16,2,3,32,128]{4,3,2,1,0:T(8,128)(2,1)} %pad_maximum_fusion.4), calls=%async_computation.4 | async-start | bytes 1572864 | tf_op jit(solution)/shard_map/all_to_all | solution.py:76
  128.9 2.1 %fusion.12 = f32[128,32,128,1,1]{0,2,4,1,3:T(8,128)} fusion(bf16[8,2,6,32,128]{4,3,2,1,0:T(8,128)(2,1)S(1)} %bitcast.170, bf16[3,8,2,6,128]{4,1,3,2,0:T(8,128)(2,1)S(1)} %select_convert_fusion), kind=kOutput, calls=%fused_computation.31 | convolution fusion | flops 100663296 | bytes 2908160 | tf_op jit(solution)/shard_map/qcht,qchkl->tkl/dot_general | solution.py:115
  131.1 15.8 %collective-permute-done.8 = bf16[16,3,32,128]{3,2,1,0:T(8,128)(2,1)S(1)} collective-permute-done((bf16[16,3,32,128]{3,2,1,0:T(8,128)(2,1)S(1)}, bf16[16,3,32,128]{3,2,1,0:T(8,128)(2,1)S(1)}, u32[]{:S(2)}, u32[]{:S(2)}) %collective-permute-start.8) | collective-permute-done | bytes 393248 | tf_op jit(solution)/shard_map/ppermute | solution.py:14
  146.9 2.4 %collective-permute-done.9 = bf16[16,3,32,128]{3,2,1,0:T(8,128)(2,1)S(1)} collective-permute-done((bf16[16,3,32,128]{3,2,1,0:T(8,128)(2,1)}, bf16[16,3,32,128]{3,2,1,0:T(8,128)(2,1)S(1)}, u32[]{:S(2)}, u32[]{:S(2)}) %collective-permute-start.9) | collective-permute-done | bytes 393248 | tf_op jit(solution)/shard_map/ppermute | solution.py:14
  151.3 5.4 %all-to-all-start.5 = ((bf16[16,2,3,32,128]{4,3,2,1,0:T(8,128)(2,1)}), bf16[16,2,3,32,128]{4,3,2,1,0:T(8,128)(2,1)}, u32[]{:S(2)}, u32[]{:S(2)}) async-start(bf16[16,2,3,32,128]{4,3,2,1,0:T(8,128)(2,1)} %copy.67), calls=%async_computation.5 | async-start | bytes 1572864 | tf_op jit(solution)/shard_map/all_to_all | solution.py:76
  159.2 12.8 %all-to-all-done.5 = bf16[16,2,3,32,128]{4,3,2,1,0:T(8,128)(2,1)} async-done(((bf16[16,2,3,32,128]{4,3,2,1,0:T(8,128)(2,1)}), bf16[16,2,3,32,128]{4,3,2,1,0:T(8,128)(2,1)}, u32[]{:S(2)}, u32[]{:S(2)}) %all-to-all-start.5) | async-done | bytes 786464 | tf_op jit(solution)/shard_map/all_to_all | solution.py:76
  176.2 1.5 fusion.8
  177.7 1.3 copy.75
  (82 shorter events, 21.8 us)
Async XLA Ops:
  0.0 87.7 %collective-permute-start.4 = (bf16[1,4096,768]{2,1,0:T(8,128)(2,1)}, bf16[1,4096,768]{2,1,0:T(8,128)(2,1)}, u32[]{:S(2)}, u32[]{:S(2)}) collective-permute-start(bf16[1,4096,768]{2,1,0:T(8,128)(2,1)} %param.8), channel_id=1, source_target_pairs={{0,1},{1,0},{2,3},{3,2},{4,5},{5,4},{6,7},{7,6},{8,9},{9,8},{10,11... | collective-permute-start | bytes 18874376 | tf_op jit(solution)/shard_map/ppermute | solution.py:20
  0.0 2.9 %copy-start.6 = (s32[2,6]{1,0:T(2,128)}, s32[2,6]{1,0:T(2,128)S(1)}, u32[]{:S(2)}) copy-start(s32[2,6]{1,0:T(2,128)S(1)} %multiply_add_fusion) | copy-start | bytes 148
  0.2 0.8 copy-start.9
  4.2 15.0 %collective-permute-start = (bf16[16,3,32,128]{3,2,1,0:T(8,128)(2,1)S(1)}, bf16[16,3,32,128]{3,2,1,0:T(8,128)(2,1)S(1)}, u32[]{:S(2)}, u32[]{:S(2)}) collective-permute-start(bf16[16,3,32,128]{3,2,1,0:T(8,128)(2,1)S(1)} %get-tuple-element.42), channel_id=1, source_target_pairs={{0,240},{16,0},{32,16},{48,32},{64,48},{80,64},{96,80},{112,96},{1... | collective-permute-start | bytes 1179656 | tf_op jit(solution)/shard_map/ppermute | solution.py:14
  7.6 22.7 %all-to-all-start = ((bf16[16,6,32,128]{3,2,1,0:T(8,128)(2,1)}), bf16[16,6,32,128]{3,2,1,0:T(8,128)(2,1)}, u32[]{:S(2)}, u32[]{:S(2)}) async-start(bf16[16,6,32,128]{3,2,1,0:T(8,128)(2,1)} %bitcast.12), calls=%async_computation | async-start | bytes 1572864 | tf_op jit(solution)/shard_map/all_to_all | solution.py:76
  13.3 14.8 %collective-permute-start.1 = (bf16[16,3,32,128]{3,2,1,0:T(8,128)(2,1)S(1)}, bf16[16,3,32,128]{3,2,1,0:T(8,128)(2,1)S(1)}, u32[]{:S(2)}, u32[]{:S(2)}) collective-permute-start(bf16[16,3,32,128]{3,2,1,0:T(8,128)(2,1)S(1)} %get-tuple-element.40), channel_id=1, source_target_pairs={{0,224},{16,240},{32,0},{48,16},{64,32},{80,48},{96,64},{112,80},{... | collective-permute-start | bytes 1179656 | tf_op jit(solution)/shard_map/ppermute | solution.py:14
  19.1 8.9 %copy-start.3 = (bf16[16,3,32,128]{3,2,1,0:T(8,128)(2,1)}, bf16[16,3,32,128]{3,2,1,0:T(8,128)(2,1)S(1)}, u32[]{:S(2)}) copy-start(bf16[16,3,32,128]{3,2,1,0:T(8,128)(2,1)S(1)} %collective-permute-done) | copy-start | bytes 1179652
  28.0 15.3 %copy-start.2 = (bf16[1,384,4096]{2,1,0:T(8,128)(2,1)S(1)}, bf16[1,384,4096]{2,1,0:T(8,128)(2,1)}, u32[]{:S(2)}) copy-start(bf16[1,384,4096]{2,1,0:T(8,128)(2,1)} %param.9) | copy-start | bytes 9437188
  30.3 25.9 %all-to-all-start.1 = ((bf16[16,2,3,32,128]{4,3,2,1,0:T(8,128)(2,1)}), bf16[16,2,3,32,128]{4,3,2,1,0:T(8,128)(2,1)}, u32[]{:S(2)}, u32[]{:S(2)}) async-start(bf16[16,2,3,32,128]{4,3,2,1,0:T(8,128)(2,1)} %copy.59), calls=%async_computation.1 | async-start | bytes 1572864 | tf_op jit(solution)/shard_map/all_to_all | solution.py:76
  37.3 17.8 %collective-permute-start.2 = (bf16[16,3,32,128]{3,2,1,0:T(8,128)(2,1)S(1)}, bf16[16,3,32,128]{3,2,1,0:T(8,128)(2,1)S(1)}, u32[]{:S(2)}, u32[]{:S(2)}) collective-permute-start(bf16[16,3,32,128]{3,2,1,0:T(8,128)(2,1)S(1)} %get-tuple-element.15), channel_id=1, source_target_pairs={{0,240},{16,0},{32,16},{48,32},{64,48},{80,64},{96,80},{112,96},{1... | collective-permute-start | bytes 1179656 | tf_op jit(solution)/shard_map/ppermute | solution.py:14
  41.1 14.0 %collective-permute-start.3 = (bf16[16,3,32,128]{3,2,1,0:T(8,128)(2,1)}, bf16[16,3,32,128]{3,2,1,0:T(8,128)(2,1)S(1)}, u32[]{:S(2)}, u32[]{:S(2)}) collective-permute-start(bf16[16,3,32,128]{3,2,1,0:T(8,128)(2,1)} %get-tuple-element.16), channel_id=1, source_target_pairs={{0,224},{16,240},{32,0},{48,16},{64,32},{80,48},{96,64},{112,80},{... | collective-permute-start | bytes 1179656 | tf_op jit(solution)/shard_map/ppermute | solution.py:14
  43.3 49.3 %collective-permute-start.5 = (bf16[1,384,4096]{2,1,0:T(8,128)(2,1)S(1)}, bf16[1,384,4096]{2,1,0:T(8,128)(2,1)}, u32[]{:S(2)}, u32[]{:S(2)}) collective-permute-start(bf16[1,384,4096]{2,1,0:T(8,128)(2,1)S(1)} %copy-done.2), channel_id=1, source_target_pairs={{0,1},{1,0},{2,3},{3,2},{4,5},{5,4},{6,7},{7,6},{8,9},{9,8},{10,11... | collective-permute-start | bytes 9437192 | tf_op jit(solution)/shard_map/ppermute | solution.py:20
  56.1 22.3 %all-to-all-start.2 = ((bf16[16,2,3,32,128]{4,3,2,1,0:T(8,128)(2,1)}), bf16[16,2,3,32,128]{4,3,2,1,0:T(8,128)(2,1)}, u32[]{:S(2)}, u32[]{:S(2)}) async-start(bf16[16,2,3,32,128]{4,3,2,1,0:T(8,128)(2,1)} %copy.60), calls=%async_computation.2 | async-start | bytes 1572864 | tf_op jit(solution)/shard_map/all_to_all | solution.py:76
  78.4 2.5 %copy-start.5 = (bf16[288,4096]{1,0:T(8,128)(2,1)S(1)}, bf16[288,4096]{1,0:T(8,128)(2,1)}, u32[]{:S(2)}) copy-start(bf16[288,4096]{1,0:T(8,128)(2,1)} %bitcast_dynamic-update-slice_fusion.2) | copy-start | bytes 7077892
  96.3 15.4 %collective-permute-start.6 = (bf16[16,3,32,128]{3,2,1,0:T(8,128)(2,1)S(1)}, bf16[16,3,32,128]{3,2,1,0:T(8,128)(2,1)S(1)}, u32[]{:S(2)}, u32[]{:S(2)}) collective-permute-start(bf16[16,3,32,128]{3,2,1,0:T(8,128)(2,1)S(1)} %get-tuple-element.34), channel_id=1, source_target_pairs={{0,16},{16,32},{32,48},{48,64},{64,80},{80,96},{96,112},{112,128},... | collective-permute-start | bytes 1179656 | tf_op jit(solution)/shard_map/ppermute | solution.py:14
  99.7 7.1 %copy-start.8 = (s32[128,8]{0,1:T(8,128)S(1)}, s32[128,8]{0,1:T(8,128)}, u32[]{:S(2)}) copy-start(s32[128,8]{0,1:T(8,128)} %param.6) | copy-start | bytes 12292
  99.7 7.1 %copy-start.10 = (s32[24]{0:T(128)S(1)}, s32[24]{0:T(128)}, u32[]{:S(2)}) copy-start(s32[24]{0:T(128)} %copy-done.9) | copy-start | bytes 292
  99.7 7.1 %copy-start.11 = (f32[128,8]{0,1:T(8,128)S(1)}, f32[128,8]{0,1:T(8,128)}, u32[]{:S(2)}) copy-start(f32[128,8]{0,1:T(8,128)} %param.7) | copy-start | bytes 12292
  99.7 7.2 %copy-start.7 = (s32[2,6]{1,0:T(2,128)S(1)}, s32[2,6]{1,0:T(2,128)}, u32[]{:S(2)}) copy-start(s32[2,6]{1,0:T(2,128)} %copy-done.6) | copy-start | bytes 148
  100.8 21.7 %all-to-all-start.3 = ((bf16[16,6,32,128]{3,2,1,0:T(8,128)(2,1)}), bf16[16,6,32,128]{3,2,1,0:T(8,128)(2,1)S(1)}, u32[]{:S(2)}, u32[]{:S(2)}) async-start(bf16[16,6,32,128]{3,2,1,0:T(8,128)(2,1)} %bitcast.105), calls=%async_computation.3 | async-start | bytes 1572864 | tf_op jit(solution)/shard_map/all_to_all | solution.py:76
  105.2 16.3 %collective-permute-start.7 = (bf16[16,3,32,128]{3,2,1,0:T(8,128)(2,1)S(1)}, bf16[16,3,32,128]{3,2,1,0:T(8,128)(2,1)S(1)}, u32[]{:S(2)}, u32[]{:S(2)}) collective-permute-start(bf16[16,3,32,128]{3,2,1,0:T(8,128)(2,1)S(1)} %get-tuple-element.32), channel_id=1, source_target_pairs={{0,32},{16,48},{32,64},{48,80},{64,96},{80,112},{96,128},{112,144}... | collective-permute-start | bytes 1179656 | tf_op jit(solution)/shard_map/ppermute | solution.py:14
  122.4 28.9 %all-to-all-start.4 = ((bf16[16,2,3,32,128]{4,3,2,1,0:T(8,128)(2,1)}), bf16[16,2,3,32,128]{4,3,2,1,0:T(8,128)(2,1)}, u32[]{:S(2)}, u32[]{:S(2)}) async-start(bf16[16,2,3,32,128]{4,3,2,1,0:T(8,128)(2,1)} %pad_maximum_fusion.4), calls=%async_computation.4 | async-start | bytes 1572864 | tf_op jit(solution)/shard_map/all_to_all | solution.py:76
  127.8 46.3 %copy-start.4 = (bf16[3,8,2,6,128]{4,1,3,2,0:T(8,128)(2,1)}, bf16[3,8,2,6,128]{4,1,3,2,0:T(8,128)(2,1)S(1)}, u32[]{:S(2)}) copy-start(bf16[3,8,2,6,128]{4,1,3,2,0:T(8,128)(2,1)S(1)} %fusion.20) | copy-start | bytes 221188
  127.8 19.1 %collective-permute-start.8 = (bf16[16,3,32,128]{3,2,1,0:T(8,128)(2,1)S(1)}, bf16[16,3,32,128]{3,2,1,0:T(8,128)(2,1)S(1)}, u32[]{:S(2)}, u32[]{:S(2)}) collective-permute-start(bf16[16,3,32,128]{3,2,1,0:T(8,128)(2,1)S(1)} %get-tuple-element.19), channel_id=1, source_target_pairs={{0,16},{16,32},{32,48},{48,64},{64,80},{80,96},{96,112},{112,128},... | collective-permute-start | bytes 1179656 | tf_op jit(solution)/shard_map/ppermute | solution.py:14
  127.9 21.4 %collective-permute-start.9 = (bf16[16,3,32,128]{3,2,1,0:T(8,128)(2,1)}, bf16[16,3,32,128]{3,2,1,0:T(8,128)(2,1)S(1)}, u32[]{:S(2)}, u32[]{:S(2)}) collective-permute-start(bf16[16,3,32,128]{3,2,1,0:T(8,128)(2,1)} %get-tuple-element.20), channel_id=1, source_target_pairs={{0,32},{16,48},{32,64},{48,80},{64,96},{80,112},{96,128},{112,144}... | collective-permute-start | bytes 1179656 | tf_op jit(solution)/shard_map/ppermute | solution.py:14
  151.3 20.7 %all-to-all-start.5 = ((bf16[16,2,3,32,128]{4,3,2,1,0:T(8,128)(2,1)}), bf16[16,2,3,32,128]{4,3,2,1,0:T(8,128)(2,1)}, u32[]{:S(2)}, u32[]{:S(2)}) async-start(bf16[16,2,3,32,128]{4,3,2,1,0:T(8,128)(2,1)} %copy.67), calls=%async_computation.5 | async-start | bytes 1572864 | tf_op jit(solution)/shard_map/all_to_all | solution.py:76
  173.5 1.1 copy-start.1
  174.6 1.6 copy-start

commit v11 on v8

--- a/solution.py
+++ b/solution.py
@@ -80,10 +80,17 @@
     near = lax.all_to_all(near, "inner", split_axis=0, concat_axis=0, tiled=True)
     far = jnp.stack(far, axis=1)
     far = lax.all_to_all(far, "inner", split_axis=0, concat_axis=0, tiled=True)
-    rows = jnp.concatenate(
-        [near.reshape(-1, width), far.transpose(1, 0, 2, 3, 4).reshape(-1, width)], axis=0
+    near_done = whole_expert(
+        near.reshape(-1, width), w_in[0], w_out[0], w_in_other[0], w_out_other[0]
     )
-    done = whole_expert(rows, w_in[0], w_out[0], w_in_other[0], w_out_other[0])
+    far_done = whole_expert(
+        far.transpose(1, 0, 2, 3, 4).reshape(-1, width),
+        w_in[0],
+        w_out[0],
+        w_in_other[0],
+        w_out_other[0],
+    )
+    done = jnp.concatenate([near_done, far_done], axis=0)
     done = done.reshape(STEPS, inner_count, half_cap, lanes_major, 128)
 
     far_back = [shifted(done[rotation], "blk", rotation) for rotation in range(1, STEPS)]

time: 171 us -> 168 us (0.982)
  waiting for transfers between devices: 89.2 us -> 71.5 us
  matrix products: 21.5 us -> 33.8 us
    ppermute x4, waiting for transfers between devices: 41.5 us -> 18.1 us  [shifted(): return lax.ppermute(value, axis, pairs)]
    all_to_all x1, waiting for transfers between devices: 0.01 us -> 10.9 us  [on_device(): lax.all_to_all(done[0], 'inner', split_axis=0, concat_axis=0, tiled=True)]
    dot_general x2 -> x4, matrix products: 9.68 us -> 17.2 us  [one_half(): projected = jnp.dot(rows, w_in_now, preferred_element_type=jnp.float32)]
    all_to_all x1, waiting for transfers between devices: 22.2 us -> 17.6 us  [on_device(): far = lax.all_to_all(far, 'inner', split_axis=0, concat_axis=0, tiled=True)]
    dot_general x2 -> x4, matrix products: 4.72 us -> 8.5 us  [one_half(): return jnp.dot(activated, w_out_now, preferred_element_type=jnp.float32)]
    dot_general x3, matrix products: 2.69 us -> 5.03 us  [on_device(): jnp.einsum('qcht,qchkl->tkl', scale_lo[rotation], back, preferred_element...]
    unnamed x16 -> x15, local copies, waits for them, and re-layouts: 5.62 us -> 3.78 us
  transfers between devices with their start and end apart: 10 -> 10, of which waited for: 7 -> 7; matrix products, arithmetic and copies ran while one was open for 17% -> 25% of each run, Pallas kernels for 0% -> 0%
where the time goes in v11:
time: 168 us; the launch traced here: 167 us
  waiting for transfers between devices  71.5 us (43%)
  starting transfers between devices  41.9 us (25%)
  matrix products  33.8 us (20%)
  local copies, waits for them, and re-layouts  14.5 us (9%)
  other arithmetic  5.32 us (3%)
    ppermute x4, starting transfers between devices, shifted(): return lax.ppermute(value, axis, pairs)  21.8 us
    all_to_all x1, waiting for transfers between devices, on_device(): lax.all_to_all(jnp.stack(far_back, axis=1), 'inner', split_axis=0, concat...  20.6 us
    ppermute x4, waiting for transfers between devices, shifted(): return lax.ppermute(value, axis, pairs)  18.1 us
    all_to_all x1, waiting for transfers between devices, on_device(): far = lax.all_to_all(far, 'inner', split_axis=0, concat_axis=0, tiled=True)  17.6 us
    dot_general x4, matrix products, one_half(): projected = jnp.dot(rows, w_in_now, preferred_element_type=jnp.float32)  17.2 us
    all_to_all x1, waiting for transfers between devices, on_device(): lax.all_to_all(done[0], 'inner', split_axis=0, concat_axis=0, tiled=True)  10.9 us
    dot_general x4, matrix products, one_half(): return jnp.dot(activated, w_out_now, preferred_element_type=jnp.float32)  8.5 us
    all_to_all x1, starting transfers between devices, on_device(): lax.all_to_all(near, 'inner', split_axis=0, concat_axis=0, tiled=True)  6.48 us
  transfers between devices with their start and end apart: 10, of which 7 were waited for; matrix products, arithmetic and copies ran while one was open for 25% of the time, Pallas kernels for 0%

profile of v11, /device:TPU:2, one launch (start us, length us, event | category | flops | bytes accessed | tf_op | source)
XLA Modules:
  0.0 167.3 jit_solution(4406001522922863745)
XLA Ops:
  1.4 1.5 copy.100
  5.0 2.3 %collective-permute-start.2 = (bf16[16,6,32,128]{3,2,1,0:T(8,128)(2,1)}, bf16[16,6,32,128]{3,2,1,0:T(8,128)(2,1)}, u32[]{:S(2)}, u32[]{:S(2)}) collective-permute-start(bf16[16,6,32,128]{3,2,1,0:T(8,128)(2,1)} %bitcast.28), channel_id=1, source_target_pairs={{0,240},{16,0},{32,16},{48,32},{64,48},{80,64},{96,80},{112,96},{1... | collective-permute-start | bytes 2359304 | tf_op jit(solution)/shard_map/ppermute | solution.py:14
  8.4 4.1 %collective-permute-start.3 = (bf16[16,6,32,128]{3,2,1,0:T(8,128)(2,1)}, bf16[16,6,32,128]{3,2,1,0:T(8,128)(2,1)}, u32[]{:S(2)}, u32[]{:S(2)}) collective-permute-start(bf16[16,6,32,128]{3,2,1,0:T(8,128)(2,1)} %bitcast.30), channel_id=1, source_target_pairs={{0,224},{16,240},{32,0},{48,16},{64,32},{80,48},{96,64},{112,80},{... | collective-permute-start | bytes 2359304 | tf_op jit(solution)/shard_map/ppermute | solution.py:14
  12.5 1.1 copy.68
  13.6 6.5 %all-to-all-start = ((bf16[16,6,32,128]{3,2,1,0:T(8,128)(2,1)}), bf16[16,6,32,128]{3,2,1,0:T(8,128)(2,1)}, u32[]{:S(2)}, u32[]{:S(2)}) async-start(bf16[16,6,32,128]{3,2,1,0:T(8,128)(2,1)} %bitcast.160), calls=%async_computation | async-start | bytes 1572864 | tf_op jit(solution)/shard_map/all_to_all | solution.py:80
  20.5 6.1 %collective-permute-done.2 = bf16[16,6,32,128]{3,2,1,0:T(8,128)(2,1)} collective-permute-done((bf16[16,6,32,128]{3,2,1,0:T(8,128)(2,1)}, bf16[16,6,32,128]{3,2,1,0:T(8,128)(2,1)}, u32[]{:S(2)}, u32[]{:S(2)}) %collective-permute-start.2) | collective-permute-done | bytes 786464 | tf_op jit(solution)/shard_map/ppermute | solution.py:14
  26.6 3.4 %collective-permute-done.3 = bf16[16,6,32,128]{3,2,1,0:T(8,128)(2,1)} collective-permute-done((bf16[16,6,32,128]{3,2,1,0:T(8,128)(2,1)}, bf16[16,6,32,128]{3,2,1,0:T(8,128)(2,1)}, u32[]{:S(2)}, u32[]{:S(2)}) %collective-permute-start.3) | collective-permute-done | bytes 786464 | tf_op jit(solution)/shard_map/ppermute | solution.py:14
  30.0 1.5 pad_maximum_fusion
  31.5 1.4 copy.73
  33.0 4.2 %all-to-all-done = bf16[16,6,32,128]{3,2,1,0:T(8,128)(2,1)} async-done(((bf16[16,6,32,128]{3,2,1,0:T(8,128)(2,1)}), bf16[16,6,32,128]{3,2,1,0:T(8,128)(2,1)}, u32[]{:S(2)}, u32[]{:S(2)}) %all-to-all-start) | async-done | bytes 786464 | tf_op jit(solution)/shard_map/all_to_all | solution.py:80
  37.1 4.4 %all-to-all-start.2 = ((bf16[16,2,6,32,128]{4,3,2,1,0:T(8,128)(2,1)}), bf16[16,2,6,32,128]{4,3,2,1,0:T(8,128)(2,1)}, u32[]{:S(2)}, u32[]{:S(2)}) async-start(bf16[16,2,6,32,128]{4,3,2,1,0:T(8,128)(2,1)} %copy.73), calls=%async_computation.2 | async-start | bytes 3145728 | tf_op jit(solution)/shard_map/all_to_all | solution.py:82
  41.5 4.2 %fusion.6 = f32[96,768]{1,0:T(8,128)S(1)} fusion(bf16[1,4096,768]{2,1,0:T(8,128)(2,1)} %param.8, bf16[12,8,32,128]{3,2,1,0:T(8,128)(2,1)} %bitcast.76), kind=kOutput, calls=%fused_computation.6 | convolution fusion | flops 603979776 | bytes 7372800 | tf_op jit(solution)/shard_map/dot_general | solution.py:27
  45.8 1.9 %fusion.14 = f32[96,4096]{1,0:T(8,128)} fusion(bf16[1,384,4096]{2,1,0:T(8,128)(2,1)S(1)} %copy-done, f32[96,768]{1,0:T(8,128)S(1)} %fusion.6), kind=kOutput, calls=%fused_computation.16 | convolution fusion | flops 302211072 | bytes 5013504 | tf_op jit(solution)/shard_map/dot_general | solution.py:31
  47.7 17.6 %all-to-all-done.2 = bf16[16,2,6,32,128]{4,3,2,1,0:T(8,128)(2,1)} async-done(((bf16[16,2,6,32,128]{4,3,2,1,0:T(8,128)(2,1)}), bf16[16,2,6,32,128]{4,3,2,1,0:T(8,128)(2,1)}, u32[]{:S(2)}, u32[]{:S(2)}) %all-to-all-start.2) | async-done | bytes 1572896 | tf_op jit(solution)/shard_map/all_to_all | solution.py:82
  65.3 1.7 %copy.74 = bf16[2,16,6,32,128]{4,3,2,1,0:T(8,128)(2,1)S(1)} copy(bf16[2,16,6,32,128]{4,3,2,0,1:T(8,128)(2,1)} %bitcast.32) | data formatting | bytes 3145728 | tf_op jit(solution)/shard_map/transpose | solution.py:87
  67.0 4.4 %fusion.4 = f32[192,768]{1,0:T(8,128)S(1)} fusion(bf16[1,4096,768]{2,1,0:T(8,128)(2,1)} %param.8, bf16[24,8,32,128]{3,2,1,0:T(8,128)(2,1)S(1)} %bitcast.161), kind=kOutput, calls=%fused_computation.4 | convolution fusion | flops 1207959552 | bytes 8454144 | tf_op jit(solution)/shard_map/dot_general | solution.py:27
  72.4 4.4 %fusion = f32[192,768]{1,0:T(8,128)S(1)} fusion(bf16[1,4096,768]{2,1,0:T(8,128)(2,1)} %collective-permute-done, bf16[24,8,32,128]{3,2,1,0:T(8,128)(2,1)S(1)} %bitcast.162), kind=kOutput, calls=%fused_computation | convolution fusion | flops 1207959552 | bytes 8454144 | tf_op jit(solution)/shard_map/dot_general | solution.py:27
  76.8 3.0 %fusion.8 = bf16[192,4096]{1,0:T(8,128)(2,1)S(1)} fusion(f32[192,4096]{1,0:T(8,128)S(1)} %fusion.12, bf16[1,384,4096]{2,1,0:T(8,128)(2,1)} %collective-permute-done.1, f32[192,768]{1,0:T(8,128)S(1)} %fusion), kind=kOutput, calls=%fused_computation.9 | convolution fusion | flops 605995008 | bytes 8454144 | tf_op jit(solution)/shard_map/dot_general | solution.py:31
  80.2 2.2 %collective-permute-start.5 = (bf16[16,6,32,128]{3,2,1,0:T(8,128)(2,1)S(1)}, bf16[16,6,32,128]{3,2,1,0:T(8,128)(2,1)S(1)}, u32[]{:S(2)}, u32[]{:S(2)}) collective-permute-start(bf16[16,6,32,128]{3,2,1,0:T(8,128)(2,1)S(1)} %bitcast.165), channel_id=1, source_target_pairs={{0,32},{16,48},{32,64},{48,80},{64,96},{80,112},{96,128},{112,144}... | collective-permute-start | bytes 2359304 | tf_op jit(solution)/shard_map/ppermute | solution.py:14
  82.4 13.2 %collective-permute-start.4 = (bf16[16,6,32,128]{3,2,1,0:T(8,128)(2,1)S(1)}, bf16[16,6,32,128]{3,2,1,0:T(8,128)(2,1)}, u32[]{:S(2)}, u32[]{:S(2)}) collective-permute-start(bf16[16,6,32,128]{3,2,1,0:T(8,128)(2,1)S(1)} %bitcast.164), channel_id=1, source_target_pairs={{0,16},{16,32},{32,48},{48,64},{64,80},{80,96},{96,112},{112,128},... | collective-permute-start | bytes 2359304 | tf_op jit(solution)/shard_map/ppermute | solution.py:14
  95.6 4.2 %fusion.2 = f32[96,768]{1,0:T(8,128)S(1)} fusion(bf16[1,4096,768]{2,1,0:T(8,128)(2,1)} %collective-permute-done, bf16[12,8,32,128]{3,2,1,0:T(8,128)(2,1)} %bitcast.76), kind=kOutput, calls=%fused_computation.2 | convolution fusion | flops 603979776 | bytes 7372800 | tf_op jit(solution)/shard_map/dot_general | solution.py:27
  99.9 2.6 %fusion.21 = bf16[12,8,32,128]{3,1,2,0:T(8,128)(2,1)S(1)} fusion(f32[96,4096]{1,0:T(8,128)S(1)} %copy-done.2, bf16[1,384,4096]{2,1,0:T(8,128)(2,1)} %collective-permute-done.1, f32[96,768]{1,0:T(8,128)S(1)} %fusion.2), kind=kOutput, calls=%fused_computation.31 | convolution fusion | flops 302997504 | bytes 5799936 | tf_op jit(solution)/shard_map/dot_general | solution.py:31
  103.5 3.6 %all-to-all-start.1 = ((bf16[16,6,32,128]{3,2,1,0:T(8,128)(2,1)}), bf16[16,6,32,128]{3,2,1,0:T(8,128)(2,1)S(1)}, u32[]{:S(2)}, u32[]{:S(2)}) async-start(bf16[16,6,32,128]{3,2,1,0:T(8,128)(2,1)} %bitcast.80), calls=%async_computation.1 | async-start | bytes 1572864 | tf_op jit(solution)/shard_map/all_to_all | solution.py:97
  107.2 8.7 %collective-permute-done.4 = bf16[16,6,32,128]{3,2,1,0:T(8,128)(2,1)} collective-permute-done((bf16[16,6,32,128]{3,2,1,0:T(8,128)(2,1)S(1)}, bf16[16,6,32,128]{3,2,1,0:T(8,128)(2,1)}, u32[]{:S(2)}, u32[]{:S(2)}) %collective-permute-start.4) | collective-permute-done | bytes 786464 | tf_op jit(solution)/shard_map/ppermute | solution.py:14
  115.8 2.4 %pad_maximum_fusion.1 = bf16[16,2,6,32,128]{4,3,2,1,0:T(8,128)(2,1)} fusion(bf16[16,1,6,32,128]{4,3,2,1,0:T(8,128)(2,1)S(1)} %bitcast.166, bf16[16,1,6,32,128]{4,3,2,1,0:T(8,128)(2,1)} %bitcast.33), kind=kLoop, calls=%fused_computation.28 | loop fusion | flops 786432 | bytes 3145728 | tf_op jit(solution)/shard_map/stack | solution.py:99
  118.3 10.9 %all-to-all-done.1 = bf16[16,6,32,128]{3,2,1,0:T(8,128)(2,1)S(1)} async-done(((bf16[16,6,32,128]{3,2,1,0:T(8,128)(2,1)}), bf16[16,6,32,128]{3,2,1,0:T(8,128)(2,1)S(1)}, u32[]{:S(2)}, u32[]{:S(2)}) %all-to-all-start.1) | async-done | bytes 786464 | tf_op jit(solution)/shard_map/all_to_all | solution.py:97
  129.2 5.1 %all-to-all-start.3 = ((bf16[16,2,6,32,128]{4,3,2,1,0:T(8,128)(2,1)}), bf16[16,2,6,32,128]{4,3,2,1,0:T(8,128)(2,1)}, u32[]{:S(2)}, u32[]{:S(2)}) async-start(bf16[16,2,6,32,128]{4,3,2,1,0:T(8,128)(2,1)} %pad_maximum_fusion.1), calls=%async_computation.3 | async-start | bytes 3145728 | tf_op jit(solution)/shard_map/all_to_all | solution.py:98
  135.4 2.1 %fusion.36 = f32[128,32,128,1,1]{0,2,4,1,3:T(8,128)} fusion(bf16[8,2,6,32,128]{4,3,2,1,0:T(8,128)(2,1)S(1)} %bitcast.153, bf16[3,8,2,6,128]{4,1,3,2,0:T(8,128)(2,1)S(1)} %fusion.42), kind=kOutput, calls=%fused_computation.46 | convolution fusion | flops 100663296 | bytes 2908160 | tf_op jit(solution)/shard_map/qcht,qchkl->tkl/dot_general | solution.py:109
  137.5 20.6 %all-to-all-done.3 = bf16[16,2,6,32,128]{4,3,2,1,0:T(8,128)(2,1)} async-done(((bf16[16,2,6,32,128]{4,3,2,1,0:T(8,128)(2,1)}), bf16[16,2,6,32,128]{4,3,2,1,0:T(8,128)(2,1)}, u32[]{:S(2)}, u32[]{:S(2)}) %all-to-all-start.3) | async-done | bytes 1572896 | tf_op jit(solution)/shard_map/all_to_all | solution.py:98
  158.1 1.6 fusion.65
  162.9 2.2 %fusion.16 = bf16[128,32,128]{0,2,1:T(8,128)(2,1)} fusion(f32[128,32,128,1,1]{0,2,4,1,3:T(8,128)S(1)} %fusion.30, f32[128,32,128,1,1]{0,2,4,1,3:T(8,128)S(1)} %fusion.32, f32[128,32,128,1,1]{0,2,4,1,3:T(8,128)S(1)} %fusion.34, f32[128,32,128,1,1]{0,2,4,1,3:T(8,128)S(1)} %copy-done.1, f32[128,32,128,1,1]{0,2,4,1,3:T(8,128)S(1)} %fusion.38, ...), kind=kOutput, calls=%fused_computation.19 | convolution fusion | flops 103809024 | bytes 12345344 | tf_op jit(solution)/shard_map/qcht,qchkl->tkl/dot_general | solution.py:109
  165.1 2.3 %copy.81 = bf16[128,4096]{1,0:T(8,128)(2,1)} copy(bf16[128,4096]{0,1:T(8,128)(2,1)} %bitcast.159) | data formatting | bytes 2097152 | tf_op jit(solution)/shard_map/convert_element_type | solution.py:113
  (42 shorter events, 11.6 us)
Async XLA Ops:
  0.0 72.4 %collective-permute-start = (bf16[1,4096,768]{2,1,0:T(8,128)(2,1)}, bf16[1,4096,768]{2,1,0:T(8,128)(2,1)}, u32[]{:S(2)}, u32[]{:S(2)}) collective-permute-start(bf16[1,4096,768]{2,1,0:T(8,128)(2,1)} %param.8), channel_id=1, source_target_pairs={{0,1},{1,0},{2,3},{3,2},{4,5},{5,4},{6,7},{7,6},{8,9},{9,8},{10,11... | collective-permute-start | bytes 18874376 | tf_op jit(solution)/shard_map/ppermute | solution.py:20
  5.0 21.6 %collective-permute-start.2 = (bf16[16,6,32,128]{3,2,1,0:T(8,128)(2,1)}, bf16[16,6,32,128]{3,2,1,0:T(8,128)(2,1)}, u32[]{:S(2)}, u32[]{:S(2)}) collective-permute-start(bf16[16,6,32,128]{3,2,1,0:T(8,128)(2,1)} %bitcast.28), channel_id=1, source_target_pairs={{0,240},{16,0},{32,16},{48,32},{64,48},{80,64},{96,80},{112,96},{1... | collective-permute-start | bytes 2359304 | tf_op jit(solution)/shard_map/ppermute | solution.py:14
  7.3 12.7 %copy-start = (bf16[1,384,4096]{2,1,0:T(8,128)(2,1)S(1)}, bf16[1,384,4096]{2,1,0:T(8,128)(2,1)}, u32[]{:S(2)}) copy-start(bf16[1,384,4096]{2,1,0:T(8,128)(2,1)} %param.9) | copy-start | bytes 9437188
  8.4 21.6 %collective-permute-start.3 = (bf16[16,6,32,128]{3,2,1,0:T(8,128)(2,1)}, bf16[16,6,32,128]{3,2,1,0:T(8,128)(2,1)}, u32[]{:S(2)}, u32[]{:S(2)}) collective-permute-start(bf16[16,6,32,128]{3,2,1,0:T(8,128)(2,1)} %bitcast.30), channel_id=1, source_target_pairs={{0,224},{16,240},{32,0},{48,16},{64,32},{80,48},{96,64},{112,80},{... | collective-permute-start | bytes 2359304 | tf_op jit(solution)/shard_map/ppermute | solution.py:14
  13.6 23.6 %all-to-all-start = ((bf16[16,6,32,128]{3,2,1,0:T(8,128)(2,1)}), bf16[16,6,32,128]{3,2,1,0:T(8,128)(2,1)}, u32[]{:S(2)}, u32[]{:S(2)}) async-start(bf16[16,6,32,128]{3,2,1,0:T(8,128)(2,1)} %bitcast.160), calls=%async_computation | async-start | bytes 1572864 | tf_op jit(solution)/shard_map/all_to_all | solution.py:80
  20.1 56.7 %collective-permute-start.1 = (bf16[1,384,4096]{2,1,0:T(8,128)(2,1)S(1)}, bf16[1,384,4096]{2,1,0:T(8,128)(2,1)}, u32[]{:S(2)}, u32[]{:S(2)}) collective-permute-start(bf16[1,384,4096]{2,1,0:T(8,128)(2,1)S(1)} %copy-done), channel_id=1, source_target_pairs={{0,1},{1,0},{2,3},{3,2},{4,5},{5,4},{6,7},{7,6},{8,9},{9,8},{10,11... | collective-permute-start | bytes 9437192 | tf_op jit(solution)/shard_map/ppermute | solution.py:20
  37.1 28.2 %all-to-all-start.2 = ((bf16[16,2,6,32,128]{4,3,2,1,0:T(8,128)(2,1)}), bf16[16,2,6,32,128]{4,3,2,1,0:T(8,128)(2,1)}, u32[]{:S(2)}, u32[]{:S(2)}) async-start(bf16[16,2,6,32,128]{4,3,2,1,0:T(8,128)(2,1)} %copy.73), calls=%async_computation.2 | async-start | bytes 3145728 | tf_op jit(solution)/shard_map/all_to_all | solution.py:82
  80.2 27.0 %collective-permute-start.5 = (bf16[16,6,32,128]{3,2,1,0:T(8,128)(2,1)S(1)}, bf16[16,6,32,128]{3,2,1,0:T(8,128)(2,1)S(1)}, u32[]{:S(2)}, u32[]{:S(2)}) collective-permute-start(bf16[16,6,32,128]{3,2,1,0:T(8,128)(2,1)S(1)} %bitcast.165), channel_id=1, source_target_pairs={{0,32},{16,48},{32,64},{48,80},{64,96},{80,112},{96,128},{112,144}... | collective-permute-start | bytes 2359304 | tf_op jit(solution)/shard_map/ppermute | solution.py:14
  82.4 17.5 %copy-start.2 = (f32[96,4096]{1,0:T(8,128)S(1)}, f32[96,4096]{1,0:T(8,128)}, u32[]{:S(2)}) copy-start(f32[96,4096]{1,0:T(8,128)} %fusion.14) | copy-start | bytes 4718596
  82.4 33.4 %collective-permute-start.4 = (bf16[16,6,32,128]{3,2,1,0:T(8,128)(2,1)S(1)}, bf16[16,6,32,128]{3,2,1,0:T(8,128)(2,1)}, u32[]{:S(2)}, u32[]{:S(2)}) collective-permute-start(bf16[16,6,32,128]{3,2,1,0:T(8,128)(2,1)S(1)} %bitcast.164), channel_id=1, source_target_pairs={{0,16},{16,32},{32,48},{48,64},{64,80},{80,96},{96,112},{112,128},... | collective-permute-start | bytes 2359304 | tf_op jit(solution)/shard_map/ppermute | solution.py:14
  103.5 25.6 %all-to-all-start.1 = ((bf16[16,6,32,128]{3,2,1,0:T(8,128)(2,1)}), bf16[16,6,32,128]{3,2,1,0:T(8,128)(2,1)S(1)}, u32[]{:S(2)}, u32[]{:S(2)}) async-start(bf16[16,6,32,128]{3,2,1,0:T(8,128)(2,1)} %bitcast.80), calls=%async_computation.1 | async-start | bytes 1572864 | tf_op jit(solution)/shard_map/all_to_all | solution.py:97
  118.3 16.0 %copy-start.3 = (s32[128,8]{0,1:T(8,128)S(1)}, s32[128,8]{0,1:T(8,128)}, u32[]{:S(2)}) copy-start(s32[128,8]{0,1:T(8,128)} %param.6) | copy-start | bytes 12292
  118.3 16.1 %copy-start.4 = (f32[128,8]{0,1:T(8,128)S(1)}, f32[128,8]{0,1:T(8,128)}, u32[]{:S(2)}) copy-start(f32[128,8]{0,1:T(8,128)} %param.7) | copy-start | bytes 12292
  129.2 28.9 %all-to-all-start.3 = ((bf16[16,2,6,32,128]{4,3,2,1,0:T(8,128)(2,1)}), bf16[16,2,6,32,128]{4,3,2,1,0:T(8,128)(2,1)}, u32[]{:S(2)}, u32[]{:S(2)}) async-start(bf16[16,2,6,32,128]{4,3,2,1,0:T(8,128)(2,1)} %pad_maximum_fusion.1), calls=%async_computation.3 | async-start | bytes 3145728 | tf_op jit(solution)/shard_map/all_to_all | solution.py:98
  161.3 1.6 copy-start.1

commit v12 on v11

--- a/solution.py
+++ b/solution.py
@@ -90,6 +90,7 @@
         w_in_other[0],
         w_out_other[0],
     )
+    near_done, far_done = lax.optimization_barrier((near_done, far_done))
     done = jnp.concatenate([near_done, far_done], axis=0)
     done = done.reshape(STEPS, inner_count, half_cap, lanes_major, 128)
 

time: 168 us -> 178 us (1.060)
  waiting for transfers between devices: 71.5 us -> 91.4 us
  starting transfers between devices: 41.9 us -> 35.1 us
  other arithmetic: 5.32 us -> 3.26 us
  local copies, waits for them, and re-layouts: 14.5 us -> 12.7 us
    ppermute x4, waiting for transfers between devices: 18.1 us -> 47 us  [shifted(): return lax.ppermute(value, axis, pairs)]
    ppermute x4, starting transfers between devices: 21.8 us -> 14.6 us  [shifted(): return lax.ppermute(value, axis, pairs)]
    all_to_all x1, waiting for transfers between devices: 4.17 us -> 0.01 us  [on_device(): lax.all_to_all(near, 'inner', split_axis=0, concat_axis=0, tiled=True)]
    all_to_all x1, waiting for transfers between devices: 10.9 us -> 6.97 us  [on_device(): lax.all_to_all(done[0], 'inner', split_axis=0, concat_axis=0, tiled=True)]
  transfers between devices with their start and end apart: 10 -> 10, of which waited for: 7 -> 7; matrix products, arithmetic and copies ran while one was open for 25% -> 20% of each run, Pallas kernels for 0% -> 0%
where the time goes in v12:
time: 178 us; the launch traced here: 177 us
  waiting for transfers between devices  91.4 us (51%)
  starting transfers between devices  35.1 us (20%)
  matrix products  34 us (19%)
  local copies, waits for them, and re-layouts  12.7 us (7%)
  other arithmetic  3.26 us (2%)
    ppermute x4, waiting for transfers between devices, shifted(): return lax.ppermute(value, axis, pairs)  47 us
    all_to_all x1, waiting for transfers between devices, on_device(): lax.all_to_all(jnp.stack(far_back, axis=1), 'inner', split_axis=0, concat...  20.4 us
    dot_general x4, matrix products, one_half(): projected = jnp.dot(rows, w_in_now, preferred_element_type=jnp.float32)  17.3 us
    all_to_all x1, waiting for transfers between devices, on_device(): far = lax.all_to_all(far, 'inner', split_axis=0, concat_axis=0, tiled=True)  17 us
    ppermute x4, starting transfers between devices, shifted(): return lax.ppermute(value, axis, pairs)  14.6 us
    dot_general x4, matrix products, one_half(): return jnp.dot(activated, w_out_now, preferred_element_type=jnp.float32)  8.49 us
    all_to_all x1, waiting for transfers between devices, on_device(): lax.all_to_all(done[0], 'inner', split_axis=0, concat_axis=0, tiled=True)  6.97 us
    all_to_all x1, starting transfers between devices, on_device(): lax.all_to_all(near, 'inner', split_axis=0, concat_axis=0, tiled=True)  6.47 us
  transfers between devices with their start and end apart: 10, of which 7 were waited for; matrix products, arithmetic and copies ran while one was open for 20% of the time, Pallas kernels for 0%

profile of v12, /device:TPU:2, one launch (start us, length us, event | category | flops | bytes accessed | tf_op | source)
XLA Modules:
  0.0 176.7 jit_solution(9997434001072096519)
XLA Ops:
  0.0 1.5 copy.100
  3.5 5.9 %collective-permute-start.3 = (bf16[16,6,32,128]{3,2,1,0:T(8,128)(2,1)S(1)}, bf16[16,6,32,128]{3,2,1,0:T(8,128)(2,1)S(1)}, u32[]{:S(2)}, u32[]{:S(2)}) collective-permute-start(bf16[16,6,32,128]{3,2,1,0:T(8,128)(2,1)S(1)} %bitcast.161), channel_id=1, source_target_pairs={{0,224},{16,240},{32,0},{48,16},{64,32},{80,48},{96,64},{112,80},{... | collective-permute-start | bytes 2359304 | tf_op jit(solution)/shard_map/ppermute | solution.py:14
  10.2 1.0 copy.68
  11.2 6.5 %all-to-all-start = ((bf16[16,6,32,128]{3,2,1,0:T(8,128)(2,1)}), bf16[16,6,32,128]{3,2,1,0:T(8,128)(2,1)}, u32[]{:S(2)}, u32[]{:S(2)}) async-start(bf16[16,6,32,128]{3,2,1,0:T(8,128)(2,1)} %bitcast.12), calls=%async_computation | async-start | bytes 1572864 | tf_op jit(solution)/shard_map/all_to_all | solution.py:80
  17.7 9.2 %collective-permute-done.3 = bf16[16,6,32,128]{3,2,1,0:T(8,128)(2,1)S(1)} collective-permute-done((bf16[16,6,32,128]{3,2,1,0:T(8,128)(2,1)S(1)}, bf16[16,6,32,128]{3,2,1,0:T(8,128)(2,1)S(1)}, u32[]{:S(2)}, u32[]{:S(2)}) %collective-permute-start.3) | collective-permute-done | bytes 786464 | tf_op jit(solution)/shard_map/ppermute | solution.py:14
  26.9 15.3 %collective-permute-done.2 = bf16[16,6,32,128]{3,2,1,0:T(8,128)(2,1)S(1)} collective-permute-done((bf16[16,6,32,128]{3,2,1,0:T(8,128)(2,1)S(1)}, bf16[16,6,32,128]{3,2,1,0:T(8,128)(2,1)S(1)}, u32[]{:S(2)}, u32[]{:S(2)}) %collective-permute-start.2) | collective-permute-done | bytes 786464 | tf_op jit(solution)/shard_map/ppermute | solution.py:14
  42.3 1.5 copy.71
  43.8 5.2 %all-to-all-start.1 = ((bf16[16,2,6,32,128]{4,3,2,1,0:T(8,128)(2,1)}), bf16[16,2,6,32,128]{4,3,2,1,0:T(8,128)(2,1)}, u32[]{:S(2)}, u32[]{:S(2)}) async-start(bf16[16,2,6,32,128]{4,3,2,1,0:T(8,128)(2,1)} %copy.71), calls=%async_computation.1 | async-start | bytes 3145728 | tf_op jit(solution)/shard_map/all_to_all | solution.py:82
  49.6 4.2 %fusion.6 = f32[96,768]{1,0:T(8,128)S(1)} fusion(bf16[1,4096,768]{2,1,0:T(8,128)(2,1)} %param.8, bf16[12,8,32,128]{3,2,1,0:T(8,128)(2,1)} %bitcast.76), kind=kOutput, calls=%fused_computation.6 | convolution fusion | flops 603979776 | bytes 7372800 | tf_op jit(solution)/shard_map/dot_general | solution.py:27
  53.8 1.9 %fusion.14 = f32[96,4096]{1,0:T(8,128)} fusion(bf16[1,384,4096]{2,1,0:T(8,128)(2,1)S(1)} %copy-done, f32[96,768]{1,0:T(8,128)S(1)} %fusion.6), kind=kOutput, calls=%fused_computation.16 | convolution fusion | flops 302211072 | bytes 5013504 | tf_op jit(solution)/shard_map/dot_general | solution.py:31
  55.7 17.0 %all-to-all-done.1 = bf16[16,2,6,32,128]{4,3,2,1,0:T(8,128)(2,1)} async-done(((bf16[16,2,6,32,128]{4,3,2,1,0:T(8,128)(2,1)}), bf16[16,2,6,32,128]{4,3,2,1,0:T(8,128)(2,1)}, u32[]{:S(2)}, u32[]{:S(2)}) %all-to-all-start.1) | async-done | bytes 1572896 | tf_op jit(solution)/shard_map/all_to_all | solution.py:82
  72.8 1.7 copy.72
  74.5 4.4 %fusion.4 = f32[192,768]{1,0:T(8,128)S(1)} fusion(bf16[1,4096,768]{2,1,0:T(8,128)(2,1)} %param.8, bf16[24,8,32,128]{3,2,1,0:T(8,128)(2,1)S(1)} %bitcast.158), kind=kOutput, calls=%fused_computation.4 | convolution fusion | flops 1207959552 | bytes 8454144 | tf_op jit(solution)/shard_map/dot_general | solution.py:27
  78.8 1.0 fusion.12
  79.9 4.2 %fusion.2 = f32[96,768]{1,0:T(8,128)S(1)} fusion(bf16[1,4096,768]{2,1,0:T(8,128)(2,1)} %collective-permute-done, bf16[12,8,32,128]{3,2,1,0:T(8,128)(2,1)} %bitcast.76), kind=kOutput, calls=%fused_computation.2 | convolution fusion | flops 603979776 | bytes 7372800 | tf_op jit(solution)/shard_map/dot_general | solution.py:27
  84.1 4.5 %fusion = f32[192,768]{1,0:T(8,128)S(1)} fusion(bf16[1,4096,768]{2,1,0:T(8,128)(2,1)} %collective-permute-done, bf16[24,8,32,128]{3,2,1,0:T(8,128)(2,1)S(1)} %bitcast.159), kind=kOutput, calls=%fused_computation | convolution fusion | flops 1207959552 | bytes 8454144 | tf_op jit(solution)/shard_map/dot_general | solution.py:27
  88.6 2.6 %fusion.9 = bf16[96,4096]{1,0:T(8,128)(2,1)S(1)} fusion(f32[96,4096]{1,0:T(8,128)S(1)} %copy-done.2, bf16[1,384,4096]{2,1,0:T(8,128)(2,1)} %collective-permute-done.1, f32[96,768]{1,0:T(8,128)S(1)} %fusion.2), kind=kOutput, calls=%fused_computation.11 | convolution fusion | flops 302997504 | bytes 5799936 | tf_op jit(solution)/shard_map/dot_general | solution.py:31
  91.3 3.0 %fusion.8 = bf16[192,4096]{1,0:T(8,128)(2,1)S(1)} fusion(f32[192,4096]{1,0:T(8,128)S(1)} %fusion.12, bf16[1,384,4096]{2,1,0:T(8,128)(2,1)} %collective-permute-done.1, f32[192,768]{1,0:T(8,128)S(1)} %fusion), kind=kOutput, calls=%fused_computation.9 | convolution fusion | flops 605995008 | bytes 8454144 | tf_op jit(solution)/shard_map/dot_general | solution.py:31
  94.5 2.0 %collective-permute-start.5 = (bf16[16,6,32,128]{3,2,1,0:T(8,128)(2,1)S(1)}, bf16[16,6,32,128]{3,2,1,0:T(8,128)(2,1)S(1)}, u32[]{:S(2)}, u32[]{:S(2)}) collective-permute-start(bf16[16,6,32,128]{3,2,1,0:T(8,128)(2,1)S(1)} %bitcast.162), channel_id=1, source_target_pairs={{0,32},{16,48},{32,64},{48,80},{64,96},{80,112},{96,128},{112,144}... | collective-permute-start | bytes 2359304 | tf_op jit(solution)/shard_map/ppermute | solution.py:14
  96.7 6.0 %collective-permute-start.4 = (bf16[16,6,32,128]{3,2,1,0:T(8,128)(2,1)S(1)}, bf16[16,6,32,128]{3,2,1,0:T(8,128)(2,1)}, u32[]{:S(2)}, u32[]{:S(2)}) collective-permute-start(bf16[16,6,32,128]{3,2,1,0:T(8,128)(2,1)S(1)} %bitcast.164), channel_id=1, source_target_pairs={{0,16},{16,32},{32,48},{48,64},{64,80},{80,96},{96,112},{112,128},... | collective-permute-start | bytes 2359304 | tf_op jit(solution)/shard_map/ppermute | solution.py:14
  102.7 1.0 copy.103
  103.7 3.6 %all-to-all-start.2 = ((bf16[16,6,32,128]{3,2,1,0:T(8,128)(2,1)}), bf16[16,6,32,128]{3,2,1,0:T(8,128)(2,1)S(1)}, u32[]{:S(2)}, u32[]{:S(2)}) async-start(bf16[16,6,32,128]{3,2,1,0:T(8,128)(2,1)} %bitcast.83), calls=%async_computation.2 | async-start | bytes 1572864 | tf_op jit(solution)/shard_map/all_to_all | solution.py:98
  107.3 12.5 %collective-permute-done.5 = bf16[16,6,32,128]{3,2,1,0:T(8,128)(2,1)S(1)} collective-permute-done((bf16[16,6,32,128]{3,2,1,0:T(8,128)(2,1)S(1)}, bf16[16,6,32,128]{3,2,1,0:T(8,128)(2,1)S(1)}, u32[]{:S(2)}, u32[]{:S(2)}) %collective-permute-start.5) | collective-permute-done | bytes 786464 | tf_op jit(solution)/shard_map/ppermute | solution.py:14
  119.9 10.0 %collective-permute-done.4 = bf16[16,6,32,128]{3,2,1,0:T(8,128)(2,1)} collective-permute-done((bf16[16,6,32,128]{3,2,1,0:T(8,128)(2,1)S(1)}, bf16[16,6,32,128]{3,2,1,0:T(8,128)(2,1)}, u32[]{:S(2)}, u32[]{:S(2)}) %collective-permute-start.4) | collective-permute-done | bytes 786464 | tf_op jit(solution)/shard_map/ppermute | solution.py:14
  129.9 2.4 %pad_maximum_fusion.1 = bf16[16,2,6,32,128]{4,3,2,1,0:T(8,128)(2,1)} fusion(bf16[16,1,6,32,128]{4,3,2,1,0:T(8,128)(2,1)S(1)} %bitcast.166, bf16[16,1,6,32,128]{4,3,2,1,0:T(8,128)(2,1)} %bitcast.33), kind=kLoop, calls=%fused_computation.28 | loop fusion | flops 786432 | bytes 3145728 | tf_op jit(solution)/shard_map/stack | solution.py:100
  132.4 7.0 %all-to-all-done.2 = bf16[16,6,32,128]{3,2,1,0:T(8,128)(2,1)S(1)} async-done(((bf16[16,6,32,128]{3,2,1,0:T(8,128)(2,1)}), bf16[16,6,32,128]{3,2,1,0:T(8,128)(2,1)S(1)}, u32[]{:S(2)}, u32[]{:S(2)}) %all-to-all-start.2) | async-done | bytes 786464 | tf_op jit(solution)/shard_map/all_to_all | solution.py:98
  139.3 4.6 %all-to-all-start.3 = ((bf16[16,2,6,32,128]{4,3,2,1,0:T(8,128)(2,1)}), bf16[16,2,6,32,128]{4,3,2,1,0:T(8,128)(2,1)}, u32[]{:S(2)}, u32[]{:S(2)}) async-start(bf16[16,2,6,32,128]{4,3,2,1,0:T(8,128)(2,1)} %pad_maximum_fusion.1), calls=%async_computation.3 | async-start | bytes 3145728 | tf_op jit(solution)/shard_map/all_to_all | solution.py:99
  145.0 2.1 %fusion.35 = f32[128,32,128,1,1]{0,2,4,1,3:T(8,128)} fusion(bf16[8,2,6,32,128]{4,3,2,1,0:T(8,128)(2,1)S(1)} %bitcast.150, bf16[3,8,2,6,128]{4,1,3,2,0:T(8,128)(2,1)S(1)} %select_convert_fusion), kind=kOutput, calls=%fused_computation.47 | convolution fusion | flops 100663296 | bytes 2908160 | tf_op jit(solution)/shard_map/qcht,qchkl->tkl/dot_general | solution.py:107
  147.1 20.4 %all-to-all-done.3 = bf16[16,2,6,32,128]{4,3,2,1,0:T(8,128)(2,1)} async-done(((bf16[16,2,6,32,128]{4,3,2,1,0:T(8,128)(2,1)}), bf16[16,2,6,32,128]{4,3,2,1,0:T(8,128)(2,1)}, u32[]{:S(2)}, u32[]{:S(2)}) %all-to-all-start.3) | async-done | bytes 1572896 | tf_op jit(solution)/shard_map/all_to_all | solution.py:99
  167.5 1.6 fusion.62
  172.3 2.2 %fusion.16 = bf16[128,32,128]{0,2,1:T(8,128)(2,1)} fusion(f32[128,32,128,1,1]{0,2,4,1,3:T(8,128)S(1)} %fusion.27, f32[128,32,128,1,1]{0,2,4,1,3:T(8,128)S(1)} %fusion.29, f32[128,32,128,1,1]{0,2,4,1,3:T(8,128)S(1)} %fusion.31, f32[128,32,128,1,1]{0,2,4,1,3:T(8,128)S(1)} %fusion.33, f32[128,32,128,1,1]{0,2,4,1,3:T(8,128)S(1)} %copy-done.1, ...), kind=kOutput, calls=%fused_computation.19 | convolution fusion | flops 103809024 | bytes 12345344 | tf_op jit(solution)/shard_map/qcht,qchkl->tkl/dot_general | solution.py:110
  174.5 2.3 %copy.81 = bf16[128,4096]{1,0:T(8,128)(2,1)} copy(bf16[128,4096]{0,1:T(8,128)(2,1)} %bitcast.156) | data formatting | bytes 2097152 | tf_op jit(solution)/shard_map/convert_element_type | solution.py:114
  (42 shorter events, 8.1 us)
Async XLA Ops:
  0.0 1.6 copy-start.3
  0.0 79.9 %collective-permute-start = (bf16[1,4096,768]{2,1,0:T(8,128)(2,1)}, bf16[1,4096,768]{2,1,0:T(8,128)(2,1)}, u32[]{:S(2)}, u32[]{:S(2)}) collective-permute-start(bf16[1,4096,768]{2,1,0:T(8,128)(2,1)} %param.8), channel_id=1, source_target_pairs={{0,1},{1,0},{2,3},{3,2},{4,5},{5,4},{6,7},{7,6},{8,9},{9,8},{10,11... | collective-permute-start | bytes 18874376 | tf_op jit(solution)/shard_map/ppermute | solution.py:20
  3.5 23.4 %collective-permute-start.3 = (bf16[16,6,32,128]{3,2,1,0:T(8,128)(2,1)S(1)}, bf16[16,6,32,128]{3,2,1,0:T(8,128)(2,1)S(1)}, u32[]{:S(2)}, u32[]{:S(2)}) collective-permute-start(bf16[16,6,32,128]{3,2,1,0:T(8,128)(2,1)S(1)} %bitcast.161), channel_id=1, source_target_pairs={{0,224},{16,240},{32,0},{48,16},{64,32},{80,48},{96,64},{112,80},{... | collective-permute-start | bytes 2359304 | tf_op jit(solution)/shard_map/ppermute | solution.py:14
  9.6 32.6 %collective-permute-start.2 = (bf16[16,6,32,128]{3,2,1,0:T(8,128)(2,1)S(1)}, bf16[16,6,32,128]{3,2,1,0:T(8,128)(2,1)S(1)}, u32[]{:S(2)}, u32[]{:S(2)}) collective-permute-start(bf16[16,6,32,128]{3,2,1,0:T(8,128)(2,1)S(1)} %bitcast.163), channel_id=1, source_target_pairs={{0,240},{16,0},{32,16},{48,32},{64,48},{80,64},{96,80},{112,96},{1... | collective-permute-start | bytes 2359304 | tf_op jit(solution)/shard_map/ppermute | solution.py:14
  11.2 32.5 %all-to-all-start = ((bf16[16,6,32,128]{3,2,1,0:T(8,128)(2,1)}), bf16[16,6,32,128]{3,2,1,0:T(8,128)(2,1)}, u32[]{:S(2)}, u32[]{:S(2)}) async-start(bf16[16,6,32,128]{3,2,1,0:T(8,128)(2,1)} %bitcast.12), calls=%async_computation | async-start | bytes 1572864 | tf_op jit(solution)/shard_map/all_to_all | solution.py:80
  43.8 5.2 %copy-start = (bf16[1,384,4096]{2,1,0:T(8,128)(2,1)S(1)}, bf16[1,384,4096]{2,1,0:T(8,128)(2,1)}, u32[]{:S(2)}) copy-start(bf16[1,384,4096]{2,1,0:T(8,128)(2,1)} %param.9) | copy-start | bytes 9437188
  43.8 29.0 %all-to-all-start.1 = ((bf16[16,2,6,32,128]{4,3,2,1,0:T(8,128)(2,1)}), bf16[16,2,6,32,128]{4,3,2,1,0:T(8,128)(2,1)}, u32[]{:S(2)}, u32[]{:S(2)}) async-start(bf16[16,2,6,32,128]{4,3,2,1,0:T(8,128)(2,1)} %copy.71), calls=%async_computation.1 | async-start | bytes 3145728 | tf_op jit(solution)/shard_map/all_to_all | solution.py:82
  49.0 39.7 %collective-permute-start.1 = (bf16[1,384,4096]{2,1,0:T(8,128)(2,1)S(1)}, bf16[1,384,4096]{2,1,0:T(8,128)(2,1)}, u32[]{:S(2)}, u32[]{:S(2)}) collective-permute-start(bf16[1,384,4096]{2,1,0:T(8,128)(2,1)S(1)} %copy-done), channel_id=1, source_target_pairs={{0,1},{1,0},{2,3},{3,2},{4,5},{5,4},{6,7},{7,6},{8,9},{9,8},{10,11... | collective-permute-start | bytes 9437192 | tf_op jit(solution)/shard_map/ppermute | solution.py:20
  84.1 4.5 %copy-start.2 = (f32[96,4096]{1,0:T(8,128)S(1)}, f32[96,4096]{1,0:T(8,128)}, u32[]{:S(2)}) copy-start(f32[96,4096]{1,0:T(8,128)} %fusion.14) | copy-start | bytes 4718596
  94.5 25.4 %collective-permute-start.5 = (bf16[16,6,32,128]{3,2,1,0:T(8,128)(2,1)S(1)}, bf16[16,6,32,128]{3,2,1,0:T(8,128)(2,1)S(1)}, u32[]{:S(2)}, u32[]{:S(2)}) collective-permute-start(bf16[16,6,32,128]{3,2,1,0:T(8,128)(2,1)S(1)} %bitcast.162), channel_id=1, source_target_pairs={{0,32},{16,48},{32,64},{48,80},{64,96},{80,112},{96,128},{112,144}... | collective-permute-start | bytes 2359304 | tf_op jit(solution)/shard_map/ppermute | solution.py:14
  96.7 33.2 %collective-permute-start.4 = (bf16[16,6,32,128]{3,2,1,0:T(8,128)(2,1)S(1)}, bf16[16,6,32,128]{3,2,1,0:T(8,128)(2,1)}, u32[]{:S(2)}, u32[]{:S(2)}) collective-permute-start(bf16[16,6,32,128]{3,2,1,0:T(8,128)(2,1)S(1)} %bitcast.164), channel_id=1, source_target_pairs={{0,16},{16,32},{32,48},{48,64},{64,80},{80,96},{96,112},{112,128},... | collective-permute-start | bytes 2359304 | tf_op jit(solution)/shard_map/ppermute | solution.py:14
  103.7 35.6 %all-to-all-start.2 = ((bf16[16,6,32,128]{3,2,1,0:T(8,128)(2,1)}), bf16[16,6,32,128]{3,2,1,0:T(8,128)(2,1)S(1)}, u32[]{:S(2)}, u32[]{:S(2)}) async-start(bf16[16,6,32,128]{3,2,1,0:T(8,128)(2,1)} %bitcast.83), calls=%async_computation.2 | async-start | bytes 1572864 | tf_op jit(solution)/shard_map/all_to_all | solution.py:98
  132.4 11.6 %copy-start.4 = (f32[128,8]{0,1:T(8,128)S(1)}, f32[128,8]{0,1:T(8,128)}, u32[]{:S(2)}) copy-start(f32[128,8]{0,1:T(8,128)} %param.7) | copy-start | bytes 12292
  139.3 28.2 %all-to-all-start.3 = ((bf16[16,2,6,32,128]{4,3,2,1,0:T(8,128)(2,1)}), bf16[16,2,6,32,128]{4,3,2,1,0:T(8,128)(2,1)}, u32[]{:S(2)}, u32[]{:S(2)}) async-start(bf16[16,2,6,32,128]{4,3,2,1,0:T(8,128)(2,1)} %pad_maximum_fusion.1), calls=%async_computation.3 | async-start | bytes 3145728 | tf_op jit(solution)/shard_map/all_to_all | solution.py:99
  170.7 1.6 copy-start.1

commit v13 on v11

--- a/solution.py
+++ b/solution.py
@@ -61,8 +61,6 @@
     scale = jnp.where(
         one_hot, weighting.T.reshape(STEPS, group_count, 1, 1, tok_rows), 0.0
     )
-    scale_hi = scale.astype(jnp.bfloat16)
-    scale_lo = (scale - scale_hi.astype(jnp.float32)).astype(jnp.bfloat16)
     lanes_major = width // 128
     dense = tokens.reshape(tok_rows, lanes_major, 128)
     picked = jnp.einsum(
@@ -98,16 +96,24 @@
     far_back = lax.all_to_all(
         jnp.stack(far_back, axis=1), "inner", split_axis=0, concat_axis=0, tiled=True
     )
-    backs = [near_back] + [far_back[:, rotation - 1] for rotation in range(1, STEPS)]
-
+    near_scale = scale[0].transpose(3, 0, 1, 2)
+    far_scale = scale[1:].transpose(4, 1, 2, 0, 3)
+    near_back = near_back.reshape(group_count, SPLIT, half_cap, lanes_major, 128)
+    far_back = far_back.reshape(group_count, SPLIT, STEPS - 1, half_cap, lanes_major, 128)
     combined = jnp.zeros((tok_rows, lanes_major, 128), jnp.float32)
-    for rotation in range(STEPS):
-        back = backs[rotation].reshape(group_count, SPLIT, half_cap, lanes_major, 128)
+    for weights in (near_scale, near_scale - near_scale.astype(jnp.bfloat16).astype(jnp.float32)):
         combined = combined + jnp.einsum(
-            "qcht,qchkl->tkl", scale_hi[rotation], back, preferred_element_type=jnp.float32
+            "tqch,qchkl->tkl",
+            weights.astype(jnp.bfloat16),
+            near_back,
+            preferred_element_type=jnp.float32,
         )
+    for weights in (far_scale, far_scale - far_scale.astype(jnp.bfloat16).astype(jnp.float32)):
         combined = combined + jnp.einsum(
-            "qcht,qchkl->tkl", scale_lo[rotation], back, preferred_element_type=jnp.float32
+            "tqcrh,qcrhkl->tkl",
+            weights.astype(jnp.bfloat16),
+            far_back,
+            preferred_element_type=jnp.float32,
         )
     combined = combined.reshape(tok_rows, width)
     return combined.astype(jnp.bfloat16)

time: 168 us -> 169 us (level)
  waiting for transfers between devices: 71.5 us -> 75.7 us
  local copies, waits for them, and re-layouts: 14.5 us -> 11.2 us
  matrix products: 33.8 us -> 35.6 us
    ppermute x4, waiting for transfers between devices: 18.1 us -> 34.5 us  [shifted(): return lax.ppermute(value, axis, pairs)]
    all_to_all x1, waiting for transfers between devices: 10.9 us -> 0.01 us  [on_device(): lax.all_to_all(done[0], 'inner', split_axis=0, concat_axis=0, tiled=True)]
    dot_general x6 -> x4, matrix products: 7.29 us -> 9.03 us  [the longest x2 4.88 us: on_device(): jnp.einsum('tqcrh,qcrhkl->tkl', weights.astype(jnp.bfloat16), far_back, p...]
where the time goes in v13:
time: 169 us
  waiting for transfers between devices  75.7 us (45%)
  starting transfers between devices  40.7 us (24%)
  matrix products  35.6 us (21%)
  local copies, waits for them, and re-layouts  11.2 us (7%)
  other arithmetic  5.21 us (3%)
    ppermute x4, waiting for transfers between devices, shifted(): return lax.ppermute(value, axis, pairs)  34.5 us
    ppermute x4, starting transfers between devices, shifted(): return lax.ppermute(value, axis, pairs)  21.9 us
    all_to_all x1, waiting for transfers between devices, on_device(): lax.all_to_all(jnp.stack(far_back, axis=1), 'inner', split_axis=0, concat...  19.4 us
    all_to_all x1, waiting for transfers between devices, on_device(): far = lax.all_to_all(far, 'inner', split_axis=0, concat_axis=0, tiled=True)  17.6 us
    dot_general x4, matrix products, one_half(): projected = jnp.dot(rows, w_in_now, preferred_element_type=jnp.float32)  17.2 us
    dot_general x4, matrix products, one_half(): return jnp.dot(activated, w_out_now, preferred_element_type=jnp.float32)  8.51 us
    all_to_all x1, starting transfers between devices, on_device(): lax.all_to_all(near, 'inner', split_axis=0, concat_axis=0, tiled=True)  6.47 us
    dot_general x2, matrix products, on_device(): jnp.einsum('tqcrh,qcrhkl->tkl', weights.astype(jnp.bfloat16), far_back, p...  4.88 us
  transfers between devices with their start and end apart: 10, of which 7 were waited for; matrix products, arithmetic and copies ran while one was open for 25% of the time, Pallas kernels for 0%

profile of v13, /device:TPU:2, one launch (start us, length us, event | category | flops | bytes accessed | tf_op | source)
XLA Modules:
  0.0 168.6 jit_solution(8785229600366904499)
XLA Ops:
  1.4 1.5 copy.94
  5.0 2.3 %collective-permute-start.2 = (bf16[16,6,32,128]{3,2,1,0:T(8,128)(2,1)}, bf16[16,6,32,128]{3,2,1,0:T(8,128)(2,1)}, u32[]{:S(2)}, u32[]{:S(2)}) collective-permute-start(bf16[16,6,32,128]{3,2,1,0:T(8,128)(2,1)} %bitcast.28), channel_id=1, source_target_pairs={{0,240},{16,0},{32,16},{48,32},{64,48},{80,64},{96,80},{112,96},{1... | collective-permute-start | bytes 2359304 | tf_op jit(solution)/shard_map/ppermute | solution.py:14
  8.4 4.1 %collective-permute-start.3 = (bf16[16,6,32,128]{3,2,1,0:T(8,128)(2,1)}, bf16[16,6,32,128]{3,2,1,0:T(8,128)(2,1)}, u32[]{:S(2)}, u32[]{:S(2)}) collective-permute-start(bf16[16,6,32,128]{3,2,1,0:T(8,128)(2,1)} %bitcast.30), channel_id=1, source_target_pairs={{0,224},{16,240},{32,0},{48,16},{64,32},{80,48},{96,64},{112,80},{... | collective-permute-start | bytes 2359304 | tf_op jit(solution)/shard_map/ppermute | solution.py:14
  13.5 6.5 %all-to-all-start = ((bf16[16,6,32,128]{3,2,1,0:T(8,128)(2,1)}), bf16[16,6,32,128]{3,2,1,0:T(8,128)(2,1)}, u32[]{:S(2)}, u32[]{:S(2)}) async-start(bf16[16,6,32,128]{3,2,1,0:T(8,128)(2,1)} %bitcast.156), calls=%async_computation | async-start | bytes 1572864 | tf_op jit(solution)/shard_map/all_to_all | solution.py:78
  20.5 6.2 %collective-permute-done.2 = bf16[16,6,32,128]{3,2,1,0:T(8,128)(2,1)} collective-permute-done((bf16[16,6,32,128]{3,2,1,0:T(8,128)(2,1)}, bf16[16,6,32,128]{3,2,1,0:T(8,128)(2,1)}, u32[]{:S(2)}, u32[]{:S(2)}) %collective-permute-start.2) | collective-permute-done | bytes 786464 | tf_op jit(solution)/shard_map/ppermute | solution.py:14
  26.6 3.3 %collective-permute-done.3 = bf16[16,6,32,128]{3,2,1,0:T(8,128)(2,1)} collective-permute-done((bf16[16,6,32,128]{3,2,1,0:T(8,128)(2,1)}, bf16[16,6,32,128]{3,2,1,0:T(8,128)(2,1)}, u32[]{:S(2)}, u32[]{:S(2)}) %collective-permute-start.3) | collective-permute-done | bytes 786464 | tf_op jit(solution)/shard_map/ppermute | solution.py:14
  30.0 1.5 pad_maximum_fusion
  31.5 1.4 copy.71
  32.9 4.2 %all-to-all-done = bf16[16,6,32,128]{3,2,1,0:T(8,128)(2,1)} async-done(((bf16[16,6,32,128]{3,2,1,0:T(8,128)(2,1)}), bf16[16,6,32,128]{3,2,1,0:T(8,128)(2,1)}, u32[]{:S(2)}, u32[]{:S(2)}) %all-to-all-start) | async-done | bytes 786464 | tf_op jit(solution)/shard_map/all_to_all | solution.py:78
  37.1 4.4 %all-to-all-start.2 = ((bf16[16,2,6,32,128]{4,3,2,1,0:T(8,128)(2,1)}), bf16[16,2,6,32,128]{4,3,2,1,0:T(8,128)(2,1)}, u32[]{:S(2)}, u32[]{:S(2)}) async-start(bf16[16,2,6,32,128]{4,3,2,1,0:T(8,128)(2,1)} %copy.71), calls=%async_computation.2 | async-start | bytes 3145728 | tf_op jit(solution)/shard_map/all_to_all | solution.py:80
  41.5 4.2 %fusion.6 = f32[96,768]{1,0:T(8,128)S(1)} fusion(bf16[1,4096,768]{2,1,0:T(8,128)(2,1)} %param.8, bf16[12,8,32,128]{3,2,1,0:T(8,128)(2,1)} %bitcast.53), kind=kOutput, calls=%fused_computation.6 | convolution fusion | flops 603979776 | bytes 7372800 | tf_op jit(solution)/shard_map/dot_general | solution.py:27
  45.8 1.9 %fusion.14 = f32[96,4096]{1,0:T(8,128)} fusion(bf16[1,384,4096]{2,1,0:T(8,128)(2,1)S(1)} %copy-done, f32[96,768]{1,0:T(8,128)S(1)} %fusion.6), kind=kOutput, calls=%fused_computation.16 | convolution fusion | flops 302211072 | bytes 5013504 | tf_op jit(solution)/shard_map/dot_general | solution.py:31
  47.7 17.6 %all-to-all-done.2 = bf16[16,2,6,32,128]{4,3,2,1,0:T(8,128)(2,1)} async-done(((bf16[16,2,6,32,128]{4,3,2,1,0:T(8,128)(2,1)}), bf16[16,2,6,32,128]{4,3,2,1,0:T(8,128)(2,1)}, u32[]{:S(2)}, u32[]{:S(2)}) %all-to-all-start.2) | async-done | bytes 1572896 | tf_op jit(solution)/shard_map/all_to_all | solution.py:80
  65.3 1.7 %copy.72 = bf16[2,16,6,32,128]{4,3,2,1,0:T(8,128)(2,1)S(1)} copy(bf16[2,16,6,32,128]{4,3,2,0,1:T(8,128)(2,1)} %bitcast.32) | data formatting | bytes 3145728 | tf_op jit(solution)/shard_map/transpose | solution.py:85
  67.0 4.4 %fusion.4 = f32[192,768]{1,0:T(8,128)S(1)} fusion(bf16[1,4096,768]{2,1,0:T(8,128)(2,1)} %param.8, bf16[24,8,32,128]{3,2,1,0:T(8,128)(2,1)S(1)} %bitcast.157), kind=kOutput, calls=%fused_computation.4 | convolution fusion | flops 1207959552 | bytes 8454144 | tf_op jit(solution)/shard_map/dot_general | solution.py:27
  72.4 4.4 %fusion = f32[192,768]{1,0:T(8,128)S(1)} fusion(bf16[1,4096,768]{2,1,0:T(8,128)(2,1)} %collective-permute-done, bf16[24,8,32,128]{3,2,1,0:T(8,128)(2,1)S(1)} %bitcast.158), kind=kOutput, calls=%fused_computation | convolution fusion | flops 1207959552 | bytes 8454144 | tf_op jit(solution)/shard_map/dot_general | solution.py:27
  76.8 3.0 %fusion.8 = bf16[192,4096]{1,0:T(8,128)(2,1)S(1)} fusion(f32[192,4096]{1,0:T(8,128)S(1)} %fusion.12, bf16[1,384,4096]{2,1,0:T(8,128)(2,1)} %collective-permute-done.1, f32[192,768]{1,0:T(8,128)S(1)} %fusion), kind=kOutput, calls=%fused_computation.9 | convolution fusion | flops 605995008 | bytes 8454144 | tf_op jit(solution)/shard_map/dot_general | solution.py:31
  80.0 13.5 %collective-permute-start.4 = (bf16[16,6,32,128]{3,2,1,0:T(8,128)(2,1)S(1)}, bf16[16,6,32,128]{3,2,1,0:T(8,128)(2,1)S(1)}, u32[]{:S(2)}, u32[]{:S(2)}) collective-permute-start(bf16[16,6,32,128]{3,2,1,0:T(8,128)(2,1)S(1)} %bitcast.160), channel_id=1, source_target_pairs={{0,16},{16,32},{32,48},{48,64},{64,80},{80,96},{96,112},{112,128},... | collective-permute-start | bytes 2359304 | tf_op jit(solution)/shard_map/ppermute | solution.py:14
  93.7 2.0 %collective-permute-start.5 = (bf16[16,6,32,128]{3,2,1,0:T(8,128)(2,1)S(1)}, bf16[16,6,32,128]{3,2,1,0:T(8,128)(2,1)}, u32[]{:S(2)}, u32[]{:S(2)}) collective-permute-start(bf16[16,6,32,128]{3,2,1,0:T(8,128)(2,1)S(1)} %bitcast.161), channel_id=1, source_target_pairs={{0,32},{16,48},{32,64},{48,80},{64,96},{80,112},{96,128},{112,144}... | collective-permute-start | bytes 2359304 | tf_op jit(solution)/shard_map/ppermute | solution.py:14
  95.7 4.2 %fusion.2 = f32[96,768]{1,0:T(8,128)S(1)} fusion(bf16[1,4096,768]{2,1,0:T(8,128)(2,1)} %collective-permute-done, bf16[12,8,32,128]{3,2,1,0:T(8,128)(2,1)} %bitcast.53), kind=kOutput, calls=%fused_computation.2 | convolution fusion | flops 603979776 | bytes 7372800 | tf_op jit(solution)/shard_map/dot_general | solution.py:27
  99.9 2.6 %fusion.24 = bf16[12,8,32,128]{3,1,2,0:T(8,128)(2,1)S(1)} fusion(f32[96,4096]{1,0:T(8,128)S(1)} %copy-done.2, bf16[1,384,4096]{2,1,0:T(8,128)(2,1)} %collective-permute-done.1, f32[96,768]{1,0:T(8,128)S(1)} %fusion.2), kind=kOutput, calls=%fused_computation.32 | convolution fusion | flops 302997504 | bytes 5799936 | tf_op jit(solution)/shard_map/dot_general | solution.py:31
  103.6 3.6 %all-to-all-start.1 = ((bf16[16,6,32,128]{3,2,1,0:T(8,128)(2,1)}), bf16[16,6,32,128]{3,2,1,0:T(8,128)(2,1)S(1)}, u32[]{:S(2)}, u32[]{:S(2)}) async-start(bf16[16,6,32,128]{3,2,1,0:T(8,128)(2,1)} %bitcast.57), calls=%async_computation.1 | async-start | bytes 1572864 | tf_op jit(solution)/shard_map/all_to_all | solution.py:95
  107.2 6.7 %collective-permute-done.4 = bf16[16,6,32,128]{3,2,1,0:T(8,128)(2,1)S(1)} collective-permute-done((bf16[16,6,32,128]{3,2,1,0:T(8,128)(2,1)S(1)}, bf16[16,6,32,128]{3,2,1,0:T(8,128)(2,1)S(1)}, u32[]{:S(2)}, u32[]{:S(2)}) %collective-permute-start.4) | collective-permute-done | bytes 786464 | tf_op jit(solution)/shard_map/ppermute | solution.py:14
  114.0 18.3 %collective-permute-done.5 = bf16[16,6,32,128]{3,2,1,0:T(8,128)(2,1)} collective-permute-done((bf16[16,6,32,128]{3,2,1,0:T(8,128)(2,1)S(1)}, bf16[16,6,32,128]{3,2,1,0:T(8,128)(2,1)}, u32[]{:S(2)}, u32[]{:S(2)}) %collective-permute-start.5) | collective-permute-done | bytes 786464 | tf_op jit(solution)/shard_map/ppermute | solution.py:14
  132.2 2.5 %pad_maximum_fusion.1 = bf16[16,2,6,32,128]{4,3,2,1,0:T(8,128)(2,1)} fusion(bf16[16,1,6,32,128]{4,3,2,1,0:T(8,128)(2,1)} %bitcast.34, bf16[16,1,6,32,128]{4,3,2,1,0:T(8,128)(2,1)S(1)} %bitcast.162), kind=kLoop, calls=%fused_computation.26 | loop fusion | flops 786432 | bytes 3145728 | tf_op jit(solution)/shard_map/stack | solution.py:97
  134.7 3.8 %all-to-all-start.3 = ((bf16[16,2,6,32,128]{4,3,2,1,0:T(8,128)(2,1)}), bf16[16,2,6,32,128]{4,3,2,1,0:T(8,128)(2,1)S(1)}, u32[]{:S(2)}, u32[]{:S(2)}) async-start(bf16[16,2,6,32,128]{4,3,2,1,0:T(8,128)(2,1)} %pad_maximum_fusion.1), calls=%async_computation.3 | async-start | bytes 3145728 | tf_op jit(solution)/shard_map/all_to_all | solution.py:96
  138.7 2.1 %fusion.32 = f32[128,32,128,1,1]{0,2,4,1,3:T(8,128)} fusion(bf16[8,2,6,32,128]{4,3,2,1,0:T(8,128)(2,1)S(1)} %bitcast.152, f32[3,8,2,6,128]{4,1,3,2,0:T(8,128)S(1)} %fusion.45), kind=kOutput, calls=%fused_computation.40 | convolution fusion | flops 100712448 | bytes 2932736 | tf_op jit(solution)/shard_map/tqch,qchkl->tkl/dot_general | solution.py:105
  140.8 2.1 %fusion.34 = f32[128,32,128,1,1]{0,2,4,1,3:T(8,128)} fusion(bf16[8,2,6,32,128]{4,3,2,1,0:T(8,128)(2,1)S(1)} %bitcast.153, f32[3,8,2,6,128]{4,1,3,2,0:T(8,128)S(1)} %fusion.45), kind=kOutput, calls=%fused_computation.42 | convolution fusion | flops 100663296 | bytes 2908160 | tf_op jit(solution)/shard_map/tqch,qchkl->tkl/dot_general | solution.py:105
  142.9 19.4 %all-to-all-done.3 = bf16[16,2,6,32,128]{4,3,2,1,0:T(8,128)(2,1)S(1)} async-done(((bf16[16,2,6,32,128]{4,3,2,1,0:T(8,128)(2,1)}), bf16[16,2,6,32,128]{4,3,2,1,0:T(8,128)(2,1)S(1)}, u32[]{:S(2)}, u32[]{:S(2)}) %all-to-all-start.3) | async-done | bytes 1572896 | tf_op jit(solution)/shard_map/all_to_all | solution.py:96
  162.3 1.5 fusion.22
  163.9 3.4 %fusion.16 = bf16[128,32,128]{0,2,1:T(8,128)(2,1)S(1)} fusion(f32[128,32,128,1,1,1]{0,2,4,1,5,3:T(8,128)S(1)} %fusion.22, f32[128,32,128,1,1]{0,2,4,1,3:T(8,128)S(1)} %copy-done.1, f32[128,32,128,1,1]{0,2,4,1,3:T(8,128)} %fusion.34, bf16[8,2,2,6,32,128]{5,4,3,2,1,0:T(8,128)(2,1)S(1)} %bitcast.151, f32[3,8,2,6,128]{4,1,3,2,0:T(8,128)S(1)} %fusion.45), kind=kOutput, calls=%fused_computation.19 | convolution fusion | flops 203522048 | bytes 9011200 | tf_op jit(solution)/shard_map/tqcrh,qcrhkl->tkl/dot_general | solution.py:112
  167.2 1.3 copy.77
  (38 shorter events, 8.8 us)
Async XLA Ops:
  0.0 72.4 %collective-permute-start = (bf16[1,4096,768]{2,1,0:T(8,128)(2,1)}, bf16[1,4096,768]{2,1,0:T(8,128)(2,1)}, u32[]{:S(2)}, u32[]{:S(2)}) collective-permute-start(bf16[1,4096,768]{2,1,0:T(8,128)(2,1)} %param.8), channel_id=1, source_target_pairs={{0,1},{1,0},{2,3},{3,2},{4,5},{5,4},{6,7},{7,6},{8,9},{9,8},{10,11... | collective-permute-start | bytes 18874376 | tf_op jit(solution)/shard_map/ppermute | solution.py:20
  5.0 21.6 %collective-permute-start.2 = (bf16[16,6,32,128]{3,2,1,0:T(8,128)(2,1)}, bf16[16,6,32,128]{3,2,1,0:T(8,128)(2,1)}, u32[]{:S(2)}, u32[]{:S(2)}) collective-permute-start(bf16[16,6,32,128]{3,2,1,0:T(8,128)(2,1)} %bitcast.28), channel_id=1, source_target_pairs={{0,240},{16,0},{32,16},{48,32},{64,48},{80,64},{96,80},{112,96},{1... | collective-permute-start | bytes 2359304 | tf_op jit(solution)/shard_map/ppermute | solution.py:14
  7.3 12.7 %copy-start = (bf16[1,384,4096]{2,1,0:T(8,128)(2,1)S(1)}, bf16[1,384,4096]{2,1,0:T(8,128)(2,1)}, u32[]{:S(2)}) copy-start(bf16[1,384,4096]{2,1,0:T(8,128)(2,1)} %param.9) | copy-start | bytes 9437188
  8.4 21.6 %collective-permute-start.3 = (bf16[16,6,32,128]{3,2,1,0:T(8,128)(2,1)}, bf16[16,6,32,128]{3,2,1,0:T(8,128)(2,1)}, u32[]{:S(2)}, u32[]{:S(2)}) collective-permute-start(bf16[16,6,32,128]{3,2,1,0:T(8,128)(2,1)} %bitcast.30), channel_id=1, source_target_pairs={{0,224},{16,240},{32,0},{48,16},{64,32},{80,48},{96,64},{112,80},{... | collective-permute-start | bytes 2359304 | tf_op jit(solution)/shard_map/ppermute | solution.py:14
  13.5 23.6 %all-to-all-start = ((bf16[16,6,32,128]{3,2,1,0:T(8,128)(2,1)}), bf16[16,6,32,128]{3,2,1,0:T(8,128)(2,1)}, u32[]{:S(2)}, u32[]{:S(2)}) async-start(bf16[16,6,32,128]{3,2,1,0:T(8,128)(2,1)} %bitcast.156), calls=%async_computation | async-start | bytes 1572864 | tf_op jit(solution)/shard_map/all_to_all | solution.py:78
  20.0 56.8 %collective-permute-start.1 = (bf16[1,384,4096]{2,1,0:T(8,128)(2,1)S(1)}, bf16[1,384,4096]{2,1,0:T(8,128)(2,1)}, u32[]{:S(2)}, u32[]{:S(2)}) collective-permute-start(bf16[1,384,4096]{2,1,0:T(8,128)(2,1)S(1)} %copy-done), channel_id=1, source_target_pairs={{0,1},{1,0},{2,3},{3,2},{4,5},{5,4},{6,7},{7,6},{8,9},{9,8},{10,11... | collective-permute-start | bytes 9437192 | tf_op jit(solution)/shard_map/ppermute | solution.py:20
  37.1 28.2 %all-to-all-start.2 = ((bf16[16,2,6,32,128]{4,3,2,1,0:T(8,128)(2,1)}), bf16[16,2,6,32,128]{4,3,2,1,0:T(8,128)(2,1)}, u32[]{:S(2)}, u32[]{:S(2)}) async-start(bf16[16,2,6,32,128]{4,3,2,1,0:T(8,128)(2,1)} %copy.71), calls=%async_computation.2 | async-start | bytes 3145728 | tf_op jit(solution)/shard_map/all_to_all | solution.py:80
  80.0 33.9 %collective-permute-start.4 = (bf16[16,6,32,128]{3,2,1,0:T(8,128)(2,1)S(1)}, bf16[16,6,32,128]{3,2,1,0:T(8,128)(2,1)S(1)}, u32[]{:S(2)}, u32[]{:S(2)}) collective-permute-start(bf16[16,6,32,128]{3,2,1,0:T(8,128)(2,1)S(1)} %bitcast.160), channel_id=1, source_target_pairs={{0,16},{16,32},{32,48},{48,64},{64,80},{80,96},{96,112},{112,128},... | collective-permute-start | bytes 2359304 | tf_op jit(solution)/shard_map/ppermute | solution.py:14
  93.7 6.2 %copy-start.2 = (f32[96,4096]{1,0:T(8,128)S(1)}, f32[96,4096]{1,0:T(8,128)}, u32[]{:S(2)}) copy-start(f32[96,4096]{1,0:T(8,128)} %fusion.14) | copy-start | bytes 4718596
  93.7 38.5 %collective-permute-start.5 = (bf16[16,6,32,128]{3,2,1,0:T(8,128)(2,1)S(1)}, bf16[16,6,32,128]{3,2,1,0:T(8,128)(2,1)}, u32[]{:S(2)}, u32[]{:S(2)}) collective-permute-start(bf16[16,6,32,128]{3,2,1,0:T(8,128)(2,1)S(1)} %bitcast.161), channel_id=1, source_target_pairs={{0,32},{16,48},{32,64},{48,80},{64,96},{80,112},{96,128},{112,144}... | collective-permute-start | bytes 2359304 | tf_op jit(solution)/shard_map/ppermute | solution.py:14
  103.6 31.1 %all-to-all-start.1 = ((bf16[16,6,32,128]{3,2,1,0:T(8,128)(2,1)}), bf16[16,6,32,128]{3,2,1,0:T(8,128)(2,1)S(1)}, u32[]{:S(2)}, u32[]{:S(2)}) async-start(bf16[16,6,32,128]{3,2,1,0:T(8,128)(2,1)} %bitcast.57), calls=%async_computation.1 | async-start | bytes 1572864 | tf_op jit(solution)/shard_map/all_to_all | solution.py:95
  134.7 3.9 %copy-start.3 = (s32[128,8]{0,1:T(8,128)S(1)}, s32[128,8]{0,1:T(8,128)}, u32[]{:S(2)}) copy-start(s32[128,8]{0,1:T(8,128)} %param.6) | copy-start | bytes 12292
  134.7 3.9 %copy-start.4 = (f32[128,8]{0,1:T(8,128)S(1)}, f32[128,8]{0,1:T(8,128)}, u32[]{:S(2)}) copy-start(f32[128,8]{0,1:T(8,128)} %param.7) | copy-start | bytes 12292
  134.7 27.6 %all-to-all-start.3 = ((bf16[16,2,6,32,128]{4,3,2,1,0:T(8,128)(2,1)}), bf16[16,2,6,32,128]{4,3,2,1,0:T(8,128)(2,1)S(1)}, u32[]{:S(2)}, u32[]{:S(2)}) async-start(bf16[16,2,6,32,128]{4,3,2,1,0:T(8,128)(2,1)} %pad_maximum_fusion.1), calls=%async_computation.3 | async-start | bytes 3145728 | tf_op jit(solution)/shard_map/all_to_all | solution.py:96
  162.3 1.6 copy-start.1

commit v14 on v8

--- a/solution.py
+++ b/solution.py
@@ -80,14 +80,18 @@
     near = lax.all_to_all(near, "inner", split_axis=0, concat_axis=0, tiled=True)
     far = jnp.stack(far, axis=1)
     far = lax.all_to_all(far, "inner", split_axis=0, concat_axis=0, tiled=True)
-    rows = jnp.concatenate(
-        [near.reshape(-1, width), far.transpose(1, 0, 2, 3, 4).reshape(-1, width)], axis=0
-    )
-    done = whole_expert(rows, w_in[0], w_out[0], w_in_other[0], w_out_other[0])
-    done = done.reshape(STEPS, inner_count, half_cap, lanes_major, 128)
 
-    far_back = [shifted(done[rotation], "blk", rotation) for rotation in range(1, STEPS)]
-    near_back = lax.all_to_all(done[0], "inner", split_axis=0, concat_axis=0, tiled=True)
+    def expert_on(part):
+        finished = whole_expert(
+            part.reshape(-1, width), w_in[0], w_out[0], w_in_other[0], w_out_other[0]
+        )
+        return finished.reshape(inner_count, half_cap, lanes_major, 128)
+
+    near_done = expert_on(near)
+    far_back = [None] * (STEPS - 1)
+    for rotation in reversed(range(1, STEPS)):
+        far_back[rotation - 1] = shifted(expert_on(far[:, rotation - 1]), "blk", rotation)
+    near_back = lax.all_to_all(near_done, "inner", split_axis=0, concat_axis=0, tiled=True)
     far_back = lax.all_to_all(
         jnp.stack(far_back, axis=1), "inner", split_axis=0, concat_axis=0, tiled=True
     )

time: 171 us -> 178 us (1.041)
  matrix products: 21.5 us -> 41.2 us
  waiting for transfers between devices: 89.2 us -> 79.1 us
    dot_general x2 -> x6, matrix products: 9.68 us -> 21.8 us  [one_half(): projected = jnp.dot(rows, w_in_now, preferred_element_type=jnp.float32)]
    ppermute x4, waiting for transfers between devices: 41.5 us -> 34.9 us  [shifted(): return lax.ppermute(value, axis, pairs)]
    dot_general x2 -> x6, matrix products: 4.72 us -> 11.3 us  [one_half(): return jnp.dot(activated, w_out_now, preferred_element_type=jnp.float32)]
    all_to_all x1, waiting for transfers between devices: 22.2 us -> 17.1 us  [on_device(): far = lax.all_to_all(far, 'inner', split_axis=0, concat_axis=0, tiled=True)]
    dot_general x3, matrix products: 2.69 us -> 5.02 us  [on_device(): jnp.einsum('qcht,qchkl->tkl', scale_lo[rotation], back, preferred_element...]
    unnamed x16 -> x18, local copies, waits for them, and re-layouts: 5.62 us -> 3.68 us
    ppermute x4, starting transfers between devices: 22.4 us -> 20.6 us  [shifted(): return lax.ppermute(value, axis, pairs)]
    slice x0 -> x1, local copies, waits for them, and re-layouts: none -> 1.8 us  [on_device(): far[:, rotation - 1]]
  transfers between devices with their start and end apart: 10 -> 10, of which waited for: 7 -> 7; matrix products, arithmetic and copies ran while one was open for 17% -> 22% of each run, Pallas kernels for 0% -> 0%
where the time goes in v14:
time: 178 us
  waiting for transfers between devices  79.1 us (44%)
  matrix products  41.2 us (23%)
  starting transfers between devices  40.3 us (23%)
  local copies, waits for them, and re-layouts  12.7 us (7%)
  other arithmetic  3.93 us (2%)
    ppermute x4, waiting for transfers between devices, shifted(): return lax.ppermute(value, axis, pairs)  34.9 us
    dot_general x6, matrix products, one_half(): projected = jnp.dot(rows, w_in_now, preferred_element_type=jnp.float32)  21.8 us
    all_to_all x1, waiting for transfers between devices, on_device(): lax.all_to_all(jnp.stack(far_back, axis=1), 'inner', split_axis=0, concat...  20.6 us
    ppermute x4, starting transfers between devices, shifted(): return lax.ppermute(value, axis, pairs)  20.6 us
    all_to_all x1, waiting for transfers between devices, on_device(): far = lax.all_to_all(far, 'inner', split_axis=0, concat_axis=0, tiled=True)  17.1 us
    dot_general x6, matrix products, one_half(): return jnp.dot(activated, w_out_now, preferred_element_type=jnp.float32)  11.3 us
    all_to_all x1, starting transfers between devices, on_device(): lax.all_to_all(near, 'inner', split_axis=0, concat_axis=0, tiled=True)  6.48 us
    all_to_all x1, waiting for transfers between devices, on_device(): lax.all_to_all(near, 'inner', split_axis=0, concat_axis=0, tiled=True)  6.45 us
  transfers between devices with their start and end apart: 10, of which 7 were waited for; matrix products, arithmetic and copies ran while one was open for 22% of the time, Pallas kernels for 0%

profile of v14, /device:TPU:2, one launch (start us, length us, event | category | flops | bytes accessed | tf_op | source)
XLA Modules:
  0.0 177.5 jit_solution(3142144174549947232)
XLA Ops:
  1.4 1.5 copy.80
  4.2 2.3 %collective-permute-start.2 = (bf16[16,6,32,128]{3,2,1,0:T(8,128)(2,1)S(1)}, bf16[16,6,32,128]{3,2,1,0:T(8,128)(2,1)S(1)}, u32[]{:S(2)}, u32[]{:S(2)}) collective-permute-start(bf16[16,6,32,128]{3,2,1,0:T(8,128)(2,1)S(1)} %bitcast.187), channel_id=1, source_target_pairs={{0,240},{16,0},{32,16},{48,32},{64,48},{80,64},{96,80},{112,96},{1... | collective-permute-start | bytes 2359304 | tf_op jit(solution)/shard_map/ppermute | solution.py:14
  6.7 4.2 %collective-permute-start.3 = (bf16[16,6,32,128]{3,2,1,0:T(8,128)(2,1)S(1)}, bf16[16,6,32,128]{3,2,1,0:T(8,128)(2,1)S(1)}, u32[]{:S(2)}, u32[]{:S(2)}) collective-permute-start(bf16[16,6,32,128]{3,2,1,0:T(8,128)(2,1)S(1)} %bitcast.188), channel_id=1, source_target_pairs={{0,224},{16,240},{32,0},{48,16},{64,32},{80,48},{96,64},{112,80},{... | collective-permute-start | bytes 2359304 | tf_op jit(solution)/shard_map/ppermute | solution.py:14
  11.9 6.5 %all-to-all-start = ((bf16[16,6,32,128]{3,2,1,0:T(8,128)(2,1)}), bf16[16,6,32,128]{3,2,1,0:T(8,128)(2,1)}, u32[]{:S(2)}, u32[]{:S(2)}) async-start(bf16[16,6,32,128]{3,2,1,0:T(8,128)(2,1)} %bitcast.12), calls=%async_computation | async-start | bytes 1572864 | tf_op jit(solution)/shard_map/all_to_all | solution.py:80
  18.4 7.1 %collective-permute-done.2 = bf16[16,6,32,128]{3,2,1,0:T(8,128)(2,1)S(1)} collective-permute-done((bf16[16,6,32,128]{3,2,1,0:T(8,128)(2,1)S(1)}, bf16[16,6,32,128]{3,2,1,0:T(8,128)(2,1)S(1)}, u32[]{:S(2)}, u32[]{:S(2)}) %collective-permute-start.2) | collective-permute-done | bytes 786464 | tf_op jit(solution)/shard_map/ppermute | solution.py:14
  25.5 2.5 %collective-permute-done.3 = bf16[16,6,32,128]{3,2,1,0:T(8,128)(2,1)S(1)} collective-permute-done((bf16[16,6,32,128]{3,2,1,0:T(8,128)(2,1)S(1)}, bf16[16,6,32,128]{3,2,1,0:T(8,128)(2,1)S(1)}, u32[]{:S(2)}, u32[]{:S(2)}) %collective-permute-start.3) | collective-permute-done | bytes 786464 | tf_op jit(solution)/shard_map/ppermute | solution.py:14
  28.2 1.4 copy.54
  29.6 6.5 %all-to-all-done = bf16[16,6,32,128]{3,2,1,0:T(8,128)(2,1)} async-done(((bf16[16,6,32,128]{3,2,1,0:T(8,128)(2,1)}), bf16[16,6,32,128]{3,2,1,0:T(8,128)(2,1)}, u32[]{:S(2)}, u32[]{:S(2)}) %all-to-all-start) | async-done | bytes 786464 | tf_op jit(solution)/shard_map/all_to_all | solution.py:80
  36.1 4.4 %all-to-all-start.2 = ((bf16[16,2,6,32,128]{4,3,2,1,0:T(8,128)(2,1)}), bf16[16,2,6,32,128]{4,3,2,1,0:T(8,128)(2,1)}, u32[]{:S(2)}, u32[]{:S(2)}) async-start(bf16[16,2,6,32,128]{4,3,2,1,0:T(8,128)(2,1)} %copy.54), calls=%async_computation.2 | async-start | bytes 3145728 | tf_op jit(solution)/shard_map/all_to_all | solution.py:82
  41.0 4.2 %fusion.10 = f32[96,768]{1,0:T(8,128)S(1)} fusion(bf16[1,4096,768]{2,1,0:T(8,128)(2,1)} %param.8, bf16[12,8,32,128]{3,2,1,0:T(8,128)(2,1)} %bitcast.75), kind=kOutput, calls=%fused_computation.10 | convolution fusion | flops 603979776 | bytes 7372800 | tf_op jit(solution)/shard_map/dot_general | solution.py:27
  45.2 1.9 %fusion.22 = f32[96,4096]{1,0:T(8,128)} fusion(bf16[1,384,4096]{2,1,0:T(8,128)(2,1)S(1)} %copy-done, f32[96,768]{1,0:T(8,128)S(1)} %fusion.10), kind=kOutput, calls=%fused_computation.25 | convolution fusion | flops 302211072 | bytes 5013504 | tf_op jit(solution)/shard_map/dot_general | solution.py:31
  47.1 17.1 %all-to-all-done.2 = bf16[16,2,6,32,128]{4,3,2,1,0:T(8,128)(2,1)} async-done(((bf16[16,2,6,32,128]{4,3,2,1,0:T(8,128)(2,1)}), bf16[16,2,6,32,128]{4,3,2,1,0:T(8,128)(2,1)}, u32[]{:S(2)}, u32[]{:S(2)}) %all-to-all-start.2) | async-done | bytes 1572896 | tf_op jit(solution)/shard_map/all_to_all | solution.py:82
  64.3 1.8 %fusion.92 = (bf16[16,1,6,32,128]{4,3,2,1,0:T(8,128)(2,1)S(1)}, bf16[16,1,6,32,128]{4,3,2,1,0:T(8,128)(2,1)S(1)}) fusion(bf16[16,2,6,32,128]{4,3,2,1,0:T(8,128)(2,1)} %all-to-all-done.2), kind=kLoop, calls=%fused_computation.115 | loop fusion | bytes 3145728 | tf_op jit(solution)/shard_map/slice | solution.py:93
  66.1 4.1 %fusion.8 = f32[96,768]{1,0:T(8,128)S(1)} fusion(bf16[1,4096,768]{2,1,0:T(8,128)(2,1)} %param.8, bf16[12,8,32,128]{3,2,1,0:T(8,128)(2,1)S(1)} %bitcast.172), kind=kOutput, calls=%fused_computation.8 | convolution fusion | flops 603979776 | bytes 7372800 | tf_op jit(solution)/shard_map/dot_general | solution.py:27
  73.0 4.0 %fusion = f32[96,768]{1,0:T(8,128)S(1)} fusion(bf16[1,4096,768]{2,1,0:T(8,128)(2,1)} %collective-permute-done, bf16[12,8,32,128]{3,2,1,0:T(8,128)(2,1)S(1)} %bitcast.175), kind=kOutput, calls=%fused_computation | convolution fusion | flops 603979776 | bytes 7372800 | tf_op jit(solution)/shard_map/dot_general | solution.py:27
  77.0 2.6 %fusion.25 = bf16[12,8,32,128]{3,1,2,0:T(8,128)(2,1)S(1)} fusion(f32[96,4096]{1,0:T(8,128)S(1)} %fusion.18, bf16[1,384,4096]{2,1,0:T(8,128)(2,1)} %collective-permute-done.1, f32[96,768]{1,0:T(8,128)S(1)} %fusion), kind=kOutput, calls=%fused_computation.36 | convolution fusion | flops 302997504 | bytes 5799936 | tf_op jit(solution)/shard_map/dot_general | solution.py:31
  79.8 4.0 %fusion.2 = f32[96,768]{1,0:T(8,128)S(1)} fusion(bf16[1,4096,768]{2,1,0:T(8,128)(2,1)} %collective-permute-done, bf16[12,8,32,128]{3,2,1,0:T(8,128)(2,1)S(1)} %bitcast.173), kind=kOutput, calls=%fused_computation.2 | convolution fusion | flops 603979776 | bytes 7372800 | tf_op jit(solution)/shard_map/dot_general | solution.py:27
  83.8 2.6 %fusion.28 = bf16[12,8,32,128]{3,1,2,0:T(8,128)(2,1)S(1)} fusion(f32[96,4096]{1,0:T(8,128)S(1)} %fusion.20, bf16[1,384,4096]{2,1,0:T(8,128)(2,1)} %collective-permute-done.1, f32[96,768]{1,0:T(8,128)S(1)} %fusion.2), kind=kOutput, calls=%fused_computation.37 | convolution fusion | flops 302997504 | bytes 5799936 | tf_op jit(solution)/shard_map/dot_general | solution.py:31
  86.6 12.1 %collective-permute-start.4 = (bf16[16,6,32,128]{3,2,1,0:T(8,128)(2,1)S(1)}, bf16[16,6,32,128]{3,2,1,0:T(8,128)(2,1)S(1)}, u32[]{:S(2)}, u32[]{:S(2)}) collective-permute-start(bf16[16,6,32,128]{3,2,1,0:T(8,128)(2,1)S(1)} %bitcast.186), channel_id=1, source_target_pairs={{0,16},{16,32},{32,48},{48,64},{64,80},{80,96},{96,112},{112,128},... | collective-permute-start | bytes 2359304 | tf_op jit(solution)/shard_map/ppermute | solution.py:14
  98.7 1.9 %collective-permute-start.5 = (bf16[16,6,32,128]{3,2,1,0:T(8,128)(2,1)S(1)}, bf16[16,6,32,128]{3,2,1,0:T(8,128)(2,1)}, u32[]{:S(2)}, u32[]{:S(2)}) collective-permute-start(bf16[16,6,32,128]{3,2,1,0:T(8,128)(2,1)S(1)} %bitcast.185), channel_id=1, source_target_pairs={{0,32},{16,48},{32,64},{48,80},{64,96},{80,112},{96,128},{112,144}... | collective-permute-start | bytes 2359304 | tf_op jit(solution)/shard_map/ppermute | solution.py:14
  100.6 4.2 %fusion.4 = f32[96,768]{1,0:T(8,128)S(1)} fusion(bf16[1,4096,768]{2,1,0:T(8,128)(2,1)} %collective-permute-done, bf16[12,8,32,128]{3,2,1,0:T(8,128)(2,1)} %bitcast.75), kind=kOutput, calls=%fused_computation.4 | convolution fusion | flops 603979776 | bytes 7372800 | tf_op jit(solution)/shard_map/dot_general | solution.py:27
  104.9 2.6 %fusion.31 = bf16[12,8,32,128]{3,1,2,0:T(8,128)(2,1)S(1)} fusion(f32[96,4096]{1,0:T(8,128)S(1)} %copy-done.2, bf16[1,384,4096]{2,1,0:T(8,128)(2,1)} %collective-permute-done.1, f32[96,768]{1,0:T(8,128)S(1)} %fusion.4), kind=kOutput, calls=%fused_computation.38 | convolution fusion | flops 302997504 | bytes 5799936 | tf_op jit(solution)/shard_map/dot_general | solution.py:31
  108.5 3.6 %all-to-all-start.1 = ((bf16[16,6,32,128]{3,2,1,0:T(8,128)(2,1)}), bf16[16,6,32,128]{3,2,1,0:T(8,128)(2,1)S(1)}, u32[]{:S(2)}, u32[]{:S(2)}) async-start(bf16[16,6,32,128]{3,2,1,0:T(8,128)(2,1)} %bitcast.79), calls=%async_computation.1 | async-start | bytes 1572864 | tf_op jit(solution)/shard_map/all_to_all | solution.py:94
  112.2 7.0 %collective-permute-done.4 = bf16[16,6,32,128]{3,2,1,0:T(8,128)(2,1)S(1)} collective-permute-done((bf16[16,6,32,128]{3,2,1,0:T(8,128)(2,1)S(1)}, bf16[16,6,32,128]{3,2,1,0:T(8,128)(2,1)S(1)}, u32[]{:S(2)}, u32[]{:S(2)}) %collective-permute-start.4) | collective-permute-done | bytes 786464 | tf_op jit(solution)/shard_map/ppermute | solution.py:14
  119.1 18.3 %collective-permute-done.5 = bf16[16,6,32,128]{3,2,1,0:T(8,128)(2,1)} collective-permute-done((bf16[16,6,32,128]{3,2,1,0:T(8,128)(2,1)S(1)}, bf16[16,6,32,128]{3,2,1,0:T(8,128)(2,1)}, u32[]{:S(2)}, u32[]{:S(2)}) %collective-permute-start.5) | collective-permute-done | bytes 786464 | tf_op jit(solution)/shard_map/ppermute | solution.py:14
  137.4 2.4 %pad_maximum_fusion.1 = bf16[16,2,6,32,128]{4,3,2,1,0:T(8,128)(2,1)} fusion(bf16[16,1,6,32,128]{4,3,2,1,0:T(8,128)(2,1)} %bitcast.33, bf16[16,1,6,32,128]{4,3,2,1,0:T(8,128)(2,1)S(1)} %bitcast.189), kind=kLoop, calls=%fused_computation.35 | loop fusion | flops 786432 | bytes 3145728 | tf_op jit(solution)/shard_map/stack | solution.py:96
  139.8 4.8 %all-to-all-start.3 = ((bf16[16,2,6,32,128]{4,3,2,1,0:T(8,128)(2,1)}), bf16[16,2,6,32,128]{4,3,2,1,0:T(8,128)(2,1)}, u32[]{:S(2)}, u32[]{:S(2)}) async-start(bf16[16,2,6,32,128]{4,3,2,1,0:T(8,128)(2,1)} %pad_maximum_fusion.1), calls=%async_computation.3 | async-start | bytes 3145728 | tf_op jit(solution)/shard_map/all_to_all | solution.py:95
  145.7 2.1 %fusion.54 = f32[128,32,128,1,1]{0,2,4,1,3:T(8,128)} fusion(bf16[8,2,6,32,128]{4,3,2,1,0:T(8,128)(2,1)S(1)} %bitcast.177, bf16[3,8,2,6,128]{4,1,3,2,0:T(8,128)(2,1)S(1)} %fusion.58), kind=kOutput, calls=%fused_computation.59 | convolution fusion | flops 100663296 | bytes 2908160 | tf_op jit(solution)/shard_map/qcht,qchkl->tkl/dot_general | solution.py:106
  147.8 20.6 %all-to-all-done.3 = bf16[16,2,6,32,128]{4,3,2,1,0:T(8,128)(2,1)} async-done(((bf16[16,2,6,32,128]{4,3,2,1,0:T(8,128)(2,1)}), bf16[16,2,6,32,128]{4,3,2,1,0:T(8,128)(2,1)}, u32[]{:S(2)}, u32[]{:S(2)}) %all-to-all-start.3) | async-done | bytes 1572896 | tf_op jit(solution)/shard_map/all_to_all | solution.py:95
  168.4 1.6 fusion.91
  173.1 2.2 %fusion.24 = bf16[128,32,128]{0,2,1:T(8,128)(2,1)} fusion(f32[128,32,128,1,1]{0,2,4,1,3:T(8,128)S(1)} %fusion.48, f32[128,32,128,1,1]{0,2,4,1,3:T(8,128)S(1)} %fusion.50, f32[128,32,128,1,1]{0,2,4,1,3:T(8,128)S(1)} %fusion.52, f32[128,32,128,1,1]{0,2,4,1,3:T(8,128)S(1)} %copy-done.1, f32[128,32,128,1,1]{0,2,4,1,3:T(8,128)S(1)} %fusion.56, ...), kind=kOutput, calls=%fused_computation.28 | convolution fusion | flops 103809024 | bytes 12345344 | tf_op jit(solution)/shard_map/qcht,qchkl->tkl/dot_general | solution.py:106
  175.3 2.3 %copy.61 = bf16[128,4096]{1,0:T(8,128)(2,1)} copy(bf16[128,4096]{0,1:T(8,128)(2,1)} %bitcast.183) | data formatting | bytes 2097152 | tf_op jit(solution)/shard_map/convert_element_type | solution.py:110
  (50 shorter events, 12.7 us)
Async XLA Ops:
  0.0 73.0 %collective-permute-start = (bf16[1,4096,768]{2,1,0:T(8,128)(2,1)}, bf16[1,4096,768]{2,1,0:T(8,128)(2,1)}, u32[]{:S(2)}, u32[]{:S(2)}) collective-permute-start(bf16[1,4096,768]{2,1,0:T(8,128)(2,1)} %param.8), channel_id=1, source_target_pairs={{0,1},{1,0},{2,3},{3,2},{4,5},{5,4},{6,7},{7,6},{8,9},{9,8},{10,11... | collective-permute-start | bytes 18874376 | tf_op jit(solution)/shard_map/ppermute | solution.py:20
  4.2 21.4 %collective-permute-start.2 = (bf16[16,6,32,128]{3,2,1,0:T(8,128)(2,1)S(1)}, bf16[16,6,32,128]{3,2,1,0:T(8,128)(2,1)S(1)}, u32[]{:S(2)}, u32[]{:S(2)}) collective-permute-start(bf16[16,6,32,128]{3,2,1,0:T(8,128)(2,1)S(1)} %bitcast.187), channel_id=1, source_target_pairs={{0,240},{16,0},{32,16},{48,32},{64,48},{80,64},{96,80},{112,96},{1... | collective-permute-start | bytes 2359304 | tf_op jit(solution)/shard_map/ppermute | solution.py:14
  6.7 21.4 %collective-permute-start.3 = (bf16[16,6,32,128]{3,2,1,0:T(8,128)(2,1)S(1)}, bf16[16,6,32,128]{3,2,1,0:T(8,128)(2,1)S(1)}, u32[]{:S(2)}, u32[]{:S(2)}) collective-permute-start(bf16[16,6,32,128]{3,2,1,0:T(8,128)(2,1)S(1)} %bitcast.188), channel_id=1, source_target_pairs={{0,224},{16,240},{32,0},{48,16},{64,32},{80,48},{96,64},{112,80},{... | collective-permute-start | bytes 2359304 | tf_op jit(solution)/shard_map/ppermute | solution.py:14
  11.9 24.2 %all-to-all-start = ((bf16[16,6,32,128]{3,2,1,0:T(8,128)(2,1)}), bf16[16,6,32,128]{3,2,1,0:T(8,128)(2,1)}, u32[]{:S(2)}, u32[]{:S(2)}) async-start(bf16[16,6,32,128]{3,2,1,0:T(8,128)(2,1)} %bitcast.12), calls=%async_computation | async-start | bytes 1572864 | tf_op jit(solution)/shard_map/all_to_all | solution.py:80
  29.6 10.9 %copy-start = (bf16[1,384,4096]{2,1,0:T(8,128)(2,1)S(1)}, bf16[1,384,4096]{2,1,0:T(8,128)(2,1)}, u32[]{:S(2)}) copy-start(bf16[1,384,4096]{2,1,0:T(8,128)(2,1)} %param.9) | copy-start | bytes 9437188
  36.1 28.2 %all-to-all-start.2 = ((bf16[16,2,6,32,128]{4,3,2,1,0:T(8,128)(2,1)}), bf16[16,2,6,32,128]{4,3,2,1,0:T(8,128)(2,1)}, u32[]{:S(2)}, u32[]{:S(2)}) async-start(bf16[16,2,6,32,128]{4,3,2,1,0:T(8,128)(2,1)} %copy.54), calls=%async_computation.2 | async-start | bytes 3145728 | tf_op jit(solution)/shard_map/all_to_all | solution.py:82
  40.5 36.4 %collective-permute-start.1 = (bf16[1,384,4096]{2,1,0:T(8,128)(2,1)S(1)}, bf16[1,384,4096]{2,1,0:T(8,128)(2,1)}, u32[]{:S(2)}, u32[]{:S(2)}) collective-permute-start(bf16[1,384,4096]{2,1,0:T(8,128)(2,1)S(1)} %copy-done), channel_id=1, source_target_pairs={{0,1},{1,0},{2,3},{3,2},{4,5},{5,4},{6,7},{7,6},{8,9},{9,8},{10,11... | collective-permute-start | bytes 9437192 | tf_op jit(solution)/shard_map/ppermute | solution.py:20
  64.3 6.7 %slice-start = ((s8[6291456]{0:T(1024)(128)(4,1)}), s8[4194304]{0:T(1024)(128)(4,1)S(1)}, s32[]{:S(2)}) async-start(s8[6291456]{0:T(1024)(128)(4,1)} %bitcast.170), calls=%async_computation.4 | async-start | bytes 8388608
  66.1 4.9 %slice-start.1 = ((s8[6291456]{0:T(1024)(128)(4,1)}), s8[2097152]{0:T(1024)(128)(4,1)S(1)}, s32[]{:S(2)}) async-start(s8[6291456]{0:T(1024)(128)(4,1)} %bitcast.170), calls=%async_computation.5 | async-start | bytes 4194304
  86.6 32.6 %collective-permute-start.4 = (bf16[16,6,32,128]{3,2,1,0:T(8,128)(2,1)S(1)}, bf16[16,6,32,128]{3,2,1,0:T(8,128)(2,1)S(1)}, u32[]{:S(2)}, u32[]{:S(2)}) collective-permute-start(bf16[16,6,32,128]{3,2,1,0:T(8,128)(2,1)S(1)} %bitcast.186), channel_id=1, source_target_pairs={{0,16},{16,32},{32,48},{48,64},{64,80},{80,96},{96,112},{112,128},... | collective-permute-start | bytes 2359304 | tf_op jit(solution)/shard_map/ppermute | solution.py:14
  98.7 6.2 %copy-start.2 = (f32[96,4096]{1,0:T(8,128)S(1)}, f32[96,4096]{1,0:T(8,128)}, u32[]{:S(2)}) copy-start(f32[96,4096]{1,0:T(8,128)} %fusion.22) | copy-start | bytes 4718596
  98.7 38.7 %collective-permute-start.5 = (bf16[16,6,32,128]{3,2,1,0:T(8,128)(2,1)S(1)}, bf16[16,6,32,128]{3,2,1,0:T(8,128)(2,1)}, u32[]{:S(2)}, u32[]{:S(2)}) collective-permute-start(bf16[16,6,32,128]{3,2,1,0:T(8,128)(2,1)S(1)} %bitcast.185), channel_id=1, source_target_pairs={{0,32},{16,48},{32,64},{48,80},{64,96},{80,112},{96,128},{112,144}... | collective-permute-start | bytes 2359304 | tf_op jit(solution)/shard_map/ppermute | solution.py:14
  108.5 31.3 %all-to-all-start.1 = ((bf16[16,6,32,128]{3,2,1,0:T(8,128)(2,1)}), bf16[16,6,32,128]{3,2,1,0:T(8,128)(2,1)S(1)}, u32[]{:S(2)}, u32[]{:S(2)}) async-start(bf16[16,6,32,128]{3,2,1,0:T(8,128)(2,1)} %bitcast.79), calls=%async_computation.1 | async-start | bytes 1572864 | tf_op jit(solution)/shard_map/all_to_all | solution.py:94
  139.8 4.8 %copy-start.3 = (s32[128,8]{0,1:T(8,128)S(1)}, s32[128,8]{0,1:T(8,128)}, u32[]{:S(2)}) copy-start(s32[128,8]{0,1:T(8,128)} %param.6) | copy-start | bytes 12292
  139.8 4.8 %copy-start.4 = (f32[128,8]{0,1:T(8,128)S(1)}, f32[128,8]{0,1:T(8,128)}, u32[]{:S(2)}) copy-start(f32[128,8]{0,1:T(8,128)} %param.7) | copy-start | bytes 12292
  139.8 28.5 %all-to-all-start.3 = ((bf16[16,2,6,32,128]{4,3,2,1,0:T(8,128)(2,1)}), bf16[16,2,6,32,128]{4,3,2,1,0:T(8,128)(2,1)}, u32[]{:S(2)}, u32[]{:S(2)}) async-start(bf16[16,2,6,32,128]{4,3,2,1,0:T(8,128)(2,1)} %pad_maximum_fusion.1), calls=%async_computation.3 | async-start | bytes 3145728 | tf_op jit(solution)/shard_map/all_to_all | solution.py:95
  171.5 1.6 copy-start.1

commit v15 on v11

--- a/solution.py
+++ b/solution.py
@@ -93,22 +93,14 @@
     done = jnp.concatenate([near_done, far_done], axis=0)
     done = done.reshape(STEPS, inner_count, half_cap, lanes_major, 128)
 
-    far_back = [shifted(done[rotation], "blk", rotation) for rotation in range(1, STEPS)]
-    near_back = lax.all_to_all(done[0], "inner", split_axis=0, concat_axis=0, tiled=True)
-    far_back = lax.all_to_all(
-        jnp.stack(far_back, axis=1), "inner", split_axis=0, concat_axis=0, tiled=True
+    results = [done[0]] + [shifted(done[r], "blk", r) for r in range(1, STEPS)]
+    returned = lax.all_to_all(
+        jnp.stack(results, axis=1), "inner", split_axis=0, concat_axis=0, tiled=True
     )
-    backs = [near_back] + [far_back[:, rotation - 1] for rotation in range(1, STEPS)]
-
-    combined = jnp.zeros((tok_rows, lanes_major, 128), jnp.float32)
-    for rotation in range(STEPS):
-        back = backs[rotation].reshape(group_count, SPLIT, half_cap, lanes_major, 128)
-        combined = combined + jnp.einsum(
-            "qcht,qchkl->tkl", scale_hi[rotation], back, preferred_element_type=jnp.float32
-        )
-        combined = combined + jnp.einsum(
-            "qcht,qchkl->tkl", scale_lo[rotation], back, preferred_element_type=jnp.float32
-        )
+    returned = returned.reshape(group_count, SPLIT, STEPS, half_cap, lanes_major, 128)
+    combined = jnp.einsum(
+        "rqcht,qcrhkl->tkl", scale_hi, returned, preferred_element_type=jnp.float32
+    ) + jnp.einsum("rqcht,qcrhkl->tkl", scale_lo, returned, preferred_element_type=jnp.float32)
     combined = combined.reshape(tok_rows, width)
     return combined.astype(jnp.bfloat16)
 

time: 168 us -> 179 us (1.065)
  waiting for transfers between devices: 71.5 us -> 92.9 us
  starting transfers between devices: 41.9 us -> 37.1 us
  local copies, waits for them, and re-layouts: 14.5 us -> 11.2 us
    ppermute x4, waiting for transfers between devices: 18.1 us -> 38.8 us  [shifted(): return lax.ppermute(value, axis, pairs)]
    all_to_all x2 -> x1, starting transfers between devices: 8.74 us -> 3.86 us  [on_device(): lax.all_to_all(jnp.stack(results, axis=1), 'inner', split_axis=0, concat_...]
    unnamed x15 -> x13, local copies, waits for them, and re-layouts: 3.78 us -> 2.1 us
    dot_general x6 -> x2, matrix products: 7.29 us -> 5.66 us  [the longest x1 3.38 us: on_device(): jnp.einsum('rqcht,qcrhkl->tkl', scale_lo, returned, preferred_element_typ...]
    all_to_all x2 -> x1, waiting for transfers between devices: 31.5 us -> 32.3 us  [on_device(): lax.all_to_all(jnp.stack(results, axis=1), 'inner', split_axis=0, concat_...]
  transfers between devices with their start and end apart: 10 -> 9, of which waited for: 7 -> 7; matrix products, arithmetic and copies ran while one was open for 25% -> 20% of each run, Pallas kernels for 0% -> 0%
where the time goes in v15:
time: 179 us; the launch traced here: 178 us
  waiting for transfers between devices  92.9 us (52%)
  starting transfers between devices  37.1 us (21%)
  matrix products  32.2 us (18%)
  local copies, waits for them, and re-layouts  11.2 us (6%)
  other arithmetic  4.32 us (2%)
    ppermute x4, waiting for transfers between devices, shifted(): return lax.ppermute(value, axis, pairs)  38.8 us
    all_to_all x1, waiting for transfers between devices, on_device(): lax.all_to_all(jnp.stack(results, axis=1), 'inner', split_axis=0, concat_...  32.3 us
    ppermute x4, starting transfers between devices, shifted(): return lax.ppermute(value, axis, pairs)  21.9 us
    all_to_all x1, waiting for transfers between devices, on_device(): far = lax.all_to_all(far, 'inner', split_axis=0, concat_axis=0, tiled=True)  17.6 us
    dot_general x4, matrix products, one_half(): projected = jnp.dot(rows, w_in_now, preferred_element_type=jnp.float32)  17.2 us
    dot_general x4, matrix products, one_half(): return jnp.dot(activated, w_out_now, preferred_element_type=jnp.float32)  8.52 us
    all_to_all x1, starting transfers between devices, on_device(): lax.all_to_all(near, 'inner', split_axis=0, concat_axis=0, tiled=True)  6.47 us
    all_to_all x1, starting transfers between devices, on_device(): far = lax.all_to_all(far, 'inner', split_axis=0, concat_axis=0, tiled=True)  4.4 us
  transfers between devices with their start and end apart: 9, of which 7 were waited for; matrix products, arithmetic and copies ran while one was open for 20% of the time, Pallas kernels for 0%

profile of v15, /device:TPU:2, one launch (start us, length us, event | category | flops | bytes accessed | tf_op | source)
XLA Modules:
  0.0 178.0 jit_solution(6540166968614590392)
XLA Ops:
  1.4 1.5 copy.79
  4.0 1.1 copy.61
  5.0 2.3 %collective-permute-start.2 = (bf16[16,6,32,128]{3,2,1,0:T(8,128)(2,1)}, bf16[16,6,32,128]{3,2,1,0:T(8,128)(2,1)}, u32[]{:S(2)}, u32[]{:S(2)}) collective-permute-start(bf16[16,6,32,128]{3,2,1,0:T(8,128)(2,1)} %bitcast.16), channel_id=1, source_target_pairs={{0,240},{16,0},{32,16},{48,32},{64,48},{80,64},{96,80},{112,96},{1... | collective-permute-start | bytes 2359304 | tf_op jit(solution)/shard_map/ppermute | solution.py:14
  7.3 1.0 copy.62
  8.3 4.1 %collective-permute-start.3 = (bf16[16,6,32,128]{3,2,1,0:T(8,128)(2,1)}, bf16[16,6,32,128]{3,2,1,0:T(8,128)(2,1)}, u32[]{:S(2)}, u32[]{:S(2)}) collective-permute-start(bf16[16,6,32,128]{3,2,1,0:T(8,128)(2,1)} %bitcast.18), channel_id=1, source_target_pairs={{0,224},{16,240},{32,0},{48,16},{64,32},{80,48},{96,64},{112,80},{... | collective-permute-start | bytes 2359304 | tf_op jit(solution)/shard_map/ppermute | solution.py:14
  12.5 1.1 copy.60
  13.5 6.5 %all-to-all-start = ((bf16[16,6,32,128]{3,2,1,0:T(8,128)(2,1)}), bf16[16,6,32,128]{3,2,1,0:T(8,128)(2,1)}, u32[]{:S(2)}, u32[]{:S(2)}) async-start(bf16[16,6,32,128]{3,2,1,0:T(8,128)(2,1)} %bitcast.103), calls=%async_computation | async-start | bytes 1572864 | tf_op jit(solution)/shard_map/all_to_all | solution.py:80
  20.5 6.2 %collective-permute-done.2 = bf16[16,6,32,128]{3,2,1,0:T(8,128)(2,1)} collective-permute-done((bf16[16,6,32,128]{3,2,1,0:T(8,128)(2,1)}, bf16[16,6,32,128]{3,2,1,0:T(8,128)(2,1)}, u32[]{:S(2)}, u32[]{:S(2)}) %collective-permute-start.2) | collective-permute-done | bytes 786464 | tf_op jit(solution)/shard_map/ppermute | solution.py:14
  26.6 3.4 %collective-permute-done.3 = bf16[16,6,32,128]{3,2,1,0:T(8,128)(2,1)} collective-permute-done((bf16[16,6,32,128]{3,2,1,0:T(8,128)(2,1)}, bf16[16,6,32,128]{3,2,1,0:T(8,128)(2,1)}, u32[]{:S(2)}, u32[]{:S(2)}) %collective-permute-start.3) | collective-permute-done | bytes 786464 | tf_op jit(solution)/shard_map/ppermute | solution.py:14
  30.0 1.5 pad_maximum_fusion.1
  31.5 1.4 copy.63
  32.9 4.2 %all-to-all-done = bf16[16,6,32,128]{3,2,1,0:T(8,128)(2,1)} async-done(((bf16[16,6,32,128]{3,2,1,0:T(8,128)(2,1)}), bf16[16,6,32,128]{3,2,1,0:T(8,128)(2,1)}, u32[]{:S(2)}, u32[]{:S(2)}) %all-to-all-start) | async-done | bytes 786464 | tf_op jit(solution)/shard_map/all_to_all | solution.py:80
  37.1 4.4 %all-to-all-start.1 = ((bf16[16,2,6,32,128]{4,3,2,1,0:T(8,128)(2,1)}), bf16[16,2,6,32,128]{4,3,2,1,0:T(8,128)(2,1)}, u32[]{:S(2)}, u32[]{:S(2)}) async-start(bf16[16,2,6,32,128]{4,3,2,1,0:T(8,128)(2,1)} %copy.63), calls=%async_computation.1 | async-start | bytes 3145728 | tf_op jit(solution)/shard_map/all_to_all | solution.py:82
  41.5 4.2 %fusion.6 = f32[96,768]{1,0:T(8,128)S(1)} fusion(bf16[1,4096,768]{2,1,0:T(8,128)(2,1)} %param.8, bf16[12,8,32,128]{3,2,1,0:T(8,128)(2,1)} %bitcast.39), kind=kOutput, calls=%fused_computation.6 | convolution fusion | flops 603979776 | bytes 7372800 | tf_op jit(solution)/shard_map/dot_general | solution.py:27
  45.7 1.9 %fusion.14 = f32[96,4096]{1,0:T(8,128)} fusion(bf16[1,384,4096]{2,1,0:T(8,128)(2,1)S(1)} %copy-done, f32[96,768]{1,0:T(8,128)S(1)} %fusion.6), kind=kOutput, calls=%fused_computation.16 | convolution fusion | flops 302211072 | bytes 5013504 | tf_op jit(solution)/shard_map/dot_general | solution.py:31
  47.6 17.6 %all-to-all-done.1 = bf16[16,2,6,32,128]{4,3,2,1,0:T(8,128)(2,1)} async-done(((bf16[16,2,6,32,128]{4,3,2,1,0:T(8,128)(2,1)}), bf16[16,2,6,32,128]{4,3,2,1,0:T(8,128)(2,1)}, u32[]{:S(2)}, u32[]{:S(2)}) %all-to-all-start.1) | async-done | bytes 1572896 | tf_op jit(solution)/shard_map/all_to_all | solution.py:82
  65.3 1.7 copy.64
  67.0 4.4 %fusion.4 = f32[192,768]{1,0:T(8,128)S(1)} fusion(bf16[1,4096,768]{2,1,0:T(8,128)(2,1)} %param.8, bf16[24,8,32,128]{3,2,1,0:T(8,128)(2,1)S(1)} %bitcast.104), kind=kOutput, calls=%fused_computation.4 | convolution fusion | flops 1207959552 | bytes 8454144 | tf_op jit(solution)/shard_map/dot_general | solution.py:27
  72.4 4.4 %fusion = f32[192,768]{1,0:T(8,128)S(1)} fusion(bf16[1,4096,768]{2,1,0:T(8,128)(2,1)} %collective-permute-done, bf16[24,8,32,128]{3,2,1,0:T(8,128)(2,1)S(1)} %bitcast.105), kind=kOutput, calls=%fused_computation | convolution fusion | flops 1207959552 | bytes 8454144 | tf_op jit(solution)/shard_map/dot_general | solution.py:27
  76.8 3.0 %fusion.8 = bf16[192,4096]{1,0:T(8,128)(2,1)S(1)} fusion(f32[192,4096]{1,0:T(8,128)S(1)} %fusion.12, bf16[1,384,4096]{2,1,0:T(8,128)(2,1)} %collective-permute-done.1, f32[192,768]{1,0:T(8,128)S(1)} %fusion), kind=kOutput, calls=%fused_computation.9 | convolution fusion | flops 605995008 | bytes 8454144 | tf_op jit(solution)/shard_map/dot_general | solution.py:31
  80.1 13.5 %collective-permute-start.4 = (bf16[16,6,32,128]{3,2,1,0:T(8,128)(2,1)S(1)}, bf16[16,6,32,128]{3,2,1,0:T(8,128)(2,1)S(1)}, u32[]{:S(2)}, u32[]{:S(2)}) collective-permute-start(bf16[16,6,32,128]{3,2,1,0:T(8,128)(2,1)S(1)} %bitcast.109), channel_id=1, source_target_pairs={{0,16},{16,32},{32,48},{48,64},{64,80},{80,96},{96,112},{112,128},... | collective-permute-start | bytes 2359304 | tf_op jit(solution)/shard_map/ppermute | solution.py:14
  93.7 2.0 %collective-permute-start.5 = (bf16[16,6,32,128]{3,2,1,0:T(8,128)(2,1)S(1)}, bf16[16,6,32,128]{3,2,1,0:T(8,128)(2,1)S(1)}, u32[]{:S(2)}, u32[]{:S(2)}) collective-permute-start(bf16[16,6,32,128]{3,2,1,0:T(8,128)(2,1)S(1)} %bitcast.110), channel_id=1, source_target_pairs={{0,32},{16,48},{32,64},{48,80},{64,96},{80,112},{96,128},{112,144}... | collective-permute-start | bytes 2359304 | tf_op jit(solution)/shard_map/ppermute | solution.py:14
  95.7 4.2 %fusion.2 = f32[96,768]{1,0:T(8,128)S(1)} fusion(bf16[1,4096,768]{2,1,0:T(8,128)(2,1)} %collective-permute-done, bf16[12,8,32,128]{3,2,1,0:T(8,128)(2,1)} %bitcast.39), kind=kOutput, calls=%fused_computation.2 | convolution fusion | flops 603979776 | bytes 7372800 | tf_op jit(solution)/shard_map/dot_general | solution.py:27
  100.0 2.7 %fusion.27 = bf16[12,8,32,128]{3,1,2,0:T(8,128)(2,1)S(1)} fusion(f32[96,4096]{1,0:T(8,128)S(1)} %copy-done.1, bf16[1,384,4096]{2,1,0:T(8,128)(2,1)} %collective-permute-done.1, f32[96,768]{1,0:T(8,128)S(1)} %fusion.2), kind=kOutput, calls=%fused_computation.31 | convolution fusion | flops 302997504 | bytes 5799936 | tf_op jit(solution)/shard_map/dot_general | solution.py:31
  102.8 10.1 %collective-permute-done.4 = bf16[16,6,32,128]{3,2,1,0:T(8,128)(2,1)S(1)} collective-permute-done((bf16[16,6,32,128]{3,2,1,0:T(8,128)(2,1)S(1)}, bf16[16,6,32,128]{3,2,1,0:T(8,128)(2,1)S(1)}, u32[]{:S(2)}, u32[]{:S(2)}) %collective-permute-start.4) | collective-permute-done | bytes 786464 | tf_op jit(solution)/shard_map/ppermute | solution.py:14
  112.9 19.2 %collective-permute-done.5 = bf16[16,6,32,128]{3,2,1,0:T(8,128)(2,1)S(1)} collective-permute-done((bf16[16,6,32,128]{3,2,1,0:T(8,128)(2,1)S(1)}, bf16[16,6,32,128]{3,2,1,0:T(8,128)(2,1)S(1)}, u32[]{:S(2)}, u32[]{:S(2)}) %collective-permute-start.5) | collective-permute-done | bytes 786464 | tf_op jit(solution)/shard_map/ppermute | solution.py:14
  132.1 1.7 pad_maximum_fusion
  133.8 3.9 %all-to-all-start.2 = ((bf16[16,3,6,32,128]{4,3,2,1,0:T(8,128)(2,1)}), bf16[16,3,6,32,128]{4,3,2,1,0:T(8,128)(2,1)S(1)}, u32[]{:S(2)}, u32[]{:S(2)}) async-start(bf16[16,3,6,32,128]{4,3,2,1,0:T(8,128)(2,1)} %pad_maximum_fusion), calls=%async_computation.2 | async-start | bytes 4718592 | tf_op jit(solution)/shard_map/all_to_all | solution.py:97
  137.7 32.3 %all-to-all-done.2 = bf16[16,3,6,32,128]{4,3,2,1,0:T(8,128)(2,1)S(1)} async-done(((bf16[16,3,6,32,128]{4,3,2,1,0:T(8,128)(2,1)}), bf16[16,3,6,32,128]{4,3,2,1,0:T(8,128)(2,1)S(1)}, u32[]{:S(2)}, u32[]{:S(2)}) %all-to-all-start.2) | async-done | bytes 2359328 | tf_op jit(solution)/shard_map/all_to_all | solution.py:97
  170.0 2.3 %fusion.19 = f32[128,32,128,1,1,1]{0,2,5,1,4,3:T(8,128)S(1)} fusion(bf16[8,2,3,6,32,128]{5,4,3,2,1,0:T(8,128)(2,1)S(1)} %bitcast.98, f32[3,8,128]{2,1,0:T(8,128)S(1)} %bitcast.114, s32[2,6]{1,0:T(2,128)S(1)} %multiply_add_fusion, s32[3,8,128]{2,1,0:T(8,128)S(1)} %bitcast.112, pred[3,8,128]{2,1,0:T(8,128)(4,1)S(1)} %bitcast.117), kind=kOutput, calls=%fused_computation.23 | convolution fusion | flops 302100480 | bytes 4484144 | tf_op jit(solution)/shard_map/rqcht,qcrhkl->tkl/dot_general | solution.py:101
  172.3 3.4 %fusion.16 = bf16[128,32,128]{0,2,1:T(8,128)(2,1)} fusion(f32[128,32,128,1,1,1]{0,2,5,1,4,3:T(8,128)S(1)} %fusion.19, bf16[8,2,3,6,32,128]{5,4,3,2,1,0:T(8,128)(2,1)S(1)} %bitcast.99, f32[3,8,128]{2,1,0:T(8,128)S(1)} %bitcast.115, s32[2,6]{1,0:T(2,128)S(1)} %multiply_add_fusion, s32[3,8,128]{2,1,0:T(8,128)S(1)} %bitcast.113, ...), kind=kOutput, calls=%fused_computation.20 | convolution fusion | flops 303296512 | bytes 5532720 | tf_op jit(solution)/shard_map/rqcht,qcrhkl->tkl/dot_general | solution.py:103
  175.7 2.3 %copy.68 = bf16[128,4096]{1,0:T(8,128)(2,1)} copy(bf16[128,4096]{0,1:T(8,128)(2,1)} %bitcast.101) | data formatting | bytes 2097152 | tf_op jit(solution)/shard_map/convert_element_type | solution.py:105
  (31 shorter events, 4.6 us)
Async XLA Ops:
  0.0 72.4 %collective-permute-start = (bf16[1,4096,768]{2,1,0:T(8,128)(2,1)}, bf16[1,4096,768]{2,1,0:T(8,128)(2,1)}, u32[]{:S(2)}, u32[]{:S(2)}) collective-permute-start(bf16[1,4096,768]{2,1,0:T(8,128)(2,1)} %param.8), channel_id=1, source_target_pairs={{0,1},{1,0},{2,3},{3,2},{4,5},{5,4},{6,7},{7,6},{8,9},{9,8},{10,11... | collective-permute-start | bytes 18874376 | tf_op jit(solution)/shard_map/ppermute | solution.py:20
  5.0 21.6 %collective-permute-start.2 = (bf16[16,6,32,128]{3,2,1,0:T(8,128)(2,1)}, bf16[16,6,32,128]{3,2,1,0:T(8,128)(2,1)}, u32[]{:S(2)}, u32[]{:S(2)}) collective-permute-start(bf16[16,6,32,128]{3,2,1,0:T(8,128)(2,1)} %bitcast.16), channel_id=1, source_target_pairs={{0,240},{16,0},{32,16},{48,32},{64,48},{80,64},{96,80},{112,96},{1... | collective-permute-start | bytes 2359304 | tf_op jit(solution)/shard_map/ppermute | solution.py:14
  7.3 12.7 %copy-start = (bf16[1,384,4096]{2,1,0:T(8,128)(2,1)S(1)}, bf16[1,384,4096]{2,1,0:T(8,128)(2,1)}, u32[]{:S(2)}) copy-start(bf16[1,384,4096]{2,1,0:T(8,128)(2,1)} %param.9) | copy-start | bytes 9437188
  8.3 21.6 %collective-permute-start.3 = (bf16[16,6,32,128]{3,2,1,0:T(8,128)(2,1)}, bf16[16,6,32,128]{3,2,1,0:T(8,128)(2,1)}, u32[]{:S(2)}, u32[]{:S(2)}) collective-permute-start(bf16[16,6,32,128]{3,2,1,0:T(8,128)(2,1)} %bitcast.18), channel_id=1, source_target_pairs={{0,224},{16,240},{32,0},{48,16},{64,32},{80,48},{96,64},{112,80},{... | collective-permute-start | bytes 2359304 | tf_op jit(solution)/shard_map/ppermute | solution.py:14
  13.5 23.6 %all-to-all-start = ((bf16[16,6,32,128]{3,2,1,0:T(8,128)(2,1)}), bf16[16,6,32,128]{3,2,1,0:T(8,128)(2,1)}, u32[]{:S(2)}, u32[]{:S(2)}) async-start(bf16[16,6,32,128]{3,2,1,0:T(8,128)(2,1)} %bitcast.103), calls=%async_computation | async-start | bytes 1572864 | tf_op jit(solution)/shard_map/all_to_all | solution.py:80
  20.0 56.8 %collective-permute-start.1 = (bf16[1,384,4096]{2,1,0:T(8,128)(2,1)S(1)}, bf16[1,384,4096]{2,1,0:T(8,128)(2,1)}, u32[]{:S(2)}, u32[]{:S(2)}) collective-permute-start(bf16[1,384,4096]{2,1,0:T(8,128)(2,1)S(1)} %copy-done), channel_id=1, source_target_pairs={{0,1},{1,0},{2,3},{3,2},{4,5},{5,4},{6,7},{7,6},{8,9},{9,8},{10,11... | collective-permute-start | bytes 9437192 | tf_op jit(solution)/shard_map/ppermute | solution.py:20
  37.1 28.2 %all-to-all-start.1 = ((bf16[16,2,6,32,128]{4,3,2,1,0:T(8,128)(2,1)}), bf16[16,2,6,32,128]{4,3,2,1,0:T(8,128)(2,1)}, u32[]{:S(2)}, u32[]{:S(2)}) async-start(bf16[16,2,6,32,128]{4,3,2,1,0:T(8,128)(2,1)} %copy.63), calls=%async_computation.1 | async-start | bytes 3145728 | tf_op jit(solution)/shard_map/all_to_all | solution.py:82
  80.1 32.8 %collective-permute-start.4 = (bf16[16,6,32,128]{3,2,1,0:T(8,128)(2,1)S(1)}, bf16[16,6,32,128]{3,2,1,0:T(8,128)(2,1)S(1)}, u32[]{:S(2)}, u32[]{:S(2)}) collective-permute-start(bf16[16,6,32,128]{3,2,1,0:T(8,128)(2,1)S(1)} %bitcast.109), channel_id=1, source_target_pairs={{0,16},{16,32},{32,48},{48,64},{64,80},{80,96},{96,112},{112,128},... | collective-permute-start | bytes 2359304 | tf_op jit(solution)/shard_map/ppermute | solution.py:14
  93.7 6.3 %copy-start.1 = (f32[96,4096]{1,0:T(8,128)S(1)}, f32[96,4096]{1,0:T(8,128)}, u32[]{:S(2)}) copy-start(f32[96,4096]{1,0:T(8,128)} %fusion.14) | copy-start | bytes 4718596
  93.7 38.4 %collective-permute-start.5 = (bf16[16,6,32,128]{3,2,1,0:T(8,128)(2,1)S(1)}, bf16[16,6,32,128]{3,2,1,0:T(8,128)(2,1)S(1)}, u32[]{:S(2)}, u32[]{:S(2)}) collective-permute-start(bf16[16,6,32,128]{3,2,1,0:T(8,128)(2,1)S(1)} %bitcast.110), channel_id=1, source_target_pairs={{0,32},{16,48},{32,64},{48,80},{64,96},{80,112},{96,128},{112,144}... | collective-permute-start | bytes 2359304 | tf_op jit(solution)/shard_map/ppermute | solution.py:14
  133.8 3.9 %copy-start.2 = (s32[128,8]{0,1:T(8,128)S(1)}, s32[128,8]{0,1:T(8,128)}, u32[]{:S(2)}) copy-start(s32[128,8]{0,1:T(8,128)} %param.6) | copy-start | bytes 12292
  133.8 3.9 %copy-start.3 = (f32[128,8]{0,1:T(8,128)S(1)}, f32[128,8]{0,1:T(8,128)}, u32[]{:S(2)}) copy-start(f32[128,8]{0,1:T(8,128)} %param.7) | copy-start | bytes 12292
  133.8 36.3 %all-to-all-start.2 = ((bf16[16,3,6,32,128]{4,3,2,1,0:T(8,128)(2,1)}), bf16[16,3,6,32,128]{4,3,2,1,0:T(8,128)(2,1)S(1)}, u32[]{:S(2)}, u32[]{:S(2)}) async-start(bf16[16,3,6,32,128]{4,3,2,1,0:T(8,128)(2,1)} %pad_maximum_fusion), calls=%async_computation.2 | async-start | bytes 4718592 | tf_op jit(solution)/shard_map/all_to_all | solution.py:97
